TPU v7x, 32 devices: a whole 2x2x4 slice. The times are simulated.
32 devices in a mesh: ctx: 16 (over z, x, core), tp: 2 (over y).
Axes of the slice: x: 2, y: 2, z: 4, core: 2. Of those that a mesh axis runs over, the one named last changes fastest.
Arguments:
- queries: bfloat16 [2048, 4096], P('ctx', 'tp'), may hold values from -100 to 100
- keys: bfloat16 [2048, 1024], P('ctx', 'tp'), may hold values from -4.5 to 4.5
- values: bfloat16 [2048, 1024], P('ctx', 'tp'), may hold values from -6 to 6
- out_weight: bfloat16 [4096, 4096], P('tp'), may hold values from -1.5 to 1.5
- group_widths: int32 [8], replicated, may hold values from 1 to 8, 16 in all
- pad_tokens: int32 [8], replicated, may hold values from 0 to 127
Outputs:
- mixed: bfloat16 [2048, 4096], P('ctx', 'tp')
Inputs may be any that keep to these rules, and one draw needn't show every extreme that they name: `group_widths`: the group widths add up to the number of ctx indices, and the widest is exactly 8.
All inputs are finite; a program needn't handle non-finite values.
Results may differ from a plain program's by a relative error of at most 0.015.
Values may be sent and summed in bfloat16 or wider, within the bound.
No kernel may reach another device: no remote copies, remote signals or barrier semaphores. Data moves between devices by JAX's collectives and lax.ppermute only.
A program may use at most 64 MiB of HBM per device.

v0:
```python
import math

import jax
import jax.numpy as jnp
from jax import lax
from jax.sharding import PartitionSpec as P

HEAD_SIZE = 128


def from_behind(array, axis, by):
    peers = lax.axis_size(axis)
    pairs = [(i, i + by) for i in range(peers) if 0 <= i + by < peers]
    return lax.ppermute(array, axis, pairs)


def rotate(block, positions):
    count = block.shape[0]
    heads = block.shape[1] // HEAD_SIZE
    half = HEAD_SIZE // 2
    pieces = block.astype(jnp.float32).reshape(count, heads, 2, half)
    freqs = 500000.0 ** (-jnp.arange(half, dtype=jnp.float32) / half)
    angles = positions.astype(jnp.float32)[:, None] * freqs[None, :]
    cosine = jnp.cos(angles)[:, None, :]
    sine = jnp.sin(angles)[:, None, :]
    first = pieces[:, :, 0, :]
    second = pieces[:, :, 1, :]
    turned = jnp.stack([first * cosine - second * sine, second * cosine + first * sine], axis=2)
    return turned.reshape(count, heads * HEAD_SIZE).astype(jnp.bfloat16)


def accumulate(carry, query_tile_rows, key_segment, value_segment, query_pos, key_pos, length):
    running, totals, summed = carry
    scores = jnp.einsum(
        "rkgd,nkd->kgrn", query_tile_rows, key_segment, preferred_element_type=jnp.float32
    ) * (1.0 / math.sqrt(HEAD_SIZE))
    allowed = (
        (key_pos[None, :] <= query_pos[:, None])
        & (key_pos[None, :] < length)
        & (key_pos[None, :] >= 0)
    )
    scores = jnp.where(allowed, scores, -1e30)
    highest = jnp.maximum(running, jnp.max(scores, axis=-1))
    weights = jnp.where(allowed, jnp.exp(scores - highest[..., None]), 0.0)
    factor = jnp.exp(running - highest)
    totals = totals * factor + jnp.sum(weights, axis=-1)
    summed = summed * factor[..., None] + jnp.einsum(
        "kgrn,nkd->kgrd",
        weights.astype(jnp.bfloat16),
        value_segment,
        preferred_element_type=jnp.float32,
    )
    return (highest, totals, summed)


def keep(state):
    return state


def on_device(queries, keys, values, out_weight, group_widths, pad_tokens):
    group_index = lax.axis_index("ctx")
    longest = lax.axis_size("ctx") // 2
    rows_here = queries.shape[0]
    prompt_ids = jnp.arange(group_widths.shape[0], dtype=jnp.int32)
    offsets = jnp.cumsum(group_widths) - group_widths
    owner = jnp.sum((offsets <= group_index).astype(jnp.int32)) - 1
    picked = prompt_ids == owner
    start = jnp.sum(jnp.where(picked, offsets, 0))
    width = jnp.sum(jnp.where(picked, group_widths, 0))
    padding = jnp.sum(jnp.where(picked, pad_tokens, 0))
    length = width * rows_here - padding
    local_rows = jnp.arange(rows_here, dtype=jnp.int32)
    local_pos = (group_index - start) * rows_here + local_rows
    heads_kv = keys.shape[1] // HEAD_SIZE
    context_group = queries.shape[1] // keys.shape[1]
    query_tile_rows = rotate(queries, local_pos).reshape(
        rows_here, heads_kv, context_group, HEAD_SIZE
    )
    stacked = jnp.stack([rotate(keys, local_pos), values])
    initial_state = (
        jnp.full((heads_kv, context_group, rows_here), -1e30, jnp.float32),
        jnp.zeros((heads_kv, context_group, rows_here), jnp.float32),
        jnp.zeros((heads_kv, context_group, rows_here, HEAD_SIZE), jnp.float32),
    )
    carry = accumulate(
        initial_state,
        query_tile_rows,
        stacked[0].reshape(rows_here, heads_kv, HEAD_SIZE),
        stacked[1].reshape(rows_here, heads_kv, HEAD_SIZE),
        local_pos,
        local_pos,
        length,
    )

    def visit(step, state):
        current, moving = state
        moving = from_behind(moving, "ctx", 1)
        source = group_index - step

        def take(inner):
            key_pos = (source - start) * rows_here + local_rows
            return accumulate(
                inner,
                query_tile_rows,
                moving[0].reshape(rows_here, heads_kv, HEAD_SIZE),
                moving[1].reshape(rows_here, heads_kv, HEAD_SIZE),
                local_pos,
                key_pos,
                length,
            )

        current = lax.cond(source >= start, take, keep, current)
        return (current, moving)

    carry, _ = lax.fori_loop(1, longest, visit, (carry, stacked))
    running, totals, summed = carry
    attended = (
        (summed / totals[..., None])
        .transpose(2, 0, 1, 3)
        .reshape(rows_here, -1)
        .astype(jnp.bfloat16)
    )
    terms = jnp.dot(attended, out_weight, preferred_element_type=jnp.float32)
    terms = terms.astype(jnp.bfloat16).astype(jnp.float32)
    return lax.psum_scatter(terms.astype(jnp.bfloat16), "tp", scatter_dimension=1, tiled=True)


def solution(mesh):
    return jax.shard_map(
        on_device,
        mesh=mesh,
        in_specs=(P("ctx", "tp"), P("ctx", "tp"), P("ctx", "tp"), P("tp", None), P(), P()),
        out_specs=P("ctx", "tp"),
        check_vma=False,
    )
```

profile of v0, /device:TPU:24, one launch (start us, length us, event | category | flops | bytes accessed | tf_op | source)
XLA Modules:
  0.0 128.9 jit_solution(16243669994780618376)
XLA Ops:
  9.2 1.4 %select_reduce_fusion.1 = (s32[]{:T(128)}, s32[]{:T(128)}, s32[]{:T(128)}) fusion(s32[8]{0:T(128)} %param.14, s32[]{:T(128)S(6)} %sub.57, s32[8,1]{0,1:T(1,128)S(1)} %reduce-window.9, s32[8]{0:T(128)} %param.15), kind=kLoop, calls=%fused_computation.50 | loop fusion | flops 61 | bytes 112 | tf_op jit(solution)/shard_map/reduce_sum | solution.py:69
  19.0 72.8 %while.20 = (s32[]{:T(128)}, f32[4,4,128]{2,1,0:T(4,128)S(1)}, f32[4,4,128]{2,1,0:T(4,128)S(1)}, f32[4,4,128,128]{3,2,1,0:T(8,128)S(1)}, bf16[2,128,512]{1,2,0:T...) while((s32[]{:T(128)}, f32[4,4,128]{2,1,0:T(4,128)S(1)}, ...), condition=%wide.region_12.13_spmd.clone, body=%wide.region_7.12_spmd.clone.sunk | while | flops 137155072 | bytes 8328035 | solution.py:115
  19.1 1.9 %collective-permute-start = (bf16[2,128,512]{1,2,0:T(8,128)(2,1)S(1)}, bf16[2,128,512]{1,2,0:T(8,128)(2,1)S(1)}, u32[]{:S(2)}, u32[]{:S(2)}) collective-permute-start(bf16[2,128,512]{1,2,0:T(8,128)(2,1)S(1)} %get-tuple-element.408), channel_id=1, source_target_pairs={{0,2},{2,4},{4,6},{6,8},{8,10},{10,12},{12,14},{14,16},{16,18},{18... | collective-permute-start | bytes 786440 | tf_op jit(solution)/shard_map/while/body/eval_jaxpr/ppermute | solution.py:14
  21.6 6.1 %collective-permute-done = bf16[2,128,512]{1,2,0:T(8,128)(2,1)S(1)} collective-permute-done((bf16[2,128,512]{1,2,0:T(8,128)(2,1)S(1)}, bf16[2,128,512]{1,2,0:T(8,128)(2,1)S(1)}, u32[]{:S(2)}, u32[]{:S(2)}) %collective-permute-start) | collective-permute-done | bytes 262176 | tf_op jit(solution)/shard_map/while/body/eval_jaxpr/ppermute | solution.py:14
  27.6 2.1 %conditional.3 = ((f32[4,4,128]{2,1,0:T(4,128)S(1)}, f32[4,4,128]{2,1,0:T(4,128)S(1)}, f32[4,4,128,128]{3,2,1,0:T(8,128)S(1)})) conditional(s32[]{:T(128)} %convert_element_type.86, (f32[4,4,128]{2,1,0:T(4,128)S(1)}, f32[4,4,128]{2,1,0:T(4,128)S(1)}, f32[4,4,128,128]{3,2,1,0:T(8,128)S(1)}) %tuple.55, (s32[]{:T(128)}, s32[]{:T(128)}, ...), branch_computations={%region_8.8_spmd, %region_9.11_spmd} | conditional | flops 137155072 | bytes 6754372 | solution.py:112
  29.8 1.9 %collective-permute-start = (bf16[2,128,512]{1,2,0:T(8,128)(2,1)S(1)}, bf16[2,128,512]{1,2,0:T(8,128)(2,1)S(1)}, u32[]{:S(2)}, u32[]{:S(2)}) collective-permute-start(bf16[2,128,512]{1,2,0:T(8,128)(2,1)S(1)} %get-tuple-element.408), channel_id=1, source_target_pairs={{0,2},{2,4},{4,6},{6,8},{8,10},{10,12},{12,14},{14,16},{16,18},{18... | collective-permute-start | bytes 786440 | tf_op jit(solution)/shard_map/while/body/eval_jaxpr/ppermute | solution.py:14
  32.2 6.1 %collective-permute-done = bf16[2,128,512]{1,2,0:T(8,128)(2,1)S(1)} collective-permute-done((bf16[2,128,512]{1,2,0:T(8,128)(2,1)S(1)}, bf16[2,128,512]{1,2,0:T(8,128)(2,1)S(1)}, u32[]{:S(2)}, u32[]{:S(2)}) %collective-permute-start) | collective-permute-done | bytes 262176 | tf_op jit(solution)/shard_map/while/body/eval_jaxpr/ppermute | solution.py:14
  38.3 2.0 %conditional.3 = ((f32[4,4,128]{2,1,0:T(4,128)S(1)}, f32[4,4,128]{2,1,0:T(4,128)S(1)}, f32[4,4,128,128]{3,2,1,0:T(8,128)S(1)})) conditional(s32[]{:T(128)} %convert_element_type.86, (f32[4,4,128]{2,1,0:T(4,128)S(1)}, f32[4,4,128]{2,1,0:T(4,128)S(1)}, f32[4,4,128,128]{3,2,1,0:T(8,128)S(1)}) %tuple.55, (s32[]{:T(128)}, s32[]{:T(128)}, ...), branch_computations={%region_8.8_spmd, %region_9.11_spmd} | conditional | flops 137155072 | bytes 6754372 | solution.py:112
  40.4 1.9 %collective-permute-start = (bf16[2,128,512]{1,2,0:T(8,128)(2,1)S(1)}, bf16[2,128,512]{1,2,0:T(8,128)(2,1)S(1)}, u32[]{:S(2)}, u32[]{:S(2)}) collective-permute-start(bf16[2,128,512]{1,2,0:T(8,128)(2,1)S(1)} %get-tuple-element.408), channel_id=1, source_target_pairs={{0,2},{2,4},{4,6},{6,8},{8,10},{10,12},{12,14},{14,16},{16,18},{18... | collective-permute-start | bytes 786440 | tf_op jit(solution)/shard_map/while/body/eval_jaxpr/ppermute | solution.py:14
  42.9 6.1 %collective-permute-done = bf16[2,128,512]{1,2,0:T(8,128)(2,1)S(1)} collective-permute-done((bf16[2,128,512]{1,2,0:T(8,128)(2,1)S(1)}, bf16[2,128,512]{1,2,0:T(8,128)(2,1)S(1)}, u32[]{:S(2)}, u32[]{:S(2)}) %collective-permute-start) | collective-permute-done | bytes 262176 | tf_op jit(solution)/shard_map/while/body/eval_jaxpr/ppermute | solution.py:14
  49.0 2.0 %conditional.3 = ((f32[4,4,128]{2,1,0:T(4,128)S(1)}, f32[4,4,128]{2,1,0:T(4,128)S(1)}, f32[4,4,128,128]{3,2,1,0:T(8,128)S(1)})) conditional(s32[]{:T(128)} %convert_element_type.86, (f32[4,4,128]{2,1,0:T(4,128)S(1)}, f32[4,4,128]{2,1,0:T(4,128)S(1)}, f32[4,4,128,128]{3,2,1,0:T(8,128)S(1)}) %tuple.55, (s32[]{:T(128)}, s32[]{:T(128)}, ...), branch_computations={%region_8.8_spmd, %region_9.11_spmd} | conditional | flops 137155072 | bytes 6754372 | solution.py:112
  51.1 1.9 %collective-permute-start = (bf16[2,128,512]{1,2,0:T(8,128)(2,1)S(1)}, bf16[2,128,512]{1,2,0:T(8,128)(2,1)S(1)}, u32[]{:S(2)}, u32[]{:S(2)}) collective-permute-start(bf16[2,128,512]{1,2,0:T(8,128)(2,1)S(1)} %get-tuple-element.408), channel_id=1, source_target_pairs={{0,2},{2,4},{4,6},{6,8},{8,10},{10,12},{12,14},{14,16},{16,18},{18... | collective-permute-start | bytes 786440 | tf_op jit(solution)/shard_map/while/body/eval_jaxpr/ppermute | solution.py:14
  53.6 6.1 %collective-permute-done = bf16[2,128,512]{1,2,0:T(8,128)(2,1)S(1)} collective-permute-done((bf16[2,128,512]{1,2,0:T(8,128)(2,1)S(1)}, bf16[2,128,512]{1,2,0:T(8,128)(2,1)S(1)}, u32[]{:S(2)}, u32[]{:S(2)}) %collective-permute-start) | collective-permute-done | bytes 262176 | tf_op jit(solution)/shard_map/while/body/eval_jaxpr/ppermute | solution.py:14
  59.7 2.1 %conditional.3 = ((f32[4,4,128]{2,1,0:T(4,128)S(1)}, f32[4,4,128]{2,1,0:T(4,128)S(1)}, f32[4,4,128,128]{3,2,1,0:T(8,128)S(1)})) conditional(s32[]{:T(128)} %convert_element_type.86, (f32[4,4,128]{2,1,0:T(4,128)S(1)}, f32[4,4,128]{2,1,0:T(4,128)S(1)}, f32[4,4,128,128]{3,2,1,0:T(8,128)S(1)}) %tuple.55, (s32[]{:T(128)}, s32[]{:T(128)}, ...), branch_computations={%region_8.8_spmd, %region_9.11_spmd} | conditional | flops 137155072 | bytes 6754372 | solution.py:112
  61.8 1.9 %collective-permute-start = (bf16[2,128,512]{1,2,0:T(8,128)(2,1)S(1)}, bf16[2,128,512]{1,2,0:T(8,128)(2,1)S(1)}, u32[]{:S(2)}, u32[]{:S(2)}) collective-permute-start(bf16[2,128,512]{1,2,0:T(8,128)(2,1)S(1)} %get-tuple-element.408), channel_id=1, source_target_pairs={{0,2},{2,4},{4,6},{6,8},{8,10},{10,12},{12,14},{14,16},{16,18},{18... | collective-permute-start | bytes 786440 | tf_op jit(solution)/shard_map/while/body/eval_jaxpr/ppermute | solution.py:14
  64.3 6.1 %collective-permute-done = bf16[2,128,512]{1,2,0:T(8,128)(2,1)S(1)} collective-permute-done((bf16[2,128,512]{1,2,0:T(8,128)(2,1)S(1)}, bf16[2,128,512]{1,2,0:T(8,128)(2,1)S(1)}, u32[]{:S(2)}, u32[]{:S(2)}) %collective-permute-start) | collective-permute-done | bytes 262176 | tf_op jit(solution)/shard_map/while/body/eval_jaxpr/ppermute | solution.py:14
  70.4 2.1 %conditional.3 = ((f32[4,4,128]{2,1,0:T(4,128)S(1)}, f32[4,4,128]{2,1,0:T(4,128)S(1)}, f32[4,4,128,128]{3,2,1,0:T(8,128)S(1)})) conditional(s32[]{:T(128)} %convert_element_type.86, (f32[4,4,128]{2,1,0:T(4,128)S(1)}, f32[4,4,128]{2,1,0:T(4,128)S(1)}, f32[4,4,128,128]{3,2,1,0:T(8,128)S(1)}) %tuple.55, (s32[]{:T(128)}, s32[]{:T(128)}, ...), branch_computations={%region_8.8_spmd, %region_9.11_spmd} | conditional | flops 137155072 | bytes 6754372 | solution.py:112
  72.5 1.9 %collective-permute-start = (bf16[2,128,512]{1,2,0:T(8,128)(2,1)S(1)}, bf16[2,128,512]{1,2,0:T(8,128)(2,1)S(1)}, u32[]{:S(2)}, u32[]{:S(2)}) collective-permute-start(bf16[2,128,512]{1,2,0:T(8,128)(2,1)S(1)} %get-tuple-element.408), channel_id=1, source_target_pairs={{0,2},{2,4},{4,6},{6,8},{8,10},{10,12},{12,14},{14,16},{16,18},{18... | collective-permute-start | bytes 786440 | tf_op jit(solution)/shard_map/while/body/eval_jaxpr/ppermute | solution.py:14
  75.0 6.1 %collective-permute-done = bf16[2,128,512]{1,2,0:T(8,128)(2,1)S(1)} collective-permute-done((bf16[2,128,512]{1,2,0:T(8,128)(2,1)S(1)}, bf16[2,128,512]{1,2,0:T(8,128)(2,1)S(1)}, u32[]{:S(2)}, u32[]{:S(2)}) %collective-permute-start) | collective-permute-done | bytes 262176 | tf_op jit(solution)/shard_map/while/body/eval_jaxpr/ppermute | solution.py:14
  81.1 2.1 %conditional.3 = ((f32[4,4,128]{2,1,0:T(4,128)S(1)}, f32[4,4,128]{2,1,0:T(4,128)S(1)}, f32[4,4,128,128]{3,2,1,0:T(8,128)S(1)})) conditional(s32[]{:T(128)} %convert_element_type.86, (f32[4,4,128]{2,1,0:T(4,128)S(1)}, f32[4,4,128]{2,1,0:T(4,128)S(1)}, f32[4,4,128,128]{3,2,1,0:T(8,128)S(1)}) %tuple.55, (s32[]{:T(128)}, s32[]{:T(128)}, ...), branch_computations={%region_8.8_spmd, %region_9.11_spmd} | conditional | flops 137155072 | bytes 6754372 | solution.py:112
  83.2 1.9 %collective-permute-start = (bf16[2,128,512]{1,2,0:T(8,128)(2,1)S(1)}, bf16[2,128,512]{1,2,0:T(8,128)(2,1)S(1)}, u32[]{:S(2)}, u32[]{:S(2)}) collective-permute-start(bf16[2,128,512]{1,2,0:T(8,128)(2,1)S(1)} %get-tuple-element.408), channel_id=1, source_target_pairs={{0,2},{2,4},{4,6},{6,8},{8,10},{10,12},{12,14},{14,16},{16,18},{18... | collective-permute-start | bytes 786440 | tf_op jit(solution)/shard_map/while/body/eval_jaxpr/ppermute | solution.py:14
  85.7 6.1 %collective-permute-done = bf16[2,128,512]{1,2,0:T(8,128)(2,1)S(1)} collective-permute-done((bf16[2,128,512]{1,2,0:T(8,128)(2,1)S(1)}, bf16[2,128,512]{1,2,0:T(8,128)(2,1)S(1)}, u32[]{:S(2)}, u32[]{:S(2)}) %collective-permute-start) | collective-permute-done | bytes 262176 | tf_op jit(solution)/shard_map/while/body/eval_jaxpr/ppermute | solution.py:14
  92.3 9.2 %convolution_convert_fusion = bf16[128,4096]{1,0:T(8,128)(2,1)} fusion(bf16[128,2048]{0,1:T(8,128)(2,1)S(1)} %bitcast.59, bf16[2048,4096]{1,0:T(8,128)(2,1)} %param.13), kind=kOutput, calls=%fused_computation.20 | convolution fusion | flops 2148007936 | bytes 18350080 | tf_op jit(solution)/shard_map/dot_general | solution.py:123
  101.5 20.5 %reduce-scatter.2.cloned.1.call-done = bf16[128,2048]{1,0:T(8,128)(2,1)} async-done(((bf16[128,4096]{1,0:T(8,128)(2,1)}), bf16[128,2048]{1,0:T(8,128)(2,1)}) %reduce-scatter.2.cloned.1.call-update) | async-done | bytes 524304 | tf_op jit(solution)/shard_map/reduce_scatter | solution.py:125
  (111 shorter events, 17.8 us)
Async XLA Ops:
  6.5 115.5 %reduce-scatter.2.cloned.1.call-start = ((), (), s32[]{:S(2)}) async-start(), calls=%async_computation.1 | async-start | bytes 1572864 | tf_op jit(solution)/shard_map/reduce_scatter | solution.py:125
  19.1 8.6 %collective-permute-start = (bf16[2,128,512]{1,2,0:T(8,128)(2,1)S(1)}, bf16[2,128,512]{1,2,0:T(8,128)(2,1)S(1)}, u32[]{:S(2)}, u32[]{:S(2)}) collective-permute-start(bf16[2,128,512]{1,2,0:T(8,128)(2,1)S(1)} %get-tuple-element.408), channel_id=1, source_target_pairs={{0,2},{2,4},{4,6},{6,8},{8,10},{10,12},{12,14},{14,16},{16,18},{18... | collective-permute-start | bytes 786440 | tf_op jit(solution)/shard_map/while/body/eval_jaxpr/ppermute | solution.py:14
  29.8 8.6 %collective-permute-start = (bf16[2,128,512]{1,2,0:T(8,128)(2,1)S(1)}, bf16[2,128,512]{1,2,0:T(8,128)(2,1)S(1)}, u32[]{:S(2)}, u32[]{:S(2)}) collective-permute-start(bf16[2,128,512]{1,2,0:T(8,128)(2,1)S(1)} %get-tuple-element.408), channel_id=1, source_target_pairs={{0,2},{2,4},{4,6},{6,8},{8,10},{10,12},{12,14},{14,16},{16,18},{18... | collective-permute-start | bytes 786440 | tf_op jit(solution)/shard_map/while/body/eval_jaxpr/ppermute | solution.py:14
  40.4 8.6 %collective-permute-start = (bf16[2,128,512]{1,2,0:T(8,128)(2,1)S(1)}, bf16[2,128,512]{1,2,0:T(8,128)(2,1)S(1)}, u32[]{:S(2)}, u32[]{:S(2)}) collective-permute-start(bf16[2,128,512]{1,2,0:T(8,128)(2,1)S(1)} %get-tuple-element.408), channel_id=1, source_target_pairs={{0,2},{2,4},{4,6},{6,8},{8,10},{10,12},{12,14},{14,16},{16,18},{18... | collective-permute-start | bytes 786440 | tf_op jit(solution)/shard_map/while/body/eval_jaxpr/ppermute | solution.py:14
  51.1 8.6 %collective-permute-start = (bf16[2,128,512]{1,2,0:T(8,128)(2,1)S(1)}, bf16[2,128,512]{1,2,0:T(8,128)(2,1)S(1)}, u32[]{:S(2)}, u32[]{:S(2)}) collective-permute-start(bf16[2,128,512]{1,2,0:T(8,128)(2,1)S(1)} %get-tuple-element.408), channel_id=1, source_target_pairs={{0,2},{2,4},{4,6},{6,8},{8,10},{10,12},{12,14},{14,16},{16,18},{18... | collective-permute-start | bytes 786440 | tf_op jit(solution)/shard_map/while/body/eval_jaxpr/ppermute | solution.py:14
  61.8 8.6 %collective-permute-start = (bf16[2,128,512]{1,2,0:T(8,128)(2,1)S(1)}, bf16[2,128,512]{1,2,0:T(8,128)(2,1)S(1)}, u32[]{:S(2)}, u32[]{:S(2)}) collective-permute-start(bf16[2,128,512]{1,2,0:T(8,128)(2,1)S(1)} %get-tuple-element.408), channel_id=1, source_target_pairs={{0,2},{2,4},{4,6},{6,8},{8,10},{10,12},{12,14},{14,16},{16,18},{18... | collective-permute-start | bytes 786440 | tf_op jit(solution)/shard_map/while/body/eval_jaxpr/ppermute | solution.py:14
  72.5 8.6 %collective-permute-start = (bf16[2,128,512]{1,2,0:T(8,128)(2,1)S(1)}, bf16[2,128,512]{1,2,0:T(8,128)(2,1)S(1)}, u32[]{:S(2)}, u32[]{:S(2)}) collective-permute-start(bf16[2,128,512]{1,2,0:T(8,128)(2,1)S(1)} %get-tuple-element.408), channel_id=1, source_target_pairs={{0,2},{2,4},{4,6},{6,8},{8,10},{10,12},{12,14},{14,16},{16,18},{18... | collective-permute-start | bytes 786440 | tf_op jit(solution)/shard_map/while/body/eval_jaxpr/ppermute | solution.py:14
  83.2 8.6 %collective-permute-start = (bf16[2,128,512]{1,2,0:T(8,128)(2,1)S(1)}, bf16[2,128,512]{1,2,0:T(8,128)(2,1)S(1)}, u32[]{:S(2)}, u32[]{:S(2)}) collective-permute-start(bf16[2,128,512]{1,2,0:T(8,128)(2,1)S(1)} %get-tuple-element.408), channel_id=1, source_target_pairs={{0,2},{2,4},{4,6},{6,8},{8,10},{10,12},{12,14},{14,16},{16,18},{18... | collective-permute-start | bytes 786440 | tf_op jit(solution)/shard_map/while/body/eval_jaxpr/ppermute | solution.py:14
Sparse Core Ops, SparseCore 0:
  101.6 20.3 reduce-scatter.1
where the time goes:
time: 131 us; the launch traced here: 129 us
  waiting for transfers between devices  63.2 us (48%)
  matrix products  16.4 us (13%)
  between operations  15.9 us (12%)
  starting transfers between devices  13.4 us (10%)
  loops' own time  7.96 us (6%)
  other arithmetic  6.74 us (5%)
  local copies, waits for them, and re-layouts  5.18 us (4%)
    ppermute x7, waiting for transfers between devices, from_behind(): return lax.ppermute(array, axis, pairs)  42.7 us
    reduce_scatter x1, waiting for transfers between devices, on_device(): lax.psum_scatter(terms.astype(jnp.bfloat16), 'tp', scatter_dimension=1, t...  20.5 us
    ppermute x7, starting transfers between devices, from_behind(): return lax.ppermute(array, axis, pairs)  13.4 us
    dot_general x1, matrix products, on_device(): terms = jnp.dot(attended, out_weight, preferred_element_type=jnp.float32)  9.15 us
    dot_general x7, matrix products, accumulate(): jnp.einsum('kgrn,nkd->kgrd', weights.astype(jnp.bfloat16), value_segment,...  4.59 us
    another operation x1, loops' own time, on_device(): carry, _ = lax.fori_loop(1, longest, visit, (carry, stacked))  4.23 us
    another operation x7, loops' own time, visit(): current = lax.cond(source >= start, take, keep, current)  3.73 us
    unnamed x4, local copies, waits for them, and re-layouts  3.64 us
  transfers between devices with their start and end apart: 8, of which 8 were waited for; matrix products, arithmetic and copies ran while one was open for 0% of the time, Pallas kernels for 0%

commit v1 on v0

v1 whole, which is shorter than its diff:
```python
import math

import jax
import jax.numpy as jnp
from jax import lax
from jax.sharding import PartitionSpec as P

HEAD_SIZE = 128
FAR = 1 << 20


def rotate(block, positions):
    count = block.shape[0]
    heads = block.shape[1] // HEAD_SIZE
    half = HEAD_SIZE // 2
    pieces = block.astype(jnp.float32).reshape(count, heads, 2, half)
    freqs = 500000.0 ** (-jnp.arange(half, dtype=jnp.float32) / half)
    angles = positions.astype(jnp.float32)[:, None] * freqs[None, :]
    cosine = jnp.cos(angles)[:, None, :]
    sine = jnp.sin(angles)[:, None, :]
    first = pieces[:, :, 0, :]
    second = pieces[:, :, 1, :]
    turned = jnp.stack([first * cosine - second * sine, second * cosine + first * sine], axis=2)
    return turned.reshape(count, heads * HEAD_SIZE).astype(jnp.bfloat16)


def gather_window(kv, n, window):
    received = []
    for s in range(1, window, 2):
        if s == 1:
            pairs = [(j, j + 1) for j in range(1, n - 1, 2)]
        else:
            pairs = [(j, j + s) for j in range(n - s)]
        received.append(lax.ppermute(kv, "ctx", pairs))
    core = lax.axis_index("ctx") % 2
    to_odd = jnp.stack([kv] + received[:-1])
    to_even = jnp.stack(received[1:] + [kv])
    outgoing = jnp.where(core == 0, to_odd, to_even)
    incoming = lax.ppermute(outgoing, "ctx", [(j, j ^ 1) for j in range(n)])
    slots = jnp.concatenate([kv[None], jnp.stack(received), incoming], axis=0)
    half = window // 2
    even_shift = [0] + [2 * m + 1 for m in range(half)] + [2 * m + 2 for m in range(half - 1)] + [FAR]
    odd_shift = [0, FAR] + [2 * m + 1 for m in range(1, half)] + [1] + [2 * m for m in range(1, half)]
    shift = jnp.where(core == 0, jnp.array(even_shift, jnp.int32), jnp.array(odd_shift, jnp.int32))
    return slots, shift


def on_device(queries, keys, values, out_weight, group_widths, pad_tokens):
    n = lax.axis_size("ctx")
    window = n // 2
    group_index = lax.axis_index("ctx")
    rows_here = queries.shape[0]
    heads_kv = keys.shape[1] // HEAD_SIZE
    context_group = queries.shape[1] // keys.shape[1]

    slots, shift = gather_window(jnp.stack([keys, values]), n, window)

    prompt_ids = jnp.arange(group_widths.shape[0], dtype=jnp.int32)
    offsets = jnp.sum(
        jnp.where(prompt_ids[None, :] < prompt_ids[:, None], group_widths[None, :], 0), axis=1
    )
    owner = jnp.sum((offsets <= group_index).astype(jnp.int32)) - 1
    picked = prompt_ids == owner
    start = jnp.sum(jnp.where(picked, offsets, 0))
    width = jnp.sum(jnp.where(picked, group_widths, 0))
    padding = jnp.sum(jnp.where(picked, pad_tokens, 0))
    length = width * rows_here - padding
    local_rows = jnp.arange(rows_here, dtype=jnp.int32)
    query_pos = (group_index - start) * rows_here + local_rows
    key_pos = ((group_index - shift - start) * rows_here)[:, None] + local_rows[None, :]
    key_pos = key_pos.reshape(-1)

    count = slots.shape[0] * rows_here
    query_rows = rotate(queries, query_pos).reshape(rows_here, heads_kv, context_group, HEAD_SIZE)
    key_rows = rotate(slots[:, 0].reshape(count, -1), key_pos).reshape(count, heads_kv, HEAD_SIZE)
    value_rows = slots[:, 1].reshape(count, heads_kv, HEAD_SIZE)

    scores = jnp.einsum(
        "rkgd,nkd->kgrn", query_rows, key_rows, preferred_element_type=jnp.float32
    ) * (1.0 / math.sqrt(HEAD_SIZE))
    allowed = (
        (key_pos[None, :] <= query_pos[:, None])
        & (key_pos[None, :] < length)
        & (key_pos[None, :] >= 0)
    )
    scores = jnp.where(allowed, scores, -1e30)
    highest = jnp.max(scores, axis=-1)
    weights = jnp.where(allowed, jnp.exp(scores - highest[..., None]), 0.0)
    totals = jnp.sum(weights, axis=-1)
    summed = jnp.einsum(
        "kgrn,nkd->kgrd", weights.astype(jnp.bfloat16), value_rows, preferred_element_type=jnp.float32
    )
    attended = (
        (summed / totals[..., None]).transpose(2, 0, 1, 3).reshape(rows_here, -1).astype(jnp.bfloat16)
    )

    n_tp = lax.axis_size("tp")
    if n_tp == 2:
        me = lax.axis_index("tp")
        part = out_weight.shape[1] // 2
        peer_weight = lax.dynamic_slice_in_dim(out_weight, (1 - me) * part, part, 1)
        peer_terms = jnp.dot(attended, peer_weight, preferred_element_type=jnp.float32)
        got = lax.ppermute(peer_terms.astype(jnp.bfloat16), "tp", [(0, 1), (1, 0)])
        own_weight = lax.dynamic_slice_in_dim(out_weight, me * part, part, 1)
        own_terms = jnp.dot(attended, own_weight, preferred_element_type=jnp.float32)
        own_terms = own_terms.astype(jnp.bfloat16).astype(jnp.float32)
        return (own_terms + got.astype(jnp.float32)).astype(jnp.bfloat16)
    terms = jnp.dot(attended, out_weight, preferred_element_type=jnp.float32)
    return lax.psum_scatter(terms.astype(jnp.bfloat16), "tp", scatter_dimension=1, tiled=True)


def solution(mesh):
    return jax.shard_map(
        on_device,
        mesh=mesh,
        in_specs=(P("ctx", "tp"), P("ctx", "tp"), P("ctx", "tp"), P("tp", None), P(), P()),
        out_specs=P("ctx", "tp"),
        check_vma=False,
    )
```

time: 131 us -> 101 us (0.77); the launches traced: 129 us -> 100 us
  waiting for transfers between devices: 63.2 us -> 22 us
  local copies, waits for them, and re-layouts: 5.18 us -> 28.7 us
  between operations: 15.9 us -> 2.73 us
  loops' own time: 7.96 us -> 0 us
  other arithmetic: 6.74 us -> 13.1 us
  matrix products: 16.4 us -> 19.8 us
    ppermute x7 -> x6, waiting for transfers between devices: 42.7 us -> 22 us  [the longest x1 12.7 us: on_device(): got = lax.ppermute(peer_terms.astype(jnp.bfloat16), 'tp', [(0, 1), (1, 0)])]
    reduce_scatter x1 -> x0, waiting for transfers between devices: 20.5 us -> none  [on_device(): lax.psum_scatter(terms.astype(jnp.bfloat16), 'tp', scatter_dimension=1, t...]
    slice x6 -> x1, local copies, waits for them, and re-layouts: 0.11 us -> 8.68 us  [rotate(): second = pieces[:, :, 1, :]]
    unnamed x4 -> x23, local copies, waits for them, and re-layouts: 3.64 us -> 11.9 us
    another operation x8 -> x0, loops' own time: 7.96 us -> none  [the longest x1 4.23 us: on_device(): carry, _ = lax.fori_loop(1, longest, visit, (carry, stacked))]
    sub x0 -> x1, matrix products: none -> 6.35 us  [on_device(): weights = jnp.where(allowed, jnp.exp(scores - highest[..., None]), 0.0)]
    convert_element_type x0 -> x1, local copies, waits for them, and re-layouts: none -> 4.57 us  [rotate(): pieces = block.astype(jnp.float32).reshape(count, heads, 2, half)]
    dot_general x15 -> x3, matrix products: 16.4 us -> 13.4 us  [the longest x1 5.47 us: on_device(): jnp.dot(attended, own_weight, preferred_element_type=jnp.float32)]
  transfers between devices with their start and end apart: 8 -> 6, of which waited for: 8 -> 3; matrix products, arithmetic and copies ran while one was open for 0% -> 11% of each run, Pallas kernels for 0% -> 0%
where the time goes in v1:
time: 101 us; the launch traced here: 100 us
  local copies, waits for them, and re-layouts  28.7 us (28%)
  waiting for transfers between devices  22 us (22%)
  matrix products  19.8 us (20%)
  starting transfers between devices  14.2 us (14%)
  other arithmetic  13.1 us (13%)
  between operations  2.73 us (3%)
    ppermute x1, waiting for transfers between devices, on_device(): got = lax.ppermute(peer_terms.astype(jnp.bfloat16), 'tp', [(0, 1), (1, 0)])  12.7 us
    unnamed x23, local copies, waits for them, and re-layouts  11.9 us
    slice x1, local copies, waits for them, and re-layouts, rotate(): second = pieces[:, :, 1, :]  8.68 us
    ppermute x4, waiting for transfers between devices, gather_window(): received.append(lax.ppermute(kv, 'ctx', pairs))  7.14 us
    ppermute x1, starting transfers between devices, gather_window(): incoming = lax.ppermute(outgoing, 'ctx', [(j, j ^ 1) for j in range(n)])  6.47 us
    sub x1, matrix products, on_device(): weights = jnp.where(allowed, jnp.exp(scores - highest[..., None]), 0.0)  6.35 us
    ppermute x4, starting transfers between devices, gather_window(): received.append(lax.ppermute(kv, 'ctx', pairs))  6.1 us
    dot_general x1, matrix products, on_device(): jnp.dot(attended, own_weight, preferred_element_type=jnp.float32)  5.47 us
  transfers between devices with their start and end apart: 6, of which 3 were waited for; matrix products, arithmetic and copies ran while one was open for 11% of the time, Pallas kernels for 0%

profile of v1, /device:TPU:24, one launch (start us, length us, event | category | flops | bytes accessed | tf_op | source)
XLA Modules:
  0.0 100.4 jit_solution(2711179175094233289)
XLA Ops:
  1.0 1.3 %collective-permute-start = (bf16[2,128,512]{2,1,0:T(8,128)(2,1)S(1)}, bf16[2,128,512]{2,1,0:T(8,128)(2,1)S(1)}, u32[]{:S(2)}, u32[]{:S(2)}) collective-permute-start(bf16[2,128,512]{2,1,0:T(8,128)(2,1)S(1)} %get-tuple-element.14), channel_id=1, source_target_pairs={{2,4},{6,8},{10,12},{14,16},{18,20},{22,24},{26,28},{3,5},{7,9},{1... | collective-permute-start | bytes 786440 | tf_op jit(solution)/shard_map/ppermute | solution.py:34
  2.3 2.2 %collective-permute-start.1 = (bf16[2,128,512]{2,1,0:T(8,128)(2,1)S(1)}, bf16[2,128,512]{2,1,0:T(8,128)(2,1)S(1)}, u32[]{:S(2)}, u32[]{:S(2)}) collective-permute-start(bf16[2,128,512]{2,1,0:T(8,128)(2,1)S(1)} %get-tuple-element.14), channel_id=1, source_target_pairs={{0,6},{2,8},{4,10},{6,12},{8,14},{10,16},{12,18},{14,20},{16,22},{... | collective-permute-start | bytes 786440 | tf_op jit(solution)/shard_map/ppermute | solution.py:34
  4.5 1.3 %collective-permute-start.2 = (bf16[2,128,512]{2,1,0:T(8,128)(2,1)S(1)}, bf16[2,128,512]{2,1,0:T(8,128)(2,1)S(1)}, u32[]{:S(2)}, u32[]{:S(2)}) collective-permute-start(bf16[2,128,512]{2,1,0:T(8,128)(2,1)S(1)} %get-tuple-element.14), channel_id=1, source_target_pairs={{0,10},{2,12},{4,14},{6,16},{8,18},{10,20},{12,22},{14,24},{16,26}... | collective-permute-start | bytes 786440 | tf_op jit(solution)/shard_map/ppermute | solution.py:34
  5.8 1.3 %collective-permute-start.3 = (bf16[2,128,512]{2,1,0:T(8,128)(2,1)S(1)}, bf16[2,128,512]{2,1,0:T(8,128)(2,1)S(1)}, u32[]{:S(2)}, u32[]{:S(2)}) collective-permute-start(bf16[2,128,512]{2,1,0:T(8,128)(2,1)S(1)} %get-tuple-element.14), channel_id=1, source_target_pairs={{0,14},{2,16},{4,18},{6,20},{8,22},{10,24},{12,26},{14,28},{16,30}... | collective-permute-start | bytes 786440 | tf_op jit(solution)/shard_map/ppermute | solution.py:34
  10.5 1.3 %fusion.35 = s32[9]{0:T(128)S(1)} fusion(s32[9]{0:T(128)} %constant.50.clone, s32[9]{0:T(128)} %constant.51.clone, pred[]{:T(512)S(6)} %eq.12, s32[]{:T(128)} %select_reduce_fusion.3, s32[]{:T(128)S(6)} %axis_index.27), kind=kLoop, calls=%fused_computation.51 | loop fusion | flops 36 | bytes 117 | tf_op jit(solution)/shard_map/mul | solution.py:70
  11.9 1.3 %select_reduce_fusion.1 = (s32[]{:T(128)}, s32[]{:T(128)}) fusion(s32[8]{0:T(128)} %param.13, s32[]{:T(128)S(6)} %sub.42, s32[8]{0:T(128)} %param.12), kind=kLoop, calls=%fused_computation.55 | loop fusion | flops 38 | bytes 76 | tf_op jit(solution)/shard_map/reduce_sum | solution.py:66
  14.5 1.9 %multiply_cosine_fusion = (f32[1152,64]{0,1:T(8,128)}, f32[1152,64]{0,1:T(8,128)}) fusion(f32[64]{0:T(128)S(1)} %multiply_power_fusion, f32[1152]{0:T(1024)S(1)} %get-tuple-element.19), kind=kLoop, calls=%fused_computation.31 | loop fusion | flops 73728 | bytes 594688 | tf_op jit(solution)/shard_map/cos | solution.py:19
  16.7 1.3 %copy.22 = bf16[128,2048]{0,1:T(8,128)(2,1)S(1)} copy(bf16[128,2048]{1,0:T(8,128)(2,1)} %param.8) | data formatting | bytes 1048576 | tf_op args[0]
  18.1 1.9 %and_and_fusion = pred[128,1152]{0,1:T(8,128)(4,1)} fusion(s32[128]{0:T(128)S(1)} %get-tuple-element.27, s32[1152]{0:T(1024)S(1)} %get-tuple-element.20, pred[1152]{0:T(1024)(128)(4,1)S(1)} %get-tuple-element.22, pred[1152]{0:T(1024)(128)(4,1)S(1)} %get-tuple-element.21), kind=kLoop, calls=%fused_computation.26 | loop fusion | flops 442368 | bytes 154880 | tf_op jit(solution)/shard_map/and | solution.py:82
  21.0 7.1 %collective-permute-done.2 = bf16[2,128,512]{2,1,0:T(8,128)(2,1)S(1)} collective-permute-done((bf16[2,128,512]{2,1,0:T(8,128)(2,1)S(1)}, bf16[2,128,512]{2,1,0:T(8,128)(2,1)S(1)}, u32[]{:S(2)}, u32[]{:S(2)}) %collective-permute-start.2) | collective-permute-done | bytes 262176 | tf_op jit(solution)/shard_map/ppermute | solution.py:34
  28.4 6.5 %collective-permute-start.4 = (bf16[4,2,128,512]{3,2,1,0:T(8,128)(2,1)S(1)}, bf16[4,2,128,512]{3,2,1,0:T(8,128)(2,1)S(1)}, u32[]{:S(2)}, u32[]{:S(2)}) collective-permute-start(bf16[4,2,128,512]{3,2,1,0:T(8,128)(2,1)S(1)} %maximum_select_fusion), channel_id=1, source_target_pairs={{0,2},{2,0},{4,6},{6,4},{8,10},{10,8},{12,14},{14,12},{16,18},{18,... | collective-permute-start | bytes 3145736 | tf_op jit(solution)/shard_map/ppermute | solution.py:39
  35.0 2.1 %collective-permute-done.4 = bf16[4,2,128,512]{3,2,1,0:T(8,128)(2,1)S(1)} collective-permute-done((bf16[4,2,128,512]{3,2,1,0:T(8,128)(2,1)S(1)}, bf16[4,2,128,512]{3,2,1,0:T(8,128)(2,1)S(1)}, u32[]{:S(2)}, u32[]{:S(2)}) %collective-permute-start.4) | collective-permute-done | bytes 1048608 | tf_op jit(solution)/shard_map/ppermute | solution.py:39
  37.3 1.4 %fusion.48 = (bf16[9,1,128,512]{3,2,1,0:T(8,128)(2,1)}, f32[9,1,128,512]{3,2,1,0:T(8,128)S(1)}) fusion(bf16[9,2,128,512]{3,2,1,0:T(8,128)(2,1)S(1)} %constant_dynamic-update-slice_fusion), kind=kLoop, calls=%fused_computation.67 | loop fusion | flops 589824 | bytes 5898240 | tf_op jit(solution)/shard_map/slice | solution.py:76
  38.7 4.6 %reshape.187 = f32[1152,4,2,64]{3,2,1,0:T(2,128)} reshape(f32[9,1,128,512]{3,2,1,0:T(8,128)S(1)} %get-tuple-element.10) | data formatting | bytes 4718592 | tf_op jit(solution)/shard_map/convert_element_type | solution.py:16
  43.3 8.7 %fusion.47 = (f32[1152,4,1,64]{3,2,1,0:T(1,128)S(1)}, f32[1152,4,1,64]{3,2,1,0:T(1,128)}) fusion(f32[1152,4,2,64]{3,2,1,0:T(2,128)} %reshape.187), kind=kLoop, calls=%fused_computation.66 | loop fusion | bytes 4718592 | tf_op jit(solution)/shard_map/slice | solution.py:22
  51.9 4.8 %copy.36 = f32[1152,4,1,64]{0,3,2,1:T(8,128)S(1)} copy(f32[1152,4,1,64]{3,2,1,0:T(1,128)} %get-tuple-element.6) | data formatting | bytes 2359296
  56.8 4.9 %copy.37 = f32[1152,4,1,64]{0,3,2,1:T(8,128)} copy(f32[1152,4,1,64]{3,2,1,0:T(1,128)S(1)} %get-tuple-element.5) | data formatting | bytes 2359296
  61.7 3.4 %reshape_squeeze.4 = bf16[1152,4,128]{2,1,0:T(4,128)(2,1)} reshape(bf16[9,1,128,512]{3,2,1,0:T(8,128)(2,1)} %get-tuple-element.9) | data formatting | bytes 2359296 | tf_op jit(solution)/shard_map/reshape;squeeze | solution.py:76
  66.4 6.4 %fusion.49 = (f32[4,4,128]{2,1,0:T(4,128)S(1)}, bf16[4,4,128,1152]{2,3,1,0:T(8,128)(2,1)}) fusion(pred[128,1152]{0,1:T(8,128)(4,1)S(1)} %copy-done.7, bf16[1152,4,128,1]{0,2,3,1:T(8,128)(2,1)S(1)} %bitcast.58, bf16[128,4,4,128]{0,3,2,1:T(8,128)(2,1)S(1)} %bitcast.63), kind=kOutput, calls=%fused_computation.68 | convolution fusion | flops 618136704 | bytes 6578176 | tf_op jit(solution)/shard_map/sub | solution.py:88
  72.7 3.3 %fusion.26 = bf16[128,4,4,128]{0,3,2,1:T(8,128)(2,1)S(1)} fusion(bf16[4,4,128,1152]{2,3,1,0:T(8,128)(2,1)} %get-tuple-element.24, bf16[1152,4,128,1]{2,1,0,3:T(4,128)(2,1)S(1)} %bitcast.57, f32[128,4,4]{0,2,1:T(4,128)S(1)} %bitcast.68), kind=kOutput, calls=%fused_computation.18 | convolution fusion | flops 604504064 | bytes 6430720 | tf_op jit(solution)/shard_map/kgrn,nkd->kgrd/dot_general | solution.py:90
  76.0 4.7 %fusion.17 = bf16[128,2048]{1,0:T(8,128)(2,1)S(1)} fusion(bf16[128,2048]{0,1:T(8,128)(2,1)S(1)} %bitcast.54, bf16[2048,4096]{1,0:T(8,128)(2,1)} %param.11, s32[]{:T(128)S(6)} %select_n.62), kind=kOutput, calls=%fused_computation.15 | convolution fusion | flops 1074003968 | bytes 9437188 | tf_op jit(solution)/shard_map/dot_general | solution.py:102
  80.7 1.6 %collective-permute-start.5 = (bf16[128,2048]{1,0:T(8,128)(2,1)S(1)}, bf16[128,2048]{1,0:T(8,128)(2,1)S(1)}, u32[]{:S(2)}, u32[]{:S(2)}) collective-permute-start(bf16[128,2048]{1,0:T(8,128)(2,1)S(1)} %fusion.17), channel_id=1, source_target_pairs={{0,1},{1,0},{2,3},{3,2},{4,5},{5,4},{6,7},{7,6},{8,9},{9,8},{10,11... | collective-permute-start | bytes 1572872 | tf_op jit(solution)/shard_map/ppermute | solution.py:103
  82.3 12.7 %collective-permute-done.5 = bf16[128,2048]{1,0:T(8,128)(2,1)S(1)} collective-permute-done((bf16[128,2048]{1,0:T(8,128)(2,1)S(1)}, bf16[128,2048]{1,0:T(8,128)(2,1)S(1)}, u32[]{:S(2)}, u32[]{:S(2)}) %collective-permute-start.5) | collective-permute-done | bytes 524320 | tf_op jit(solution)/shard_map/ppermute | solution.py:103
  95.0 5.5 %add_convert_fusion.1 = bf16[128,2048]{1,0:T(8,128)(2,1)} fusion(bf16[128,2048]{1,0:T(8,128)(2,1)S(1)} %collective-permute-done.5, bf16[128,2048]{0,1:T(8,128)(2,1)S(1)} %bitcast.55, bf16[2048,4096]{1,0:T(8,128)(2,1)} %param.11, s32[]{:T(128)S(6)} %select_n.61), kind=kOutput, calls=%fused_computation.25 | convolution fusion | flops 1075052544 | bytes 9961476 | tf_op jit(solution)/shard_map/dot_general | solution.py:105
  (40 shorter events, 6.2 us)
Async XLA Ops:
  1.0 20.0 %collective-permute-start = (bf16[2,128,512]{2,1,0:T(8,128)(2,1)S(1)}, bf16[2,128,512]{2,1,0:T(8,128)(2,1)S(1)}, u32[]{:S(2)}, u32[]{:S(2)}) collective-permute-start(bf16[2,128,512]{2,1,0:T(8,128)(2,1)S(1)} %get-tuple-element.14), channel_id=1, source_target_pairs={{2,4},{6,8},{10,12},{14,16},{18,20},{22,24},{26,28},{3,5},{7,9},{1... | collective-permute-start | bytes 786440 | tf_op jit(solution)/shard_map/ppermute | solution.py:34
  2.3 18.7 %collective-permute-start.1 = (bf16[2,128,512]{2,1,0:T(8,128)(2,1)S(1)}, bf16[2,128,512]{2,1,0:T(8,128)(2,1)S(1)}, u32[]{:S(2)}, u32[]{:S(2)}) collective-permute-start(bf16[2,128,512]{2,1,0:T(8,128)(2,1)S(1)} %get-tuple-element.14), channel_id=1, source_target_pairs={{0,6},{2,8},{4,10},{6,12},{8,14},{10,16},{12,18},{14,20},{16,22},{... | collective-permute-start | bytes 786440 | tf_op jit(solution)/shard_map/ppermute | solution.py:34
  4.5 23.6 %collective-permute-start.2 = (bf16[2,128,512]{2,1,0:T(8,128)(2,1)S(1)}, bf16[2,128,512]{2,1,0:T(8,128)(2,1)S(1)}, u32[]{:S(2)}, u32[]{:S(2)}) collective-permute-start(bf16[2,128,512]{2,1,0:T(8,128)(2,1)S(1)} %get-tuple-element.14), channel_id=1, source_target_pairs={{0,10},{2,12},{4,14},{6,16},{8,18},{10,20},{12,22},{14,24},{16,26}... | collective-permute-start | bytes 786440 | tf_op jit(solution)/shard_map/ppermute | solution.py:34
  5.8 22.3 %collective-permute-start.3 = (bf16[2,128,512]{2,1,0:T(8,128)(2,1)S(1)}, bf16[2,128,512]{2,1,0:T(8,128)(2,1)S(1)}, u32[]{:S(2)}, u32[]{:S(2)}) collective-permute-start(bf16[2,128,512]{2,1,0:T(8,128)(2,1)S(1)} %get-tuple-element.14), channel_id=1, source_target_pairs={{0,14},{2,16},{4,18},{6,20},{8,22},{10,24},{12,26},{14,28},{16,30}... | collective-permute-start | bytes 786440 | tf_op jit(solution)/shard_map/ppermute | solution.py:34
  20.0 14.9 %copy-start.5 = (bf16[128,512]{1,0:T(8,128)(2,1)S(1)}, bf16[128,512]{1,0:T(8,128)(2,1)}, u32[]{:S(2)}) copy-start(bf16[128,512]{1,0:T(8,128)(2,1)} %param.10) | copy-start | bytes 393220
  20.0 14.9 %copy-start.6 = (bf16[128,512]{1,0:T(8,128)(2,1)S(1)}, bf16[128,512]{1,0:T(8,128)(2,1)}, u32[]{:S(2)}) copy-start(bf16[128,512]{1,0:T(8,128)(2,1)} %param.9) | copy-start | bytes 393220
  28.4 8.8 %collective-permute-start.4 = (bf16[4,2,128,512]{3,2,1,0:T(8,128)(2,1)S(1)}, bf16[4,2,128,512]{3,2,1,0:T(8,128)(2,1)S(1)}, u32[]{:S(2)}, u32[]{:S(2)}) collective-permute-start(bf16[4,2,128,512]{3,2,1,0:T(8,128)(2,1)S(1)} %maximum_select_fusion), channel_id=1, source_target_pairs={{0,2},{2,0},{4,6},{6,4},{8,10},{10,8},{12,14},{14,12},{16,18},{18,... | collective-permute-start | bytes 3145736 | tf_op jit(solution)/shard_map/ppermute | solution.py:39
  61.6 3.5 %copy-start = (f32[1152,4,1,64]{0,3,2,1:T(8,128)S(1)}, f32[1152,4,1,64]{0,3,2,1:T(8,128)}, u32[]{:S(2)}) copy-start(f32[1152,4,1,64]{0,3,2,1:T(8,128)} %copy.37) | copy-start | bytes 3538948
  61.6 3.5 %copy-start.1 = (f32[1152,64]{0,1:T(8,128)S(1)}, f32[1152,64]{0,1:T(8,128)}, u32[]{:S(2)}) copy-start(f32[1152,64]{0,1:T(8,128)} %get-tuple-element.15) | copy-start | bytes 884740
  61.7 3.5 %copy-start.2 = (f32[1152,64]{0,1:T(8,128)S(1)}, f32[1152,64]{0,1:T(8,128)}, u32[]{:S(2)}) copy-start(f32[1152,64]{0,1:T(8,128)} %get-tuple-element.16) | copy-start | bytes 884740
  65.1 1.0 %copy-start.4 = (bf16[128,16,2,64]{0,3,2,1:T(8,128)(2,1)S(1)}, bf16[128,16,2,64]{0,3,2,1:T(8,128)(2,1)}, u32[]{:S(2)}) copy-start(bf16[128,16,2,64]{0,3,2,1:T(8,128)(2,1)} %pad_maximum_fusion.1) | copy-start | bytes 1572868
  65.4 0.9 copy-start.7
  66.4 6.4 %copy-start.3 = (bf16[1152,4,128]{2,1,0:T(4,128)(2,1)S(1)}, bf16[1152,4,128]{2,1,0:T(4,128)(2,1)}, u32[]{:S(2)}) copy-start(bf16[1152,4,128]{2,1,0:T(4,128)(2,1)} %reshape_squeeze.4) | copy-start | bytes 3538948
  80.7 14.3 %collective-permute-start.5 = (bf16[128,2048]{1,0:T(8,128)(2,1)S(1)}, bf16[128,2048]{1,0:T(8,128)(2,1)S(1)}, u32[]{:S(2)}, u32[]{:S(2)}) collective-permute-start(bf16[128,2048]{1,0:T(8,128)(2,1)S(1)} %fusion.17), channel_id=1, source_target_pairs={{0,1},{1,0},{2,3},{3,2},{4,5},{5,4},{6,7},{7,6},{8,9},{9,8},{10,11... | collective-permute-start | bytes 1572872 | tf_op jit(solution)/shard_map/ppermute | solution.py:103

commit v2 on v1

--- a/solution.py
+++ b/solution.py
@@ -3,6 +3,8 @@
 import jax
 import jax.numpy as jnp
 from jax import lax
+from jax.experimental import pallas as pl
+from jax.experimental.pallas import tpu as pltpu
 from jax.sharding import PartitionSpec as P
 
 HEAD_SIZE = 128
@@ -45,6 +47,48 @@
     return slots, shift
 
 
+def attention_kernel(query_pos_ref, key_limit_ref, query_ref, key_ref, value_ref, out_ref):
+    keys = key_ref[...]
+    values = value_ref[...].reshape(keys.shape[0], HEAD_SIZE)
+    allowed = key_limit_ref[...] <= query_pos_ref[...]
+    for g in range(query_ref.shape[1] // HEAD_SIZE):
+        columns = slice(g * HEAD_SIZE, (g + 1) * HEAD_SIZE)
+        scores = lax.dot_general(
+            query_ref[:, columns], keys, (((1,), (1,)), ((), ())), preferred_element_type=jnp.float32
+        ) * (1.0 / math.sqrt(HEAD_SIZE))
+        scores = jnp.where(allowed, scores, -1e30)
+        highest = jnp.max(scores, axis=1, keepdims=True)
+        weights = jnp.where(allowed, jnp.exp(scores - highest), 0.0)
+        totals = jnp.sum(weights, axis=1, keepdims=True)
+        summed = jnp.dot(weights.astype(jnp.bfloat16), values, preferred_element_type=jnp.float32)
+        out_ref[:, columns] = (summed / totals).astype(out_ref.dtype)
+
+
+def attend(query_pos, key_limit, query_rows, key_rows, slots, heads_kv):
+    rows, width = query_rows.shape
+    count = key_rows.shape[0]
+    group = width // heads_kv
+    n_slots = slots.shape[0]
+    flops = 4 * rows * count * width
+    return pl.pallas_call(
+        attention_kernel,
+        out_shape=jax.ShapeDtypeStruct((rows, width), jnp.bfloat16),
+        grid=(heads_kv,),
+        in_specs=[
+            pl.BlockSpec((rows, 1), lambda h: (0, 0)),
+            pl.BlockSpec((1, count), lambda h: (0, 0)),
+            pl.BlockSpec((rows, group), lambda h: (0, h)),
+            pl.BlockSpec((count, HEAD_SIZE), lambda h: (0, h)),
+            pl.BlockSpec((n_slots, None, slots.shape[2], HEAD_SIZE), lambda h: (0, 1, 0, h)),
+        ],
+        out_specs=pl.BlockSpec((rows, group), lambda h: (0, h)),
+        cost_estimate=pl.CostEstimate(
+            flops=flops, transcendentals=rows * count * width // HEAD_SIZE,
+            bytes_accessed=2 * (2 * rows * width + 2 * count * heads_kv * HEAD_SIZE),
+        ),
+    )(query_pos, key_limit, query_rows, key_rows, slots)
+
+
 def on_device(queries, keys, values, out_weight, group_widths, pad_tokens):
     n = lax.axis_size("ctx")
     window = n // 2
@@ -71,28 +115,11 @@
     key_pos = key_pos.reshape(-1)
 
     count = slots.shape[0] * rows_here
-    query_rows = rotate(queries, query_pos).reshape(rows_here, heads_kv, context_group, HEAD_SIZE)
-    key_rows = rotate(slots[:, 0].reshape(count, -1), key_pos).reshape(count, heads_kv, HEAD_SIZE)
-    value_rows = slots[:, 1].reshape(count, heads_kv, HEAD_SIZE)
-
-    scores = jnp.einsum(
-        "rkgd,nkd->kgrn", query_rows, key_rows, preferred_element_type=jnp.float32
-    ) * (1.0 / math.sqrt(HEAD_SIZE))
-    allowed = (
-        (key_pos[None, :] <= query_pos[:, None])
-        & (key_pos[None, :] < length)
-        & (key_pos[None, :] >= 0)
-    )
-    scores = jnp.where(allowed, scores, -1e30)
-    highest = jnp.max(scores, axis=-1)
-    weights = jnp.where(allowed, jnp.exp(scores - highest[..., None]), 0.0)
-    totals = jnp.sum(weights, axis=-1)
-    summed = jnp.einsum(
-        "kgrn,nkd->kgrd", weights.astype(jnp.bfloat16), value_rows, preferred_element_type=jnp.float32
-    )
-    attended = (
-        (summed / totals[..., None]).transpose(2, 0, 1, 3).reshape(rows_here, -1).astype(jnp.bfloat16)
-    )
+    query_rows = rotate(queries, query_pos)
+    key_rows = rotate(slots[:, 0].reshape(count, -1), key_pos)
+    usable = (key_pos >= 0) & (key_pos < length)
+    key_limit = jnp.where(usable, key_pos, FAR * rows_here).reshape(1, count)
+    attended = attend(query_pos.reshape(rows_here, 1), key_limit, query_rows, key_rows, slots, heads_kv)
 
     n_tp = lax.axis_size("tp")
     if n_tp == 2:
@@ -103,7 +130,7 @@
         got = lax.ppermute(peer_terms.astype(jnp.bfloat16), "tp", [(0, 1), (1, 0)])
         own_weight = lax.dynamic_slice_in_dim(out_weight, me * part, part, 1)
         own_terms = jnp.dot(attended, own_weight, preferred_element_type=jnp.float32)
-        own_terms = own_terms.astype(jnp.bfloat16).astype(jnp.float32)
+        own_terms = lax.optimization_barrier(own_terms.astype(jnp.bfloat16)).astype(jnp.float32)
         return (own_terms + got.astype(jnp.float32)).astype(jnp.bfloat16)
     terms = jnp.dot(attended, out_weight, preferred_element_type=jnp.float32)
     return lax.psum_scatter(terms.astype(jnp.bfloat16), "tp", scatter_dimension=1, tiled=True)

time: 101 us -> 95.4 us (0.945)
  matrix products: 19.8 us -> 9.5 us
  Pallas kernels: 0 us -> 9.4 us
  waiting for transfers between devices: 22 us -> 17.7 us
    pallas_call x0 -> x1, Pallas kernels: none -> 9.4 us  [attend(): pl.pallas_call(attention_kernel, out_shape=jax.ShapeDtypeStruct((rows, wi...]
    sub x1 -> x0, matrix products: 6.35 us -> none  [on_device(): weights = jnp.where(allowed, jnp.exp(scores - highest[..., None]), 0.0)]
    ppermute x1, waiting for transfers between devices: 12.7 us -> 8.02 us  [on_device(): got = lax.ppermute(peer_terms.astype(jnp.bfloat16), 'tp', [(0, 1), (1, 0)])]
    another operation x1 -> x0, local copies, waits for them, and re-layouts: 3.45 us -> none  [on_device(): value_rows = slots[:, 1].reshape(count, heads_kv, HEAD_SIZE)]
    dot_general x1 -> x0, matrix products: 3.27 us -> none  [on_device(): jnp.einsum('kgrn,nkd->kgrd', weights.astype(jnp.bfloat16), value_rows, pr...]
    convert_element_type x0 -> x2, local copies, waits for them, and re-layouts: none -> 2.47 us  [rotate(): return turned.reshape(count, heads * HEAD_SIZE).astype(jnp.bfloat16)]
    and x1 -> x0, other arithmetic: 1.93 us -> none  [on_device(): (key_pos[None, :] <= query_pos[:, None]) & (key_pos[None, :] < length)]
    slice x1 -> x0, other arithmetic: 1.44 us -> none  [on_device(): value_rows = slots[:, 1].reshape(count, heads_kv, HEAD_SIZE)]
  transfers between devices with their start and end apart: 6 -> 6, of which waited for: 3 -> 3; matrix products, arithmetic and copies ran while one was open for 11% -> 16% of each run, Pallas kernels for 0% -> 0%
where the time goes in v2:
time: 95.4 us; the launch traced here: 94.8 us
  local copies, waits for them, and re-layouts  28.4 us (30%)
  waiting for transfers between devices  17.7 us (19%)
  starting transfers between devices  14.2 us (15%)
  other arithmetic  12.8 us (13%)
  matrix products  9.5 us (10%)
  Pallas kernels  9.4 us (10%)
  between operations  2.82 us (3%)
    unnamed x15, local copies, waits for them, and re-layouts  12.5 us
    pallas_call x1, Pallas kernels, attend(): pl.pallas_call(attention_kernel, out_shape=jax.ShapeDtypeStruct((rows, wi...  9.4 us
    slice x1, local copies, waits for them, and re-layouts, rotate(): second = pieces[:, :, 1, :]  8.72 us
    ppermute x4, waiting for transfers between devices, gather_window(): received.append(lax.ppermute(kv, 'ctx', pairs))  8.15 us
    ppermute x1, waiting for transfers between devices, on_device(): got = lax.ppermute(peer_terms.astype(jnp.bfloat16), 'tp', [(0, 1), (1, 0)])  8.02 us
    ppermute x1, starting transfers between devices, gather_window(): incoming = lax.ppermute(outgoing, 'ctx', [(j, j ^ 1) for j in range(n)])  6.47 us
    ppermute x4, starting transfers between devices, gather_window(): received.append(lax.ppermute(kv, 'ctx', pairs))  6.1 us
    dot_general x1, matrix products, on_device(): jnp.dot(attended, peer_weight, preferred_element_type=jnp.float32)  4.86 us
  transfers between devices with their start and end apart: 6, of which 3 were waited for; matrix products, arithmetic and copies ran while one was open for 16% of the time, Pallas kernels for 0%

profile of v2, /device:TPU:24, one launch (start us, length us, event | category | flops | bytes accessed | tf_op | source)
XLA Modules:
  0.0 94.8 jit_solution(9137034455444087517)
XLA Ops:
  1.0 1.3 %collective-permute-start = (bf16[2,128,512]{2,1,0:T(8,128)(2,1)S(1)}, bf16[2,128,512]{2,1,0:T(8,128)(2,1)S(1)}, u32[]{:S(2)}, u32[]{:S(2)}) collective-permute-start(bf16[2,128,512]{2,1,0:T(8,128)(2,1)S(1)} %get-tuple-element.12), channel_id=1, source_target_pairs={{2,4},{6,8},{10,12},{14,16},{18,20},{22,24},{26,28},{3,5},{7,9},{1... | collective-permute-start | bytes 786440 | tf_op jit(solution)/shard_map/ppermute | solution.py:36
  2.3 2.2 %collective-permute-start.1 = (bf16[2,128,512]{2,1,0:T(8,128)(2,1)S(1)}, bf16[2,128,512]{2,1,0:T(8,128)(2,1)S(1)}, u32[]{:S(2)}, u32[]{:S(2)}) collective-permute-start(bf16[2,128,512]{2,1,0:T(8,128)(2,1)S(1)} %get-tuple-element.12), channel_id=1, source_target_pairs={{0,6},{2,8},{4,10},{6,12},{8,14},{10,16},{12,18},{14,20},{16,22},{... | collective-permute-start | bytes 786440 | tf_op jit(solution)/shard_map/ppermute | solution.py:36
  4.5 1.3 %collective-permute-start.2 = (bf16[2,128,512]{2,1,0:T(8,128)(2,1)S(1)}, bf16[2,128,512]{2,1,0:T(8,128)(2,1)S(1)}, u32[]{:S(2)}, u32[]{:S(2)}) collective-permute-start(bf16[2,128,512]{2,1,0:T(8,128)(2,1)S(1)} %get-tuple-element.12), channel_id=1, source_target_pairs={{0,10},{2,12},{4,14},{6,16},{8,18},{10,20},{12,22},{14,24},{16,26}... | collective-permute-start | bytes 786440 | tf_op jit(solution)/shard_map/ppermute | solution.py:36
  5.8 1.3 %collective-permute-start.3 = (bf16[2,128,512]{2,1,0:T(8,128)(2,1)S(1)}, bf16[2,128,512]{2,1,0:T(8,128)(2,1)S(1)}, u32[]{:S(2)}, u32[]{:S(2)}) collective-permute-start(bf16[2,128,512]{2,1,0:T(8,128)(2,1)S(1)} %get-tuple-element.12), channel_id=1, source_target_pairs={{0,14},{2,16},{4,18},{6,20},{8,22},{10,24},{12,26},{14,28},{16,30}... | collective-permute-start | bytes 786440 | tf_op jit(solution)/shard_map/ppermute | solution.py:36
  10.5 1.3 %fusion.13 = s32[9]{0:T(128)S(1)} fusion(s32[9]{0:T(128)} %constant.44.clone, s32[9]{0:T(128)} %constant.45.clone, pred[]{:T(512)S(6)} %eq.14, s32[]{:T(128)} %select_reduce_fusion.3, s32[]{:T(128)S(6)} %axis_index.27), kind=kLoop, calls=%fused_computation.37 | loop fusion | flops 36 | bytes 117 | tf_op jit(solution)/shard_map/mul | solution.py:114
  11.9 1.3 %select_reduce_fusion.1 = (s32[]{:T(128)}, s32[]{:T(128)}) fusion(s32[8]{0:T(128)} %param.13, s32[]{:T(128)S(6)} %sub.32, s32[8]{0:T(128)} %param.12), kind=kLoop, calls=%fused_computation.41 | loop fusion | flops 38 | bytes 76 | tf_op jit(solution)/shard_map/reduce_sum | solution.py:110
  13.9 1.9 %multiply_cosine_fusion = (f32[1152,64]{0,1:T(8,128)}, f32[1152,64]{0,1:T(8,128)}) fusion(f32[64]{0:T(128)S(1)} %multiply_power_fusion, f32[1152]{0:T(1024)S(1)} %get-tuple-element.17), kind=kLoop, calls=%fused_computation.16 | loop fusion | flops 73728 | bytes 594688 | tf_op jit(solution)/shard_map/cos | solution.py:21
  16.0 1.3 %copy.13 = bf16[128,2048]{0,1:T(8,128)(2,1)S(1)} copy(bf16[128,2048]{1,0:T(8,128)(2,1)} %param.8) | data formatting | bytes 1048576 | tf_op args[0]
  19.0 1.0 %copy.15.query_ref = bf16[128,2048]{1,0:T(8,128)(2,1)} copy(bf16[128,2048]{0,1:T(8,128)(2,1)S(1)} %bitcast.30) | data formatting | bytes 1048576 | tf_op jit(solution)/shard_map/convert_element_type | solution.py:26
  20.0 8.1 %collective-permute-done.2 = bf16[2,128,512]{2,1,0:T(8,128)(2,1)S(1)} collective-permute-done((bf16[2,128,512]{2,1,0:T(8,128)(2,1)S(1)}, bf16[2,128,512]{2,1,0:T(8,128)(2,1)S(1)}, u32[]{:S(2)}, u32[]{:S(2)}) %collective-permute-start.2) | collective-permute-done | bytes 262176 | tf_op jit(solution)/shard_map/ppermute | solution.py:36
  28.4 6.5 %collective-permute-start.4 = (bf16[4,2,128,512]{3,2,1,0:T(8,128)(2,1)S(1)}, bf16[4,2,128,512]{3,2,1,0:T(8,128)(2,1)S(1)}, u32[]{:S(2)}, u32[]{:S(2)}) collective-permute-start(bf16[4,2,128,512]{3,2,1,0:T(8,128)(2,1)S(1)} %maximum_select_fusion), channel_id=1, source_target_pairs={{0,2},{2,0},{4,6},{6,4},{8,10},{10,8},{12,14},{14,12},{16,18},{18,... | collective-permute-start | bytes 3145736 | tf_op jit(solution)/shard_map/ppermute | solution.py:41
  35.6 1.6 %collective-permute-done.4 = bf16[4,2,128,512]{3,2,1,0:T(8,128)(2,1)S(1)} collective-permute-done((bf16[4,2,128,512]{3,2,1,0:T(8,128)(2,1)S(1)}, bf16[4,2,128,512]{3,2,1,0:T(8,128)(2,1)S(1)}, u32[]{:S(2)}, u32[]{:S(2)}) %collective-permute-start.4) | collective-permute-done | bytes 1048608 | tf_op jit(solution)/shard_map/ppermute | solution.py:41
  37.3 1.4 %copy-done = bf16[9,2,128,512]{3,2,1,0:T(8,128)(2,1)} copy-done((bf16[9,2,128,512]{3,2,1,0:T(8,128)(2,1)}, bf16[9,2,128,512]{3,2,1,0:T(8,128)(2,1)S(1)}, u32[]{:S(2)}) %copy-start) | copy-done | bytes 2359320
  39.0 4.6 %reshape.178 = f32[1152,4,2,64]{3,2,1,0:T(2,128)} reshape(f32[9,1,128,512]{3,2,1,0:T(8,128)S(1)} %slice_convert_fusion) | data formatting | bytes 4718592 | tf_op jit(solution)/shard_map/convert_element_type | solution.py:18
  43.6 8.7 %fusion.18 = (f32[1152,4,1,64]{3,2,1,0:T(1,128)S(1)}, f32[1152,4,1,64]{3,2,1,0:T(1,128)}) fusion(f32[1152,4,2,64]{3,2,1,0:T(2,128)} %reshape.178), kind=kLoop, calls=%fused_computation.48 | loop fusion | bytes 4718592 | tf_op jit(solution)/shard_map/slice | solution.py:24
  52.3 4.8 %copy.18 = f32[1152,4,1,64]{0,3,2,1:T(8,128)S(1)} copy(f32[1152,4,1,64]{3,2,1,0:T(1,128)} %get-tuple-element.6) | data formatting | bytes 2359296
  57.2 4.9 %copy.19 = f32[1152,4,1,64]{0,3,2,1:T(8,128)} copy(f32[1152,4,1,64]{3,2,1,0:T(1,128)S(1)} %get-tuple-element.5) | data formatting | bytes 2359296
  62.0 1.7 %subtract_convert_fusion = (bf16[1152,4,1,64]{0,3,2,1:T(8,128)(2,1)S(1)}, bf16[1152,4,1,64]{0,3,2,1:T(8,128)(2,1)S(1)}) fusion(f32[1152,4,1,64]{0,3,2,1:T(8,128)} %copy.19, f32[1152,4,1,64]{0,3,2,1:T(8,128)S(1)} %copy.18, f32[1152,64]{0,1:T(8,128)} %get-tuple-element.14, f32[1152,64]{0,1:T(8,128)} %get-tuple-element.13), kind=kLoop, calls=%fused_computation.9 | loop fusion | flops 2359296 | bytes 4128768 | tf_op jit(solution)/shard_map/convert.2
  63.9 1.5 %copy.16.key_ref = bf16[1152,512]{1,0:T(8,128)(2,1)} copy(bf16[1152,512]{0,1:T(8,128)(2,1)S(1)} %bitcast.28) | data formatting | bytes 2359296 | tf_op jit(solution)/shard_map/convert_element_type | solution.py:26
  65.3 9.4 %shard_map.82 = bf16[128,2048]{1,0:T(8,128)(2,1)} custom-call(s32[128,1]{1,0:T(8,128)} %iota_add_fusion.query_pos_ref, s32[1,1152]{1,0:T(1,128)} %and_select_fusion.key_limit_ref, bf16[128,2048]{1,0:T(8,128)(2,1)} %copy.15.query_ref, bf16[1152,512]{1,0:T(8,128)(2,1)} %copy.16.key_ref, bf16[9,2,128,512]{3,2,1,0:T(8,128)(2,1)} %copy-done), custom_call_target="tpu_custom_call" | custom-call | flops 1207959552 | bytes 3407872 | tf_op jit(solution)/shard_map/pallas_call | solution.py:73
  74.7 4.9 %fusion.7 = bf16[128,2048]{1,0:T(8,128)(2,1)S(1)} fusion(bf16[128,2048]{1,0:T(8,128)(2,1)} %shard_map.82, bf16[2048,4096]{1,0:T(8,128)(2,1)} %param.11, s32[]{:T(128)S(6)} %select_n.65), kind=kOutput, calls=%fused_computation.5 | convolution fusion | flops 1074003968 | bytes 9437188 | tf_op jit(solution)/shard_map/dot_general | solution.py:129
  79.6 1.6 %collective-permute-start.5 = (bf16[128,2048]{1,0:T(8,128)(2,1)S(1)}, bf16[128,2048]{1,0:T(8,128)(2,1)S(1)}, u32[]{:S(2)}, u32[]{:S(2)}) collective-permute-start(bf16[128,2048]{1,0:T(8,128)(2,1)S(1)} %fusion.7), channel_id=1, source_target_pairs={{0,1},{1,0},{2,3},{3,2},{4,5},{5,4},{6,7},{7,6},{8,9},{9,8},{10,11... | collective-permute-start | bytes 1572872 | tf_op jit(solution)/shard_map/ppermute | solution.py:130
  81.2 4.6 %fusion.4 = bf16[128,2048]{1,0:T(8,128)(2,1)S(1)} fusion(bf16[128,2048]{1,0:T(8,128)(2,1)S(1)} %copy-done.1, bf16[2048,4096]{1,0:T(8,128)(2,1)} %param.11, s32[]{:T(128)S(6)} %select_n.64), kind=kOutput, calls=%fused_computation.4 | convolution fusion | flops 1074003968 | bytes 9437188 | tf_op jit(solution)/shard_map/dot_general | solution.py:132
  85.8 8.0 %collective-permute-done.5 = bf16[128,2048]{1,0:T(8,128)(2,1)S(1)} collective-permute-done((bf16[128,2048]{1,0:T(8,128)(2,1)S(1)}, bf16[128,2048]{1,0:T(8,128)(2,1)S(1)}, u32[]{:S(2)}, u32[]{:S(2)}) %collective-permute-start.5) | collective-permute-done | bytes 524320 | tf_op jit(solution)/shard_map/ppermute | solution.py:130
  (33 shorter events, 6.6 us)
Async XLA Ops:
  1.0 19.0 %collective-permute-start = (bf16[2,128,512]{2,1,0:T(8,128)(2,1)S(1)}, bf16[2,128,512]{2,1,0:T(8,128)(2,1)S(1)}, u32[]{:S(2)}, u32[]{:S(2)}) collective-permute-start(bf16[2,128,512]{2,1,0:T(8,128)(2,1)S(1)} %get-tuple-element.12), channel_id=1, source_target_pairs={{2,4},{6,8},{10,12},{14,16},{18,20},{22,24},{26,28},{3,5},{7,9},{1... | collective-permute-start | bytes 786440 | tf_op jit(solution)/shard_map/ppermute | solution.py:36
  2.3 17.7 %collective-permute-start.1 = (bf16[2,128,512]{2,1,0:T(8,128)(2,1)S(1)}, bf16[2,128,512]{2,1,0:T(8,128)(2,1)S(1)}, u32[]{:S(2)}, u32[]{:S(2)}) collective-permute-start(bf16[2,128,512]{2,1,0:T(8,128)(2,1)S(1)} %get-tuple-element.12), channel_id=1, source_target_pairs={{0,6},{2,8},{4,10},{6,12},{8,14},{10,16},{12,18},{14,20},{16,22},{... | collective-permute-start | bytes 786440 | tf_op jit(solution)/shard_map/ppermute | solution.py:36
  4.5 23.6 %collective-permute-start.2 = (bf16[2,128,512]{2,1,0:T(8,128)(2,1)S(1)}, bf16[2,128,512]{2,1,0:T(8,128)(2,1)S(1)}, u32[]{:S(2)}, u32[]{:S(2)}) collective-permute-start(bf16[2,128,512]{2,1,0:T(8,128)(2,1)S(1)} %get-tuple-element.12), channel_id=1, source_target_pairs={{0,10},{2,12},{4,14},{6,16},{8,18},{10,20},{12,22},{14,24},{16,26}... | collective-permute-start | bytes 786440 | tf_op jit(solution)/shard_map/ppermute | solution.py:36
  5.8 22.3 %collective-permute-start.3 = (bf16[2,128,512]{2,1,0:T(8,128)(2,1)S(1)}, bf16[2,128,512]{2,1,0:T(8,128)(2,1)S(1)}, u32[]{:S(2)}, u32[]{:S(2)}) collective-permute-start(bf16[2,128,512]{2,1,0:T(8,128)(2,1)S(1)} %get-tuple-element.12), channel_id=1, source_target_pairs={{0,14},{2,16},{4,18},{6,20},{8,22},{10,24},{12,26},{14,28},{16,30}... | collective-permute-start | bytes 786440 | tf_op jit(solution)/shard_map/ppermute | solution.py:36
  17.3 2.6 %copy-start.2 = (bf16[128,512]{1,0:T(8,128)(2,1)S(1)}, bf16[128,512]{1,0:T(8,128)(2,1)}, u32[]{:S(2)}) copy-start(bf16[128,512]{1,0:T(8,128)(2,1)} %param.10) | copy-start | bytes 393220
  17.4 2.6 %copy-start.3 = (bf16[128,512]{1,0:T(8,128)(2,1)S(1)}, bf16[128,512]{1,0:T(8,128)(2,1)}, u32[]{:S(2)}) copy-start(bf16[128,512]{1,0:T(8,128)(2,1)} %param.9) | copy-start | bytes 393220
  28.4 8.8 %collective-permute-start.4 = (bf16[4,2,128,512]{3,2,1,0:T(8,128)(2,1)S(1)}, bf16[4,2,128,512]{3,2,1,0:T(8,128)(2,1)S(1)}, u32[]{:S(2)}, u32[]{:S(2)}) collective-permute-start(bf16[4,2,128,512]{3,2,1,0:T(8,128)(2,1)S(1)} %maximum_select_fusion), channel_id=1, source_target_pairs={{0,2},{2,0},{4,6},{6,4},{8,10},{10,8},{12,14},{14,12},{16,18},{18,... | collective-permute-start | bytes 3145736 | tf_op jit(solution)/shard_map/ppermute | solution.py:41
  37.3 1.4 %copy-start = (bf16[9,2,128,512]{3,2,1,0:T(8,128)(2,1)}, bf16[9,2,128,512]{3,2,1,0:T(8,128)(2,1)S(1)}, u32[]{:S(2)}) copy-start(bf16[9,2,128,512]{3,2,1,0:T(8,128)(2,1)S(1)} %constant_dynamic-update-slice_fusion.value_ref) | copy-start | bytes 7077892
  74.7 6.5 %copy-start.1 = (bf16[128,2048]{1,0:T(8,128)(2,1)S(1)}, bf16[128,2048]{1,0:T(8,128)(2,1)}, u32[]{:S(2)}) copy-start(bf16[128,2048]{1,0:T(8,128)(2,1)} %shard_map.82) | copy-start | bytes 1572868
  79.6 14.3 %collective-permute-start.5 = (bf16[128,2048]{1,0:T(8,128)(2,1)S(1)}, bf16[128,2048]{1,0:T(8,128)(2,1)S(1)}, u32[]{:S(2)}, u32[]{:S(2)}) collective-permute-start(bf16[128,2048]{1,0:T(8,128)(2,1)S(1)} %fusion.7), channel_id=1, source_target_pairs={{0,1},{1,0},{2,3},{3,2},{4,5},{5,4},{6,7},{7,6},{8,9},{9,8},{10,11... | collective-permute-start | bytes 1572872 | tf_op jit(solution)/shard_map/ppermute | solution.py:130

commit v3 on v2

--- a/solution.py
+++ b/solution.py
@@ -9,21 +9,6 @@
 
 HEAD_SIZE = 128
 FAR = 1 << 20
-
-
-def rotate(block, positions):
-    count = block.shape[0]
-    heads = block.shape[1] // HEAD_SIZE
-    half = HEAD_SIZE // 2
-    pieces = block.astype(jnp.float32).reshape(count, heads, 2, half)
-    freqs = 500000.0 ** (-jnp.arange(half, dtype=jnp.float32) / half)
-    angles = positions.astype(jnp.float32)[:, None] * freqs[None, :]
-    cosine = jnp.cos(angles)[:, None, :]
-    sine = jnp.sin(angles)[:, None, :]
-    first = pieces[:, :, 0, :]
-    second = pieces[:, :, 1, :]
-    turned = jnp.stack([first * cosine - second * sine, second * cosine + first * sine], axis=2)
-    return turned.reshape(count, heads * HEAD_SIZE).astype(jnp.bfloat16)
 
 
 def gather_window(kv, n, window):
@@ -47,46 +32,71 @@
     return slots, shift
 
 
-def attention_kernel(query_pos_ref, key_limit_ref, query_ref, key_ref, value_ref, out_ref):
-    keys = key_ref[...]
-    values = value_ref[...].reshape(keys.shape[0], HEAD_SIZE)
+def turn(rows, cosine, sine):
+    rows = rows.astype(jnp.float32)
+    return (rows * cosine + pltpu.roll(rows, HEAD_SIZE // 2, 1) * sine).astype(jnp.bfloat16)
+
+
+def attention_kernel(
+    query_pos_ref, key_limit_ref, query_cos_ref, query_sin_ref, key_cos_ref, key_sin_ref,
+    query_ref, key_ref, value_ref, out_ref,
+):
+    count = key_ref.shape[0] * key_ref.shape[1]
+    keys = turn(key_ref[...].reshape(count, HEAD_SIZE), key_cos_ref[...], key_sin_ref[...])
+    values = value_ref[...].reshape(count, HEAD_SIZE)
     allowed = key_limit_ref[...] <= query_pos_ref[...]
     for g in range(query_ref.shape[1] // HEAD_SIZE):
         columns = slice(g * HEAD_SIZE, (g + 1) * HEAD_SIZE)
+        query = turn(query_ref[:, columns], query_cos_ref[...], query_sin_ref[...])
         scores = lax.dot_general(
-            query_ref[:, columns], keys, (((1,), (1,)), ((), ())), preferred_element_type=jnp.float32
+            query, keys, (((1,), (1,)), ((), ())), preferred_element_type=jnp.float32
         ) * (1.0 / math.sqrt(HEAD_SIZE))
         scores = jnp.where(allowed, scores, -1e30)
         highest = jnp.max(scores, axis=1, keepdims=True)
-        weights = jnp.where(allowed, jnp.exp(scores - highest), 0.0)
+        weights = jnp.exp(scores - highest)
         totals = jnp.sum(weights, axis=1, keepdims=True)
         summed = jnp.dot(weights.astype(jnp.bfloat16), values, preferred_element_type=jnp.float32)
         out_ref[:, columns] = (summed / totals).astype(out_ref.dtype)
 
 
-def attend(query_pos, key_limit, query_rows, key_rows, slots, heads_kv):
-    rows, width = query_rows.shape
-    count = key_rows.shape[0]
+def tables(positions):
+    half = HEAD_SIZE // 2
+    freqs = 500000.0 ** (-jnp.arange(half, dtype=jnp.float32) / half)
+    angles = positions.astype(jnp.float32)[:, None] * freqs[None, :]
+    cosine = jnp.cos(angles)
+    sine = jnp.sin(angles)
+    return jnp.concatenate([cosine, cosine], axis=1), jnp.concatenate([-sine, sine], axis=1)
+
+
+def attend(query_pos, key_pos, key_limit, queries, slots, heads_kv):
+    rows, width = queries.shape
+    n_slots, _, block, _ = slots.shape
+    count = n_slots * block
     group = width // heads_kv
-    n_slots = slots.shape[0]
-    flops = 4 * rows * count * width
+    query_cos, query_sin = tables(query_pos)
+    key_cos, key_sin = tables(key_pos)
+    whole = lambda h: (0, 0)
     return pl.pallas_call(
         attention_kernel,
         out_shape=jax.ShapeDtypeStruct((rows, width), jnp.bfloat16),
         grid=(heads_kv,),
         in_specs=[
-            pl.BlockSpec((rows, 1), lambda h: (0, 0)),
-            pl.BlockSpec((1, count), lambda h: (0, 0)),
+            pl.BlockSpec((rows, 1), whole),
+            pl.BlockSpec((1, count), whole),
+            pl.BlockSpec((rows, HEAD_SIZE), whole),
+            pl.BlockSpec((rows, HEAD_SIZE), whole),
+            pl.BlockSpec((count, HEAD_SIZE), whole),
+            pl.BlockSpec((count, HEAD_SIZE), whole),
             pl.BlockSpec((rows, group), lambda h: (0, h)),
-            pl.BlockSpec((count, HEAD_SIZE), lambda h: (0, h)),
-            pl.BlockSpec((n_slots, None, slots.shape[2], HEAD_SIZE), lambda h: (0, 1, 0, h)),
+            pl.BlockSpec((n_slots, None, block, HEAD_SIZE), lambda h: (0, 0, 0, h)),
+            pl.BlockSpec((n_slots, None, block, HEAD_SIZE), lambda h: (0, 1, 0, h)),
         ],
         out_specs=pl.BlockSpec((rows, group), lambda h: (0, h)),
         cost_estimate=pl.CostEstimate(
-            flops=flops, transcendentals=rows * count * width // HEAD_SIZE,
+            flops=4 * rows * count * width, transcendentals=rows * count * width // HEAD_SIZE,
             bytes_accessed=2 * (2 * rows * width + 2 * count * heads_kv * HEAD_SIZE),
         ),
-    )(query_pos, key_limit, query_rows, key_rows, slots)
+    )(query_pos.reshape(rows, 1), key_limit, query_cos, query_sin, key_cos, key_sin, queries, slots, slots)
 
 
 def on_device(queries, keys, values, out_weight, group_widths, pad_tokens):
@@ -114,12 +124,9 @@
     key_pos = ((group_index - shift - start) * rows_here)[:, None] + local_rows[None, :]
     key_pos = key_pos.reshape(-1)
 
-    count = slots.shape[0] * rows_here
-    query_rows = rotate(queries, query_pos)
-    key_rows = rotate(slots[:, 0].reshape(count, -1), key_pos)
     usable = (key_pos >= 0) & (key_pos < length)
-    key_limit = jnp.where(usable, key_pos, FAR * rows_here).reshape(1, count)
-    attended = attend(query_pos.reshape(rows_here, 1), key_limit, query_rows, key_rows, slots, heads_kv)
+    key_limit = jnp.where(usable, key_pos, FAR * rows_here).reshape(1, -1)
+    attended = attend(query_pos, key_pos, key_limit, queries, slots, heads_kv)
 
     n_tp = lax.axis_size("tp")
     if n_tp == 2:

time: 95.4 us -> 74.5 us (0.78)
  the two profiles are of different devices: /device:TPU:24 before, /device:TPU:0 now
where the time goes in v3:
time: 74.5 us; the launch traced here: 73.9 us
  other arithmetic  21.5 us (29%)
  starting transfers between devices  17.6 us (24%)
  Pallas kernels  9.7 us (13%)
  matrix products  9.5 us (13%)
  waiting for transfers between devices  7.69 us (10%)
  local copies, waits for them, and re-layouts  5.4 us (7%)
  between operations  2.52 us (3%)
    ppermute x4, starting transfers between devices, gather_window(): received.append(lax.ppermute(kv, 'ctx', pairs))  14.9 us
    pallas_call x1, Pallas kernels, attend(): pl.pallas_call(attention_kernel, out_shape=jax.ShapeDtypeStruct((rows, wi...  9.7 us
    ppermute x1, waiting for transfers between devices, on_device(): got = lax.ppermute(peer_terms.astype(jnp.bfloat16), 'tp', [(0, 1), (1, 0)])  7.67 us
    neg x2, other arithmetic, tables(): -sine  5.35 us
    unnamed x10, local copies, waits for them, and re-layouts  5.3 us
    dot_general x1, matrix products, on_device(): jnp.dot(attended, peer_weight, preferred_element_type=jnp.float32)  4.86 us
    dot_general x1, matrix products, on_device(): jnp.dot(attended, own_weight, preferred_element_type=jnp.float32)  4.64 us
    concatenate x2, other arithmetic, tables(): jnp.concatenate([cosine, cosine], axis=1)  4.36 us
  transfers between devices with their start and end apart: 6, of which 1 were waited for; matrix products, arithmetic and copies ran while one was open for 35% of the time, Pallas kernels for 0%

profile of v3, /device:TPU:0, one launch (start us, length us, event | category | flops | bytes accessed | tf_op | source)
XLA Modules:
  0.0 73.9 jit_solution(13801303925405542218)
XLA Ops:
  0.0 1.8 %fusion.19 = (bf16[1,2,128,512]{3,2,1,0:T(8,128)(2,1)}, bf16[2,128,512]{2,1,0:T(8,128)(2,1)}) fusion(bf16[1,128,512]{2,1,0:T(8,128)(2,1)} %bitcast.22, bf16[1,128,512]{2,1,0:T(8,128)(2,1)} %bitcast.24), kind=kLoop, calls=%fused_computation.46 | loop fusion | flops 131072 | bytes 786432 | tf_op jit(solution)/shard_map/broadcast_in_dim | solution.py:27
  1.8 1.3 %collective-permute-start = (bf16[2,128,512]{2,1,0:T(8,128)(2,1)}, bf16[2,128,512]{2,1,0:T(8,128)(2,1)}, u32[]{:S(2)}, u32[]{:S(2)}) collective-permute-start(bf16[2,128,512]{2,1,0:T(8,128)(2,1)} %get-tuple-element.6), channel_id=1, source_target_pairs={{2,4},{6,8},{10,12},{14,16},{18,20},{22,24},{26,28},{3,5},{7,9},{1... | collective-permute-start | bytes 786440 | tf_op jit(solution)/shard_map/ppermute | solution.py:21
  3.1 8.1 %collective-permute-start.1 = (bf16[2,128,512]{2,1,0:T(8,128)(2,1)}, bf16[2,128,512]{2,1,0:T(8,128)(2,1)}, u32[]{:S(2)}, u32[]{:S(2)}) collective-permute-start(bf16[2,128,512]{2,1,0:T(8,128)(2,1)} %get-tuple-element.6), channel_id=1, source_target_pairs={{0,6},{2,8},{4,10},{6,12},{8,14},{10,16},{12,18},{14,20},{16,22},{... | collective-permute-start | bytes 786440 | tf_op jit(solution)/shard_map/ppermute | solution.py:21
  11.2 2.0 %collective-permute-start.2 = (bf16[2,128,512]{2,1,0:T(8,128)(2,1)}, bf16[2,128,512]{2,1,0:T(8,128)(2,1)}, u32[]{:S(2)}, u32[]{:S(2)}) collective-permute-start(bf16[2,128,512]{2,1,0:T(8,128)(2,1)} %get-tuple-element.6), channel_id=1, source_target_pairs={{0,10},{2,12},{4,14},{6,16},{8,18},{10,20},{12,22},{14,24},{16,26}... | collective-permute-start | bytes 786440 | tf_op jit(solution)/shard_map/ppermute | solution.py:21
  13.2 3.6 %collective-permute-start.3 = (bf16[2,128,512]{2,1,0:T(8,128)(2,1)}, bf16[2,128,512]{2,1,0:T(8,128)(2,1)}, u32[]{:S(2)}, u32[]{:S(2)}) collective-permute-start(bf16[2,128,512]{2,1,0:T(8,128)(2,1)} %get-tuple-element.6), channel_id=1, source_target_pairs={{0,14},{2,16},{4,18},{6,20},{8,22},{10,24},{12,26},{14,28},{16,30}... | collective-permute-start | bytes 786440 | tf_op jit(solution)/shard_map/ppermute | solution.py:21
  16.7 1.0 %constant_dynamic-update-slice_fusion.5 = bf16[9,2,128,512]{3,2,1,0:T(8,128)(2,1)S(1)} fusion(bf16[1,128,512]{2,1,0:T(8,128)(2,1)} %bitcast.23, bf16[1,128,512]{2,1,0:T(8,128)(2,1)} %bitcast.25), kind=kLoop, calls=%fused_computation.26 | loop fusion | flops 524287 | bytes 524288
  21.5 1.3 %fusion.15 = s32[9]{0:T(128)S(1)} fusion(s32[9]{0:T(128)} %constant.44.clone, s32[9]{0:T(128)} %constant.45.clone, pred[]{:T(512)S(6)} %eq.14, s32[]{:T(128)} %select_reduce_fusion.3, s32[]{:T(128)S(6)} %axis_index.27), kind=kLoop, calls=%fused_computation.36 | loop fusion | flops 36 | bytes 117 | tf_op jit(solution)/shard_map/mul | solution.py:124
  22.9 1.3 %select_reduce_fusion.1 = (s32[]{:T(128)}, s32[]{:T(128)}) fusion(s32[8]{0:T(128)} %param.13, s32[]{:T(128)S(6)} %sub.24, s32[8]{0:T(128)} %param.12), kind=kLoop, calls=%fused_computation.40 | loop fusion | flops 38 | bytes 76 | tf_op jit(solution)/shard_map/reduce_sum | solution.py:120
  24.9 3.8 %fusion.10 = (f32[1152,64]{1,0:T(8,128)S(1)}, f32[1152,64]{1,0:T(8,128)S(1)}, f32[1152,64]{1,0:T(8,128)}) fusion(f32[64]{0:T(128)} %multiply_power_fusion, f32[1152]{0:T(1024)S(1)} %get-tuple-element.13), kind=kLoop, calls=%fused_computation.13 | loop fusion | flops 147456 | bytes 889600 | tf_op jit(solution)/shard_map/neg | solution.py:68
  28.6 1.6 %fusion.11 = (f32[128,64]{1,0:T(8,128)}, f32[128,64]{1,0:T(8,128)}, f32[128,64]{1,0:T(8,128)}) fusion(f32[64]{0:T(128)} %multiply_power_fusion, f32[128]{0:T(128)S(1)} %add_convert_fusion.1), kind=kLoop, calls=%fused_computation.19 | loop fusion | flops 16384 | bytes 99072 | tf_op jit(solution)/shard_map/neg | solution.py:68
  31.4 1.7 %pad_maximum_fusion.3 = (f32[128,128]{1,0:T(8,128)}, f32[128,128]{1,0:T(8,128)}) fusion(f32[128,64]{1,0:T(8,128)} %get-tuple-element.12, f32[128,64]{1,0:T(8,128)} %get-tuple-element.11, f32[128,64]{1,0:T(8,128)} %get-tuple-element.10), kind=kLoop, calls=%fused_computation.16 | loop fusion | flops 32768 | bytes 229376 | tf_op jit(solution)/shard_map/concatenate | solution.py:68
  33.1 2.6 %pad_maximum_fusion = (f32[1152,128]{1,0:T(8,128)}, f32[1152,128]{1,0:T(8,128)}) fusion(f32[1152,64]{1,0:T(8,128)} %get-tuple-element.9, f32[1152,64]{1,0:T(8,128)S(1)} %get-tuple-element.8, f32[1152,64]{1,0:T(8,128)S(1)} %get-tuple-element.7), kind=kLoop, calls=%fused_computation.10 | loop fusion | flops 294912 | bytes 2064384 | tf_op jit(solution)/shard_map/concatenate | solution.py:68
  35.8 1.6 %maximum_select_fusion = bf16[4,2,128,512]{3,2,1,0:T(8,128)(2,1)S(1)} fusion(bf16[1,2,128,512]{3,2,1,0:T(8,128)(2,1)} %bitcast.6, bf16[1,2,128,512]{3,2,1,0:T(8,128)(2,1)} %bitcast.5, bf16[1,2,128,512]{3,2,1,0:T(8,128)(2,1)} %bitcast.4, bf16[1,2,128,512]{3,2,1,0:T(8,128)(2,1)S(1)} %copy-done.2, bf16[1,2,128,512]{3,2,1,0:T(8,128)(2,1)} %bitcast.7, pred[]{:T(512)S(6)} %eq.14), kind=kLoop, calls=%fused_computation.6 | loop fusion | flops 3670016 | bytes 2359297 | tf_op jit(solution)/shard_map/jit(_where)/select_n | solution.py:25
  37.4 1.1 %collective-permute-start.4 = (bf16[4,2,128,512]{3,2,1,0:T(8,128)(2,1)S(1)}, bf16[4,2,128,512]{3,2,1,0:T(8,128)(2,1)S(1)}, u32[]{:S(2)}, u32[]{:S(2)}) collective-permute-start(bf16[4,2,128,512]{3,2,1,0:T(8,128)(2,1)S(1)} %maximum_select_fusion), channel_id=1, source_target_pairs={{0,2},{2,0},{4,6},{6,4},{8,10},{10,8},{12,14},{14,12},{16,18},{18,... | collective-permute-start | bytes 3145736 | tf_op jit(solution)/shard_map/ppermute | solution.py:26
  39.1 1.0 %constant_dynamic-update-slice_fusion.4 = bf16[9,2,128,512]{3,2,1,0:T(8,128)(2,1)S(1)} fusion(bf16[9,2,128,512]{3,2,1,0:T(8,128)(2,1)S(1)} %constant_dynamic-update-slice_fusion.5, bf16[2,128,512]{2,1,0:T(8,128)(2,1)} %collective-permute-done), kind=kLoop, calls=%fused_computation.25 | loop fusion | bytes 524288
  40.0 1.0 %constant_dynamic-update-slice_fusion.3 = bf16[9,2,128,512]{3,2,1,0:T(8,128)(2,1)S(1)} fusion(bf16[9,2,128,512]{3,2,1,0:T(8,128)(2,1)S(1)} %constant_dynamic-update-slice_fusion.4, bf16[2,128,512]{2,1,0:T(8,128)(2,1)} %collective-permute-done.1), kind=kLoop, calls=%fused_computation.24 | loop fusion | bytes 524288
  41.0 1.0 %constant_dynamic-update-slice_fusion.2 = bf16[9,2,128,512]{3,2,1,0:T(8,128)(2,1)S(1)} fusion(bf16[9,2,128,512]{3,2,1,0:T(8,128)(2,1)S(1)} %constant_dynamic-update-slice_fusion.3, bf16[2,128,512]{2,1,0:T(8,128)(2,1)} %collective-permute-done.2), kind=kLoop, calls=%fused_computation.23 | loop fusion | bytes 524288
  42.0 1.0 %constant_dynamic-update-slice_fusion.1 = bf16[9,2,128,512]{3,2,1,0:T(8,128)(2,1)S(1)} fusion(bf16[9,2,128,512]{3,2,1,0:T(8,128)(2,1)S(1)} %constant_dynamic-update-slice_fusion.2, bf16[2,128,512]{2,1,0:T(8,128)(2,1)} %collective-permute-done.3), kind=kLoop, calls=%fused_computation.22 | loop fusion | bytes 524288
  43.1 1.4 %copy-done = bf16[9,2,128,512]{3,2,1,0:T(8,128)(2,1)} copy-done((bf16[9,2,128,512]{3,2,1,0:T(8,128)(2,1)}, bf16[9,2,128,512]{3,2,1,0:T(8,128)(2,1)S(1)}, u32[]{:S(2)}) %copy-start) | copy-done | bytes 2359320
  44.5 9.7 %shard_map.82 = bf16[128,2048]{1,0:T(8,128)(2,1)} custom-call(s32[128,1]{1,0:T(8,128)} %iota_add_fusion.query_pos_ref, s32[1,1152]{1,0:T(1,128)} %and_select_fusion.key_limit_ref, f32[128,128]{1,0:T(8,128)} %get-tuple-element.17.query_cos_ref, f32[128,128]{1,0:T(8,128)} %get-tuple-element.18.query_sin_ref, f32[1152,128]{1,0:T(8,128)} %get-tuple-element.19.key_cos_ref, ...), custom_call_target="tpu_custom_call" | custom-call | flops 1207959552 | bytes 3407872 | tf_op jit(solution)/shard_map/pallas_call | solution.py:79
  54.2 4.9 %fusion.7 = bf16[128,2048]{1,0:T(8,128)(2,1)S(1)} fusion(bf16[128,2048]{1,0:T(8,128)(2,1)} %shard_map.82, bf16[2048,4096]{1,0:T(8,128)(2,1)} %param.11, s32[]{:T(128)S(6)} %select_n.65), kind=kOutput, calls=%fused_computation.5 | convolution fusion | flops 1074003968 | bytes 9437188 | tf_op jit(solution)/shard_map/dot_general | solution.py:136
  59.1 1.6 %collective-permute-start.5 = (bf16[128,2048]{1,0:T(8,128)(2,1)S(1)}, bf16[128,2048]{1,0:T(8,128)(2,1)S(1)}, u32[]{:S(2)}, u32[]{:S(2)}) collective-permute-start(bf16[128,2048]{1,0:T(8,128)(2,1)S(1)} %fusion.7), channel_id=1, source_target_pairs={{0,1},{1,0},{2,3},{3,2},{4,5},{5,4},{6,7},{7,6},{8,9},{9,8},{10,11... | collective-permute-start | bytes 1572872 | tf_op jit(solution)/shard_map/ppermute | solution.py:137
  60.7 4.6 %fusion.4 = bf16[128,2048]{1,0:T(8,128)(2,1)S(1)} fusion(bf16[128,2048]{1,0:T(8,128)(2,1)S(1)} %copy-done.1, bf16[2048,4096]{1,0:T(8,128)(2,1)} %param.11, s32[]{:T(128)S(6)} %select_n.64), kind=kOutput, calls=%fused_computation.4 | convolution fusion | flops 1074003968 | bytes 9437188 | tf_op jit(solution)/shard_map/dot_general | solution.py:139
  65.3 7.7 %collective-permute-done.5 = bf16[128,2048]{1,0:T(8,128)(2,1)S(1)} collective-permute-done((bf16[128,2048]{1,0:T(8,128)(2,1)S(1)}, bf16[128,2048]{1,0:T(8,128)(2,1)S(1)}, u32[]{:S(2)}, u32[]{:S(2)}) %collective-permute-start.5) | collective-permute-done | bytes 524320 | tf_op jit(solution)/shard_map/ppermute | solution.py:137
  (20 shorter events, 4.9 us)
Async XLA Ops:
  1.8 33.9 %collective-permute-start = (bf16[2,128,512]{2,1,0:T(8,128)(2,1)}, bf16[2,128,512]{2,1,0:T(8,128)(2,1)}, u32[]{:S(2)}, u32[]{:S(2)}) collective-permute-start(bf16[2,128,512]{2,1,0:T(8,128)(2,1)} %get-tuple-element.6), channel_id=1, source_target_pairs={{2,4},{6,8},{10,12},{14,16},{18,20},{22,24},{26,28},{3,5},{7,9},{1... | collective-permute-start | bytes 786440 | tf_op jit(solution)/shard_map/ppermute | solution.py:21
  3.1 32.6 %collective-permute-start.1 = (bf16[2,128,512]{2,1,0:T(8,128)(2,1)}, bf16[2,128,512]{2,1,0:T(8,128)(2,1)}, u32[]{:S(2)}, u32[]{:S(2)}) collective-permute-start(bf16[2,128,512]{2,1,0:T(8,128)(2,1)} %get-tuple-element.6), channel_id=1, source_target_pairs={{0,6},{2,8},{4,10},{6,12},{8,14},{10,16},{12,18},{14,20},{16,22},{... | collective-permute-start | bytes 786440 | tf_op jit(solution)/shard_map/ppermute | solution.py:21
  11.2 24.5 %collective-permute-start.2 = (bf16[2,128,512]{2,1,0:T(8,128)(2,1)}, bf16[2,128,512]{2,1,0:T(8,128)(2,1)}, u32[]{:S(2)}, u32[]{:S(2)}) collective-permute-start(bf16[2,128,512]{2,1,0:T(8,128)(2,1)} %get-tuple-element.6), channel_id=1, source_target_pairs={{0,10},{2,12},{4,14},{6,16},{8,18},{10,20},{12,22},{14,24},{16,26}... | collective-permute-start | bytes 786440 | tf_op jit(solution)/shard_map/ppermute | solution.py:21
  13.2 22.6 %collective-permute-start.3 = (bf16[2,128,512]{2,1,0:T(8,128)(2,1)}, bf16[2,128,512]{2,1,0:T(8,128)(2,1)}, u32[]{:S(2)}, u32[]{:S(2)}) collective-permute-start(bf16[2,128,512]{2,1,0:T(8,128)(2,1)} %get-tuple-element.6), channel_id=1, source_target_pairs={{0,14},{2,16},{4,18},{6,20},{8,22},{10,24},{12,26},{14,28},{16,30}... | collective-permute-start | bytes 786440 | tf_op jit(solution)/shard_map/ppermute | solution.py:21
  31.4 4.4 %copy-start.2 = (bf16[1,2,128,512]{3,2,1,0:T(8,128)(2,1)S(1)}, bf16[1,2,128,512]{3,2,1,0:T(8,128)(2,1)}, u32[]{:S(2)}) copy-start(bf16[1,2,128,512]{3,2,1,0:T(8,128)(2,1)} %get-tuple-element.5) | copy-start | bytes 786436
  37.4 5.6 %collective-permute-start.4 = (bf16[4,2,128,512]{3,2,1,0:T(8,128)(2,1)S(1)}, bf16[4,2,128,512]{3,2,1,0:T(8,128)(2,1)S(1)}, u32[]{:S(2)}, u32[]{:S(2)}) collective-permute-start(bf16[4,2,128,512]{3,2,1,0:T(8,128)(2,1)S(1)} %maximum_select_fusion), channel_id=1, source_target_pairs={{0,2},{2,0},{4,6},{6,4},{8,10},{10,8},{12,14},{14,12},{16,18},{18,... | collective-permute-start | bytes 3145736 | tf_op jit(solution)/shard_map/ppermute | solution.py:26
  43.1 1.4 %copy-start = (bf16[9,2,128,512]{3,2,1,0:T(8,128)(2,1)}, bf16[9,2,128,512]{3,2,1,0:T(8,128)(2,1)S(1)}, u32[]{:S(2)}) copy-start(bf16[9,2,128,512]{3,2,1,0:T(8,128)(2,1)S(1)} %constant_dynamic-update-slice_fusion.key_ref.value_ref) | copy-start | bytes 7077892
  54.2 6.5 %copy-start.1 = (bf16[128,2048]{1,0:T(8,128)(2,1)S(1)}, bf16[128,2048]{1,0:T(8,128)(2,1)}, u32[]{:S(2)}) copy-start(bf16[128,2048]{1,0:T(8,128)(2,1)} %shard_map.82) | copy-start | bytes 1572868
  59.1 13.9 %collective-permute-start.5 = (bf16[128,2048]{1,0:T(8,128)(2,1)S(1)}, bf16[128,2048]{1,0:T(8,128)(2,1)S(1)}, u32[]{:S(2)}, u32[]{:S(2)}) collective-permute-start(bf16[128,2048]{1,0:T(8,128)(2,1)S(1)} %fusion.7), channel_id=1, source_target_pairs={{0,1},{1,0},{2,3},{3,2},{4,5},{5,4},{6,7},{7,6},{8,9},{9,8},{10,11... | collective-permute-start | bytes 1572872 | tf_op jit(solution)/shard_map/ppermute | solution.py:137

commit v4 on v3

v4 whole, which is shorter than its diff:
```python
import functools
import math

import jax
import jax.numpy as jnp
from jax import lax
from jax.experimental import pallas as pl
from jax.experimental.pallas import tpu as pltpu
from jax.sharding import PartitionSpec as P

HEAD_SIZE = 128
FAR = 1 << 20


def gather_window(kv, n, window):
    received = []
    for s in range(1, window, 2):
        if s == 1:
            pairs = [(j, j + 1) for j in range(1, n - 1, 2)]
        else:
            pairs = [(j, j + s) for j in range(n - s)]
        received.append(lax.ppermute(kv, "ctx", pairs))
    across = [(j, j ^ 1) for j in range(n)]
    passed = [lax.ppermute(block, "ctx", across) for block in [kv] + received]
    half = window // 2
    even_shift = [0] + [2 * m + 1 for m in range(half)] + [FAR, FAR] + [2 * m for m in range(1, half)]
    odd_shift = [0, FAR] + [2 * m + 1 for m in range(1, half)] + [1] + [2 * m + 2 for m in range(half)]
    core = lax.axis_index("ctx") % 2
    shift = jnp.where(core == 0, jnp.array(even_shift, jnp.int32), jnp.array(odd_shift, jnp.int32))
    return [kv] + received + passed, shift


def turn(rows, cosine, sine):
    rows = rows.astype(jnp.float32)
    return (rows * cosine + pltpu.roll(rows, HEAD_SIZE // 2, 1) * sine).astype(jnp.bfloat16)


def attention_kernel(n_slots, project, peer_ref, query_pos_ref, key_limit_ref, query_cos_ref, query_sin_ref,
                     key_cos_ref, key_sin_ref, query_ref, *refs):
    key_refs = refs[:n_slots]
    value_refs = refs[n_slots:2 * n_slots]
    keys = turn(jnp.concatenate([r[...] for r in key_refs], axis=0), key_cos_ref[...], key_sin_ref[...])
    values = jnp.concatenate([r[...] for r in value_refs], axis=0)
    allowed = key_limit_ref[...] <= query_pos_ref[...]
    out_ref = refs[2 * n_slots + 1] if project else refs[2 * n_slots]
    for g in range(query_ref.shape[1] // HEAD_SIZE):
        columns = slice(g * HEAD_SIZE, (g + 1) * HEAD_SIZE)
        query = turn(query_ref[:, columns], query_cos_ref[...], query_sin_ref[...])
        scores = lax.dot_general(
            query, keys, (((1,), (1,)), ((), ())), preferred_element_type=jnp.float32
        ) * (1.0 / math.sqrt(HEAD_SIZE))
        scores = jnp.where(allowed, scores, -1e30)
        highest = jnp.max(scores, axis=1, keepdims=True)
        weights = jnp.exp(scores - highest)
        totals = jnp.sum(weights, axis=1, keepdims=True)
        summed = jnp.dot(weights.astype(jnp.bfloat16), values, preferred_element_type=jnp.float32)
        out_ref[:, columns] = (summed / totals).astype(out_ref.dtype)
    if project:
        weight_ref = refs[2 * n_slots]
        peer_out_ref, total_ref = refs[2 * n_slots + 2], refs[2 * n_slots + 3]
        step = pl.program_id(0)

        @pl.when(step == 0)
        def _():
            total_ref[...] = jnp.zeros_like(total_ref)

        total_ref[...] += jnp.dot(out_ref[...], weight_ref[...], preferred_element_type=jnp.float32)

        @pl.when(step == pl.num_programs(0) - 1)
        def _():
            peer_out_ref[...] = total_ref[...].astype(peer_out_ref.dtype)


def tables(positions):
    half = HEAD_SIZE // 2
    freqs = 500000.0 ** (-jnp.arange(half, dtype=jnp.float32) / half)
    angles = positions.astype(jnp.float32)[:, None] * freqs[None, :]
    cosine = jnp.cos(angles)
    sine = jnp.sin(angles)
    return jnp.concatenate([cosine, cosine], axis=1), jnp.concatenate([-sine, sine], axis=1)


def attend(query_pos, key_pos, key_limit, queries, slots, heads_kv, out_weight, peer):
    rows, width = queries.shape
    block = slots[0].shape[1]
    n_slots = len(slots)
    count = n_slots * block
    group = width // heads_kv
    project = out_weight is not None
    query_cos, query_sin = tables(query_pos)
    key_cos, key_sin = tables(key_pos)
    whole = lambda h, p: (0, 0)
    in_specs = [
        pl.BlockSpec((rows, 1), whole),
        pl.BlockSpec((1, count), whole),
        pl.BlockSpec((rows, HEAD_SIZE), whole),
        pl.BlockSpec((rows, HEAD_SIZE), whole),
        pl.BlockSpec((count, HEAD_SIZE), whole),
        pl.BlockSpec((count, HEAD_SIZE), whole),
        pl.BlockSpec((rows, group), lambda h, p: (0, h)),
    ]
    in_specs += [pl.BlockSpec((None, block, HEAD_SIZE), lambda h, p: (0, 0, h))] * n_slots
    in_specs += [pl.BlockSpec((None, block, HEAD_SIZE), lambda h, p: (1, 0, h))] * n_slots
    out_shape = [jax.ShapeDtypeStruct((rows, width), jnp.bfloat16)]
    out_specs = [pl.BlockSpec((rows, group), lambda h, p: (0, h))]
    scratch = []
    args = [peer.reshape(1), query_pos.reshape(rows, 1), key_limit, query_cos, query_sin, key_cos, key_sin,
            queries] + slots + slots
    flops = 4 * rows * count * width
    moved = 2 * (2 * rows * width + 2 * count * heads_kv * HEAD_SIZE)
    if project:
        part = out_weight.shape[1] // 2
        in_specs.append(pl.BlockSpec((group, part), lambda h, p: (h, p[0])))
        out_shape.append(jax.ShapeDtypeStruct((rows, part), jnp.bfloat16))
        out_specs.append(pl.BlockSpec((rows, part), whole))
        scratch.append(pltpu.VMEM((rows, part), jnp.float32))
        args.append(out_weight)
        flops += 2 * rows * width * part
        moved += 2 * (width * part + rows * part)
    return pl.pallas_call(
        functools.partial(attention_kernel, n_slots, project),
        out_shape=out_shape,
        grid_spec=pltpu.PrefetchScalarGridSpec(
            num_scalar_prefetch=1, grid=(heads_kv,), in_specs=in_specs, out_specs=out_specs,
            scratch_shapes=scratch,
        ),
        cost_estimate=pl.CostEstimate(
            flops=flops, transcendentals=rows * count * width // HEAD_SIZE, bytes_accessed=moved
        ),
    )(*args)


def on_device(queries, keys, values, out_weight, group_widths, pad_tokens):
    n = lax.axis_size("ctx")
    window = n // 2
    group_index = lax.axis_index("ctx")
    rows_here = queries.shape[0]
    heads_kv = keys.shape[1] // HEAD_SIZE
    context_group = queries.shape[1] // keys.shape[1]

    slots, shift = gather_window(jnp.stack([keys, values]), n, window)

    prompt_ids = jnp.arange(group_widths.shape[0], dtype=jnp.int32)
    offsets = jnp.sum(
        jnp.where(prompt_ids[None, :] < prompt_ids[:, None], group_widths[None, :], 0), axis=1
    )
    owner = jnp.sum((offsets <= group_index).astype(jnp.int32)) - 1
    picked = prompt_ids == owner
    start = jnp.sum(jnp.where(picked, offsets, 0))
    width = jnp.sum(jnp.where(picked, group_widths, 0))
    padding = jnp.sum(jnp.where(picked, pad_tokens, 0))
    length = width * rows_here - padding
    local_rows = jnp.arange(rows_here, dtype=jnp.int32)
    query_pos = (group_index - start) * rows_here + local_rows
    key_pos = ((group_index - shift - start) * rows_here)[:, None] + local_rows[None, :]
    key_pos = key_pos.reshape(-1)

    usable = (key_pos >= 0) & (key_pos < length)
    key_limit = jnp.where(usable, key_pos, FAR * rows_here).reshape(1, -1)

    n_tp = lax.axis_size("tp")
    if n_tp == 2:
        me = lax.axis_index("tp")
        attended, peer_terms = attend(
            query_pos, key_pos, key_limit, queries, slots, heads_kv, out_weight, 1 - me
        )
        got = lax.ppermute(peer_terms, "tp", [(0, 1), (1, 0)])
        part = out_weight.shape[1] // 2
        own_weight = lax.dynamic_slice_in_dim(out_weight, me * part, part, 1)
        own_terms = jnp.dot(attended, own_weight, preferred_element_type=jnp.float32)
        own_terms = lax.optimization_barrier(own_terms.astype(jnp.bfloat16)).astype(jnp.float32)
        return (own_terms + got.astype(jnp.float32)).astype(jnp.bfloat16)
    (attended,) = attend(query_pos, key_pos, key_limit, queries, slots, heads_kv, None, jnp.int32(0))
    terms = jnp.dot(attended, out_weight, preferred_element_type=jnp.float32)
    return lax.psum_scatter(terms.astype(jnp.bfloat16), "tp", scatter_dimension=1, tiled=True)


def solution(mesh):
    return jax.shard_map(
        on_device,
        mesh=mesh,
        in_specs=(P("ctx", "tp"), P("ctx", "tp"), P("ctx", "tp"), P("tp", None), P(), P()),
        out_specs=P("ctx", "tp"),
        check_vma=False,
    )
```

time: 74.5 us -> 66.1 us (0.89)
  the two profiles are of different devices: /device:TPU:0 before, /device:TPU:24 now
where the time goes in v4:
time: 66.1 us; the launch traced here: 65.7 us
  other arithmetic  16.7 us (25%)
  starting transfers between devices  16 us (24%)
  Pallas kernels  13.1 us (20%)
  waiting for transfers between devices  10.9 us (16%)
  matrix products  4.82 us (7%)
  between operations  2.77 us (4%)
  local copies, waits for them, and re-layouts  1.4 us (2%)
    pallas_call x1, Pallas kernels, attend(): pl.pallas_call(functools.partial(attention_kernel, n_slots, project), out...  13.1 us
    ppermute x5, starting transfers between devices, gather_window(): passed = [lax.ppermute(block, 'ctx', across) for block in [kv] + received]  8.32 us
    ppermute x1, waiting for transfers between devices, on_device(): got = lax.ppermute(peer_terms, 'tp', [(0, 1), (1, 0)])  7.68 us
    ppermute x4, starting transfers between devices, gather_window(): received.append(lax.ppermute(kv, 'ctx', pairs))  6.1 us
    dot_general x1, matrix products, on_device(): jnp.dot(attended, own_weight, preferred_element_type=jnp.float32)  4.82 us
    neg x2, other arithmetic, tables(): -sine  4.54 us
    concatenate x2, other arithmetic, tables(): jnp.concatenate([cosine, cosine], axis=1)  3.2 us
    ppermute x4, waiting for transfers between devices, gather_window(): received.append(lax.ppermute(kv, 'ctx', pairs))  3.17 us
  transfers between devices with their start and end apart: 10, of which 2 were waited for; matrix products, arithmetic and copies ran while one was open for 30% of the time, Pallas kernels for 0%

profile of v4, /device:TPU:24, one launch (start us, length us, event | category | flops | bytes accessed | tf_op | source)
XLA Modules:
  0.0 65.7 jit_solution(6269692774428890917)
XLA Ops:
  0.0 1.0 %pad_maximum_fusion.2.refs_0_.refs_10_ = bf16[2,128,512]{2,1,0:T(8,128)(2,1)S(1)} fusion(bf16[1,128,512]{2,1,0:T(8,128)(2,1)} %bitcast.11, bf16[1,128,512]{2,1,0:T(8,128)(2,1)} %bitcast.12), kind=kLoop, calls=%fused_computation.8 | loop fusion | flops 131072 | bytes 524288 | tf_op jit(solution)/shard_map/stack | solution.py:141
  1.0 1.3 %collective-permute-start = (bf16[2,128,512]{2,1,0:T(8,128)(2,1)S(1)}, bf16[2,128,512]{2,1,0:T(8,128)(2,1)S(1)}, u32[]{:S(2)}, u32[]{:S(2)}) collective-permute-start(bf16[2,128,512]{2,1,0:T(8,128)(2,1)S(1)} %pad_maximum_fusion.2.refs_0_.refs_10_), channel_id=1, source_target_pairs={{2,4},{6,8},{10,12},{14,16},{18,20},{22,24},{26,28},{3,5},{7,9},{1... | collective-permute-start | bytes 786440 | tf_op jit(solution)/shard_map/ppermute | solution.py:22
  2.3 2.2 %collective-permute-start.1 = (bf16[2,128,512]{2,1,0:T(8,128)(2,1)S(1)}, bf16[2,128,512]{2,1,0:T(8,128)(2,1)S(1)}, u32[]{:S(2)}, u32[]{:S(2)}) collective-permute-start(bf16[2,128,512]{2,1,0:T(8,128)(2,1)S(1)} %pad_maximum_fusion.2.refs_0_.refs_10_), channel_id=1, source_target_pairs={{0,6},{2,8},{4,10},{6,12},{8,14},{10,16},{12,18},{14,20},{16,22},{... | collective-permute-start | bytes 786440 | tf_op jit(solution)/shard_map/ppermute | solution.py:22
  4.5 1.3 %collective-permute-start.2 = (bf16[2,128,512]{2,1,0:T(8,128)(2,1)S(1)}, bf16[2,128,512]{2,1,0:T(8,128)(2,1)S(1)}, u32[]{:S(2)}, u32[]{:S(2)}) collective-permute-start(bf16[2,128,512]{2,1,0:T(8,128)(2,1)S(1)} %pad_maximum_fusion.2.refs_0_.refs_10_), channel_id=1, source_target_pairs={{0,10},{2,12},{4,14},{6,16},{8,18},{10,20},{12,22},{14,24},{16,26}... | collective-permute-start | bytes 786440 | tf_op jit(solution)/shard_map/ppermute | solution.py:22
  5.8 1.3 %collective-permute-start.3 = (bf16[2,128,512]{2,1,0:T(8,128)(2,1)S(1)}, bf16[2,128,512]{2,1,0:T(8,128)(2,1)S(1)}, u32[]{:S(2)}, u32[]{:S(2)}) collective-permute-start(bf16[2,128,512]{2,1,0:T(8,128)(2,1)S(1)} %pad_maximum_fusion.2.refs_0_.refs_10_), channel_id=1, source_target_pairs={{0,14},{2,16},{4,18},{6,20},{8,22},{10,24},{12,26},{14,28},{16,30}... | collective-permute-start | bytes 786440 | tf_op jit(solution)/shard_map/ppermute | solution.py:22
  7.1 1.4 %collective-permute-start.4 = (bf16[2,128,512]{2,1,0:T(8,128)(2,1)S(1)}, bf16[2,128,512]{2,1,0:T(8,128)(2,1)S(1)}, u32[]{:S(2)}, u32[]{:S(2)}) collective-permute-start(bf16[2,128,512]{2,1,0:T(8,128)(2,1)S(1)} %pad_maximum_fusion.2.refs_0_.refs_10_), channel_id=1, source_target_pairs={{0,2},{2,0},{4,6},{6,4},{8,10},{10,8},{12,14},{14,12},{16,18},{18,... | collective-permute-start | bytes 786440 | tf_op jit(solution)/shard_map/ppermute | solution.py:24
  9.0 0.8 %select_reduce_fusion = s32[8]{0:T(128)S(1)} fusion(s32[8]{0:T(128)} %param.12), kind=kLoop, calls=%fused_computation.20 | loop fusion | flops 184 | bytes 64 | tf_op jit(solution)/shard_map/reduce_sum | solution.py:144
  9.8 0.6 fusion.11
  11.1 0.6 select_reduce_fusion.3
  12.4 1.3 %fusion.10 = s32[10]{0:T(128)S(1)} fusion(s32[10]{0:T(128)} %constant.44.clone, s32[10]{0:T(128)} %constant.45.clone, pred[]{:T(512)S(6)} %eq.13, s32[]{:T(128)} %select_reduce_fusion.3, s32[]{:T(128)S(6)} %axis_index.29), kind=kLoop, calls=%fused_computation.26 | loop fusion | flops 40 | bytes 129 | tf_op jit(solution)/shard_map/mul | solution.py:155
  13.8 1.3 %select_reduce_fusion.1 = (s32[]{:T(128)}, s32[]{:T(128)}) fusion(s32[8]{0:T(128)} %param.13, s32[]{:T(128)S(6)} %sub.25, s32[8]{0:T(128)} %param.12), kind=kLoop, calls=%fused_computation.30 | loop fusion | flops 38 | bytes 76 | tf_op jit(solution)/shard_map/reduce_sum | solution.py:151
  16.3 3.0 %fusion.5 = (f32[1280,64]{1,0:T(8,128)S(1)}, f32[1280,64]{1,0:T(8,128)S(1)}, f32[1280,64]{1,0:T(8,128)S(1)}) fusion(f32[64]{0:T(128)} %multiply_power_fusion, f32[1280]{0:T(1024)S(1)} %get-tuple-element.15), kind=kLoop, calls=%fused_computation.9 | loop fusion | flops 163840 | bytes 988416 | tf_op jit(solution)/shard_map/neg | solution.py:80
  20.5 1.6 %fusion.6 = (f32[128,64]{1,0:T(8,128)}, f32[128,64]{1,0:T(8,128)}, f32[128,64]{1,0:T(8,128)}) fusion(f32[64]{0:T(128)} %multiply_power_fusion, f32[128]{0:T(128)} %add_convert_fusion.1), kind=kLoop, calls=%fused_computation.15 | loop fusion | flops 16384 | bytes 99072 | tf_op jit(solution)/shard_map/neg | solution.py:80
  22.1 0.6 iota_add_fusion.query_pos_ref
  22.7 1.7 %pad_maximum_fusion.3 = (f32[128,128]{1,0:T(8,128)}, f32[128,128]{1,0:T(8,128)}) fusion(f32[128,64]{1,0:T(8,128)} %get-tuple-element.14, f32[128,64]{1,0:T(8,128)} %get-tuple-element.13, f32[128,64]{1,0:T(8,128)} %get-tuple-element.12), kind=kLoop, calls=%fused_computation.12 | loop fusion | flops 32768 | bytes 229376 | tf_op jit(solution)/shard_map/concatenate | solution.py:80
  25.0 3.2 %collective-permute-done.2.refs_3_.refs_13_ = bf16[2,128,512]{2,1,0:T(8,128)(2,1)S(1)} collective-permute-done((bf16[2,128,512]{2,1,0:T(8,128)(2,1)S(1)}, bf16[2,128,512]{2,1,0:T(8,128)(2,1)S(1)}, u32[]{:S(2)}, u32[]{:S(2)}) %collective-permute-start.2) | collective-permute-done | bytes 262176 | tf_op jit(solution)/shard_map/ppermute | solution.py:22
  28.2 6.4 %collective-permute-start.8 = (bf16[2,128,512]{2,1,0:T(8,128)(2,1)S(1)}, bf16[2,128,512]{2,1,0:T(8,128)(2,1)S(1)}, u32[]{:S(2)}, u32[]{:S(2)}) collective-permute-start(bf16[2,128,512]{2,1,0:T(8,128)(2,1)S(1)} %collective-permute-done.3.refs_4_.refs_14_), channel_id=1, source_target_pairs={{0,2},{2,0},{4,6},{6,4},{8,10},{10,8},{12,14},{14,12},{16,18},{18,... | collective-permute-start | bytes 786440 | tf_op jit(solution)/shard_map/ppermute | solution.py:24
  34.6 1.5 %pad_maximum_fusion = (f32[1280,128]{1,0:T(8,128)}, f32[1280,128]{1,0:T(8,128)}) fusion(f32[1280,64]{1,0:T(8,128)S(1)} %get-tuple-element.11, f32[1280,64]{1,0:T(8,128)S(1)} %get-tuple-element.10, f32[1280,64]{1,0:T(8,128)S(1)} %get-tuple-element.9), kind=kLoop, calls=%fused_computation.6 | loop fusion | flops 327680 | bytes 2293760 | tf_op jit(solution)/shard_map/concatenate | solution.py:80
  36.2 0.7 %copy-done.6 = bf16[2,128,512]{2,1,0:T(8,128)(2,1)} copy-done((bf16[2,128,512]{2,1,0:T(8,128)(2,1)}, bf16[2,128,512]{2,1,0:T(8,128)(2,1)S(1)}, u32[]{:S(2)}) %copy-start.6) | copy-done | bytes 262168
  37.6 13.1 %shard_map.82 = (bf16[128,2048]{1,0:T(8,128)(2,1)}, bf16[128,2048]{1,0:T(8,128)(2,1)}) custom-call(s32[1]{0:T(128)} %bitcast.peer_ref, s32[128,1]{1,0:T(8,128)} %iota_add_fusion.query_pos_ref, s32[1,1280]{1,0:T(1,128)} %and_select_fusion.key_limit_ref, f32[128,128]{1,0:T(8,128)} %get-tuple-element.19.query_cos_ref, ...), custom_call_target="tpu_custom_call" | custom-call | flops 2415919104 | bytes 12582912 | tf_op jit(solution)/shard_map/pallas_call | solution.py:120
  50.7 1.6 %collective-permute-start.9 = (bf16[128,2048]{1,0:T(8,128)(2,1)}, bf16[128,2048]{1,0:T(8,128)(2,1)S(1)}, u32[]{:S(2)}, u32[]{:S(2)}) collective-permute-start(bf16[128,2048]{1,0:T(8,128)(2,1)} %get-tuple-element.8), channel_id=1, source_target_pairs={{0,1},{1,0},{2,3},{3,2},{4,5},{5,4},{6,7},{7,6},{8,9},{9,8},{10,11... | collective-permute-start | bytes 1572872 | tf_op jit(solution)/shard_map/ppermute | solution.py:167
  52.3 4.8 %fusion.2 = bf16[128,2048]{1,0:T(8,128)(2,1)S(1)} fusion(bf16[128,2048]{1,0:T(8,128)(2,1)} %get-tuple-element.7, bf16[2048,4096]{1,0:T(8,128)(2,1)} %refs_20_.1, s32[]{:T(128)S(6)} %select_n.51), kind=kOutput, calls=%fused_computation.2 | convolution fusion | flops 1074003968 | bytes 9437188 | tf_op jit(solution)/shard_map/dot_general | solution.py:170
  57.1 7.7 %collective-permute-done.9 = bf16[128,2048]{1,0:T(8,128)(2,1)S(1)} collective-permute-done((bf16[128,2048]{1,0:T(8,128)(2,1)}, bf16[128,2048]{1,0:T(8,128)(2,1)S(1)}, u32[]{:S(2)}, u32[]{:S(2)}) %collective-permute-start.9) | collective-permute-done | bytes 524320 | tf_op jit(solution)/shard_map/ppermute | solution.py:167
  64.8 0.9 %add_convert_fusion = bf16[128,2048]{1,0:T(8,128)(2,1)} fusion(bf16[128,2048]{1,0:T(8,128)(2,1)S(1)} %collective-permute-done.9, bf16[128,2048]{1,0:T(8,128)(2,1)S(1)} %fusion.2), kind=kLoop, calls=%fused_computation.3 | loop fusion | flops 1048576 | bytes 1572864 | tf_op jit(solution)/shard_map/convert_element_type | solution.py:172
  (34 shorter events, 3.0 us)
Async XLA Ops:
  1.0 36.5 %copy-start = (bf16[2,128,512]{2,1,0:T(8,128)(2,1)}, bf16[2,128,512]{2,1,0:T(8,128)(2,1)S(1)}, u32[]{:S(2)}) copy-start(bf16[2,128,512]{2,1,0:T(8,128)(2,1)S(1)} %pad_maximum_fusion.2.refs_0_.refs_10_) | copy-start | bytes 786436
  1.0 23.4 %collective-permute-start = (bf16[2,128,512]{2,1,0:T(8,128)(2,1)S(1)}, bf16[2,128,512]{2,1,0:T(8,128)(2,1)S(1)}, u32[]{:S(2)}, u32[]{:S(2)}) collective-permute-start(bf16[2,128,512]{2,1,0:T(8,128)(2,1)S(1)} %pad_maximum_fusion.2.refs_0_.refs_10_), channel_id=1, source_target_pairs={{2,4},{6,8},{10,12},{14,16},{18,20},{22,24},{26,28},{3,5},{7,9},{1... | collective-permute-start | bytes 786440 | tf_op jit(solution)/shard_map/ppermute | solution.py:22
  2.3 22.2 %collective-permute-start.1 = (bf16[2,128,512]{2,1,0:T(8,128)(2,1)S(1)}, bf16[2,128,512]{2,1,0:T(8,128)(2,1)S(1)}, u32[]{:S(2)}, u32[]{:S(2)}) collective-permute-start(bf16[2,128,512]{2,1,0:T(8,128)(2,1)S(1)} %pad_maximum_fusion.2.refs_0_.refs_10_), channel_id=1, source_target_pairs={{0,6},{2,8},{4,10},{6,12},{8,14},{10,16},{12,18},{14,20},{16,22},{... | collective-permute-start | bytes 786440 | tf_op jit(solution)/shard_map/ppermute | solution.py:22
  4.5 23.6 %collective-permute-start.2 = (bf16[2,128,512]{2,1,0:T(8,128)(2,1)S(1)}, bf16[2,128,512]{2,1,0:T(8,128)(2,1)S(1)}, u32[]{:S(2)}, u32[]{:S(2)}) collective-permute-start(bf16[2,128,512]{2,1,0:T(8,128)(2,1)S(1)} %pad_maximum_fusion.2.refs_0_.refs_10_), channel_id=1, source_target_pairs={{0,10},{2,12},{4,14},{6,16},{8,18},{10,20},{12,22},{14,24},{16,26}... | collective-permute-start | bytes 786440 | tf_op jit(solution)/shard_map/ppermute | solution.py:22
  5.8 22.3 %collective-permute-start.3 = (bf16[2,128,512]{2,1,0:T(8,128)(2,1)S(1)}, bf16[2,128,512]{2,1,0:T(8,128)(2,1)S(1)}, u32[]{:S(2)}, u32[]{:S(2)}) collective-permute-start(bf16[2,128,512]{2,1,0:T(8,128)(2,1)S(1)} %pad_maximum_fusion.2.refs_0_.refs_10_), channel_id=1, source_target_pairs={{0,14},{2,16},{4,18},{6,20},{8,22},{10,24},{12,26},{14,28},{16,30}... | collective-permute-start | bytes 786440 | tf_op jit(solution)/shard_map/ppermute | solution.py:22
  7.1 28.9 %collective-permute-start.4 = (bf16[2,128,512]{2,1,0:T(8,128)(2,1)S(1)}, bf16[2,128,512]{2,1,0:T(8,128)(2,1)S(1)}, u32[]{:S(2)}, u32[]{:S(2)}) collective-permute-start(bf16[2,128,512]{2,1,0:T(8,128)(2,1)S(1)} %pad_maximum_fusion.2.refs_0_.refs_10_), channel_id=1, source_target_pairs={{0,2},{2,0},{4,6},{6,4},{8,10},{10,8},{12,14},{14,12},{16,18},{18,... | collective-permute-start | bytes 786440 | tf_op jit(solution)/shard_map/ppermute | solution.py:24
  24.4 13.1 %copy-start.1 = (bf16[2,128,512]{2,1,0:T(8,128)(2,1)}, bf16[2,128,512]{2,1,0:T(8,128)(2,1)S(1)}, u32[]{:S(2)}) copy-start(bf16[2,128,512]{2,1,0:T(8,128)(2,1)S(1)} %collective-permute-done.refs_1_.refs_11_) | copy-start | bytes 786436
  24.4 11.6 %collective-permute-start.5 = (bf16[2,128,512]{2,1,0:T(8,128)(2,1)S(1)}, bf16[2,128,512]{2,1,0:T(8,128)(2,1)S(1)}, u32[]{:S(2)}, u32[]{:S(2)}) collective-permute-start(bf16[2,128,512]{2,1,0:T(8,128)(2,1)S(1)} %collective-permute-done.refs_1_.refs_11_), channel_id=1, source_target_pairs={{0,2},{2,0},{4,6},{6,4},{8,10},{10,8},{12,14},{14,12},{16,18},{18,... | collective-permute-start | bytes 786440 | tf_op jit(solution)/shard_map/ppermute | solution.py:24
  24.5 13.0 %copy-start.2 = (bf16[2,128,512]{2,1,0:T(8,128)(2,1)}, bf16[2,128,512]{2,1,0:T(8,128)(2,1)S(1)}, u32[]{:S(2)}) copy-start(bf16[2,128,512]{2,1,0:T(8,128)(2,1)S(1)} %collective-permute-done.1.refs_2_.refs_12_) | copy-start | bytes 786436
  24.5 11.6 %collective-permute-start.6 = (bf16[2,128,512]{2,1,0:T(8,128)(2,1)S(1)}, bf16[2,128,512]{2,1,0:T(8,128)(2,1)S(1)}, u32[]{:S(2)}, u32[]{:S(2)}) collective-permute-start(bf16[2,128,512]{2,1,0:T(8,128)(2,1)S(1)} %collective-permute-done.1.refs_2_.refs_12_), channel_id=1, source_target_pairs={{0,2},{2,0},{4,6},{6,4},{8,10},{10,8},{12,14},{14,12},{16,18},{18,... | collective-permute-start | bytes 786440 | tf_op jit(solution)/shard_map/ppermute | solution.py:24
  28.2 9.4 %copy-start.3 = (bf16[2,128,512]{2,1,0:T(8,128)(2,1)}, bf16[2,128,512]{2,1,0:T(8,128)(2,1)S(1)}, u32[]{:S(2)}) copy-start(bf16[2,128,512]{2,1,0:T(8,128)(2,1)S(1)} %collective-permute-done.2.refs_3_.refs_13_) | copy-start | bytes 786436
  28.2 7.9 %collective-permute-start.7 = (bf16[2,128,512]{2,1,0:T(8,128)(2,1)S(1)}, bf16[2,128,512]{2,1,0:T(8,128)(2,1)S(1)}, u32[]{:S(2)}, u32[]{:S(2)}) collective-permute-start(bf16[2,128,512]{2,1,0:T(8,128)(2,1)S(1)} %collective-permute-done.2.refs_3_.refs_13_), channel_id=1, source_target_pairs={{0,2},{2,0},{4,6},{6,4},{8,10},{10,8},{12,14},{14,12},{16,18},{18,... | collective-permute-start | bytes 786440 | tf_op jit(solution)/shard_map/ppermute | solution.py:24
  28.2 9.4 %copy-start.4 = (bf16[2,128,512]{2,1,0:T(8,128)(2,1)}, bf16[2,128,512]{2,1,0:T(8,128)(2,1)S(1)}, u32[]{:S(2)}) copy-start(bf16[2,128,512]{2,1,0:T(8,128)(2,1)S(1)} %collective-permute-done.3.refs_4_.refs_14_) | copy-start | bytes 786436
  28.2 8.0 %collective-permute-start.8 = (bf16[2,128,512]{2,1,0:T(8,128)(2,1)S(1)}, bf16[2,128,512]{2,1,0:T(8,128)(2,1)S(1)}, u32[]{:S(2)}, u32[]{:S(2)}) collective-permute-start(bf16[2,128,512]{2,1,0:T(8,128)(2,1)S(1)} %collective-permute-done.3.refs_4_.refs_14_), channel_id=1, source_target_pairs={{0,2},{2,0},{4,6},{6,4},{8,10},{10,8},{12,14},{14,12},{16,18},{18,... | collective-permute-start | bytes 786440 | tf_op jit(solution)/shard_map/ppermute | solution.py:24
  36.1 1.5 %copy-start.5 = (bf16[2,128,512]{2,1,0:T(8,128)(2,1)}, bf16[2,128,512]{2,1,0:T(8,128)(2,1)S(1)}, u32[]{:S(2)}) copy-start(bf16[2,128,512]{2,1,0:T(8,128)(2,1)S(1)} %collective-permute-done.4.refs_5_.refs_15_) | copy-start | bytes 786436
  36.1 0.7 %copy-start.6 = (bf16[2,128,512]{2,1,0:T(8,128)(2,1)}, bf16[2,128,512]{2,1,0:T(8,128)(2,1)S(1)}, u32[]{:S(2)}) copy-start(bf16[2,128,512]{2,1,0:T(8,128)(2,1)S(1)} %collective-permute-done.5.refs_6_.refs_16_) | copy-start | bytes 786436
  36.1 0.8 %copy-start.7 = (bf16[2,128,512]{2,1,0:T(8,128)(2,1)}, bf16[2,128,512]{2,1,0:T(8,128)(2,1)S(1)}, u32[]{:S(2)}) copy-start(bf16[2,128,512]{2,1,0:T(8,128)(2,1)S(1)} %collective-permute-done.6.refs_7_.refs_17_) | copy-start | bytes 786436
  36.1 0.9 %copy-start.8 = (bf16[2,128,512]{2,1,0:T(8,128)(2,1)}, bf16[2,128,512]{2,1,0:T(8,128)(2,1)S(1)}, u32[]{:S(2)}) copy-start(bf16[2,128,512]{2,1,0:T(8,128)(2,1)S(1)} %collective-permute-done.7.refs_8_.refs_18_) | copy-start | bytes 786436
  36.8 0.7 %copy-start.9 = (bf16[2,128,512]{2,1,0:T(8,128)(2,1)}, bf16[2,128,512]{2,1,0:T(8,128)(2,1)S(1)}, u32[]{:S(2)}) copy-start(bf16[2,128,512]{2,1,0:T(8,128)(2,1)S(1)} %collective-permute-done.8.refs_9_.refs_19_) | copy-start | bytes 786436
  50.7 14.1 %collective-permute-start.9 = (bf16[128,2048]{1,0:T(8,128)(2,1)}, bf16[128,2048]{1,0:T(8,128)(2,1)S(1)}, u32[]{:S(2)}, u32[]{:S(2)}) collective-permute-start(bf16[128,2048]{1,0:T(8,128)(2,1)} %get-tuple-element.8), channel_id=1, source_target_pairs={{0,1},{1,0},{2,3},{3,2},{4,5},{5,4},{6,7},{7,6},{8,9},{9,8},{10,11... | collective-permute-start | bytes 1572872 | tf_op jit(solution)/shard_map/ppermute | solution.py:167

commit v5 on v4

v5 whole, which is shorter than its diff:
```python
import functools
import math

import jax
import jax.numpy as jnp
from jax import lax
from jax.experimental import pallas as pl
from jax.experimental.pallas import tpu as pltpu
from jax.sharding import PartitionSpec as P

HEAD_SIZE = 128
FAR = 1 << 20


def gather_window(kv, n, window):
    half = window // 2
    received = [None] * half
    for m in reversed(range(half)):
        s = 2 * m + 1
        if s == 1:
            pairs = [(j, j + 1) for j in range(1, n - 1, 2)]
        else:
            pairs = [(j, j + s) for j in range(n - s)]
        received[m] = lax.ppermute(kv, "ctx", pairs)
    up = [(j, j + 1) for j in range(0, n, 2)]
    down = [(j + 1, j) for j in range(0, n, 2)]
    passed = [lax.ppermute(kv, "ctx", up)]
    for m in range(half):
        pairs = (up if m < half - 1 else []) + (down if m > 0 else [])
        passed.append(lax.ppermute(received[m], "ctx", pairs))
    slots = [kv] + received + passed
    even_use = [0] + [1 + m for m in range(half)] + [2 + half + m for m in range(1, half)]
    odd_use = [0] + [1 + m for m in range(1, half)] + [1 + half] + [2 + half + m for m in range(half - 1)]
    even_shift = [0] + [2 * m + 1 for m in range(half)] + [2 * m for m in range(1, half)]
    odd_shift = [0] + [2 * m + 1 for m in range(1, half)] + [1] + [2 * m + 2 for m in range(half - 1)]
    core = lax.axis_index("ctx") % 2
    shift = jnp.where(core == 0, jnp.array(even_shift, jnp.int32), jnp.array(odd_shift, jnp.int32))
    return slots, (even_use, odd_use), shift


def turn(rows, cosine, sine):
    rows = rows.astype(jnp.float32)
    return (rows * cosine + pltpu.roll(rows, HEAD_SIZE // 2, 1) * sine).astype(jnp.bfloat16)


def attention_kernel(n_slots, uses, project, peer_ref, core_ref, query_pos_ref, key_limit_ref, query_cos_ref,
                     query_sin_ref, key_cos_ref, key_sin_ref, query_ref, *refs):
    key_refs = refs[:n_slots]
    value_refs = refs[n_slots:2 * n_slots]
    out_ref = refs[2 * n_slots + 1] if project else refs[2 * n_slots]

    def attend_with(use):
        keys = turn(jnp.concatenate([key_refs[j][...] for j in use], axis=0), key_cos_ref[...], key_sin_ref[...])
        values = jnp.concatenate([value_refs[j][...] for j in use], axis=0)
        allowed = key_limit_ref[...] <= query_pos_ref[...]
        for g in range(query_ref.shape[1] // HEAD_SIZE):
            columns = slice(g * HEAD_SIZE, (g + 1) * HEAD_SIZE)
            query = turn(query_ref[:, columns], query_cos_ref[...], query_sin_ref[...])
            scores = lax.dot_general(
                query, keys, (((1,), (1,)), ((), ())), preferred_element_type=jnp.float32
            ) * (1.0 / math.sqrt(HEAD_SIZE))
            scores = jnp.where(allowed, scores, -1e30)
            highest = jnp.max(scores, axis=1, keepdims=True)
            weights = jnp.exp(scores - highest)
            totals = jnp.sum(weights, axis=1, keepdims=True)
            summed = jnp.dot(weights.astype(jnp.bfloat16), values, preferred_element_type=jnp.float32)
            out_ref[:, columns] = (summed / totals).astype(out_ref.dtype)

    for parity, use in enumerate(uses):
        pl.when(core_ref[0] == parity)(functools.partial(attend_with, use))
    if project:
        weight_ref = refs[2 * n_slots]
        peer_out_ref, total_ref = refs[2 * n_slots + 2], refs[2 * n_slots + 3]
        step = pl.program_id(0)

        @pl.when(step == 0)
        def _():
            total_ref[...] = jnp.zeros_like(total_ref)

        total_ref[...] += jnp.dot(out_ref[...], weight_ref[...], preferred_element_type=jnp.float32)

        @pl.when(step == pl.num_programs(0) - 1)
        def _():
            peer_out_ref[...] = total_ref[...].astype(peer_out_ref.dtype)


def tables(positions):
    half = HEAD_SIZE // 2
    freqs = 500000.0 ** (-jnp.arange(half, dtype=jnp.float32) / half)
    angles = positions.astype(jnp.float32)[:, None] * freqs[None, :]
    cosine = jnp.cos(angles)
    sine = jnp.sin(angles)
    return jnp.concatenate([cosine, cosine], axis=1), jnp.concatenate([-sine, sine], axis=1)


def attend(query_pos, key_pos, key_limit, queries, slots, uses, heads_kv, out_weight, peer):
    rows, width = queries.shape
    block = slots[0].shape[1]
    n_slots = len(slots)
    count = len(uses[0]) * block
    group = width // heads_kv
    project = out_weight is not None
    query_cos, query_sin = tables(query_pos)
    key_cos, key_sin = tables(key_pos)
    whole = lambda h, p, c: (0, 0)
    in_specs = [
        pl.BlockSpec((rows, 1), whole),
        pl.BlockSpec((1, count), whole),
        pl.BlockSpec((rows, HEAD_SIZE), whole),
        pl.BlockSpec((rows, HEAD_SIZE), whole),
        pl.BlockSpec((count, HEAD_SIZE), whole),
        pl.BlockSpec((count, HEAD_SIZE), whole),
        pl.BlockSpec((rows, group), lambda h, p, c: (0, h)),
    ]
    in_specs += [pl.BlockSpec((None, block, HEAD_SIZE), lambda h, p, c: (0, 0, h))] * n_slots
    in_specs += [pl.BlockSpec((None, block, HEAD_SIZE), lambda h, p, c: (1, 0, h))] * n_slots
    out_shape = [jax.ShapeDtypeStruct((rows, width), jnp.bfloat16)]
    out_specs = [pl.BlockSpec((rows, group), lambda h, p, c: (0, h))]
    scratch = []
    core = (lax.axis_index("ctx") % 2).astype(jnp.int32)
    args = [peer.reshape(1), core.reshape(1), query_pos.reshape(rows, 1), key_limit, query_cos, query_sin, key_cos, key_sin,
            queries] + slots + slots
    flops = 4 * rows * count * width
    moved = 2 * (2 * rows * width + 2 * count * heads_kv * HEAD_SIZE)
    if project:
        part = out_weight.shape[1] // 2
        in_specs.append(pl.BlockSpec((group, part), lambda h, p, c: (h, p[0])))
        out_shape.append(jax.ShapeDtypeStruct((rows, part), jnp.bfloat16))
        out_specs.append(pl.BlockSpec((rows, part), whole))
        scratch.append(pltpu.VMEM((rows, part), jnp.float32))
        args.append(out_weight)
        flops += 2 * rows * width * part
        moved += 2 * (width * part + rows * part)
    return pl.pallas_call(
        functools.partial(attention_kernel, n_slots, uses, project),
        out_shape=out_shape,
        grid_spec=pltpu.PrefetchScalarGridSpec(
            num_scalar_prefetch=2, grid=(heads_kv,), in_specs=in_specs, out_specs=out_specs,
            scratch_shapes=scratch,
        ),
        cost_estimate=pl.CostEstimate(
            flops=flops, transcendentals=rows * count * width // HEAD_SIZE, bytes_accessed=moved
        ),
    )(*args)


def on_device(queries, keys, values, out_weight, group_widths, pad_tokens):
    n = lax.axis_size("ctx")
    window = n // 2
    group_index = lax.axis_index("ctx")
    rows_here = queries.shape[0]
    heads_kv = keys.shape[1] // HEAD_SIZE
    context_group = queries.shape[1] // keys.shape[1]

    slots, uses, shift = gather_window(jnp.stack([keys, values]), n, window)

    prompt_ids = jnp.arange(group_widths.shape[0], dtype=jnp.int32)
    offsets = jnp.sum(
        jnp.where(prompt_ids[None, :] < prompt_ids[:, None], group_widths[None, :], 0), axis=1
    )
    owner = jnp.sum((offsets <= group_index).astype(jnp.int32)) - 1
    picked = prompt_ids == owner
    start = jnp.sum(jnp.where(picked, offsets, 0))
    width = jnp.sum(jnp.where(picked, group_widths, 0))
    padding = jnp.sum(jnp.where(picked, pad_tokens, 0))
    length = width * rows_here - padding
    local_rows = jnp.arange(rows_here, dtype=jnp.int32)
    query_pos = (group_index - start) * rows_here + local_rows
    key_pos = ((group_index - shift - start) * rows_here)[:, None] + local_rows[None, :]
    key_pos = key_pos.reshape(-1)

    usable = (key_pos >= 0) & (key_pos < length)
    key_limit = jnp.where(usable, key_pos, FAR * rows_here).reshape(1, -1)

    n_tp = lax.axis_size("tp")
    if n_tp == 2:
        me = lax.axis_index("tp")
        attended, peer_terms = attend(
            query_pos, key_pos, key_limit, queries, slots, uses, heads_kv, out_weight, 1 - me
        )
        got = lax.ppermute(peer_terms, "tp", [(0, 1), (1, 0)])
        part = out_weight.shape[1] // 2
        own_weight = lax.dynamic_slice_in_dim(out_weight, me * part, part, 1)
        own_terms = jnp.dot(attended, own_weight, preferred_element_type=jnp.float32)
        own_terms = lax.optimization_barrier(own_terms.astype(jnp.bfloat16)).astype(jnp.float32)
        return (own_terms + got.astype(jnp.float32)).astype(jnp.bfloat16)
    (attended,) = attend(query_pos, key_pos, key_limit, queries, slots, uses, heads_kv, None, jnp.int32(0))
    terms = jnp.dot(attended, out_weight, preferred_element_type=jnp.float32)
    return lax.psum_scatter(terms.astype(jnp.bfloat16), "tp", scatter_dimension=1, tiled=True)


def solution(mesh):
    return jax.shard_map(
        on_device,
        mesh=mesh,
        in_specs=(P("ctx", "tp"), P("ctx", "tp"), P("ctx", "tp"), P("tp", None), P(), P()),
        out_specs=P("ctx", "tp"),
        check_vma=False,
    )
```

time: 66.1 us -> 67.5 us (1.021)
  the two profiles are of different devices: /device:TPU:24 before, /device:TPU:11 now
where the time goes in v5:
time: 67.5 us; the launch traced here: 67.1 us
  starting transfers between devices  20.9 us (31%)
  waiting for transfers between devices  13.1 us (19%)
  other arithmetic  12.2 us (18%)
  Pallas kernels  12.2 us (18%)
  matrix products  4.82 us (7%)
  between operations  2.85 us (4%)
  local copies, waits for them, and re-layouts  0.98 us (1%)
    pallas_call x1, Pallas kernels, attend(): pl.pallas_call(functools.partial(attention_kernel, n_slots, uses, project...  12.2 us
    ppermute x4, starting transfers between devices, gather_window(): received[m] = lax.ppermute(kv, 'ctx', pairs)  10.2 us
    ppermute x4, starting transfers between devices, gather_window(): passed.append(lax.ppermute(received[m], 'ctx', pairs))  8.1 us
    ppermute x1, waiting for transfers between devices, on_device(): got = lax.ppermute(peer_terms, 'tp', [(0, 1), (1, 0)])  7.84 us
    ppermute x4, waiting for transfers between devices, gather_window(): received[m] = lax.ppermute(kv, 'ctx', pairs)  5.27 us
    dot_general x1, matrix products, on_device(): jnp.dot(attended, own_weight, preferred_element_type=jnp.float32)  4.82 us
    neg x2, other arithmetic, tables(): -sine  2.21 us
    concatenate x2, other arithmetic, tables(): jnp.concatenate([cosine, cosine], axis=1)  2.08 us
  transfers between devices with their start and end apart: 10, of which 3 were waited for; matrix products, arithmetic and copies ran while one was open for 23% of the time, Pallas kernels for 0%

profile of v5, /device:TPU:11, one launch (start us, length us, event | category | flops | bytes accessed | tf_op | source)
XLA Modules:
  0.0 67.1 jit_solution(12732592125764905721)
XLA Ops:
  0.0 1.0 %pad_maximum_fusion.2.refs_0_.refs_10_ = bf16[2,128,512]{2,1,0:T(8,128)(2,1)S(1)} fusion(bf16[1,128,512]{2,1,0:T(8,128)(2,1)} %bitcast.8, bf16[1,128,512]{2,1,0:T(8,128)(2,1)} %bitcast.9), kind=kLoop, calls=%fused_computation.8 | loop fusion | flops 131072 | bytes 524288 | tf_op jit(solution)/shard_map/stack | solution.py:155
  1.0 3.7 %collective-permute-start = (bf16[2,128,512]{2,1,0:T(8,128)(2,1)S(1)}, bf16[2,128,512]{2,1,0:T(8,128)(2,1)S(1)}, u32[]{:S(2)}, u32[]{:S(2)}) collective-permute-start(bf16[2,128,512]{2,1,0:T(8,128)(2,1)S(1)} %pad_maximum_fusion.2.refs_0_.refs_10_), channel_id=1, source_target_pairs={{2,4},{6,8},{10,12},{14,16},{18,20},{22,24},{26,28},{3,5},{7,9},{1... | collective-permute-start | bytes 786440 | tf_op jit(solution)/shard_map/ppermute | solution.py:24
  4.8 1.9 %collective-permute-start.1 = (bf16[2,128,512]{2,1,0:T(8,128)(2,1)S(1)}, bf16[2,128,512]{2,1,0:T(8,128)(2,1)S(1)}, u32[]{:S(2)}, u32[]{:S(2)}) collective-permute-start(bf16[2,128,512]{2,1,0:T(8,128)(2,1)S(1)} %pad_maximum_fusion.2.refs_0_.refs_10_), channel_id=1, source_target_pairs={{0,6},{2,8},{4,10},{6,12},{8,14},{10,16},{12,18},{14,20},{16,22},{... | collective-permute-start | bytes 786440 | tf_op jit(solution)/shard_map/ppermute | solution.py:24
  6.7 2.6 %collective-permute-start.2 = (bf16[2,128,512]{2,1,0:T(8,128)(2,1)S(1)}, bf16[2,128,512]{2,1,0:T(8,128)(2,1)S(1)}, u32[]{:S(2)}, u32[]{:S(2)}) collective-permute-start(bf16[2,128,512]{2,1,0:T(8,128)(2,1)S(1)} %pad_maximum_fusion.2.refs_0_.refs_10_), channel_id=1, source_target_pairs={{0,10},{2,12},{4,14},{6,16},{8,18},{10,20},{12,22},{14,24},{16,26}... | collective-permute-start | bytes 786440 | tf_op jit(solution)/shard_map/ppermute | solution.py:24
  9.3 1.9 %collective-permute-start.3 = (bf16[2,128,512]{2,1,0:T(8,128)(2,1)S(1)}, bf16[2,128,512]{2,1,0:T(8,128)(2,1)S(1)}, u32[]{:S(2)}, u32[]{:S(2)}) collective-permute-start(bf16[2,128,512]{2,1,0:T(8,128)(2,1)S(1)} %pad_maximum_fusion.2.refs_0_.refs_10_), channel_id=1, source_target_pairs={{0,14},{2,16},{4,18},{6,20},{8,22},{10,24},{12,26},{14,28},{16,30}... | collective-permute-start | bytes 786440 | tf_op jit(solution)/shard_map/ppermute | solution.py:24
  11.2 1.3 %collective-permute-start.4 = (bf16[2,128,512]{2,1,0:T(8,128)(2,1)S(1)}, bf16[2,128,512]{2,1,0:T(8,128)(2,1)S(1)}, u32[]{:S(2)}, u32[]{:S(2)}) collective-permute-start(bf16[2,128,512]{2,1,0:T(8,128)(2,1)S(1)} %pad_maximum_fusion.2.refs_0_.refs_10_), channel_id=1, source_target_pairs={{0,2},{4,6},{8,10},{12,14},{16,18},{20,22},{24,26},{28,30},{1,3},{... | collective-permute-start | bytes 786440 | tf_op jit(solution)/shard_map/ppermute | solution.py:27
  12.6 0.8 %select_reduce_fusion = s32[8]{0:T(128)S(1)} fusion(s32[8]{0:T(128)} %param.12), kind=kLoop, calls=%fused_computation.19 | loop fusion | flops 184 | bytes 64 | tf_op jit(solution)/shard_map/reduce_sum | solution.py:158
  13.3 0.6 fusion.10
  15.9 1.3 %fusion.9 = s32[8]{0:T(128)S(1)} fusion(s32[8]{0:T(128)} %constant.46.clone, s32[8]{0:T(128)} %constant.47.clone, pred[]{:T(512)S(6)} %eq.14, s32[]{:T(128)} %select_reduce_fusion.3, s32[]{:T(128)S(6)} %axis_index.33), kind=kLoop, calls=%fused_computation.25 | loop fusion | flops 32 | bytes 105 | tf_op jit(solution)/shard_map/mul | solution.py:169
  17.3 1.9 %fusion.5 = (f32[1024,64]{1,0:T(8,128)S(1)}, f32[1024,64]{1,0:T(8,128)S(1)}, f32[1024,64]{1,0:T(8,128)S(1)}) fusion(f32[64]{0:T(128)S(1)} %multiply_power_fusion, f32[1024]{0:T(1024)S(1)} %get-tuple-element.15), kind=kLoop, calls=%fused_computation.9 | loop fusion | flops 131072 | bytes 790784 | tf_op jit(solution)/shard_map/neg | solution.py:93
  20.2 0.8 %pad_maximum_fusion.3 = (f32[128,128]{1,0:T(8,128)}, f32[128,128]{1,0:T(8,128)}) fusion(f32[128,64]{1,0:T(8,128)S(1)} %get-tuple-element.14, f32[128,64]{1,0:T(8,128)S(1)} %get-tuple-element.13, f32[128,64]{1,0:T(8,128)S(1)} %get-tuple-element.12), kind=kLoop, calls=%fused_computation.12 | loop fusion | flops 32768 | bytes 229376 | tf_op jit(solution)/shard_map/concatenate | solution.py:93
  20.9 1.3 %pad_maximum_fusion = (f32[1024,128]{1,0:T(8,128)}, f32[1024,128]{1,0:T(8,128)}) fusion(f32[1024,64]{1,0:T(8,128)S(1)} %get-tuple-element.11, f32[1024,64]{1,0:T(8,128)S(1)} %get-tuple-element.10, f32[1024,64]{1,0:T(8,128)S(1)} %get-tuple-element.9), kind=kLoop, calls=%fused_computation.6 | loop fusion | flops 262144 | bytes 1835008 | tf_op jit(solution)/shard_map/concatenate | solution.py:93
  22.2 1.3 %collective-permute-start.5 = (bf16[2,128,512]{2,1,0:T(8,128)(2,1)S(1)}, bf16[2,128,512]{2,1,0:T(8,128)(2,1)S(1)}, u32[]{:S(2)}, u32[]{:S(2)}) collective-permute-start(bf16[2,128,512]{2,1,0:T(8,128)(2,1)S(1)} %collective-permute-done.refs_1_.refs_11_), channel_id=1, source_target_pairs={{0,2},{4,6},{8,10},{12,14},{16,18},{20,22},{24,26},{28,30},{1,3},{... | collective-permute-start | bytes 786440 | tf_op jit(solution)/shard_map/ppermute | solution.py:30
  23.5 1.2 %collective-permute-start.6 = (bf16[2,128,512]{2,1,0:T(8,128)(2,1)S(1)}, bf16[2,128,512]{2,1,0:T(8,128)(2,1)S(1)}, u32[]{:S(2)}, u32[]{:S(2)}) collective-permute-start(bf16[2,128,512]{2,1,0:T(8,128)(2,1)S(1)} %collective-permute-done.1.refs_2_.refs_12_), channel_id=1, source_target_pairs={{0,2},{4,6},{8,10},{12,14},{16,18},{20,22},{24,26},{28,30},{2,0},{... | collective-permute-start | bytes 786440 | tf_op jit(solution)/shard_map/ppermute | solution.py:30
  24.8 2.0 %collective-permute-done.2.refs_3_.refs_13_ = bf16[2,128,512]{2,1,0:T(8,128)(2,1)S(1)} collective-permute-done((bf16[2,128,512]{2,1,0:T(8,128)(2,1)S(1)}, bf16[2,128,512]{2,1,0:T(8,128)(2,1)S(1)}, u32[]{:S(2)}, u32[]{:S(2)}) %collective-permute-start.2) | collective-permute-done | bytes 262176 | tf_op jit(solution)/shard_map/ppermute | solution.py:24
  26.7 2.3 %collective-permute-start.7 = (bf16[2,128,512]{2,1,0:T(8,128)(2,1)S(1)}, bf16[2,128,512]{2,1,0:T(8,128)(2,1)S(1)}, u32[]{:S(2)}, u32[]{:S(2)}) collective-permute-start(bf16[2,128,512]{2,1,0:T(8,128)(2,1)S(1)} %collective-permute-done.2.refs_3_.refs_13_), channel_id=1, source_target_pairs={{0,2},{4,6},{8,10},{12,14},{16,18},{20,22},{24,26},{28,30},{2,0},{... | collective-permute-start | bytes 786440 | tf_op jit(solution)/shard_map/ppermute | solution.py:30
  29.1 3.3 %collective-permute-done.3.refs_4_.refs_14_ = bf16[2,128,512]{2,1,0:T(8,128)(2,1)S(1)} collective-permute-done((bf16[2,128,512]{2,1,0:T(8,128)(2,1)S(1)}, bf16[2,128,512]{2,1,0:T(8,128)(2,1)S(1)}, u32[]{:S(2)}, u32[]{:S(2)}) %collective-permute-start.3) | collective-permute-done | bytes 262176 | tf_op jit(solution)/shard_map/ppermute | solution.py:24
  32.4 3.3 %collective-permute-start.8 = (bf16[2,128,512]{2,1,0:T(8,128)(2,1)S(1)}, bf16[2,128,512]{2,1,0:T(8,128)(2,1)S(1)}, u32[]{:S(2)}, u32[]{:S(2)}) collective-permute-start(bf16[2,128,512]{2,1,0:T(8,128)(2,1)S(1)} %collective-permute-done.3.refs_4_.refs_14_), channel_id=1, source_target_pairs={{2,0},{6,4},{10,8},{14,12},{18,16},{22,20},{26,24},{30,28},{3,1},{... | collective-permute-start | bytes 786440 | tf_op jit(solution)/shard_map/ppermute | solution.py:30
  35.6 1.4 %select_reduce_fusion.1 = (s32[]{:T(128)}, s32[]{:T(128)}) fusion(s32[8]{0:T(128)} %param.13, s32[]{:T(128)S(6)} %sub.23, s32[8]{0:T(128)} %param.12), kind=kLoop, calls=%fused_computation.29 | loop fusion | flops 38 | bytes 76 | tf_op jit(solution)/shard_map/reduce_sum | solution.py:165
  40.0 12.2 %shard_map.82 = (bf16[128,2048]{1,0:T(8,128)(2,1)}, bf16[128,2048]{1,0:T(8,128)(2,1)}) custom-call(s32[1]{0:T(128)} %bitcast.peer_ref, s32[1]{0:T(128)} %bitcast.1.core_ref, s32[128,1]{1,0:T(8,128)} %iota_add_fusion.query_pos_ref, s32[1,1024]{1,0:T(1,128)} %and_select_fusion.key_limit_ref, f32[128,128]{1,0:T(8,128)} %get-tuple-element.19.query_cos_ref, ...), custom_call_target="tpu_custom_call" | custom-call | flops 2147483648 | bytes 12058624 | tf_op jit(solution)/shard_map/pallas_call | solution.py:134
  52.2 1.3 %collective-permute-start.9 = (bf16[128,2048]{1,0:T(8,128)(2,1)}, bf16[128,2048]{1,0:T(8,128)(2,1)S(1)}, u32[]{:S(2)}, u32[]{:S(2)}) collective-permute-start(bf16[128,2048]{1,0:T(8,128)(2,1)} %get-tuple-element.8), channel_id=1, source_target_pairs={{0,1},{1,0},{2,3},{3,2},{4,5},{5,4},{6,7},{7,6},{8,9},{9,8},{10,11... | collective-permute-start | bytes 1572872 | tf_op jit(solution)/shard_map/ppermute | solution.py:181
  53.5 4.8 %fusion.2 = bf16[128,2048]{1,0:T(8,128)(2,1)S(1)} fusion(bf16[128,2048]{1,0:T(8,128)(2,1)} %get-tuple-element.7, bf16[2048,4096]{1,0:T(8,128)(2,1)} %refs_20_.1, s32[]{:T(128)S(6)} %select_n.53), kind=kOutput, calls=%fused_computation.2 | convolution fusion | flops 1074003968 | bytes 9437188 | tf_op jit(solution)/shard_map/dot_general | solution.py:184
  58.3 7.8 %collective-permute-done.9 = bf16[128,2048]{1,0:T(8,128)(2,1)S(1)} collective-permute-done((bf16[128,2048]{1,0:T(8,128)(2,1)}, bf16[128,2048]{1,0:T(8,128)(2,1)S(1)}, u32[]{:S(2)}, u32[]{:S(2)}) %collective-permute-start.9) | collective-permute-done | bytes 524320 | tf_op jit(solution)/shard_map/ppermute | solution.py:181
  66.2 0.9 %add_convert_fusion = bf16[128,2048]{1,0:T(8,128)(2,1)} fusion(bf16[128,2048]{1,0:T(8,128)(2,1)S(1)} %collective-permute-done.9, bf16[128,2048]{1,0:T(8,128)(2,1)S(1)} %fusion.2), kind=kLoop, calls=%fused_computation.3 | loop fusion | flops 1048576 | bytes 1572864 | tf_op jit(solution)/shard_map/convert_element_type | solution.py:186
  (34 shorter events, 3.3 us)
Async XLA Ops:
  1.0 38.0 %copy-start = (bf16[2,128,512]{2,1,0:T(8,128)(2,1)}, bf16[2,128,512]{2,1,0:T(8,128)(2,1)S(1)}, u32[]{:S(2)}) copy-start(bf16[2,128,512]{2,1,0:T(8,128)(2,1)S(1)} %pad_maximum_fusion.2.refs_0_.refs_10_) | copy-start | bytes 786436
  1.0 21.2 %collective-permute-start = (bf16[2,128,512]{2,1,0:T(8,128)(2,1)S(1)}, bf16[2,128,512]{2,1,0:T(8,128)(2,1)S(1)}, u32[]{:S(2)}, u32[]{:S(2)}) collective-permute-start(bf16[2,128,512]{2,1,0:T(8,128)(2,1)S(1)} %pad_maximum_fusion.2.refs_0_.refs_10_), channel_id=1, source_target_pairs={{2,4},{6,8},{10,12},{14,16},{18,20},{22,24},{26,28},{3,5},{7,9},{1... | collective-permute-start | bytes 786440 | tf_op jit(solution)/shard_map/ppermute | solution.py:24
  4.8 18.8 %collective-permute-start.1 = (bf16[2,128,512]{2,1,0:T(8,128)(2,1)S(1)}, bf16[2,128,512]{2,1,0:T(8,128)(2,1)S(1)}, u32[]{:S(2)}, u32[]{:S(2)}) collective-permute-start(bf16[2,128,512]{2,1,0:T(8,128)(2,1)S(1)} %pad_maximum_fusion.2.refs_0_.refs_10_), channel_id=1, source_target_pairs={{0,6},{2,8},{4,10},{6,12},{8,14},{10,16},{12,18},{14,20},{16,22},{... | collective-permute-start | bytes 786440 | tf_op jit(solution)/shard_map/ppermute | solution.py:24
  6.7 20.0 %collective-permute-start.2 = (bf16[2,128,512]{2,1,0:T(8,128)(2,1)S(1)}, bf16[2,128,512]{2,1,0:T(8,128)(2,1)S(1)}, u32[]{:S(2)}, u32[]{:S(2)}) collective-permute-start(bf16[2,128,512]{2,1,0:T(8,128)(2,1)S(1)} %pad_maximum_fusion.2.refs_0_.refs_10_), channel_id=1, source_target_pairs={{0,10},{2,12},{4,14},{6,16},{8,18},{10,20},{12,22},{14,24},{16,26}... | collective-permute-start | bytes 786440 | tf_op jit(solution)/shard_map/ppermute | solution.py:24
  9.3 23.1 %collective-permute-start.3 = (bf16[2,128,512]{2,1,0:T(8,128)(2,1)S(1)}, bf16[2,128,512]{2,1,0:T(8,128)(2,1)S(1)}, u32[]{:S(2)}, u32[]{:S(2)}) collective-permute-start(bf16[2,128,512]{2,1,0:T(8,128)(2,1)S(1)} %pad_maximum_fusion.2.refs_0_.refs_10_), channel_id=1, source_target_pairs={{0,14},{2,16},{4,18},{6,20},{8,22},{10,24},{12,26},{14,28},{16,30}... | collective-permute-start | bytes 786440 | tf_op jit(solution)/shard_map/ppermute | solution.py:24
  11.2 27.7 %collective-permute-start.4 = (bf16[2,128,512]{2,1,0:T(8,128)(2,1)S(1)}, bf16[2,128,512]{2,1,0:T(8,128)(2,1)S(1)}, u32[]{:S(2)}, u32[]{:S(2)}) collective-permute-start(bf16[2,128,512]{2,1,0:T(8,128)(2,1)S(1)} %pad_maximum_fusion.2.refs_0_.refs_10_), channel_id=1, source_target_pairs={{0,2},{4,6},{8,10},{12,14},{16,18},{20,22},{24,26},{28,30},{1,3},{... | collective-permute-start | bytes 786440 | tf_op jit(solution)/shard_map/ppermute | solution.py:27
  22.2 16.8 %copy-start.1 = (bf16[2,128,512]{2,1,0:T(8,128)(2,1)}, bf16[2,128,512]{2,1,0:T(8,128)(2,1)S(1)}, u32[]{:S(2)}) copy-start(bf16[2,128,512]{2,1,0:T(8,128)(2,1)S(1)} %collective-permute-done.refs_1_.refs_11_) | copy-start | bytes 786436
  22.2 16.7 %collective-permute-start.5 = (bf16[2,128,512]{2,1,0:T(8,128)(2,1)S(1)}, bf16[2,128,512]{2,1,0:T(8,128)(2,1)S(1)}, u32[]{:S(2)}, u32[]{:S(2)}) collective-permute-start(bf16[2,128,512]{2,1,0:T(8,128)(2,1)S(1)} %collective-permute-done.refs_1_.refs_11_), channel_id=1, source_target_pairs={{0,2},{4,6},{8,10},{12,14},{16,18},{20,22},{24,26},{28,30},{1,3},{... | collective-permute-start | bytes 786440 | tf_op jit(solution)/shard_map/ppermute | solution.py:30
  23.5 15.5 %copy-start.2 = (bf16[2,128,512]{2,1,0:T(8,128)(2,1)}, bf16[2,128,512]{2,1,0:T(8,128)(2,1)S(1)}, u32[]{:S(2)}) copy-start(bf16[2,128,512]{2,1,0:T(8,128)(2,1)S(1)} %collective-permute-done.1.refs_2_.refs_12_) | copy-start | bytes 786436
  23.5 15.4 %collective-permute-start.6 = (bf16[2,128,512]{2,1,0:T(8,128)(2,1)S(1)}, bf16[2,128,512]{2,1,0:T(8,128)(2,1)S(1)}, u32[]{:S(2)}, u32[]{:S(2)}) collective-permute-start(bf16[2,128,512]{2,1,0:T(8,128)(2,1)S(1)} %collective-permute-done.1.refs_2_.refs_12_), channel_id=1, source_target_pairs={{0,2},{4,6},{8,10},{12,14},{16,18},{20,22},{24,26},{28,30},{2,0},{... | collective-permute-start | bytes 786440 | tf_op jit(solution)/shard_map/ppermute | solution.py:30
  26.7 12.3 %copy-start.3 = (bf16[2,128,512]{2,1,0:T(8,128)(2,1)}, bf16[2,128,512]{2,1,0:T(8,128)(2,1)S(1)}, u32[]{:S(2)}) copy-start(bf16[2,128,512]{2,1,0:T(8,128)(2,1)S(1)} %collective-permute-done.2.refs_3_.refs_13_) | copy-start | bytes 786436
  26.7 12.2 %collective-permute-start.7 = (bf16[2,128,512]{2,1,0:T(8,128)(2,1)S(1)}, bf16[2,128,512]{2,1,0:T(8,128)(2,1)S(1)}, u32[]{:S(2)}, u32[]{:S(2)}) collective-permute-start(bf16[2,128,512]{2,1,0:T(8,128)(2,1)S(1)} %collective-permute-done.2.refs_3_.refs_13_), channel_id=1, source_target_pairs={{0,2},{4,6},{8,10},{12,14},{16,18},{20,22},{24,26},{28,30},{2,0},{... | collective-permute-start | bytes 786440 | tf_op jit(solution)/shard_map/ppermute | solution.py:30
  32.4 6.7 %copy-start.4 = (bf16[2,128,512]{2,1,0:T(8,128)(2,1)}, bf16[2,128,512]{2,1,0:T(8,128)(2,1)S(1)}, u32[]{:S(2)}) copy-start(bf16[2,128,512]{2,1,0:T(8,128)(2,1)S(1)} %collective-permute-done.3.refs_4_.refs_14_) | copy-start | bytes 786436
  32.4 6.6 %collective-permute-start.8 = (bf16[2,128,512]{2,1,0:T(8,128)(2,1)S(1)}, bf16[2,128,512]{2,1,0:T(8,128)(2,1)S(1)}, u32[]{:S(2)}, u32[]{:S(2)}) collective-permute-start(bf16[2,128,512]{2,1,0:T(8,128)(2,1)S(1)} %collective-permute-done.3.refs_4_.refs_14_), channel_id=1, source_target_pairs={{2,0},{6,4},{10,8},{14,12},{18,16},{22,20},{26,24},{30,28},{3,1},{... | collective-permute-start | bytes 786440 | tf_op jit(solution)/shard_map/ppermute | solution.py:30
  38.9 0.7 %copy-start.5 = (bf16[2,128,512]{2,1,0:T(8,128)(2,1)}, bf16[2,128,512]{2,1,0:T(8,128)(2,1)S(1)}, u32[]{:S(2)}) copy-start(bf16[2,128,512]{2,1,0:T(8,128)(2,1)S(1)} %collective-permute-done.4.refs_5_.refs_15_) | copy-start | bytes 786436
  38.9 0.8 %copy-start.6 = (bf16[2,128,512]{2,1,0:T(8,128)(2,1)}, bf16[2,128,512]{2,1,0:T(8,128)(2,1)S(1)}, u32[]{:S(2)}) copy-start(bf16[2,128,512]{2,1,0:T(8,128)(2,1)S(1)} %collective-permute-done.5.refs_6_.refs_16_) | copy-start | bytes 786436
  38.9 0.9 %copy-start.7 = (bf16[2,128,512]{2,1,0:T(8,128)(2,1)}, bf16[2,128,512]{2,1,0:T(8,128)(2,1)S(1)}, u32[]{:S(2)}) copy-start(bf16[2,128,512]{2,1,0:T(8,128)(2,1)S(1)} %collective-permute-done.6.refs_7_.refs_17_) | copy-start | bytes 786436
  39.0 0.9 %copy-start.8 = (bf16[2,128,512]{2,1,0:T(8,128)(2,1)}, bf16[2,128,512]{2,1,0:T(8,128)(2,1)S(1)}, u32[]{:S(2)}) copy-start(bf16[2,128,512]{2,1,0:T(8,128)(2,1)S(1)} %collective-permute-done.7.refs_8_.refs_18_) | copy-start | bytes 786436
  39.0 1.0 %copy-start.9 = (bf16[2,128,512]{2,1,0:T(8,128)(2,1)}, bf16[2,128,512]{2,1,0:T(8,128)(2,1)S(1)}, u32[]{:S(2)}) copy-start(bf16[2,128,512]{2,1,0:T(8,128)(2,1)S(1)} %collective-permute-done.8.refs_9_.refs_19_) | copy-start | bytes 786436
  52.2 14.0 %collective-permute-start.9 = (bf16[128,2048]{1,0:T(8,128)(2,1)}, bf16[128,2048]{1,0:T(8,128)(2,1)S(1)}, u32[]{:S(2)}, u32[]{:S(2)}) collective-permute-start(bf16[128,2048]{1,0:T(8,128)(2,1)} %get-tuple-element.8), channel_id=1, source_target_pairs={{0,1},{1,0},{2,3},{3,2},{4,5},{5,4},{6,7},{7,6},{8,9},{9,8},{10,11... | collective-permute-start | bytes 1572872 | tf_op jit(solution)/shard_map/ppermute | solution.py:181

commit v6 on v5

--- a/solution.py
+++ b/solution.py
@@ -10,6 +10,7 @@
 
 HEAD_SIZE = 128
 FAR = 1 << 20
+CHUNK = 32
 
 
 def gather_window(kv, n, window):
@@ -47,30 +48,43 @@
                      query_sin_ref, key_cos_ref, key_sin_ref, query_ref, *refs):
     key_refs = refs[:n_slots]
     value_refs = refs[n_slots:2 * n_slots]
-    out_ref = refs[2 * n_slots + 1] if project else refs[2 * n_slots]
-
-    def attend_with(use):
-        keys = turn(jnp.concatenate([key_refs[j][...] for j in use], axis=0), key_cos_ref[...], key_sin_ref[...])
-        values = jnp.concatenate([value_refs[j][...] for j in use], axis=0)
-        allowed = key_limit_ref[...] <= query_pos_ref[...]
-        for g in range(query_ref.shape[1] // HEAD_SIZE):
-            columns = slice(g * HEAD_SIZE, (g + 1) * HEAD_SIZE)
-            query = turn(query_ref[:, columns], query_cos_ref[...], query_sin_ref[...])
-            scores = lax.dot_general(
-                query, keys, (((1,), (1,)), ((), ())), preferred_element_type=jnp.float32
-            ) * (1.0 / math.sqrt(HEAD_SIZE))
-            scores = jnp.where(allowed, scores, -1e30)
-            highest = jnp.max(scores, axis=1, keepdims=True)
-            weights = jnp.exp(scores - highest)
-            totals = jnp.sum(weights, axis=1, keepdims=True)
-            summed = jnp.dot(weights.astype(jnp.bfloat16), values, preferred_element_type=jnp.float32)
-            out_ref[:, columns] = (summed / totals).astype(out_ref.dtype)
+    rest = refs[2 * n_slots:]
+    if project:
+        weight_ref, out_ref, peer_out_ref, total_ref, keys_ref, values_ref = rest
+    else:
+        out_ref, keys_ref, values_ref = rest
+    block = key_refs[0].shape[0]
+
+    def fill(use):
+        for j, slot in enumerate(use):
+            rows = slice(j * block, (j + 1) * block)
+            keys_ref[rows, :] = turn(key_refs[slot][...], key_cos_ref[rows, :], key_sin_ref[rows, :])
+            values_ref[rows, :] = value_refs[slot][...]
 
     for parity, use in enumerate(uses):
-        pl.when(core_ref[0] == parity)(functools.partial(attend_with, use))
+        pl.when(core_ref[0] == parity)(functools.partial(fill, use))
+
+    chunks = query_ref.shape[0] // CHUNK
+
+    def one(step, carry):
+        g, r = step // chunks, step % chunks
+        rows = pl.ds(pl.multiple_of(r * CHUNK, CHUNK), CHUNK)
+        columns = pl.ds(pl.multiple_of(g * HEAD_SIZE, HEAD_SIZE), HEAD_SIZE)
+        query = turn(query_ref[rows, columns], query_cos_ref[rows, :], query_sin_ref[rows, :])
+        scores = lax.dot_general(
+            query, keys_ref[...], (((1,), (1,)), ((), ())), preferred_element_type=jnp.float32
+        ) * (1.0 / math.sqrt(HEAD_SIZE))
+        allowed = key_limit_ref[...] <= query_pos_ref[rows, :]
+        scores = jnp.where(allowed, scores, -1e30)
+        highest = jnp.max(scores, axis=1, keepdims=True)
+        weights = jnp.exp(scores - highest)
+        totals = jnp.sum(weights, axis=1, keepdims=True)
+        summed = jnp.dot(weights.astype(jnp.bfloat16), values_ref[...], preferred_element_type=jnp.float32)
+        out_ref[rows, columns] = (summed / totals).astype(out_ref.dtype)
+        return carry
+
+    lax.fori_loop(0, (query_ref.shape[1] // HEAD_SIZE) * chunks, one, 0)
     if project:
-        weight_ref = refs[2 * n_slots]
-        peer_out_ref, total_ref = refs[2 * n_slots + 2], refs[2 * n_slots + 3]
         step = pl.program_id(0)
 
         @pl.when(step == 0)
@@ -131,6 +145,7 @@
         args.append(out_weight)
         flops += 2 * rows * width * part
         moved += 2 * (width * part + rows * part)
+    scratch += [pltpu.VMEM((count, HEAD_SIZE), jnp.bfloat16), pltpu.VMEM((count, HEAD_SIZE), jnp.bfloat16)]
     return pl.pallas_call(
         functools.partial(attention_kernel, n_slots, uses, project),
         out_shape=out_shape,

time: 67.5 us -> 92.3 us (1.37)
  the two profiles are of different devices: /device:TPU:11 before, /device:TPU:15 now
where the time goes in v6:
time: 92.3 us; the launch traced here: 92 us
  Pallas kernels  37.2 us (40%)
  starting transfers between devices  19.9 us (22%)
  waiting for transfers between devices  14 us (15%)
  other arithmetic  12.2 us (13%)
  matrix products  4.82 us (5%)
  between operations  2.85 us (3%)
  local copies, waits for them, and re-layouts  0.98 us (1%)
    pallas_call x1, Pallas kernels, attend(): pl.pallas_call(functools.partial(attention_kernel, n_slots, uses, project...  37.2 us
    ppermute x4, starting transfers between devices, gather_window(): received[m] = lax.ppermute(kv, 'ctx', pairs)  10.2 us
    ppermute x1, waiting for transfers between devices, on_device(): got = lax.ppermute(peer_terms, 'tp', [(0, 1), (1, 0)])  8.71 us
    ppermute x4, starting transfers between devices, gather_window(): passed.append(lax.ppermute(received[m], 'ctx', pairs))  8.1 us
    ppermute x4, waiting for transfers between devices, gather_window(): received[m] = lax.ppermute(kv, 'ctx', pairs)  5.27 us
    dot_general x1, matrix products, on_device(): jnp.dot(attended, own_weight, preferred_element_type=jnp.float32)  4.82 us
    neg x2, other arithmetic, tables(): -sine  2.21 us
    concatenate x2, other arithmetic, tables(): jnp.concatenate([cosine, cosine], axis=1)  2.08 us
  transfers between devices with their start and end apart: 10, of which 3 were waited for; matrix products, arithmetic and copies ran while one was open for 16% of the time, Pallas kernels for 0%

profile of v6, /device:TPU:15, one launch (start us, length us, event | category | flops | bytes accessed | tf_op | source)
XLA Modules:
  0.0 92.0 jit_solution(820838425723240501)
XLA Ops:
  0.0 1.0 %pad_maximum_fusion.2.refs_0_.refs_10_ = bf16[2,128,512]{2,1,0:T(8,128)(2,1)S(1)} fusion(bf16[1,128,512]{2,1,0:T(8,128)(2,1)} %bitcast.8, bf16[1,128,512]{2,1,0:T(8,128)(2,1)} %bitcast.9), kind=kLoop, calls=%fused_computation.8 | loop fusion | flops 131072 | bytes 524288 | tf_op jit(solution)/shard_map/stack | solution.py:170
  1.0 3.7 %collective-permute-start = (bf16[2,128,512]{2,1,0:T(8,128)(2,1)S(1)}, bf16[2,128,512]{2,1,0:T(8,128)(2,1)S(1)}, u32[]{:S(2)}, u32[]{:S(2)}) collective-permute-start(bf16[2,128,512]{2,1,0:T(8,128)(2,1)S(1)} %pad_maximum_fusion.2.refs_0_.refs_10_), channel_id=1, source_target_pairs={{2,4},{6,8},{10,12},{14,16},{18,20},{22,24},{26,28},{3,5},{7,9},{1... | collective-permute-start | bytes 786440 | tf_op jit(solution)/shard_map/ppermute | solution.py:25
  4.8 1.9 %collective-permute-start.1 = (bf16[2,128,512]{2,1,0:T(8,128)(2,1)S(1)}, bf16[2,128,512]{2,1,0:T(8,128)(2,1)S(1)}, u32[]{:S(2)}, u32[]{:S(2)}) collective-permute-start(bf16[2,128,512]{2,1,0:T(8,128)(2,1)S(1)} %pad_maximum_fusion.2.refs_0_.refs_10_), channel_id=1, source_target_pairs={{0,6},{2,8},{4,10},{6,12},{8,14},{10,16},{12,18},{14,20},{16,22},{... | collective-permute-start | bytes 786440 | tf_op jit(solution)/shard_map/ppermute | solution.py:25
  6.7 2.6 %collective-permute-start.2 = (bf16[2,128,512]{2,1,0:T(8,128)(2,1)S(1)}, bf16[2,128,512]{2,1,0:T(8,128)(2,1)S(1)}, u32[]{:S(2)}, u32[]{:S(2)}) collective-permute-start(bf16[2,128,512]{2,1,0:T(8,128)(2,1)S(1)} %pad_maximum_fusion.2.refs_0_.refs_10_), channel_id=1, source_target_pairs={{0,10},{2,12},{4,14},{6,16},{8,18},{10,20},{12,22},{14,24},{16,26}... | collective-permute-start | bytes 786440 | tf_op jit(solution)/shard_map/ppermute | solution.py:25
  9.3 1.9 %collective-permute-start.3 = (bf16[2,128,512]{2,1,0:T(8,128)(2,1)S(1)}, bf16[2,128,512]{2,1,0:T(8,128)(2,1)S(1)}, u32[]{:S(2)}, u32[]{:S(2)}) collective-permute-start(bf16[2,128,512]{2,1,0:T(8,128)(2,1)S(1)} %pad_maximum_fusion.2.refs_0_.refs_10_), channel_id=1, source_target_pairs={{0,14},{2,16},{4,18},{6,20},{8,22},{10,24},{12,26},{14,28},{16,30}... | collective-permute-start | bytes 786440 | tf_op jit(solution)/shard_map/ppermute | solution.py:25
  11.2 1.3 %collective-permute-start.4 = (bf16[2,128,512]{2,1,0:T(8,128)(2,1)S(1)}, bf16[2,128,512]{2,1,0:T(8,128)(2,1)S(1)}, u32[]{:S(2)}, u32[]{:S(2)}) collective-permute-start(bf16[2,128,512]{2,1,0:T(8,128)(2,1)S(1)} %pad_maximum_fusion.2.refs_0_.refs_10_), channel_id=1, source_target_pairs={{0,2},{4,6},{8,10},{12,14},{16,18},{20,22},{24,26},{28,30},{1,3},{... | collective-permute-start | bytes 786440 | tf_op jit(solution)/shard_map/ppermute | solution.py:28
  12.6 0.8 select_reduce_fusion
  13.3 0.6 fusion.10
  14.6 0.6 select_reduce_fusion.3
  15.9 1.3 %fusion.9 = s32[8]{0:T(128)S(1)} fusion(s32[8]{0:T(128)} %constant.46.clone, s32[8]{0:T(128)} %constant.47.clone, pred[]{:T(512)S(6)} %eq.14, s32[]{:T(128)} %select_reduce_fusion.3, s32[]{:T(128)S(6)} %axis_index.33), kind=kLoop, calls=%fused_computation.25 | loop fusion | flops 32 | bytes 105 | tf_op jit(solution)/shard_map/mul | solution.py:184
  17.3 1.9 %fusion.5 = (f32[1024,64]{1,0:T(8,128)S(1)}, f32[1024,64]{1,0:T(8,128)S(1)}, f32[1024,64]{1,0:T(8,128)S(1)}) fusion(f32[64]{0:T(128)S(1)} %multiply_power_fusion, f32[1024]{0:T(1024)S(1)} %get-tuple-element.15), kind=kLoop, calls=%fused_computation.9 | loop fusion | flops 131072 | bytes 790784 | tf_op jit(solution)/shard_map/neg | solution.py:107
  20.2 0.8 pad_maximum_fusion.3
  20.9 1.3 %pad_maximum_fusion = (f32[1024,128]{1,0:T(8,128)}, f32[1024,128]{1,0:T(8,128)}) fusion(f32[1024,64]{1,0:T(8,128)S(1)} %get-tuple-element.11, f32[1024,64]{1,0:T(8,128)S(1)} %get-tuple-element.10, f32[1024,64]{1,0:T(8,128)S(1)} %get-tuple-element.9), kind=kLoop, calls=%fused_computation.6 | loop fusion | flops 262144 | bytes 1835008 | tf_op jit(solution)/shard_map/concatenate | solution.py:107
  22.2 1.3 %collective-permute-start.5 = (bf16[2,128,512]{2,1,0:T(8,128)(2,1)S(1)}, bf16[2,128,512]{2,1,0:T(8,128)(2,1)S(1)}, u32[]{:S(2)}, u32[]{:S(2)}) collective-permute-start(bf16[2,128,512]{2,1,0:T(8,128)(2,1)S(1)} %collective-permute-done.refs_1_.refs_11_), channel_id=1, source_target_pairs={{0,2},{4,6},{8,10},{12,14},{16,18},{20,22},{24,26},{28,30},{1,3},{... | collective-permute-start | bytes 786440 | tf_op jit(solution)/shard_map/ppermute | solution.py:31
  23.5 1.2 %collective-permute-start.6 = (bf16[2,128,512]{2,1,0:T(8,128)(2,1)S(1)}, bf16[2,128,512]{2,1,0:T(8,128)(2,1)S(1)}, u32[]{:S(2)}, u32[]{:S(2)}) collective-permute-start(bf16[2,128,512]{2,1,0:T(8,128)(2,1)S(1)} %collective-permute-done.1.refs_2_.refs_12_), channel_id=1, source_target_pairs={{0,2},{4,6},{8,10},{12,14},{16,18},{20,22},{24,26},{28,30},{2,0},{... | collective-permute-start | bytes 786440 | tf_op jit(solution)/shard_map/ppermute | solution.py:31
  24.8 2.0 %collective-permute-done.2.refs_3_.refs_13_ = bf16[2,128,512]{2,1,0:T(8,128)(2,1)S(1)} collective-permute-done((bf16[2,128,512]{2,1,0:T(8,128)(2,1)S(1)}, bf16[2,128,512]{2,1,0:T(8,128)(2,1)S(1)}, u32[]{:S(2)}, u32[]{:S(2)}) %collective-permute-start.2) | collective-permute-done | bytes 262176 | tf_op jit(solution)/shard_map/ppermute | solution.py:25
  26.7 2.3 %collective-permute-start.7 = (bf16[2,128,512]{2,1,0:T(8,128)(2,1)S(1)}, bf16[2,128,512]{2,1,0:T(8,128)(2,1)S(1)}, u32[]{:S(2)}, u32[]{:S(2)}) collective-permute-start(bf16[2,128,512]{2,1,0:T(8,128)(2,1)S(1)} %collective-permute-done.2.refs_3_.refs_13_), channel_id=1, source_target_pairs={{0,2},{4,6},{8,10},{12,14},{16,18},{20,22},{24,26},{28,30},{2,0},{... | collective-permute-start | bytes 786440 | tf_op jit(solution)/shard_map/ppermute | solution.py:31
  29.1 3.3 %collective-permute-done.3.refs_4_.refs_14_ = bf16[2,128,512]{2,1,0:T(8,128)(2,1)S(1)} collective-permute-done((bf16[2,128,512]{2,1,0:T(8,128)(2,1)S(1)}, bf16[2,128,512]{2,1,0:T(8,128)(2,1)S(1)}, u32[]{:S(2)}, u32[]{:S(2)}) %collective-permute-start.3) | collective-permute-done | bytes 262176 | tf_op jit(solution)/shard_map/ppermute | solution.py:25
  32.4 3.3 %collective-permute-start.8 = (bf16[2,128,512]{2,1,0:T(8,128)(2,1)S(1)}, bf16[2,128,512]{2,1,0:T(8,128)(2,1)S(1)}, u32[]{:S(2)}, u32[]{:S(2)}) collective-permute-start(bf16[2,128,512]{2,1,0:T(8,128)(2,1)S(1)} %collective-permute-done.3.refs_4_.refs_14_), channel_id=1, source_target_pairs={{2,0},{6,4},{10,8},{14,12},{18,16},{22,20},{26,24},{30,28},{3,1},{... | collective-permute-start | bytes 786440 | tf_op jit(solution)/shard_map/ppermute | solution.py:31
  35.6 1.4 %select_reduce_fusion.1 = (s32[]{:T(128)}, s32[]{:T(128)}) fusion(s32[8]{0:T(128)} %param.13, s32[]{:T(128)S(6)} %sub.23, s32[8]{0:T(128)} %param.12), kind=kLoop, calls=%fused_computation.29 | loop fusion | flops 38 | bytes 76 | tf_op jit(solution)/shard_map/reduce_sum | solution.py:180
  40.0 37.2 %shard_map.82 = (bf16[128,2048]{1,0:T(8,128)(2,1)}, bf16[128,2048]{1,0:T(8,128)(2,1)}) custom-call(s32[1]{0:T(128)} %bitcast.peer_ref, s32[1]{0:T(128)} %bitcast.1.core_ref, s32[128,1]{1,0:T(8,128)} %iota_add_fusion.query_pos_ref, s32[1,1024]{1,0:T(1,128)} %and_select_fusion.key_limit_ref, f32[128,128]{1,0:T(8,128)} %get-tuple-element.19.query_cos_ref, ...), custom_call_target="tpu_custom_call" | custom-call | flops 2147483648 | bytes 12058624 | tf_op jit(solution)/shard_map/pallas_call | solution.py:149
  77.5 4.8 %fusion.2 = bf16[128,2048]{1,0:T(8,128)(2,1)S(1)} fusion(bf16[128,2048]{1,0:T(8,128)(2,1)} %get-tuple-element.7, bf16[2048,4096]{1,0:T(8,128)(2,1)} %refs_20_.1, s32[]{:T(128)S(6)} %select_n.53), kind=kOutput, calls=%fused_computation.2 | convolution fusion | flops 1074003968 | bytes 9437188 | tf_op jit(solution)/shard_map/dot_general | solution.py:199
  82.4 8.7 %collective-permute-done.9 = bf16[128,2048]{1,0:T(8,128)(2,1)S(1)} collective-permute-done((bf16[128,2048]{1,0:T(8,128)(2,1)}, bf16[128,2048]{1,0:T(8,128)(2,1)S(1)}, u32[]{:S(2)}, u32[]{:S(2)}) %collective-permute-start.9) | collective-permute-done | bytes 524320 | tf_op jit(solution)/shard_map/ppermute | solution.py:196
  91.1 0.9 %add_convert_fusion = bf16[128,2048]{1,0:T(8,128)(2,1)} fusion(bf16[128,2048]{1,0:T(8,128)(2,1)S(1)} %collective-permute-done.9, bf16[128,2048]{1,0:T(8,128)(2,1)S(1)} %fusion.2), kind=kLoop, calls=%fused_computation.3 | loop fusion | flops 1048576 | bytes 1572864 | tf_op jit(solution)/shard_map/convert_element_type | solution.py:201
  (34 shorter events, 2.9 us)
Async XLA Ops:
  1.0 38.0 %copy-start = (bf16[2,128,512]{2,1,0:T(8,128)(2,1)}, bf16[2,128,512]{2,1,0:T(8,128)(2,1)S(1)}, u32[]{:S(2)}) copy-start(bf16[2,128,512]{2,1,0:T(8,128)(2,1)S(1)} %pad_maximum_fusion.2.refs_0_.refs_10_) | copy-start | bytes 786436
  1.0 21.2 %collective-permute-start = (bf16[2,128,512]{2,1,0:T(8,128)(2,1)S(1)}, bf16[2,128,512]{2,1,0:T(8,128)(2,1)S(1)}, u32[]{:S(2)}, u32[]{:S(2)}) collective-permute-start(bf16[2,128,512]{2,1,0:T(8,128)(2,1)S(1)} %pad_maximum_fusion.2.refs_0_.refs_10_), channel_id=1, source_target_pairs={{2,4},{6,8},{10,12},{14,16},{18,20},{22,24},{26,28},{3,5},{7,9},{1... | collective-permute-start | bytes 786440 | tf_op jit(solution)/shard_map/ppermute | solution.py:25
  4.8 18.8 %collective-permute-start.1 = (bf16[2,128,512]{2,1,0:T(8,128)(2,1)S(1)}, bf16[2,128,512]{2,1,0:T(8,128)(2,1)S(1)}, u32[]{:S(2)}, u32[]{:S(2)}) collective-permute-start(bf16[2,128,512]{2,1,0:T(8,128)(2,1)S(1)} %pad_maximum_fusion.2.refs_0_.refs_10_), channel_id=1, source_target_pairs={{0,6},{2,8},{4,10},{6,12},{8,14},{10,16},{12,18},{14,20},{16,22},{... | collective-permute-start | bytes 786440 | tf_op jit(solution)/shard_map/ppermute | solution.py:25
  6.7 20.0 %collective-permute-start.2 = (bf16[2,128,512]{2,1,0:T(8,128)(2,1)S(1)}, bf16[2,128,512]{2,1,0:T(8,128)(2,1)S(1)}, u32[]{:S(2)}, u32[]{:S(2)}) collective-permute-start(bf16[2,128,512]{2,1,0:T(8,128)(2,1)S(1)} %pad_maximum_fusion.2.refs_0_.refs_10_), channel_id=1, source_target_pairs={{0,10},{2,12},{4,14},{6,16},{8,18},{10,20},{12,22},{14,24},{16,26}... | collective-permute-start | bytes 786440 | tf_op jit(solution)/shard_map/ppermute | solution.py:25
  9.3 23.1 %collective-permute-start.3 = (bf16[2,128,512]{2,1,0:T(8,128)(2,1)S(1)}, bf16[2,128,512]{2,1,0:T(8,128)(2,1)S(1)}, u32[]{:S(2)}, u32[]{:S(2)}) collective-permute-start(bf16[2,128,512]{2,1,0:T(8,128)(2,1)S(1)} %pad_maximum_fusion.2.refs_0_.refs_10_), channel_id=1, source_target_pairs={{0,14},{2,16},{4,18},{6,20},{8,22},{10,24},{12,26},{14,28},{16,30}... | collective-permute-start | bytes 786440 | tf_op jit(solution)/shard_map/ppermute | solution.py:25
  11.2 27.7 %collective-permute-start.4 = (bf16[2,128,512]{2,1,0:T(8,128)(2,1)S(1)}, bf16[2,128,512]{2,1,0:T(8,128)(2,1)S(1)}, u32[]{:S(2)}, u32[]{:S(2)}) collective-permute-start(bf16[2,128,512]{2,1,0:T(8,128)(2,1)S(1)} %pad_maximum_fusion.2.refs_0_.refs_10_), channel_id=1, source_target_pairs={{0,2},{4,6},{8,10},{12,14},{16,18},{20,22},{24,26},{28,30},{1,3},{... | collective-permute-start | bytes 786440 | tf_op jit(solution)/shard_map/ppermute | solution.py:28
  22.2 16.8 %copy-start.1 = (bf16[2,128,512]{2,1,0:T(8,128)(2,1)}, bf16[2,128,512]{2,1,0:T(8,128)(2,1)S(1)}, u32[]{:S(2)}) copy-start(bf16[2,128,512]{2,1,0:T(8,128)(2,1)S(1)} %collective-permute-done.refs_1_.refs_11_) | copy-start | bytes 786436
  22.2 16.7 %collective-permute-start.5 = (bf16[2,128,512]{2,1,0:T(8,128)(2,1)S(1)}, bf16[2,128,512]{2,1,0:T(8,128)(2,1)S(1)}, u32[]{:S(2)}, u32[]{:S(2)}) collective-permute-start(bf16[2,128,512]{2,1,0:T(8,128)(2,1)S(1)} %collective-permute-done.refs_1_.refs_11_), channel_id=1, source_target_pairs={{0,2},{4,6},{8,10},{12,14},{16,18},{20,22},{24,26},{28,30},{1,3},{... | collective-permute-start | bytes 786440 | tf_op jit(solution)/shard_map/ppermute | solution.py:31
  23.5 15.5 %copy-start.2 = (bf16[2,128,512]{2,1,0:T(8,128)(2,1)}, bf16[2,128,512]{2,1,0:T(8,128)(2,1)S(1)}, u32[]{:S(2)}) copy-start(bf16[2,128,512]{2,1,0:T(8,128)(2,1)S(1)} %collective-permute-done.1.refs_2_.refs_12_) | copy-start | bytes 786436
  23.5 15.4 %collective-permute-start.6 = (bf16[2,128,512]{2,1,0:T(8,128)(2,1)S(1)}, bf16[2,128,512]{2,1,0:T(8,128)(2,1)S(1)}, u32[]{:S(2)}, u32[]{:S(2)}) collective-permute-start(bf16[2,128,512]{2,1,0:T(8,128)(2,1)S(1)} %collective-permute-done.1.refs_2_.refs_12_), channel_id=1, source_target_pairs={{0,2},{4,6},{8,10},{12,14},{16,18},{20,22},{24,26},{28,30},{2,0},{... | collective-permute-start | bytes 786440 | tf_op jit(solution)/shard_map/ppermute | solution.py:31
  26.7 12.3 %copy-start.3 = (bf16[2,128,512]{2,1,0:T(8,128)(2,1)}, bf16[2,128,512]{2,1,0:T(8,128)(2,1)S(1)}, u32[]{:S(2)}) copy-start(bf16[2,128,512]{2,1,0:T(8,128)(2,1)S(1)} %collective-permute-done.2.refs_3_.refs_13_) | copy-start | bytes 786436
  26.7 12.2 %collective-permute-start.7 = (bf16[2,128,512]{2,1,0:T(8,128)(2,1)S(1)}, bf16[2,128,512]{2,1,0:T(8,128)(2,1)S(1)}, u32[]{:S(2)}, u32[]{:S(2)}) collective-permute-start(bf16[2,128,512]{2,1,0:T(8,128)(2,1)S(1)} %collective-permute-done.2.refs_3_.refs_13_), channel_id=1, source_target_pairs={{0,2},{4,6},{8,10},{12,14},{16,18},{20,22},{24,26},{28,30},{2,0},{... | collective-permute-start | bytes 786440 | tf_op jit(solution)/shard_map/ppermute | solution.py:31
  32.4 6.7 %copy-start.4 = (bf16[2,128,512]{2,1,0:T(8,128)(2,1)}, bf16[2,128,512]{2,1,0:T(8,128)(2,1)S(1)}, u32[]{:S(2)}) copy-start(bf16[2,128,512]{2,1,0:T(8,128)(2,1)S(1)} %collective-permute-done.3.refs_4_.refs_14_) | copy-start | bytes 786436
  32.4 6.6 %collective-permute-start.8 = (bf16[2,128,512]{2,1,0:T(8,128)(2,1)S(1)}, bf16[2,128,512]{2,1,0:T(8,128)(2,1)S(1)}, u32[]{:S(2)}, u32[]{:S(2)}) collective-permute-start(bf16[2,128,512]{2,1,0:T(8,128)(2,1)S(1)} %collective-permute-done.3.refs_4_.refs_14_), channel_id=1, source_target_pairs={{2,0},{6,4},{10,8},{14,12},{18,16},{22,20},{26,24},{30,28},{3,1},{... | collective-permute-start | bytes 786440 | tf_op jit(solution)/shard_map/ppermute | solution.py:31
  38.9 0.7 copy-start.5
  38.9 0.8 copy-start.6
  38.9 0.9 copy-start.7
  39.0 0.9 %copy-start.8 = (bf16[2,128,512]{2,1,0:T(8,128)(2,1)}, bf16[2,128,512]{2,1,0:T(8,128)(2,1)S(1)}, u32[]{:S(2)}) copy-start(bf16[2,128,512]{2,1,0:T(8,128)(2,1)S(1)} %collective-permute-done.7.refs_8_.refs_18_) | copy-start | bytes 786436
  39.0 1.0 %copy-start.9 = (bf16[2,128,512]{2,1,0:T(8,128)(2,1)}, bf16[2,128,512]{2,1,0:T(8,128)(2,1)S(1)}, u32[]{:S(2)}) copy-start(bf16[2,128,512]{2,1,0:T(8,128)(2,1)S(1)} %collective-permute-done.8.refs_9_.refs_19_) | copy-start | bytes 786436
  77.2 13.8 %collective-permute-start.9 = (bf16[128,2048]{1,0:T(8,128)(2,1)}, bf16[128,2048]{1,0:T(8,128)(2,1)S(1)}, u32[]{:S(2)}, u32[]{:S(2)}) collective-permute-start(bf16[128,2048]{1,0:T(8,128)(2,1)} %get-tuple-element.8), channel_id=1, source_target_pairs={{0,1},{1,0},{2,3},{3,2},{4,5},{5,4},{6,7},{7,6},{8,9},{9,8},{10,11... | collective-permute-start | bytes 1572872 | tf_op jit(solution)/shard_map/ppermute | solution.py:196

commit v7 on v5

v7 whole, which is shorter than its diff:
```python
import functools
import math

import jax
import jax.numpy as jnp
from jax import lax
from jax.experimental import pallas as pl
from jax.experimental.pallas import tpu as pltpu
from jax.sharding import PartitionSpec as P

HEAD_SIZE = 128
FAR = 1 << 20


def gather_window(kv, n, window):
    half = window // 2
    received = [None] * half
    for m in reversed(range(half)):
        s = 2 * m + 1
        if s == 1:
            pairs = [(j, j + 1) for j in range(1, n - 1, 2)]
        else:
            pairs = [(j, j + s) for j in range(n - s)]
        received[m] = lax.ppermute(kv, "ctx", pairs)
    up = [(j, j + 1) for j in range(0, n, 2)]
    down = [(j + 1, j) for j in range(0, n, 2)]
    passed = [lax.ppermute(kv, "ctx", up)]
    for m in range(half - 1):
        pairs = up + (down if m > 0 else [])
        passed.append(lax.ppermute(received[m], "ctx", pairs))
    slots = [kv] + received + passed

    def pass_last(block):
        return lax.ppermute(block, "ctx", down)
    even = [(0, 0)] + [(1 + m, 2 * m + 1) for m in range(half - 1)] + [(2 + half + m, 2 * m) for m in range(1, half - 1)]
    even += [(half, 2 * half - 1), (2 * half + 1, 2 * half - 2)]
    odd = [(0, 0)] + [(1 + m, 2 * m + 1) for m in range(1, half - 1)] + [(1 + half, 1)]
    odd += [(2 + half + m, 2 * m + 2) for m in range(half - 2)] + [(half, 2 * half - 1), (2 * half, 2 * half - 2)]
    return slots, (even, odd), pass_last


def turn(rows, cosine, sine):
    rows = rows.astype(jnp.float32)
    return (rows * cosine + pltpu.roll(rows, HEAD_SIZE // 2, 1) * sine).astype(jnp.bfloat16)


def scores_of(query_ref, query_cos_ref, query_sin_ref, keys, allowed, g):
    columns = slice(g * HEAD_SIZE, (g + 1) * HEAD_SIZE)
    query = turn(query_ref[:, columns], query_cos_ref[...], query_sin_ref[...])
    scores = lax.dot_general(
        query, keys, (((1,), (1,)), ((), ())), preferred_element_type=jnp.float32
    ) * (1.0 / math.sqrt(HEAD_SIZE))
    return columns, jnp.where(allowed, scores, -1e30)


def attention_kernel(n_slots, uses, late, project, peer_ref, core_ref, query_pos_ref, key_limit_ref, query_cos_ref,
                     query_sin_ref, key_cos_ref, key_sin_ref, query_ref, *refs):
    if late:
        acc_in_ref, max_in_ref, sum_in_ref = refs[:3]
        refs = refs[3:]
    key_refs = refs[:n_slots]
    value_refs = refs[n_slots:2 * n_slots]
    rest = refs[2 * n_slots:]

    def body(use):
        keys = turn(jnp.concatenate([key_refs[j][...] for j in use], axis=0), key_cos_ref[...], key_sin_ref[...])
        values = jnp.concatenate([value_refs[j][...] for j in use], axis=0)
        allowed = key_limit_ref[...] <= query_pos_ref[...]
        for g in range(query_ref.shape[1] // HEAD_SIZE):
            columns, scores = scores_of(query_ref, query_cos_ref, query_sin_ref, keys, allowed, g)
            highest = jnp.max(scores, axis=1, keepdims=True)
            if late:
                before = max_in_ref[:, g:g + 1]
                highest = jnp.maximum(before, highest)
                factor = jnp.exp(before - highest)
            weights = jnp.exp(scores - highest)
            totals = jnp.sum(weights, axis=1, keepdims=True)
            summed = jnp.dot(weights.astype(jnp.bfloat16), values, preferred_element_type=jnp.float32)
            if late:
                totals = sum_in_ref[:, g:g + 1] * factor + totals
                summed = acc_in_ref[:, columns] * factor + summed
                out_ref[:, columns] = (summed / totals).astype(out_ref.dtype)
            else:
                acc_ref[:, columns] = summed
                max_ref[:, g:g + 1] = highest
                sum_ref[:, g:g + 1] = totals

    if late:
        if project:
            weight_ref, out_ref, peer_out_ref, total_ref = rest
        else:
            (out_ref,) = rest
    else:
        acc_ref, max_ref, sum_ref = rest
    for parity, use in enumerate(uses):
        pl.when(core_ref[0] == parity)(functools.partial(body, use))
    if late and project:
        step = pl.program_id(0)

        @pl.when(step == 0)
        def _():
            total_ref[...] = jnp.zeros_like(total_ref)

        total_ref[...] += jnp.dot(out_ref[...], weight_ref[...], preferred_element_type=jnp.float32)

        @pl.when(step == pl.num_programs(0) - 1)
        def _():
            peer_out_ref[...] = total_ref[...].astype(peer_out_ref.dtype)


def tables(positions):
    half = HEAD_SIZE // 2
    freqs = 500000.0 ** (-jnp.arange(half, dtype=jnp.float32) / half)
    angles = positions.astype(jnp.float32)[:, None] * freqs[None, :]
    cosine = jnp.cos(angles)
    sine = jnp.sin(angles)
    return jnp.concatenate([cosine, cosine], axis=1), jnp.concatenate([-sine, sine], axis=1)


def attend_stage(place, queries, slots, chosen, heads_kv, carry=None, out_weight=None, peer=None):
    query_pos, key_position, length, core = place
    rows, width = queries.shape
    block = slots[0].shape[1]
    present = sorted({s for pairs in chosen for s, _ in pairs})
    uses = [[present.index(s) for s, _ in pairs] for pairs in chosen]
    shift = jnp.where(core == 0, *[jnp.array([t for _, t in pairs], jnp.int32) for pairs in chosen])
    key_pos = key_position(shift)
    usable = (key_pos >= 0) & (key_pos < length)
    key_limit = jnp.where(usable, key_pos, FAR * rows).reshape(1, -1)
    count = key_pos.shape[0]
    group = width // heads_kv
    heads_here = group // HEAD_SIZE
    late = carry is not None
    project = out_weight is not None
    query_cos, query_sin = tables(query_pos)
    key_cos, key_sin = tables(key_pos)
    whole = lambda h, p, c: (0, 0)
    by_head = lambda h, p, c: (0, h)
    stats = lambda h, p, c: (h, 0, 0)
    in_specs = [
        pl.BlockSpec((rows, 1), whole),
        pl.BlockSpec((1, count), whole),
        pl.BlockSpec((rows, HEAD_SIZE), whole),
        pl.BlockSpec((rows, HEAD_SIZE), whole),
        pl.BlockSpec((count, HEAD_SIZE), whole),
        pl.BlockSpec((count, HEAD_SIZE), whole),
        pl.BlockSpec((rows, group), by_head),
    ]
    args = [peer.reshape(1), core.astype(jnp.int32).reshape(1), query_pos.reshape(rows, 1), key_limit,
            query_cos, query_sin, key_cos, key_sin, queries]
    if late:
        in_specs += [pl.BlockSpec((rows, group), by_head), pl.BlockSpec((None, rows, heads_here), stats),
                     pl.BlockSpec((None, rows, heads_here), stats)]
        args += list(carry)
    picked = [slots[s] for s in present]
    in_specs += [pl.BlockSpec((None, block, HEAD_SIZE), lambda h, p, c: (0, 0, h))] * len(picked)
    in_specs += [pl.BlockSpec((None, block, HEAD_SIZE), lambda h, p, c: (1, 0, h))] * len(picked)
    args += picked + picked
    flops = 4 * rows * count * width
    moved = 2 * (2 * rows * width + 2 * count * heads_kv * HEAD_SIZE)
    scratch = []
    if late:
        out_shape = [jax.ShapeDtypeStruct((rows, width), jnp.bfloat16)]
        out_specs = [pl.BlockSpec((rows, group), by_head)]
        if project:
            part = out_weight.shape[1] // 2
            in_specs.append(pl.BlockSpec((group, part), lambda h, p, c: (h, p[0])))
            out_shape.append(jax.ShapeDtypeStruct((rows, part), jnp.bfloat16))
            out_specs.append(pl.BlockSpec((rows, part), whole))
            scratch.append(pltpu.VMEM((rows, part), jnp.float32))
            args.append(out_weight)
            flops += 2 * rows * width * part
            moved += 2 * (width * part + rows * part)
    else:
        out_shape = [jax.ShapeDtypeStruct((rows, width), jnp.float32),
                     jax.ShapeDtypeStruct((heads_kv, rows, heads_here), jnp.float32),
                     jax.ShapeDtypeStruct((heads_kv, rows, heads_here), jnp.float32)]
        out_specs = [pl.BlockSpec((rows, group), by_head), pl.BlockSpec((None, rows, heads_here), stats),
                     pl.BlockSpec((None, rows, heads_here), stats)]
    return pl.pallas_call(
        functools.partial(attention_kernel, len(picked), uses, late, project),
        out_shape=out_shape,
        grid_spec=pltpu.PrefetchScalarGridSpec(
            num_scalar_prefetch=2, grid=(heads_kv,), in_specs=in_specs, out_specs=out_specs,
            scratch_shapes=scratch,
        ),
        cost_estimate=pl.CostEstimate(
            flops=flops, transcendentals=rows * count * width // HEAD_SIZE, bytes_accessed=moved
        ),
    )(*args)


def on_device(queries, keys, values, out_weight, group_widths, pad_tokens):
    n = lax.axis_size("ctx")
    window = n // 2
    group_index = lax.axis_index("ctx")
    rows_here = queries.shape[0]
    heads_kv = keys.shape[1] // HEAD_SIZE
    context_group = queries.shape[1] // keys.shape[1]

    slots, chosen, pass_last = gather_window(jnp.stack([keys, values]), n, window)
    half = window // 2
    first = [pairs[:-2] for pairs in chosen]
    last = [pairs[-2:] for pairs in chosen]

    prompt_ids = jnp.arange(group_widths.shape[0], dtype=jnp.int32)
    offsets = jnp.sum(
        jnp.where(prompt_ids[None, :] < prompt_ids[:, None], group_widths[None, :], 0), axis=1
    )
    owner = jnp.sum((offsets <= group_index).astype(jnp.int32)) - 1
    picked = prompt_ids == owner
    start = jnp.sum(jnp.where(picked, offsets, 0))
    width = jnp.sum(jnp.where(picked, group_widths, 0))
    padding = jnp.sum(jnp.where(picked, pad_tokens, 0))
    length = width * rows_here - padding
    local_rows = jnp.arange(rows_here, dtype=jnp.int32)
    query_pos = (group_index - start) * rows_here + local_rows

    def key_position(shift):
        return (((group_index - shift - start) * rows_here)[:, None] + local_rows[None, :]).reshape(-1)

    place = (query_pos, key_position, length, group_index % 2)
    zero = jnp.int32(0)
    carry = attend_stage(place, queries, slots, first, heads_kv, peer=zero)
    newest, carry = lax.optimization_barrier((slots[half], carry))
    slots = slots[:half] + [newest] + slots[half + 1:] + [pass_last(newest)]

    n_tp = lax.axis_size("tp")
    if n_tp == 2:
        me = lax.axis_index("tp")
        attended, peer_terms = attend_stage(
            place, queries, slots, last, heads_kv, carry=carry, out_weight=out_weight, peer=1 - me
        )
        got = lax.ppermute(peer_terms, "tp", [(0, 1), (1, 0)])
        part = out_weight.shape[1] // 2
        own_weight = lax.dynamic_slice_in_dim(out_weight, me * part, part, 1)
        own_terms = jnp.dot(attended, own_weight, preferred_element_type=jnp.float32)
        own_terms = lax.optimization_barrier(own_terms.astype(jnp.bfloat16)).astype(jnp.float32)
        return (own_terms + got.astype(jnp.float32)).astype(jnp.bfloat16)
    (attended,) = attend_stage(place, queries, slots, last, heads_kv, carry=carry, peer=zero)
    terms = jnp.dot(attended, out_weight, preferred_element_type=jnp.float32)
    return lax.psum_scatter(terms.astype(jnp.bfloat16), "tp", scatter_dimension=1, tiled=True)


def solution(mesh):
    return jax.shard_map(
        on_device,
        mesh=mesh,
        in_specs=(P("ctx", "tp"), P("ctx", "tp"), P("ctx", "tp"), P("tp", None), P(), P()),
        out_specs=P("ctx", "tp"),
        check_vma=False,
    )
```

time: 67.5 us -> 74.8 us (1.11)
  the two profiles are of different devices: /device:TPU:11 before, /device:TPU:18 now
where the time goes in v7:
time: 74.8 us; the launch traced here: 74.4 us
  Pallas kernels  19.3 us (26%)
  starting transfers between devices  15.8 us (21%)
  other arithmetic  15 us (20%)
  waiting for transfers between devices  15 us (20%)
  matrix products  4.82 us (6%)
  between operations  2.83 us (4%)
  local copies, waits for them, and re-layouts  1.61 us (2%)
    pallas_call x2, Pallas kernels, attend_stage(): pl.pallas_call(functools.partial(attention_kernel, len(picked), uses, lat...  19.3 us
    ppermute x4, starting transfers between devices, gather_window(): received[m] = lax.ppermute(kv, 'ctx', pairs)  9.17 us
    ppermute x1, waiting for transfers between devices, on_device(): got = lax.ppermute(peer_terms, 'tp', [(0, 1), (1, 0)])  8.17 us
    ppermute x4, waiting for transfers between devices, gather_window(): received[m] = lax.ppermute(kv, 'ctx', pairs)  6.15 us
    dot_general x1, matrix products, on_device(): jnp.dot(attended, own_weight, preferred_element_type=jnp.float32)  4.82 us
    concatenate x3, other arithmetic, tables(): jnp.concatenate([cosine, cosine], axis=1)  2.74 us
    mul x2, other arithmetic, key_position(): (group_index - shift - start) * rows_here  2.62 us
    ppermute x3, starting transfers between devices, gather_window(): passed.append(lax.ppermute(received[m], 'ctx', pairs))  2.46 us
  transfers between devices with their start and end apart: 10, of which 3 were waited for; matrix products, arithmetic and copies ran while one was open for 24% of the time, Pallas kernels for 12%

profile of v7, /device:TPU:18, one launch (start us, length us, event | category | flops | bytes accessed | tf_op | source)
XLA Modules:
  0.0 74.4 jit_solution(11814565689762179649)
XLA Ops:
  0.0 1.0 %pad_maximum_fusion.2.refs_0_.refs_8_ = bf16[2,128,512]{2,1,0:T(8,128)(2,1)S(1)} fusion(bf16[1,128,512]{2,1,0:T(8,128)(2,1)} %bitcast.15, bf16[1,128,512]{2,1,0:T(8,128)(2,1)} %bitcast.16), kind=kLoop, calls=%fused_computation.8 | loop fusion | flops 131072 | bytes 524288 | tf_op jit(solution)/shard_map/stack | solution.py:201
  1.0 2.9 %collective-permute-start.3 = (bf16[2,128,512]{2,1,0:T(8,128)(2,1)S(1)}, bf16[2,128,512]{2,1,0:T(8,128)(2,1)S(1)}, u32[]{:S(2)}, u32[]{:S(2)}) collective-permute-start(bf16[2,128,512]{2,1,0:T(8,128)(2,1)S(1)} %pad_maximum_fusion.2.refs_0_.refs_8_), channel_id=1, source_target_pairs={{0,10},{2,12},{4,14},{6,16},{8,18},{10,20},{12,22},{14,24},{16,26}... | collective-permute-start | bytes 786440 | tf_op jit(solution)/shard_map/ppermute | solution.py:24
  3.9 1.3 %collective-permute-start.1 = (bf16[2,128,512]{2,1,0:T(8,128)(2,1)S(1)}, bf16[2,128,512]{2,1,0:T(8,128)(2,1)S(1)}, u32[]{:S(2)}, u32[]{:S(2)}) collective-permute-start(bf16[2,128,512]{2,1,0:T(8,128)(2,1)S(1)} %pad_maximum_fusion.2.refs_0_.refs_8_), channel_id=1, source_target_pairs={{2,4},{6,8},{10,12},{14,16},{18,20},{22,24},{26,28},{3,5},{7,9},{1... | collective-permute-start | bytes 786440 | tf_op jit(solution)/shard_map/ppermute | solution.py:24
  5.2 3.7 %collective-permute-start.2 = (bf16[2,128,512]{2,1,0:T(8,128)(2,1)S(1)}, bf16[2,128,512]{2,1,0:T(8,128)(2,1)S(1)}, u32[]{:S(2)}, u32[]{:S(2)}) collective-permute-start(bf16[2,128,512]{2,1,0:T(8,128)(2,1)S(1)} %pad_maximum_fusion.2.refs_0_.refs_8_), channel_id=1, source_target_pairs={{0,6},{2,8},{4,10},{6,12},{8,14},{10,16},{12,18},{14,20},{16,22},{... | collective-permute-start | bytes 786440 | tf_op jit(solution)/shard_map/ppermute | solution.py:24
  8.9 1.3 %collective-permute-start.4 = (bf16[2,128,512]{2,1,0:T(8,128)(2,1)S(1)}, bf16[2,128,512]{2,1,0:T(8,128)(2,1)S(1)}, u32[]{:S(2)}, u32[]{:S(2)}) collective-permute-start(bf16[2,128,512]{2,1,0:T(8,128)(2,1)S(1)} %pad_maximum_fusion.2.refs_0_.refs_8_), channel_id=1, source_target_pairs={{0,2},{4,6},{8,10},{12,14},{16,18},{20,22},{24,26},{28,30},{1,3},{... | collective-permute-start | bytes 786440 | tf_op jit(solution)/shard_map/ppermute | solution.py:27
  10.2 1.3 %collective-permute-start = (bf16[2,128,512]{2,1,0:T(8,128)(2,1)S(1)}, bf16[2,128,512]{2,1,0:T(8,128)(2,1)S(1)}, u32[]{:S(2)}, u32[]{:S(2)}) collective-permute-start(bf16[2,128,512]{2,1,0:T(8,128)(2,1)S(1)} %pad_maximum_fusion.2.refs_0_.refs_8_), channel_id=1, source_target_pairs={{0,14},{2,16},{4,18},{6,20},{8,22},{10,24},{12,26},{14,28},{16,30}... | collective-permute-start | bytes 786440 | tf_op jit(solution)/shard_map/ppermute | solution.py:24
  11.6 0.8 %select_reduce_fusion = s32[8]{0:T(128)S(1)} fusion(s32[8]{0:T(128)} %param.14), kind=kLoop, calls=%fused_computation.25 | loop fusion | flops 184 | bytes 64 | tf_op jit(solution)/shard_map/reduce_sum | solution.py:207
  14.9 1.3 %fusion.11 = s32[6]{0:T(128)S(1)} fusion(s32[6]{0:T(128)} %constant.50.clone, s32[6]{0:T(128)} %constant.51.clone, pred[]{:T(512)S(6)} %eq.14, s32[]{:T(128)} %select_reduce_fusion.3, s32[]{:T(128)S(6)} %axis_index.25), kind=kLoop, calls=%fused_computation.34 | loop fusion | flops 24 | bytes 81 | tf_op jit(solution)/shard_map/mul | solution.py:220
  16.3 1.4 %fusion.5 = (f32[768,64]{1,0:T(8,128)S(1)}, f32[768,64]{1,0:T(8,128)S(1)}, f32[768,64]{1,0:T(8,128)S(1)}) fusion(f32[64]{0:T(128)S(1)} %multiply_power_fusion, f32[768]{0:T(1024)S(1)} %get-tuple-element.32), kind=kLoop, calls=%fused_computation.13 | loop fusion | flops 98304 | bytes 593152 | tf_op jit(solution)/shard_map/neg | solution.py:117
  18.1 1.3 %fusion.13 = s32[2]{0:T(128)S(1)} fusion(s32[2]{0:T(128)} %constant.53, s32[]{:T(128)} %select_reduce_fusion.3, s32[]{:T(128)S(6)} %axis_index.25), kind=kLoop, calls=%fused_computation.37 | loop fusion | flops 6 | bytes 24 | tf_op jit(solution)/shard_map/mul | solution.py:220
  19.4 1.2 %pad_maximum_fusion = (f32[768,128]{1,0:T(8,128)}, f32[768,128]{1,0:T(8,128)}) fusion(f32[768,64]{1,0:T(8,128)S(1)} %get-tuple-element.25, f32[768,64]{1,0:T(8,128)S(1)} %get-tuple-element.24, f32[768,64]{1,0:T(8,128)S(1)} %get-tuple-element.23), kind=kLoop, calls=%fused_computation.6 | loop fusion | flops 196608 | bytes 1376256 | tf_op jit(solution)/shard_map/concatenate | solution.py:117
  20.6 0.7 %pad_maximum_fusion.5 = (f32[128,128]{1,0:T(8,128)}, f32[128,128]{1,0:T(8,128)}) fusion(f32[128,64]{1,0:T(8,128)S(1)} %get-tuple-element.31, f32[128,64]{1,0:T(8,128)S(1)} %get-tuple-element.30, f32[128,64]{1,0:T(8,128)S(1)} %get-tuple-element.29), kind=kLoop, calls=%fused_computation.16 | loop fusion | flops 32768 | bytes 229376 | tf_op jit(solution)/shard_map/concatenate | solution.py:117
  22.6 2.4 %collective-permute-start.5 = (bf16[2,128,512]{2,1,0:T(8,128)(2,1)S(1)}, bf16[2,128,512]{2,1,0:T(8,128)(2,1)S(1)}, u32[]{:S(2)}, u32[]{:S(2)}) collective-permute-start(bf16[2,128,512]{2,1,0:T(8,128)(2,1)S(1)} %collective-permute-done.1.refs_1_.refs_9_), channel_id=1, source_target_pairs={{0,2},{4,6},{8,10},{12,14},{16,18},{20,22},{24,26},{28,30},{1,3},{... | collective-permute-start | bytes 786440 | tf_op jit(solution)/shard_map/ppermute | solution.py:30
  25.0 6.1 %collective-permute-done.2.refs_2_.refs_10_ = bf16[2,128,512]{2,1,0:T(8,128)(2,1)S(1)} collective-permute-done((bf16[2,128,512]{2,1,0:T(8,128)(2,1)S(1)}, bf16[2,128,512]{2,1,0:T(8,128)(2,1)S(1)}, u32[]{:S(2)}, u32[]{:S(2)}) %collective-permute-start.2) | collective-permute-done | bytes 262176 | tf_op jit(solution)/shard_map/ppermute | solution.py:24
  31.2 1.4 %select_reduce_fusion.1 = (s32[]{:T(128)}, s32[]{:T(128)}) fusion(s32[8]{0:T(128)} %param.15, s32[]{:T(128)S(6)} %sub.37, s32[8]{0:T(128)} %param.14), kind=kLoop, calls=%fused_computation.40 | loop fusion | flops 38 | bytes 76 | tf_op jit(solution)/shard_map/reduce_sum | solution.py:214
  35.4 8.6 %shard_map.100 = (f32[128,2048]{1,0:T(8,128)}, f32[4,128,4]{2,1,0:T(8,128)}, f32[4,128,4]{2,1,0:T(8,128)}) custom-call(s32[1]{0:T(128)} %constant.47.clone.1.peer_ref, s32[1]{0:T(128)} %bitcast.1.core_ref, s32[128,1]{1,0:T(8,128)} %iota_add_fusion.query_pos_ref, s32[1,768]{1,0:T(1,128)} %and_select_fusion.key_limit_ref, ...), custom_call_target="tpu_custom_call" | custom-call | flops 805306368 | bytes 2621440 | tf_op jit(solution)/shard_map/pallas_call | solution.py:180
  44.0 1.3 %collective-permute-start.8 = (bf16[2,128,512]{2,1,0:T(8,128)(2,1)S(1)}, bf16[2,128,512]{2,1,0:T(8,128)(2,1)S(1)}, u32[]{:S(2)}, u32[]{:S(2)}) collective-permute-start(bf16[2,128,512]{2,1,0:T(8,128)(2,1)S(1)} %collective-permute-done.refs_3_.refs_6_), channel_id=1, source_target_pairs={{2,0},{6,4},{10,8},{14,12},{18,16},{22,20},{26,24},{30,28},{3,1},{... | collective-permute-start | bytes 786440 | tf_op jit(solution)/shard_map/ppermute | solution.py:34
  45.3 0.8 %pad_maximum_fusion.3 = (f32[256,128]{1,0:T(8,128)}, f32[256,128]{1,0:T(8,128)}) fusion(f32[256,64]{1,0:T(8,128)S(1)} %get-tuple-element.28, f32[256,64]{1,0:T(8,128)S(1)} %get-tuple-element.27, f32[256,64]{1,0:T(8,128)S(1)} %get-tuple-element.26), kind=kLoop, calls=%fused_computation.11 | loop fusion | flops 65536 | bytes 458752 | tf_op jit(solution)/shard_map/concatenate | solution.py:117
  47.4 0.7 copy-done.3
  48.1 10.7 %shard_map.101 = (bf16[128,2048]{1,0:T(8,128)(2,1)}, bf16[128,2048]{1,0:T(8,128)(2,1)}) custom-call(s32[1]{0:T(128)} %bitcast.peer_ref, s32[1]{0:T(128)} %bitcast.1.core_ref, s32[128,1]{1,0:T(8,128)} %iota_add_fusion.query_pos_ref, s32[1,256]{1,0:T(1,128)} %and_select_fusion.1.key_limit_ref, f32[128,128]{1,0:T(8,128)} %get-tuple-element.38.query_cos_ref, ...), custom_call_target="tpu_custom_call" | custom-call | flops 1342177280 | bytes 10485760 | tf_op jit(solution)/shard_map/pallas_call | solution.py:180
  58.9 1.6 %collective-permute-start.9 = (bf16[128,2048]{1,0:T(8,128)(2,1)}, bf16[128,2048]{1,0:T(8,128)(2,1)S(1)}, u32[]{:S(2)}, u32[]{:S(2)}) collective-permute-start(bf16[128,2048]{1,0:T(8,128)(2,1)} %get-tuple-element.22), channel_id=1, source_target_pairs={{0,1},{1,0},{2,3},{3,2},{4,5},{5,4},{6,7},{7,6},{8,9},{9,8},{10,11... | collective-permute-start | bytes 1572872 | tf_op jit(solution)/shard_map/ppermute | solution.py:234
  60.5 4.8 %fusion.2 = bf16[128,2048]{1,0:T(8,128)(2,1)S(1)} fusion(bf16[128,2048]{1,0:T(8,128)(2,1)} %get-tuple-element.21, bf16[2048,4096]{1,0:T(8,128)(2,1)} %refs_9_.1, s32[]{:T(128)S(6)} %select_n.73), kind=kOutput, calls=%fused_computation.2 | convolution fusion | flops 1074003968 | bytes 9437188 | tf_op jit(solution)/shard_map/dot_general | solution.py:237
  65.3 8.2 %collective-permute-done.9 = bf16[128,2048]{1,0:T(8,128)(2,1)S(1)} collective-permute-done((bf16[128,2048]{1,0:T(8,128)(2,1)}, bf16[128,2048]{1,0:T(8,128)(2,1)S(1)}, u32[]{:S(2)}, u32[]{:S(2)}) %collective-permute-start.9) | collective-permute-done | bytes 524320 | tf_op jit(solution)/shard_map/ppermute | solution.py:234
  73.5 0.9 %add_convert_fusion = bf16[128,2048]{1,0:T(8,128)(2,1)} fusion(bf16[128,2048]{1,0:T(8,128)(2,1)S(1)} %collective-permute-done.9, bf16[128,2048]{1,0:T(8,128)(2,1)S(1)} %fusion.2), kind=kLoop, calls=%fused_computation.3 | loop fusion | flops 1048576 | bytes 1572864 | tf_op jit(solution)/shard_map/convert_element_type | solution.py:239
  (40 shorter events, 5.8 us)
Async XLA Ops:
  1.0 33.5 %copy-start.1 = (bf16[2,128,512]{2,1,0:T(8,128)(2,1)}, bf16[2,128,512]{2,1,0:T(8,128)(2,1)S(1)}, u32[]{:S(2)}) copy-start(bf16[2,128,512]{2,1,0:T(8,128)(2,1)S(1)} %pad_maximum_fusion.2.refs_0_.refs_8_) | copy-start | bytes 786436
  1.0 21.5 %collective-permute-start.3 = (bf16[2,128,512]{2,1,0:T(8,128)(2,1)S(1)}, bf16[2,128,512]{2,1,0:T(8,128)(2,1)S(1)}, u32[]{:S(2)}, u32[]{:S(2)}) collective-permute-start(bf16[2,128,512]{2,1,0:T(8,128)(2,1)S(1)} %pad_maximum_fusion.2.refs_0_.refs_8_), channel_id=1, source_target_pairs={{0,10},{2,12},{4,14},{6,16},{8,18},{10,20},{12,22},{14,24},{16,26}... | collective-permute-start | bytes 786440 | tf_op jit(solution)/shard_map/ppermute | solution.py:24
  3.9 18.7 %collective-permute-start.1 = (bf16[2,128,512]{2,1,0:T(8,128)(2,1)S(1)}, bf16[2,128,512]{2,1,0:T(8,128)(2,1)S(1)}, u32[]{:S(2)}, u32[]{:S(2)}) collective-permute-start(bf16[2,128,512]{2,1,0:T(8,128)(2,1)S(1)} %pad_maximum_fusion.2.refs_0_.refs_8_), channel_id=1, source_target_pairs={{2,4},{6,8},{10,12},{14,16},{18,20},{22,24},{26,28},{3,5},{7,9},{1... | collective-permute-start | bytes 786440 | tf_op jit(solution)/shard_map/ppermute | solution.py:24
  5.2 25.9 %collective-permute-start.2 = (bf16[2,128,512]{2,1,0:T(8,128)(2,1)S(1)}, bf16[2,128,512]{2,1,0:T(8,128)(2,1)S(1)}, u32[]{:S(2)}, u32[]{:S(2)}) collective-permute-start(bf16[2,128,512]{2,1,0:T(8,128)(2,1)S(1)} %pad_maximum_fusion.2.refs_0_.refs_8_), channel_id=1, source_target_pairs={{0,6},{2,8},{4,10},{6,12},{8,14},{10,16},{12,18},{14,20},{16,22},{... | collective-permute-start | bytes 786440 | tf_op jit(solution)/shard_map/ppermute | solution.py:24
  8.9 25.5 %collective-permute-start.4 = (bf16[2,128,512]{2,1,0:T(8,128)(2,1)S(1)}, bf16[2,128,512]{2,1,0:T(8,128)(2,1)S(1)}, u32[]{:S(2)}, u32[]{:S(2)}) collective-permute-start(bf16[2,128,512]{2,1,0:T(8,128)(2,1)S(1)} %pad_maximum_fusion.2.refs_0_.refs_8_), channel_id=1, source_target_pairs={{0,2},{4,6},{8,10},{12,14},{16,18},{20,22},{24,26},{28,30},{1,3},{... | collective-permute-start | bytes 786440 | tf_op jit(solution)/shard_map/ppermute | solution.py:27
  10.2 33.8 %collective-permute-start = (bf16[2,128,512]{2,1,0:T(8,128)(2,1)S(1)}, bf16[2,128,512]{2,1,0:T(8,128)(2,1)S(1)}, u32[]{:S(2)}, u32[]{:S(2)}) collective-permute-start(bf16[2,128,512]{2,1,0:T(8,128)(2,1)S(1)} %pad_maximum_fusion.2.refs_0_.refs_8_), channel_id=1, source_target_pairs={{0,14},{2,16},{4,18},{6,20},{8,22},{10,24},{12,26},{14,28},{16,30}... | collective-permute-start | bytes 786440 | tf_op jit(solution)/shard_map/ppermute | solution.py:24
  22.5 12.0 %copy-start.4 = (bf16[2,128,512]{2,1,0:T(8,128)(2,1)}, bf16[2,128,512]{2,1,0:T(8,128)(2,1)S(1)}, u32[]{:S(2)}) copy-start(bf16[2,128,512]{2,1,0:T(8,128)(2,1)S(1)} %collective-permute-done.3.refs_3_.refs_11_) | copy-start | bytes 786436
  22.5 11.9 %collective-permute-start.7 = (bf16[2,128,512]{2,1,0:T(8,128)(2,1)S(1)}, bf16[2,128,512]{2,1,0:T(8,128)(2,1)S(1)}, u32[]{:S(2)}, u32[]{:S(2)}) collective-permute-start(bf16[2,128,512]{2,1,0:T(8,128)(2,1)S(1)} %collective-permute-done.3.refs_3_.refs_11_), channel_id=1, source_target_pairs={{0,2},{4,6},{8,10},{12,14},{16,18},{20,22},{24,26},{28,30},{2,0},{... | collective-permute-start | bytes 786440 | tf_op jit(solution)/shard_map/ppermute | solution.py:30
  22.6 11.9 %copy-start.5 = (bf16[2,128,512]{2,1,0:T(8,128)(2,1)}, bf16[2,128,512]{2,1,0:T(8,128)(2,1)S(1)}, u32[]{:S(2)}) copy-start(bf16[2,128,512]{2,1,0:T(8,128)(2,1)S(1)} %collective-permute-done.1.refs_1_.refs_9_) | copy-start | bytes 786436
  22.6 11.8 %collective-permute-start.5 = (bf16[2,128,512]{2,1,0:T(8,128)(2,1)S(1)}, bf16[2,128,512]{2,1,0:T(8,128)(2,1)S(1)}, u32[]{:S(2)}, u32[]{:S(2)}) collective-permute-start(bf16[2,128,512]{2,1,0:T(8,128)(2,1)S(1)} %collective-permute-done.1.refs_1_.refs_9_), channel_id=1, source_target_pairs={{0,2},{4,6},{8,10},{12,14},{16,18},{20,22},{24,26},{28,30},{1,3},{... | collective-permute-start | bytes 786440 | tf_op jit(solution)/shard_map/ppermute | solution.py:30
  31.2 3.3 %copy-start.6 = (bf16[2,128,512]{2,1,0:T(8,128)(2,1)}, bf16[2,128,512]{2,1,0:T(8,128)(2,1)S(1)}, u32[]{:S(2)}) copy-start(bf16[2,128,512]{2,1,0:T(8,128)(2,1)S(1)} %collective-permute-done.2.refs_2_.refs_10_) | copy-start | bytes 786436
  31.2 3.3 %collective-permute-start.6 = (bf16[2,128,512]{2,1,0:T(8,128)(2,1)S(1)}, bf16[2,128,512]{2,1,0:T(8,128)(2,1)S(1)}, u32[]{:S(2)}, u32[]{:S(2)}) collective-permute-start(bf16[2,128,512]{2,1,0:T(8,128)(2,1)S(1)} %collective-permute-done.2.refs_2_.refs_10_), channel_id=1, source_target_pairs={{0,2},{4,6},{8,10},{12,14},{16,18},{20,22},{24,26},{28,30},{2,0},{... | collective-permute-start | bytes 786440 | tf_op jit(solution)/shard_map/ppermute | solution.py:30
  34.4 0.7 copy-start.7
  34.4 0.8 %copy-start = (bf16[2,128,512]{2,1,0:T(8,128)(2,1)}, bf16[2,128,512]{2,1,0:T(8,128)(2,1)S(1)}, u32[]{:S(2)}) copy-start(bf16[2,128,512]{2,1,0:T(8,128)(2,1)S(1)} %collective-permute-done.7.refs_7_.refs_15_.refs_4_) | copy-start | bytes 786436
  34.5 0.9 %copy-start.8 = (bf16[2,128,512]{2,1,0:T(8,128)(2,1)}, bf16[2,128,512]{2,1,0:T(8,128)(2,1)S(1)}, u32[]{:S(2)}) copy-start(bf16[2,128,512]{2,1,0:T(8,128)(2,1)S(1)} %collective-permute-done.5.refs_5_.refs_13_) | copy-start | bytes 786436
  34.5 0.9 %copy-start.9 = (bf16[2,128,512]{2,1,0:T(8,128)(2,1)}, bf16[2,128,512]{2,1,0:T(8,128)(2,1)S(1)}, u32[]{:S(2)}) copy-start(bf16[2,128,512]{2,1,0:T(8,128)(2,1)S(1)} %collective-permute-done.6.refs_6_.refs_14_) | copy-start | bytes 786436
  44.0 3.4 %copy-start.2 = (bf16[2,128,512]{2,1,0:T(8,128)(2,1)}, bf16[2,128,512]{2,1,0:T(8,128)(2,1)S(1)}, u32[]{:S(2)}) copy-start(bf16[2,128,512]{2,1,0:T(8,128)(2,1)S(1)} %collective-permute-done.refs_3_.refs_6_) | copy-start | bytes 786436
  44.0 3.4 %collective-permute-start.8 = (bf16[2,128,512]{2,1,0:T(8,128)(2,1)S(1)}, bf16[2,128,512]{2,1,0:T(8,128)(2,1)S(1)}, u32[]{:S(2)}, u32[]{:S(2)}) collective-permute-start(bf16[2,128,512]{2,1,0:T(8,128)(2,1)S(1)} %collective-permute-done.refs_3_.refs_6_), channel_id=1, source_target_pairs={{2,0},{6,4},{10,8},{14,12},{18,16},{22,20},{26,24},{30,28},{3,1},{... | collective-permute-start | bytes 786440 | tf_op jit(solution)/shard_map/ppermute | solution.py:34
  47.4 0.7 copy-start.3
  58.9 14.6 %collective-permute-start.9 = (bf16[128,2048]{1,0:T(8,128)(2,1)}, bf16[128,2048]{1,0:T(8,128)(2,1)S(1)}, u32[]{:S(2)}, u32[]{:S(2)}) collective-permute-start(bf16[128,2048]{1,0:T(8,128)(2,1)} %get-tuple-element.22), channel_id=1, source_target_pairs={{0,1},{1,0},{2,3},{3,2},{4,5},{5,4},{6,7},{7,6},{8,9},{9,8},{10,11... | collective-permute-start | bytes 1572872 | tf_op jit(solution)/shard_map/ppermute | solution.py:234

commit v8 on v5

--- a/solution.py
+++ b/solution.py
@@ -43,45 +43,58 @@
     return (rows * cosine + pltpu.roll(rows, HEAD_SIZE // 2, 1) * sine).astype(jnp.bfloat16)
 
 
-def attention_kernel(n_slots, uses, project, peer_ref, core_ref, query_pos_ref, key_limit_ref, query_cos_ref,
-                     query_sin_ref, key_cos_ref, key_sin_ref, query_ref, *refs):
-    key_refs = refs[:n_slots]
-    value_refs = refs[n_slots:2 * n_slots]
-    out_ref = refs[2 * n_slots + 1] if project else refs[2 * n_slots]
-
-    def attend_with(use):
-        keys = turn(jnp.concatenate([key_refs[j][...] for j in use], axis=0), key_cos_ref[...], key_sin_ref[...])
-        values = jnp.concatenate([value_refs[j][...] for j in use], axis=0)
-        allowed = key_limit_ref[...] <= query_pos_ref[...]
-        for g in range(query_ref.shape[1] // HEAD_SIZE):
-            columns = slice(g * HEAD_SIZE, (g + 1) * HEAD_SIZE)
-            query = turn(query_ref[:, columns], query_cos_ref[...], query_sin_ref[...])
-            scores = lax.dot_general(
-                query, keys, (((1,), (1,)), ((), ())), preferred_element_type=jnp.float32
-            ) * (1.0 / math.sqrt(HEAD_SIZE))
-            scores = jnp.where(allowed, scores, -1e30)
-            highest = jnp.max(scores, axis=1, keepdims=True)
-            weights = jnp.exp(scores - highest)
-            totals = jnp.sum(weights, axis=1, keepdims=True)
-            summed = jnp.dot(weights.astype(jnp.bfloat16), values, preferred_element_type=jnp.float32)
-            out_ref[:, columns] = (summed / totals).astype(out_ref.dtype)
+def attention_kernel(n_slots, uses, heads_kv, project, peer_ref, core_ref, query_pos_ref, key_limit_ref,
+                     query_cos_ref, query_sin_ref, key_cos_ref, key_sin_ref, query_ref, *refs):
+    slot_refs = refs[:n_slots]
+    if project:
+        weight_hbm, out_ref, peer_out_ref, weight_ref, copy_sem = refs[n_slots:]
+        group = query_ref.shape[1] // heads_kv
+        part = weight_ref.shape[1]
+        copies = [
+            pltpu.make_async_copy(
+                weight_hbm.at[pl.ds(h * group, group), pl.ds(pl.multiple_of(peer_ref[0] * part, part), part)],
+                weight_ref.at[pl.ds(h * group, group), :],
+                copy_sem.at[h],
+            )
+            for h in range(heads_kv)
+        ]
+        for copy in copies:
+            copy.start()
+    else:
+        (out_ref,) = refs[n_slots:]
+    allowed = key_limit_ref[...] <= query_pos_ref[...]
+    heads_here = query_ref.shape[1] // HEAD_SIZE // heads_kv
+
+    def body(use):
+        for h in range(heads_kv):
+            head = slice(h * HEAD_SIZE, (h + 1) * HEAD_SIZE)
+            keys = turn(jnp.concatenate([slot_refs[j][0, :, head] for j in use], axis=0),
+                        key_cos_ref[...], key_sin_ref[...])
+            values = jnp.concatenate([slot_refs[j][1, :, head] for j in use], axis=0)
+            for g in range(heads_here):
+                q = h * heads_here + g
+                columns = slice(q * HEAD_SIZE, (q + 1) * HEAD_SIZE)
+                query = turn(query_ref[:, columns], query_cos_ref[...], query_sin_ref[...])
+                scores = lax.dot_general(
+                    query, keys, (((1,), (1,)), ((), ())), preferred_element_type=jnp.float32
+                ) * (1.0 / math.sqrt(HEAD_SIZE))
+                scores = jnp.where(allowed, scores, -1e30)
+                highest = jnp.max(scores, axis=1, keepdims=True)
+                weights = jnp.exp(scores - highest)
+                totals = jnp.sum(weights, axis=1, keepdims=True)
+                summed = jnp.dot(weights.astype(jnp.bfloat16), values, preferred_element_type=jnp.float32)
+                out_ref[:, columns] = (summed / totals).astype(out_ref.dtype)
 
     for parity, use in enumerate(uses):
-        pl.when(core_ref[0] == parity)(functools.partial(attend_with, use))
+        pl.when(core_ref[0] == parity)(functools.partial(body, use))
     if project:
-        weight_ref = refs[2 * n_slots]
-        peer_out_ref, total_ref = refs[2 * n_slots + 2], refs[2 * n_slots + 3]
-        step = pl.program_id(0)
-
-        @pl.when(step == 0)
-        def _():
-            total_ref[...] = jnp.zeros_like(total_ref)
-
-        total_ref[...] += jnp.dot(out_ref[...], weight_ref[...], preferred_element_type=jnp.float32)
-
-        @pl.when(step == pl.num_programs(0) - 1)
-        def _():
-            peer_out_ref[...] = total_ref[...].astype(peer_out_ref.dtype)
+        total = None
+        for h in range(heads_kv):
+            copies[h].wait()
+            rows = slice(h * group, (h + 1) * group)
+            term = jnp.dot(out_ref[:, rows], weight_ref[rows, :], preferred_element_type=jnp.float32)
+            total = term if total is None else total + term
+        peer_out_ref[...] = total.astype(peer_out_ref.dtype)
 
 
 def tables(positions):
@@ -95,49 +108,38 @@
 
 def attend(query_pos, key_pos, key_limit, queries, slots, uses, heads_kv, out_weight, peer):
     rows, width = queries.shape
-    block = slots[0].shape[1]
     n_slots = len(slots)
-    count = len(uses[0]) * block
-    group = width // heads_kv
+    count = key_pos.shape[0]
     project = out_weight is not None
     query_cos, query_sin = tables(query_pos)
     key_cos, key_sin = tables(key_pos)
-    whole = lambda h, p, c: (0, 0)
-    in_specs = [
-        pl.BlockSpec((rows, 1), whole),
-        pl.BlockSpec((1, count), whole),
-        pl.BlockSpec((rows, HEAD_SIZE), whole),
-        pl.BlockSpec((rows, HEAD_SIZE), whole),
-        pl.BlockSpec((count, HEAD_SIZE), whole),
-        pl.BlockSpec((count, HEAD_SIZE), whole),
-        pl.BlockSpec((rows, group), lambda h, p, c: (0, h)),
-    ]
-    in_specs += [pl.BlockSpec((None, block, HEAD_SIZE), lambda h, p, c: (0, 0, h))] * n_slots
-    in_specs += [pl.BlockSpec((None, block, HEAD_SIZE), lambda h, p, c: (1, 0, h))] * n_slots
+    vmem = pl.BlockSpec(memory_space=pltpu.VMEM)
+    smem = pl.BlockSpec(memory_space=pltpu.SMEM)
+    core = (lax.axis_index("ctx") % 2).astype(jnp.int32)
+    args = [peer.reshape(1), core.reshape(1), query_pos.reshape(rows, 1), key_limit, query_cos, query_sin,
+            key_cos, key_sin, queries] + slots
+    in_specs = [smem, smem] + [vmem] * (7 + n_slots)
     out_shape = [jax.ShapeDtypeStruct((rows, width), jnp.bfloat16)]
-    out_specs = [pl.BlockSpec((rows, group), lambda h, p, c: (0, h))]
+    out_specs = [vmem]
     scratch = []
-    core = (lax.axis_index("ctx") % 2).astype(jnp.int32)
-    args = [peer.reshape(1), core.reshape(1), query_pos.reshape(rows, 1), key_limit, query_cos, query_sin, key_cos, key_sin,
-            queries] + slots + slots
     flops = 4 * rows * count * width
     moved = 2 * (2 * rows * width + 2 * count * heads_kv * HEAD_SIZE)
     if project:
         part = out_weight.shape[1] // 2
-        in_specs.append(pl.BlockSpec((group, part), lambda h, p, c: (h, p[0])))
+        args.append(out_weight)
+        in_specs.append(pl.BlockSpec(memory_space=pl.ANY))
         out_shape.append(jax.ShapeDtypeStruct((rows, part), jnp.bfloat16))
-        out_specs.append(pl.BlockSpec((rows, part), whole))
-        scratch.append(pltpu.VMEM((rows, part), jnp.float32))
-        args.append(out_weight)
+        out_specs.append(vmem)
+        scratch += [pltpu.VMEM((width, part), jnp.bfloat16), pltpu.SemaphoreType.DMA((heads_kv,))]
         flops += 2 * rows * width * part
         moved += 2 * (width * part + rows * part)
     return pl.pallas_call(
-        functools.partial(attention_kernel, n_slots, uses, project),
+        functools.partial(attention_kernel, n_slots, uses, heads_kv, project),
         out_shape=out_shape,
-        grid_spec=pltpu.PrefetchScalarGridSpec(
-            num_scalar_prefetch=2, grid=(heads_kv,), in_specs=in_specs, out_specs=out_specs,
-            scratch_shapes=scratch,
-        ),
+        in_specs=in_specs,
+        out_specs=out_specs,
+        scratch_shapes=scratch,
+        compiler_params=pltpu.CompilerParams(vmem_limit_bytes=48 * 1024 * 1024),
         cost_estimate=pl.CostEstimate(
             flops=flops, transcendentals=rows * count * width // HEAD_SIZE, bytes_accessed=moved
         ),

time: 67.5 us -> 68.4 us (1.013)
  local copies, waits for them, and re-layouts: 0.98 us -> 5.19 us
  Pallas kernels: 12.2 us -> 9.65 us
  other arithmetic: 12.2 us -> 9.96 us
  waiting for transfers between devices: 13.1 us -> 14.1 us
  starting transfers between devices: 20.9 us -> 21.6 us
    unnamed x20 -> x12, local copies, waits for them, and re-layouts: 0.98 us -> 5.19 us
    pallas_call x1, Pallas kernels: 12.2 us -> 9.65 us  [attend(): pl.pallas_call(functools.partial(attention_kernel, n_slots, uses, heads_k...]
    concatenate x2, other arithmetic: 2.08 us -> 0.44 us  [tables(): jnp.concatenate([cosine, cosine], axis=1)]
    ppermute x4, waiting for transfers between devices: 5.27 us -> 6.89 us  [gather_window(): received[m] = lax.ppermute(kv, 'ctx', pairs)]
    ppermute x4, starting transfers between devices: 8.1 us -> 8.8 us  [gather_window(): passed.append(lax.ppermute(received[m], 'ctx', pairs))]
  transfers between devices with their start and end apart: 10 -> 10, of which waited for: 3 -> 3; matrix products, arithmetic and copies ran while one was open for 23% -> 19% of each run, Pallas kernels for 0% -> 0%
where the time goes in v8:
time: 68.4 us; the launch traced here: 67.9 us
  starting transfers between devices  21.6 us (32%)
  waiting for transfers between devices  14.1 us (21%)
  other arithmetic  9.96 us (15%)
  Pallas kernels  9.65 us (14%)
  local copies, waits for them, and re-layouts  5.19 us (8%)
  matrix products  4.64 us (7%)
  between operations  2.77 us (4%)
    ppermute x4, starting transfers between devices, gather_window(): received[m] = lax.ppermute(kv, 'ctx', pairs)  10.2 us
    pallas_call x1, Pallas kernels, attend(): pl.pallas_call(functools.partial(attention_kernel, n_slots, uses, heads_k...  9.65 us
    ppermute x4, starting transfers between devices, gather_window(): passed.append(lax.ppermute(received[m], 'ctx', pairs))  8.8 us
    ppermute x1, waiting for transfers between devices, on_device(): got = lax.ppermute(peer_terms, 'tp', [(0, 1), (1, 0)])  7.16 us
    ppermute x4, waiting for transfers between devices, gather_window(): received[m] = lax.ppermute(kv, 'ctx', pairs)  6.89 us
    unnamed x12, local copies, waits for them, and re-layouts  5.19 us
    dot_general x1, matrix products, on_device(): jnp.dot(attended, own_weight, preferred_element_type=jnp.float32)  4.64 us
    neg x2, other arithmetic, tables(): -sine  2.21 us
  transfers between devices with their start and end apart: 10, of which 3 were waited for; matrix products, arithmetic and copies ran while one was open for 19% of the time, Pallas kernels for 0%

profile of v8, /device:TPU:11, one launch (start us, length us, event | category | flops | bytes accessed | tf_op | source)
XLA Modules:
  0.0 67.9 jit_solution(7988535873600904649)
XLA Ops:
  0.0 1.0 %pad_maximum_fusion.2.refs_0_ = bf16[2,128,512]{2,1,0:T(8,128)(2,1)S(1)} fusion(bf16[1,128,512]{2,1,0:T(8,128)(2,1)} %bitcast.8, bf16[1,128,512]{2,1,0:T(8,128)(2,1)} %bitcast.9), kind=kLoop, calls=%fused_computation.8 | loop fusion | flops 131072 | bytes 524288 | tf_op jit(solution)/shard_map/stack | solution.py:157
  1.0 3.7 %collective-permute-start = (bf16[2,128,512]{2,1,0:T(8,128)(2,1)S(1)}, bf16[2,128,512]{2,1,0:T(8,128)(2,1)S(1)}, u32[]{:S(2)}, u32[]{:S(2)}) collective-permute-start(bf16[2,128,512]{2,1,0:T(8,128)(2,1)S(1)} %pad_maximum_fusion.2.refs_0_), channel_id=1, source_target_pairs={{2,4},{6,8},{10,12},{14,16},{18,20},{22,24},{26,28},{3,5},{7,9},{1... | collective-permute-start | bytes 786440 | tf_op jit(solution)/shard_map/ppermute | solution.py:24
  4.8 1.9 %collective-permute-start.1 = (bf16[2,128,512]{2,1,0:T(8,128)(2,1)S(1)}, bf16[2,128,512]{2,1,0:T(8,128)(2,1)S(1)}, u32[]{:S(2)}, u32[]{:S(2)}) collective-permute-start(bf16[2,128,512]{2,1,0:T(8,128)(2,1)S(1)} %pad_maximum_fusion.2.refs_0_), channel_id=1, source_target_pairs={{0,6},{2,8},{4,10},{6,12},{8,14},{10,16},{12,18},{14,20},{16,22},{... | collective-permute-start | bytes 786440 | tf_op jit(solution)/shard_map/ppermute | solution.py:24
  6.7 2.6 %collective-permute-start.2 = (bf16[2,128,512]{2,1,0:T(8,128)(2,1)S(1)}, bf16[2,128,512]{2,1,0:T(8,128)(2,1)S(1)}, u32[]{:S(2)}, u32[]{:S(2)}) collective-permute-start(bf16[2,128,512]{2,1,0:T(8,128)(2,1)S(1)} %pad_maximum_fusion.2.refs_0_), channel_id=1, source_target_pairs={{0,10},{2,12},{4,14},{6,16},{8,18},{10,20},{12,22},{14,24},{16,26}... | collective-permute-start | bytes 786440 | tf_op jit(solution)/shard_map/ppermute | solution.py:24
  9.3 1.9 %collective-permute-start.3 = (bf16[2,128,512]{2,1,0:T(8,128)(2,1)S(1)}, bf16[2,128,512]{2,1,0:T(8,128)(2,1)S(1)}, u32[]{:S(2)}, u32[]{:S(2)}) collective-permute-start(bf16[2,128,512]{2,1,0:T(8,128)(2,1)S(1)} %pad_maximum_fusion.2.refs_0_), channel_id=1, source_target_pairs={{0,14},{2,16},{4,18},{6,20},{8,22},{10,24},{12,26},{14,28},{16,30}... | collective-permute-start | bytes 786440 | tf_op jit(solution)/shard_map/ppermute | solution.py:24
  11.2 1.3 %collective-permute-start.4 = (bf16[2,128,512]{2,1,0:T(8,128)(2,1)S(1)}, bf16[2,128,512]{2,1,0:T(8,128)(2,1)S(1)}, u32[]{:S(2)}, u32[]{:S(2)}) collective-permute-start(bf16[2,128,512]{2,1,0:T(8,128)(2,1)S(1)} %pad_maximum_fusion.2.refs_0_), channel_id=1, source_target_pairs={{0,2},{4,6},{8,10},{12,14},{16,18},{20,22},{24,26},{28,30},{1,3},{... | collective-permute-start | bytes 786440 | tf_op jit(solution)/shard_map/ppermute | solution.py:27
  15.9 1.3 %fusion.9 = s32[8]{0:T(128)S(1)} fusion(s32[8]{0:T(128)} %constant.46.clone, s32[8]{0:T(128)} %constant.47.clone, pred[]{:T(512)S(6)} %eq.14, s32[]{:T(128)} %select_reduce_fusion.3, s32[]{:T(128)S(6)} %axis_index.33), kind=kLoop, calls=%fused_computation.25 | loop fusion | flops 32 | bytes 105 | tf_op jit(solution)/shard_map/mul | solution.py:171
  17.3 1.9 %fusion.5 = (f32[1024,64]{1,0:T(8,128)S(1)}, f32[1024,64]{1,0:T(8,128)S(1)}, f32[1024,64]{1,0:T(8,128)S(1)}) fusion(f32[64]{0:T(128)S(1)} %multiply_power_fusion, f32[1024]{0:T(1024)S(1)} %get-tuple-element.15), kind=kLoop, calls=%fused_computation.9 | loop fusion | flops 131072 | bytes 790784 | tf_op jit(solution)/shard_map/neg | solution.py:106
  20.6 1.3 %collective-permute-start.5 = (bf16[2,128,512]{2,1,0:T(8,128)(2,1)S(1)}, bf16[2,128,512]{2,1,0:T(8,128)(2,1)S(1)}, u32[]{:S(2)}, u32[]{:S(2)}) collective-permute-start(bf16[2,128,512]{2,1,0:T(8,128)(2,1)S(1)} %collective-permute-done.refs_1_), channel_id=1, source_target_pairs={{0,2},{4,6},{8,10},{12,14},{16,18},{20,22},{24,26},{28,30},{1,3},{... | collective-permute-start | bytes 786440 | tf_op jit(solution)/shard_map/ppermute | solution.py:30
  21.9 1.2 %collective-permute-start.6 = (bf16[2,128,512]{2,1,0:T(8,128)(2,1)S(1)}, bf16[2,128,512]{2,1,0:T(8,128)(2,1)S(1)}, u32[]{:S(2)}, u32[]{:S(2)}) collective-permute-start(bf16[2,128,512]{2,1,0:T(8,128)(2,1)S(1)} %collective-permute-done.1.refs_2_), channel_id=1, source_target_pairs={{0,2},{4,6},{8,10},{12,14},{16,18},{20,22},{24,26},{28,30},{2,0},{... | collective-permute-start | bytes 786440 | tf_op jit(solution)/shard_map/ppermute | solution.py:30
  23.1 3.6 %collective-permute-done.2.refs_3_ = bf16[2,128,512]{2,1,0:T(8,128)(2,1)S(1)} collective-permute-done((bf16[2,128,512]{2,1,0:T(8,128)(2,1)S(1)}, bf16[2,128,512]{2,1,0:T(8,128)(2,1)S(1)}, u32[]{:S(2)}, u32[]{:S(2)}) %collective-permute-start.2) | collective-permute-done | bytes 262176 | tf_op jit(solution)/shard_map/ppermute | solution.py:24
  26.7 2.3 %collective-permute-start.7 = (bf16[2,128,512]{2,1,0:T(8,128)(2,1)S(1)}, bf16[2,128,512]{2,1,0:T(8,128)(2,1)S(1)}, u32[]{:S(2)}, u32[]{:S(2)}) collective-permute-start(bf16[2,128,512]{2,1,0:T(8,128)(2,1)S(1)} %collective-permute-done.2.refs_3_), channel_id=1, source_target_pairs={{0,2},{4,6},{8,10},{12,14},{16,18},{20,22},{24,26},{28,30},{2,0},{... | collective-permute-start | bytes 786440 | tf_op jit(solution)/shard_map/ppermute | solution.py:30
  29.1 3.3 %collective-permute-done.3.refs_4_ = bf16[2,128,512]{2,1,0:T(8,128)(2,1)S(1)} collective-permute-done((bf16[2,128,512]{2,1,0:T(8,128)(2,1)S(1)}, bf16[2,128,512]{2,1,0:T(8,128)(2,1)S(1)}, u32[]{:S(2)}, u32[]{:S(2)}) %collective-permute-start.3) | collective-permute-done | bytes 262176 | tf_op jit(solution)/shard_map/ppermute | solution.py:24
  32.3 4.0 %collective-permute-start.8 = (bf16[2,128,512]{2,1,0:T(8,128)(2,1)S(1)}, bf16[2,128,512]{2,1,0:T(8,128)(2,1)}, u32[]{:S(2)}, u32[]{:S(2)}) collective-permute-start(bf16[2,128,512]{2,1,0:T(8,128)(2,1)S(1)} %collective-permute-done.3.refs_4_), channel_id=1, source_target_pairs={{2,0},{6,4},{10,8},{14,12},{18,16},{22,20},{26,24},{30,28},{3,1},{... | collective-permute-start | bytes 786440 | tf_op jit(solution)/shard_map/ppermute | solution.py:30
  36.3 1.3 %select_reduce_fusion.1 = (s32[]{:T(128)}, s32[]{:T(128)}) fusion(s32[8]{0:T(128)} %param.13, s32[]{:T(128)S(6)} %sub.23, s32[8]{0:T(128)} %param.12), kind=kLoop, calls=%fused_computation.29 | loop fusion | flops 38 | bytes 76 | tf_op jit(solution)/shard_map/reduce_sum | solution.py:167
  40.4 1.0 %copy-done = bf16[128,2048]{1,0:T(8,128)(2,1)S(1)} copy-done((bf16[128,2048]{1,0:T(8,128)(2,1)S(1)}, bf16[128,2048]{1,0:T(8,128)(2,1)}, u32[]{:S(2)}) %copy-start) | copy-done | bytes 524312
  41.4 0.9 %copy-done.2 = bf16[2,128,512]{2,1,0:T(8,128)(2,1)S(1)} copy-done((bf16[2,128,512]{2,1,0:T(8,128)(2,1)S(1)}, bf16[2,128,512]{2,1,0:T(8,128)(2,1)}, u32[]{:S(2)}) %copy-start.2) | copy-done | bytes 262168
  42.4 0.9 %copy-done.4 = bf16[2,128,512]{2,1,0:T(8,128)(2,1)S(1)} copy-done((bf16[2,128,512]{2,1,0:T(8,128)(2,1)S(1)}, bf16[2,128,512]{2,1,0:T(8,128)(2,1)}, u32[]{:S(2)}) %copy-start.4) | copy-done | bytes 262168
  43.3 0.8 %copy-done.5 = s32[128,1]{1,0:T(8,128)S(1)} copy-done((s32[128,1]{1,0:T(8,128)S(1)}, s32[128,1]{1,0:T(8,128)}, u32[]{:S(2)}) %copy-start.5) | copy-done | bytes 536
  44.2 9.7 %shard_map.82 = (bf16[128,2048]{1,0:T(8,128)(2,1)S(1)}, bf16[128,2048]{1,0:T(8,128)(2,1)}) custom-call(s32[1]{0:T(128)} %bitcast.peer_ref, s32[1]{0:T(128)} %bitcast.1.core_ref, s32[128,1]{1,0:T(8,128)S(1)} %copy-done.5, s32[1,1024]{1,0:T(1,128)S(1)} %and_select_fusion.key_limit_ref, f32[128,128]{1,0:T(8,128)S(1)} %get-tuple-element.19.query_cos_ref, ...), custom_call_target="tpu_custom_call" | custom-call | flops 2147483648 | bytes 12058624 | tf_op jit(solution)/shard_map/pallas_call | solution.py:136
  53.8 1.3 %collective-permute-start.9 = (bf16[128,2048]{1,0:T(8,128)(2,1)}, bf16[128,2048]{1,0:T(8,128)(2,1)S(1)}, u32[]{:S(2)}, u32[]{:S(2)}) collective-permute-start(bf16[128,2048]{1,0:T(8,128)(2,1)} %get-tuple-element.8), channel_id=1, source_target_pairs={{0,1},{1,0},{2,3},{3,2},{4,5},{5,4},{6,7},{7,6},{8,9},{9,8},{10,11... | collective-permute-start | bytes 1572872 | tf_op jit(solution)/shard_map/ppermute | solution.py:183
  55.1 4.6 %fusion.2 = bf16[128,2048]{1,0:T(8,128)(2,1)S(1)} fusion(bf16[128,2048]{1,0:T(8,128)(2,1)S(1)} %get-tuple-element.7, bf16[2048,4096]{1,0:T(8,128)(2,1)} %refs_10_.1, s32[]{:T(128)S(6)} %select_n.53), kind=kOutput, calls=%fused_computation.2 | convolution fusion | flops 1074003968 | bytes 9437188 | tf_op jit(solution)/shard_map/dot_general | solution.py:186
  59.8 7.2 %collective-permute-done.9 = bf16[128,2048]{1,0:T(8,128)(2,1)S(1)} collective-permute-done((bf16[128,2048]{1,0:T(8,128)(2,1)}, bf16[128,2048]{1,0:T(8,128)(2,1)S(1)}, u32[]{:S(2)}, u32[]{:S(2)}) %collective-permute-start.9) | collective-permute-done | bytes 524320 | tf_op jit(solution)/shard_map/ppermute | solution.py:183
  66.9 0.9 %add_convert_fusion = bf16[128,2048]{1,0:T(8,128)(2,1)} fusion(bf16[128,2048]{1,0:T(8,128)(2,1)S(1)} %collective-permute-done.9, bf16[128,2048]{1,0:T(8,128)(2,1)S(1)} %fusion.2), kind=kLoop, calls=%fused_computation.3 | loop fusion | flops 1048576 | bytes 1572864 | tf_op jit(solution)/shard_map/convert_element_type | solution.py:188
  (26 shorter events, 4.9 us)
Async XLA Ops:
  1.0 19.6 %collective-permute-start = (bf16[2,128,512]{2,1,0:T(8,128)(2,1)S(1)}, bf16[2,128,512]{2,1,0:T(8,128)(2,1)S(1)}, u32[]{:S(2)}, u32[]{:S(2)}) collective-permute-start(bf16[2,128,512]{2,1,0:T(8,128)(2,1)S(1)} %pad_maximum_fusion.2.refs_0_), channel_id=1, source_target_pairs={{2,4},{6,8},{10,12},{14,16},{18,20},{22,24},{26,28},{3,5},{7,9},{1... | collective-permute-start | bytes 786440 | tf_op jit(solution)/shard_map/ppermute | solution.py:24
  4.8 17.1 %collective-permute-start.1 = (bf16[2,128,512]{2,1,0:T(8,128)(2,1)S(1)}, bf16[2,128,512]{2,1,0:T(8,128)(2,1)S(1)}, u32[]{:S(2)}, u32[]{:S(2)}) collective-permute-start(bf16[2,128,512]{2,1,0:T(8,128)(2,1)S(1)} %pad_maximum_fusion.2.refs_0_), channel_id=1, source_target_pairs={{0,6},{2,8},{4,10},{6,12},{8,14},{10,16},{12,18},{14,20},{16,22},{... | collective-permute-start | bytes 786440 | tf_op jit(solution)/shard_map/ppermute | solution.py:24
  6.7 20.0 %collective-permute-start.2 = (bf16[2,128,512]{2,1,0:T(8,128)(2,1)S(1)}, bf16[2,128,512]{2,1,0:T(8,128)(2,1)S(1)}, u32[]{:S(2)}, u32[]{:S(2)}) collective-permute-start(bf16[2,128,512]{2,1,0:T(8,128)(2,1)S(1)} %pad_maximum_fusion.2.refs_0_), channel_id=1, source_target_pairs={{0,10},{2,12},{4,14},{6,16},{8,18},{10,20},{12,22},{14,24},{16,26}... | collective-permute-start | bytes 786440 | tf_op jit(solution)/shard_map/ppermute | solution.py:24
  9.3 23.1 %collective-permute-start.3 = (bf16[2,128,512]{2,1,0:T(8,128)(2,1)S(1)}, bf16[2,128,512]{2,1,0:T(8,128)(2,1)S(1)}, u32[]{:S(2)}, u32[]{:S(2)}) collective-permute-start(bf16[2,128,512]{2,1,0:T(8,128)(2,1)S(1)} %pad_maximum_fusion.2.refs_0_), channel_id=1, source_target_pairs={{0,14},{2,16},{4,18},{6,20},{8,22},{10,24},{12,26},{14,28},{16,30}... | collective-permute-start | bytes 786440 | tf_op jit(solution)/shard_map/ppermute | solution.py:24
  11.2 27.7 %collective-permute-start.4 = (bf16[2,128,512]{2,1,0:T(8,128)(2,1)S(1)}, bf16[2,128,512]{2,1,0:T(8,128)(2,1)S(1)}, u32[]{:S(2)}, u32[]{:S(2)}) collective-permute-start(bf16[2,128,512]{2,1,0:T(8,128)(2,1)S(1)} %pad_maximum_fusion.2.refs_0_), channel_id=1, source_target_pairs={{0,2},{4,6},{8,10},{12,14},{16,18},{20,22},{24,26},{28,30},{1,3},{... | collective-permute-start | bytes 786440 | tf_op jit(solution)/shard_map/ppermute | solution.py:27
  20.6 18.3 %collective-permute-start.5 = (bf16[2,128,512]{2,1,0:T(8,128)(2,1)S(1)}, bf16[2,128,512]{2,1,0:T(8,128)(2,1)S(1)}, u32[]{:S(2)}, u32[]{:S(2)}) collective-permute-start(bf16[2,128,512]{2,1,0:T(8,128)(2,1)S(1)} %collective-permute-done.refs_1_), channel_id=1, source_target_pairs={{0,2},{4,6},{8,10},{12,14},{16,18},{20,22},{24,26},{28,30},{1,3},{... | collective-permute-start | bytes 786440 | tf_op jit(solution)/shard_map/ppermute | solution.py:30
  21.9 17.0 %collective-permute-start.6 = (bf16[2,128,512]{2,1,0:T(8,128)(2,1)S(1)}, bf16[2,128,512]{2,1,0:T(8,128)(2,1)S(1)}, u32[]{:S(2)}, u32[]{:S(2)}) collective-permute-start(bf16[2,128,512]{2,1,0:T(8,128)(2,1)S(1)} %collective-permute-done.1.refs_2_), channel_id=1, source_target_pairs={{0,2},{4,6},{8,10},{12,14},{16,18},{20,22},{24,26},{28,30},{2,0},{... | collective-permute-start | bytes 786440 | tf_op jit(solution)/shard_map/ppermute | solution.py:30
  26.7 12.9 %collective-permute-start.7 = (bf16[2,128,512]{2,1,0:T(8,128)(2,1)S(1)}, bf16[2,128,512]{2,1,0:T(8,128)(2,1)S(1)}, u32[]{:S(2)}, u32[]{:S(2)}) collective-permute-start(bf16[2,128,512]{2,1,0:T(8,128)(2,1)S(1)} %collective-permute-done.2.refs_3_), channel_id=1, source_target_pairs={{0,2},{4,6},{8,10},{12,14},{16,18},{20,22},{24,26},{28,30},{2,0},{... | collective-permute-start | bytes 786440 | tf_op jit(solution)/shard_map/ppermute | solution.py:30
  32.3 8.0 %collective-permute-start.8 = (bf16[2,128,512]{2,1,0:T(8,128)(2,1)S(1)}, bf16[2,128,512]{2,1,0:T(8,128)(2,1)}, u32[]{:S(2)}, u32[]{:S(2)}) collective-permute-start(bf16[2,128,512]{2,1,0:T(8,128)(2,1)S(1)} %collective-permute-done.3.refs_4_), channel_id=1, source_target_pairs={{2,0},{6,4},{10,8},{14,12},{18,16},{22,20},{26,24},{30,28},{3,1},{... | collective-permute-start | bytes 786440 | tf_op jit(solution)/shard_map/ppermute | solution.py:30
  39.0 0.7 %copy-start.1 = (bf16[2,128,512]{2,1,0:T(8,128)(2,1)}, bf16[2,128,512]{2,1,0:T(8,128)(2,1)S(1)}, u32[]{:S(2)}) copy-start(bf16[2,128,512]{2,1,0:T(8,128)(2,1)S(1)} %collective-permute-done.6.refs_7_) | copy-start | bytes 786436
  39.7 0.7 %copy-start.3 = (bf16[2,128,512]{2,1,0:T(8,128)(2,1)}, bf16[2,128,512]{2,1,0:T(8,128)(2,1)S(1)}, u32[]{:S(2)}) copy-start(bf16[2,128,512]{2,1,0:T(8,128)(2,1)S(1)} %collective-permute-done.7.refs_8_) | copy-start | bytes 786436
  40.4 1.0 %copy-start = (bf16[128,2048]{1,0:T(8,128)(2,1)S(1)}, bf16[128,2048]{1,0:T(8,128)(2,1)}, u32[]{:S(2)}) copy-start(bf16[128,2048]{1,0:T(8,128)(2,1)} %query_ref.1) | copy-start | bytes 1572868
  41.4 0.9 %copy-start.2 = (bf16[2,128,512]{2,1,0:T(8,128)(2,1)S(1)}, bf16[2,128,512]{2,1,0:T(8,128)(2,1)}, u32[]{:S(2)}) copy-start(bf16[2,128,512]{2,1,0:T(8,128)(2,1)} %copy-done.1) | copy-start | bytes 786436
  42.4 0.9 %copy-start.4 = (bf16[2,128,512]{2,1,0:T(8,128)(2,1)S(1)}, bf16[2,128,512]{2,1,0:T(8,128)(2,1)}, u32[]{:S(2)}) copy-start(bf16[2,128,512]{2,1,0:T(8,128)(2,1)} %copy-done.3) | copy-start | bytes 786436
  43.3 0.8 %copy-start.5 = (s32[128,1]{1,0:T(8,128)S(1)}, s32[128,1]{1,0:T(8,128)}, u32[]{:S(2)}) copy-start(s32[128,1]{1,0:T(8,128)} %iota_add_fusion.query_pos_ref) | copy-start | bytes 1540
  53.8 13.1 %collective-permute-start.9 = (bf16[128,2048]{1,0:T(8,128)(2,1)}, bf16[128,2048]{1,0:T(8,128)(2,1)S(1)}, u32[]{:S(2)}, u32[]{:S(2)}) collective-permute-start(bf16[128,2048]{1,0:T(8,128)(2,1)} %get-tuple-element.8), channel_id=1, source_target_pairs={{0,1},{1,0},{2,3},{3,2},{4,5},{5,4},{6,7},{7,6},{8,9},{9,8},{10,11... | collective-permute-start | bytes 1572872 | tf_op jit(solution)/shard_map/ppermute | solution.py:183

commit v9 on v8

--- a/solution.py
+++ b/solution.py
@@ -22,20 +22,22 @@
         else:
             pairs = [(j, j + s) for j in range(n - s)]
         received[m] = lax.ppermute(kv, "ctx", pairs)
+        if m == half - 1:
+            direct = lax.ppermute(kv, "ctx", [(j, j + s - 1) for j in range(0, n - s + 1, 2)])
     up = [(j, j + 1) for j in range(0, n, 2)]
     down = [(j + 1, j) for j in range(0, n, 2)]
     passed = [lax.ppermute(kv, "ctx", up)]
-    for m in range(half):
-        pairs = (up if m < half - 1 else []) + (down if m > 0 else [])
-        passed.append(lax.ppermute(received[m], "ctx", pairs))
-    slots = [kv] + received + passed
-    even_use = [0] + [1 + m for m in range(half)] + [2 + half + m for m in range(1, half)]
-    odd_use = [0] + [1 + m for m in range(1, half)] + [1 + half] + [2 + half + m for m in range(half - 1)]
-    even_shift = [0] + [2 * m + 1 for m in range(half)] + [2 * m for m in range(1, half)]
-    odd_shift = [0] + [2 * m + 1 for m in range(1, half)] + [1] + [2 * m + 2 for m in range(half - 1)]
+    for m in range(half - 1):
+        passed.append(lax.ppermute(received[m], "ctx", up + (down if m > 0 else [])))
+    slots = [kv] + received + [direct] + passed
+    even = [(0, 0)] + [(1 + m, 2 * m + 1) for m in range(half)]
+    even += [(3 + half + m, 2 * m) for m in range(1, half - 1)] + [(1 + half, window - 2)]
+    odd = [(0, 0)] + [(1 + m, 2 * m + 1) for m in range(1, half)] + [(2 + half, 1)]
+    odd += [(3 + half + m, 2 * m + 2) for m in range(half - 1)]
     core = lax.axis_index("ctx") % 2
-    shift = jnp.where(core == 0, jnp.array(even_shift, jnp.int32), jnp.array(odd_shift, jnp.int32))
-    return slots, (even_use, odd_use), shift
+    shift = jnp.where(core == 0, jnp.array([t for _, t in even], jnp.int32),
+                      jnp.array([t for _, t in odd], jnp.int32))
+    return slots, ([s for s, _ in even], [s for s, _ in odd]), shift
 
 
 def turn(rows, cosine, sine):
@@ -44,10 +46,11 @@
 
 
 def attention_kernel(n_slots, uses, heads_kv, project, peer_ref, core_ref, query_pos_ref, key_limit_ref,
-                     query_cos_ref, query_sin_ref, key_cos_ref, key_sin_ref, query_ref, *refs):
-    slot_refs = refs[:n_slots]
+                     query_cos_ref, query_sin_ref, key_cos_ref, key_sin_ref, query_any, *refs):
+    slot_any = refs[:n_slots]
+    refs = refs[n_slots:]
     if project:
-        weight_hbm, out_ref, peer_out_ref, weight_ref, copy_sem = refs[n_slots:]
+        weight_hbm, out_ref, peer_out_ref, query_ref, slot_ref, load_sem, weight_ref, copy_sem = refs
         group = query_ref.shape[1] // heads_kv
         part = weight_ref.shape[1]
         copies = [
@@ -61,16 +64,22 @@
         for copy in copies:
             copy.start()
     else:
-        (out_ref,) = refs[n_slots:]
+        out_ref, query_ref, slot_ref, load_sem = refs
+    loads = [pltpu.make_async_copy(query_any, query_ref, load_sem.at[n_slots])]
+    loads += [pltpu.make_async_copy(slot_any[j], slot_ref.at[j], load_sem.at[j]) for j in range(n_slots)]
+    for load in loads:
+        load.start()
+    for load in loads:
+        load.wait()
     allowed = key_limit_ref[...] <= query_pos_ref[...]
     heads_here = query_ref.shape[1] // HEAD_SIZE // heads_kv
 
     def body(use):
         for h in range(heads_kv):
             head = slice(h * HEAD_SIZE, (h + 1) * HEAD_SIZE)
-            keys = turn(jnp.concatenate([slot_refs[j][0, :, head] for j in use], axis=0),
+            keys = turn(jnp.concatenate([slot_ref[j, 0, :, head] for j in use], axis=0),
                         key_cos_ref[...], key_sin_ref[...])
-            values = jnp.concatenate([slot_refs[j][1, :, head] for j in use], axis=0)
+            values = jnp.concatenate([slot_ref[j, 1, :, head] for j in use], axis=0)
             for g in range(heads_here):
                 q = h * heads_here + g
                 columns = slice(q * HEAD_SIZE, (q + 1) * HEAD_SIZE)
@@ -113,23 +122,28 @@
     project = out_weight is not None
     query_cos, query_sin = tables(query_pos)
     key_cos, key_sin = tables(key_pos)
-    vmem = pl.BlockSpec(memory_space=pltpu.VMEM)
     smem = pl.BlockSpec(memory_space=pltpu.SMEM)
+
+    def vmem(shape):
+        return pl.BlockSpec(shape, lambda: (0,) * len(shape))
+
     core = (lax.axis_index("ctx") % 2).astype(jnp.int32)
     args = [peer.reshape(1), core.reshape(1), query_pos.reshape(rows, 1), key_limit, query_cos, query_sin,
             key_cos, key_sin, queries] + slots
-    in_specs = [smem, smem] + [vmem] * (7 + n_slots)
+    anywhere = pl.BlockSpec(memory_space=pl.ANY)
+    in_specs = [smem, smem] + [vmem(x.shape) for x in args[2:8]] + [anywhere] * (1 + n_slots)
     out_shape = [jax.ShapeDtypeStruct((rows, width), jnp.bfloat16)]
-    out_specs = [vmem]
-    scratch = []
+    out_specs = [vmem((rows, width))]
+    scratch = [pltpu.VMEM((rows, width), jnp.bfloat16), pltpu.VMEM((n_slots,) + slots[0].shape, jnp.bfloat16),
+               pltpu.SemaphoreType.DMA((n_slots + 1,))]
     flops = 4 * rows * count * width
     moved = 2 * (2 * rows * width + 2 * count * heads_kv * HEAD_SIZE)
     if project:
         part = out_weight.shape[1] // 2
         args.append(out_weight)
-        in_specs.append(pl.BlockSpec(memory_space=pl.ANY))
+        in_specs.append(anywhere)
         out_shape.append(jax.ShapeDtypeStruct((rows, part), jnp.bfloat16))
-        out_specs.append(vmem)
+        out_specs.append(vmem((rows, part)))
         scratch += [pltpu.VMEM((width, part), jnp.bfloat16), pltpu.SemaphoreType.DMA((heads_kv,))]
         flops += 2 * rows * width * part
         moved += 2 * (width * part + rows * part)

time: 68.4 us -> 73 us (1.067)
  the two profiles are of different devices: /device:TPU:11 before, /device:TPU:24 now
where the time goes in v9:
time: 73 us; the launch traced here: 72.5 us
  starting transfers between devices  19.3 us (26%)
  waiting for transfers between devices  18.4 us (25%)
  Pallas kernels  12.2 us (17%)
  other arithmetic  9.96 us (14%)
  local copies, waits for them, and re-layouts  5.2 us (7%)
  matrix products  4.64 us (6%)
  between operations  2.75 us (4%)
    pallas_call x1, Pallas kernels, attend(): pl.pallas_call(functools.partial(attention_kernel, n_slots, uses, heads_k...  12.2 us
    ppermute x4, waiting for transfers between devices, gather_window(): received[m] = lax.ppermute(kv, 'ctx', pairs)  10.5 us
    ppermute x3, starting transfers between devices, gather_window(): lax.ppermute(received[m], 'ctx', up + (down if m > 0 else []))  7.71 us
    ppermute x1, waiting for transfers between devices, on_device(): got = lax.ppermute(peer_terms, 'tp', [(0, 1), (1, 0)])  7.53 us
    ppermute x4, starting transfers between devices, gather_window(): received[m] = lax.ppermute(kv, 'ctx', pairs)  6.1 us
    unnamed x12, local copies, waits for them, and re-layouts  5.2 us
    dot_general x1, matrix products, on_device(): jnp.dot(attended, own_weight, preferred_element_type=jnp.float32)  4.64 us
    ppermute x1, starting transfers between devices, gather_window(): passed = [lax.ppermute(kv, 'ctx', up)]  2.61 us
  transfers between devices with their start and end apart: 10, of which 3 were waited for; matrix products, arithmetic and copies ran while one was open for 17% of the time, Pallas kernels for 0%

profile of v9, /device:TPU:24, one launch (start us, length us, event | category | flops | bytes accessed | tf_op | source)
XLA Modules:
  0.0 72.5 jit_solution(9056546359039527541)
XLA Ops:
  0.0 1.0 %pad_maximum_fusion.2.refs_0_ = bf16[2,128,512]{2,1,0:T(8,128)(2,1)S(1)} fusion(bf16[1,128,512]{2,1,0:T(8,128)(2,1)} %bitcast.8, bf16[1,128,512]{2,1,0:T(8,128)(2,1)} %bitcast.9), kind=kLoop, calls=%fused_computation.8 | loop fusion | flops 131072 | bytes 524288 | tf_op jit(solution)/shard_map/stack | solution.py:171
  1.0 1.3 %collective-permute-start = (bf16[2,128,512]{2,1,0:T(8,128)(2,1)S(1)}, bf16[2,128,512]{2,1,0:T(8,128)(2,1)S(1)}, u32[]{:S(2)}, u32[]{:S(2)}) collective-permute-start(bf16[2,128,512]{2,1,0:T(8,128)(2,1)S(1)} %pad_maximum_fusion.2.refs_0_), channel_id=1, source_target_pairs={{2,4},{6,8},{10,12},{14,16},{18,20},{22,24},{26,28},{3,5},{7,9},{1... | collective-permute-start | bytes 786440 | tf_op jit(solution)/shard_map/ppermute | solution.py:24
  2.3 2.2 %collective-permute-start.1 = (bf16[2,128,512]{2,1,0:T(8,128)(2,1)S(1)}, bf16[2,128,512]{2,1,0:T(8,128)(2,1)S(1)}, u32[]{:S(2)}, u32[]{:S(2)}) collective-permute-start(bf16[2,128,512]{2,1,0:T(8,128)(2,1)S(1)} %pad_maximum_fusion.2.refs_0_), channel_id=1, source_target_pairs={{0,6},{2,8},{4,10},{6,12},{8,14},{10,16},{12,18},{14,20},{16,22},{... | collective-permute-start | bytes 786440 | tf_op jit(solution)/shard_map/ppermute | solution.py:24
  4.5 1.3 %collective-permute-start.2 = (bf16[2,128,512]{2,1,0:T(8,128)(2,1)S(1)}, bf16[2,128,512]{2,1,0:T(8,128)(2,1)S(1)}, u32[]{:S(2)}, u32[]{:S(2)}) collective-permute-start(bf16[2,128,512]{2,1,0:T(8,128)(2,1)S(1)} %pad_maximum_fusion.2.refs_0_), channel_id=1, source_target_pairs={{0,10},{2,12},{4,14},{6,16},{8,18},{10,20},{12,22},{14,24},{16,26}... | collective-permute-start | bytes 786440 | tf_op jit(solution)/shard_map/ppermute | solution.py:24
  5.8 1.3 %collective-permute-start.3 = (bf16[2,128,512]{2,1,0:T(8,128)(2,1)S(1)}, bf16[2,128,512]{2,1,0:T(8,128)(2,1)S(1)}, u32[]{:S(2)}, u32[]{:S(2)}) collective-permute-start(bf16[2,128,512]{2,1,0:T(8,128)(2,1)S(1)} %pad_maximum_fusion.2.refs_0_), channel_id=1, source_target_pairs={{0,14},{2,16},{4,18},{6,20},{8,22},{10,24},{12,26},{14,28},{16,30}... | collective-permute-start | bytes 786440 | tf_op jit(solution)/shard_map/ppermute | solution.py:24
  7.1 1.3 %collective-permute-start.4 = (bf16[2,128,512]{2,1,0:T(8,128)(2,1)S(1)}, bf16[2,128,512]{2,1,0:T(8,128)(2,1)S(1)}, u32[]{:S(2)}, u32[]{:S(2)}) collective-permute-start(bf16[2,128,512]{2,1,0:T(8,128)(2,1)S(1)} %pad_maximum_fusion.2.refs_0_), channel_id=1, source_target_pairs={{0,12},{4,16},{8,20},{12,24},{16,28},{1,13},{5,17},{9,21},{13,25},... | collective-permute-start | bytes 786440 | tf_op jit(solution)/shard_map/ppermute | solution.py:26
  8.5 0.8 %select_reduce_fusion = s32[8]{0:T(128)S(1)} fusion(s32[8]{0:T(128)} %param.12), kind=kLoop, calls=%fused_computation.19 | loop fusion | flops 184 | bytes 64 | tf_op jit(solution)/shard_map/reduce_sum | solution.py:174
  11.8 1.3 %fusion.9 = s32[8]{0:T(128)S(1)} fusion(s32[8]{0:T(128)} %constant.46.clone, s32[8]{0:T(128)} %constant.47.clone, pred[]{:T(512)S(6)} %eq.14, s32[]{:T(128)} %select_reduce_fusion.3, s32[]{:T(128)S(6)} %axis_index.33), kind=kLoop, calls=%fused_computation.25 | loop fusion | flops 32 | bytes 105 | tf_op jit(solution)/shard_map/mul | solution.py:185
  13.2 1.9 %fusion.5 = (f32[1024,64]{1,0:T(8,128)S(1)}, f32[1024,64]{1,0:T(8,128)S(1)}, f32[1024,64]{1,0:T(8,128)S(1)}) fusion(f32[64]{0:T(128)S(1)} %multiply_power_fusion, f32[1024]{0:T(1024)S(1)} %get-tuple-element.15), kind=kLoop, calls=%fused_computation.9 | loop fusion | flops 131072 | bytes 790784 | tf_op jit(solution)/shard_map/neg | solution.py:115
  16.5 2.6 %collective-permute-start.5 = (bf16[2,128,512]{2,1,0:T(8,128)(2,1)S(1)}, bf16[2,128,512]{2,1,0:T(8,128)(2,1)S(1)}, u32[]{:S(2)}, u32[]{:S(2)}) collective-permute-start(bf16[2,128,512]{2,1,0:T(8,128)(2,1)S(1)} %pad_maximum_fusion.2.refs_0_), channel_id=1, source_target_pairs={{0,2},{4,6},{8,10},{12,14},{16,18},{20,22},{24,26},{28,30},{1,3},{... | collective-permute-start | bytes 786440 | tf_op jit(solution)/shard_map/ppermute | solution.py:29
  19.1 1.3 %collective-permute-start.6 = (bf16[2,128,512]{2,1,0:T(8,128)(2,1)S(1)}, bf16[2,128,512]{2,1,0:T(8,128)(2,1)S(1)}, u32[]{:S(2)}, u32[]{:S(2)}) collective-permute-start(bf16[2,128,512]{2,1,0:T(8,128)(2,1)S(1)} %collective-permute-done.refs_1_), channel_id=1, source_target_pairs={{0,2},{4,6},{8,10},{12,14},{16,18},{20,22},{24,26},{28,30},{1,3},{... | collective-permute-start | bytes 786440 | tf_op jit(solution)/shard_map/ppermute | solution.py:31
  20.5 10.5 %collective-permute-done.2.refs_3_ = bf16[2,128,512]{2,1,0:T(8,128)(2,1)S(1)} collective-permute-done((bf16[2,128,512]{2,1,0:T(8,128)(2,1)S(1)}, bf16[2,128,512]{2,1,0:T(8,128)(2,1)S(1)}, u32[]{:S(2)}, u32[]{:S(2)}) %collective-permute-start.2) | collective-permute-done | bytes 262176 | tf_op jit(solution)/shard_map/ppermute | solution.py:24
  31.0 6.4 %collective-permute-start.8 = (bf16[2,128,512]{2,1,0:T(8,128)(2,1)S(1)}, bf16[2,128,512]{2,1,0:T(8,128)(2,1)}, u32[]{:S(2)}, u32[]{:S(2)}) collective-permute-start(bf16[2,128,512]{2,1,0:T(8,128)(2,1)S(1)} %collective-permute-done.2.refs_3_), channel_id=1, source_target_pairs={{0,2},{4,6},{8,10},{12,14},{16,18},{20,22},{24,26},{28,30},{2,0},{... | collective-permute-start | bytes 786440 | tf_op jit(solution)/shard_map/ppermute | solution.py:31
  37.4 1.3 %select_reduce_fusion.1 = (s32[]{:T(128)}, s32[]{:T(128)}) fusion(s32[8]{0:T(128)} %param.13, s32[]{:T(128)S(6)} %sub.23, s32[8]{0:T(128)} %param.12), kind=kLoop, calls=%fused_computation.29 | loop fusion | flops 38 | bytes 76 | tf_op jit(solution)/shard_map/reduce_sum | solution.py:181
  41.1 0.7 copy-done.3
  41.8 1.0 %copy-done = bf16[128,2048]{1,0:T(8,128)(2,1)S(1)} copy-done((bf16[128,2048]{1,0:T(8,128)(2,1)S(1)}, bf16[128,2048]{1,0:T(8,128)(2,1)}, u32[]{:S(2)}) %copy-start) | copy-done | bytes 524312
  42.8 0.9 %copy-done.2 = bf16[2,128,512]{2,1,0:T(8,128)(2,1)S(1)} copy-done((bf16[2,128,512]{2,1,0:T(8,128)(2,1)S(1)}, bf16[2,128,512]{2,1,0:T(8,128)(2,1)}, u32[]{:S(2)}) %copy-start.2) | copy-done | bytes 262168
  43.8 0.9 %copy-done.4 = bf16[2,128,512]{2,1,0:T(8,128)(2,1)S(1)} copy-done((bf16[2,128,512]{2,1,0:T(8,128)(2,1)S(1)}, bf16[2,128,512]{2,1,0:T(8,128)(2,1)}, u32[]{:S(2)}) %copy-start.4) | copy-done | bytes 262168
  44.7 0.8 %copy-done.5 = s32[128,1]{1,0:T(8,128)S(1)} copy-done((s32[128,1]{1,0:T(8,128)S(1)}, s32[128,1]{1,0:T(8,128)}, u32[]{:S(2)}) %copy-start.5) | copy-done | bytes 536
  45.6 12.2 %shard_map.82 = (bf16[128,2048]{1,0:T(8,128)(2,1)S(1)}, bf16[128,2048]{1,0:T(8,128)(2,1)}) custom-call(s32[1]{0:T(128)} %bitcast.peer_ref, s32[1]{0:T(128)} %bitcast.1.core_ref, s32[128,1]{1,0:T(8,128)S(1)} %copy-done.5, s32[1,1024]{1,0:T(1,128)S(1)} %and_select_fusion.key_limit_ref, f32[128,128]{1,0:T(8,128)S(1)} %get-tuple-element.19.query_cos_ref, ...), custom_call_target="tpu_custom_call" | custom-call | flops 2147483648 | bytes 12058624 | tf_op jit(solution)/shard_map/pallas_call | solution.py:150
  57.8 1.6 %collective-permute-start.9 = (bf16[128,2048]{1,0:T(8,128)(2,1)}, bf16[128,2048]{1,0:T(8,128)(2,1)S(1)}, u32[]{:S(2)}, u32[]{:S(2)}) collective-permute-start(bf16[128,2048]{1,0:T(8,128)(2,1)} %get-tuple-element.8), channel_id=1, source_target_pairs={{0,1},{1,0},{2,3},{3,2},{4,5},{5,4},{6,7},{7,6},{8,9},{9,8},{10,11... | collective-permute-start | bytes 1572872 | tf_op jit(solution)/shard_map/ppermute | solution.py:197
  59.4 4.6 %fusion.2 = bf16[128,2048]{1,0:T(8,128)(2,1)S(1)} fusion(bf16[128,2048]{1,0:T(8,128)(2,1)S(1)} %get-tuple-element.7, bf16[2048,4096]{1,0:T(8,128)(2,1)} %refs_10_.1, s32[]{:T(128)S(6)} %select_n.53), kind=kOutput, calls=%fused_computation.2 | convolution fusion | flops 1074003968 | bytes 9437188 | tf_op jit(solution)/shard_map/dot_general | solution.py:200
  64.0 7.5 %collective-permute-done.9 = bf16[128,2048]{1,0:T(8,128)(2,1)S(1)} collective-permute-done((bf16[128,2048]{1,0:T(8,128)(2,1)}, bf16[128,2048]{1,0:T(8,128)(2,1)S(1)}, u32[]{:S(2)}, u32[]{:S(2)}) %collective-permute-start.9) | collective-permute-done | bytes 524320 | tf_op jit(solution)/shard_map/ppermute | solution.py:197
  71.5 0.9 %add_convert_fusion = bf16[128,2048]{1,0:T(8,128)(2,1)} fusion(bf16[128,2048]{1,0:T(8,128)(2,1)S(1)} %collective-permute-done.9, bf16[128,2048]{1,0:T(8,128)(2,1)S(1)} %fusion.2), kind=kLoop, calls=%fused_computation.3 | loop fusion | flops 1048576 | bytes 1572864 | tf_op jit(solution)/shard_map/convert_element_type | solution.py:202
  (26 shorter events, 3.8 us)
Async XLA Ops:
  1.0 15.5 %collective-permute-start = (bf16[2,128,512]{2,1,0:T(8,128)(2,1)S(1)}, bf16[2,128,512]{2,1,0:T(8,128)(2,1)S(1)}, u32[]{:S(2)}, u32[]{:S(2)}) collective-permute-start(bf16[2,128,512]{2,1,0:T(8,128)(2,1)S(1)} %pad_maximum_fusion.2.refs_0_), channel_id=1, source_target_pairs={{2,4},{6,8},{10,12},{14,16},{18,20},{22,24},{26,28},{3,5},{7,9},{1... | collective-permute-start | bytes 786440 | tf_op jit(solution)/shard_map/ppermute | solution.py:24
  2.3 16.8 %collective-permute-start.1 = (bf16[2,128,512]{2,1,0:T(8,128)(2,1)S(1)}, bf16[2,128,512]{2,1,0:T(8,128)(2,1)S(1)}, u32[]{:S(2)}, u32[]{:S(2)}) collective-permute-start(bf16[2,128,512]{2,1,0:T(8,128)(2,1)S(1)} %pad_maximum_fusion.2.refs_0_), channel_id=1, source_target_pairs={{0,6},{2,8},{4,10},{6,12},{8,14},{10,16},{12,18},{14,20},{16,22},{... | collective-permute-start | bytes 786440 | tf_op jit(solution)/shard_map/ppermute | solution.py:24
  4.5 26.4 %collective-permute-start.2 = (bf16[2,128,512]{2,1,0:T(8,128)(2,1)S(1)}, bf16[2,128,512]{2,1,0:T(8,128)(2,1)S(1)}, u32[]{:S(2)}, u32[]{:S(2)}) collective-permute-start(bf16[2,128,512]{2,1,0:T(8,128)(2,1)S(1)} %pad_maximum_fusion.2.refs_0_), channel_id=1, source_target_pairs={{0,10},{2,12},{4,14},{6,16},{8,18},{10,20},{12,22},{14,24},{16,26}... | collective-permute-start | bytes 786440 | tf_op jit(solution)/shard_map/ppermute | solution.py:24
  5.8 25.2 %collective-permute-start.3 = (bf16[2,128,512]{2,1,0:T(8,128)(2,1)S(1)}, bf16[2,128,512]{2,1,0:T(8,128)(2,1)S(1)}, u32[]{:S(2)}, u32[]{:S(2)}) collective-permute-start(bf16[2,128,512]{2,1,0:T(8,128)(2,1)S(1)} %pad_maximum_fusion.2.refs_0_), channel_id=1, source_target_pairs={{0,14},{2,16},{4,18},{6,20},{8,22},{10,24},{12,26},{14,28},{16,30}... | collective-permute-start | bytes 786440 | tf_op jit(solution)/shard_map/ppermute | solution.py:24
  7.1 33.2 %collective-permute-start.4 = (bf16[2,128,512]{2,1,0:T(8,128)(2,1)S(1)}, bf16[2,128,512]{2,1,0:T(8,128)(2,1)S(1)}, u32[]{:S(2)}, u32[]{:S(2)}) collective-permute-start(bf16[2,128,512]{2,1,0:T(8,128)(2,1)S(1)} %pad_maximum_fusion.2.refs_0_), channel_id=1, source_target_pairs={{0,12},{4,16},{8,20},{12,24},{16,28},{1,13},{5,17},{9,21},{13,25},... | collective-permute-start | bytes 786440 | tf_op jit(solution)/shard_map/ppermute | solution.py:26
  16.5 23.9 %collective-permute-start.5 = (bf16[2,128,512]{2,1,0:T(8,128)(2,1)S(1)}, bf16[2,128,512]{2,1,0:T(8,128)(2,1)S(1)}, u32[]{:S(2)}, u32[]{:S(2)}) collective-permute-start(bf16[2,128,512]{2,1,0:T(8,128)(2,1)S(1)} %pad_maximum_fusion.2.refs_0_), channel_id=1, source_target_pairs={{0,2},{4,6},{8,10},{12,14},{16,18},{20,22},{24,26},{28,30},{1,3},{... | collective-permute-start | bytes 786440 | tf_op jit(solution)/shard_map/ppermute | solution.py:29
  19.1 21.2 %collective-permute-start.6 = (bf16[2,128,512]{2,1,0:T(8,128)(2,1)S(1)}, bf16[2,128,512]{2,1,0:T(8,128)(2,1)S(1)}, u32[]{:S(2)}, u32[]{:S(2)}) collective-permute-start(bf16[2,128,512]{2,1,0:T(8,128)(2,1)S(1)} %collective-permute-done.refs_1_), channel_id=1, source_target_pairs={{0,2},{4,6},{8,10},{12,14},{16,18},{20,22},{24,26},{28,30},{1,3},{... | collective-permute-start | bytes 786440 | tf_op jit(solution)/shard_map/ppermute | solution.py:31
  31.0 10.1 %collective-permute-start.7 = (bf16[2,128,512]{2,1,0:T(8,128)(2,1)S(1)}, bf16[2,128,512]{2,1,0:T(8,128)(2,1)S(1)}, u32[]{:S(2)}, u32[]{:S(2)}) collective-permute-start(bf16[2,128,512]{2,1,0:T(8,128)(2,1)S(1)} %collective-permute-done.1.refs_2_), channel_id=1, source_target_pairs={{0,2},{4,6},{8,10},{12,14},{16,18},{20,22},{24,26},{28,30},{2,0},{... | collective-permute-start | bytes 786440 | tf_op jit(solution)/shard_map/ppermute | solution.py:31
  31.0 10.8 %collective-permute-start.8 = (bf16[2,128,512]{2,1,0:T(8,128)(2,1)S(1)}, bf16[2,128,512]{2,1,0:T(8,128)(2,1)}, u32[]{:S(2)}, u32[]{:S(2)}) collective-permute-start(bf16[2,128,512]{2,1,0:T(8,128)(2,1)S(1)} %collective-permute-done.2.refs_3_), channel_id=1, source_target_pairs={{0,2},{4,6},{8,10},{12,14},{16,18},{20,22},{24,26},{28,30},{2,0},{... | collective-permute-start | bytes 786440 | tf_op jit(solution)/shard_map/ppermute | solution.py:31
  40.4 0.7 copy-start.1
  41.1 0.7 copy-start.3
  41.8 1.0 %copy-start = (bf16[128,2048]{1,0:T(8,128)(2,1)S(1)}, bf16[128,2048]{1,0:T(8,128)(2,1)}, u32[]{:S(2)}) copy-start(bf16[128,2048]{1,0:T(8,128)(2,1)} %query_any.1) | copy-start | bytes 1572868
  42.8 0.9 %copy-start.2 = (bf16[2,128,512]{2,1,0:T(8,128)(2,1)S(1)}, bf16[2,128,512]{2,1,0:T(8,128)(2,1)}, u32[]{:S(2)}) copy-start(bf16[2,128,512]{2,1,0:T(8,128)(2,1)} %copy-done.1) | copy-start | bytes 786436
  43.8 0.9 %copy-start.4 = (bf16[2,128,512]{2,1,0:T(8,128)(2,1)S(1)}, bf16[2,128,512]{2,1,0:T(8,128)(2,1)}, u32[]{:S(2)}) copy-start(bf16[2,128,512]{2,1,0:T(8,128)(2,1)} %copy-done.3) | copy-start | bytes 786436
  44.7 0.8 %copy-start.5 = (s32[128,1]{1,0:T(8,128)S(1)}, s32[128,1]{1,0:T(8,128)}, u32[]{:S(2)}) copy-start(s32[128,1]{1,0:T(8,128)} %iota_add_fusion.query_pos_ref) | copy-start | bytes 1540
  57.8 13.8 %collective-permute-start.9 = (bf16[128,2048]{1,0:T(8,128)(2,1)}, bf16[128,2048]{1,0:T(8,128)(2,1)S(1)}, u32[]{:S(2)}, u32[]{:S(2)}) collective-permute-start(bf16[128,2048]{1,0:T(8,128)(2,1)} %get-tuple-element.8), channel_id=1, source_target_pairs={{0,1},{1,0},{2,3},{3,2},{4,5},{5,4},{6,7},{7,6},{8,9},{9,8},{10,11... | collective-permute-start | bytes 1572872 | tf_op jit(solution)/shard_map/ppermute | solution.py:197

commit v10 on v8

--- a/solution.py
+++ b/solution.py
@@ -13,29 +13,21 @@
 
 
 def gather_window(kv, n, window):
-    half = window // 2
-    received = [None] * half
-    for m in reversed(range(half)):
-        s = 2 * m + 1
+    received = []
+    for s in range(1, window, 2):
         if s == 1:
             pairs = [(j, j + 1) for j in range(1, n - 1, 2)]
         else:
             pairs = [(j, j + s) for j in range(n - s)]
-        received[m] = lax.ppermute(kv, "ctx", pairs)
-    up = [(j, j + 1) for j in range(0, n, 2)]
-    down = [(j + 1, j) for j in range(0, n, 2)]
-    passed = [lax.ppermute(kv, "ctx", up)]
-    for m in range(half):
-        pairs = (up if m < half - 1 else []) + (down if m > 0 else [])
-        passed.append(lax.ppermute(received[m], "ctx", pairs))
-    slots = [kv] + received + passed
-    even_use = [0] + [1 + m for m in range(half)] + [2 + half + m for m in range(1, half)]
-    odd_use = [0] + [1 + m for m in range(1, half)] + [1 + half] + [2 + half + m for m in range(half - 1)]
-    even_shift = [0] + [2 * m + 1 for m in range(half)] + [2 * m for m in range(1, half)]
-    odd_shift = [0] + [2 * m + 1 for m in range(1, half)] + [1] + [2 * m + 2 for m in range(half - 1)]
+        received.append(lax.ppermute(kv, "ctx", pairs))
+    across = [(j, j ^ 1) for j in range(n)]
+    passed = [lax.ppermute(block, "ctx", across) for block in [kv] + received]
+    half = window // 2
+    even_shift = [0] + [2 * m + 1 for m in range(half)] + [FAR, FAR] + [2 * m for m in range(1, half)]
+    odd_shift = [0, FAR] + [2 * m + 1 for m in range(1, half)] + [1] + [2 * m + 2 for m in range(half)]
     core = lax.axis_index("ctx") % 2
     shift = jnp.where(core == 0, jnp.array(even_shift, jnp.int32), jnp.array(odd_shift, jnp.int32))
-    return slots, (even_use, odd_use), shift
+    return [kv] + received + passed, shift
 
 
 def turn(rows, cosine, sine):
@@ -85,8 +77,7 @@
                 summed = jnp.dot(weights.astype(jnp.bfloat16), values, preferred_element_type=jnp.float32)
                 out_ref[:, columns] = (summed / totals).astype(out_ref.dtype)
 
-    for parity, use in enumerate(uses):
-        pl.when(core_ref[0] == parity)(functools.partial(body, use))
+    body(uses)
     if project:
         total = None
         for h in range(heads_kv):
@@ -154,7 +145,7 @@
     heads_kv = keys.shape[1] // HEAD_SIZE
     context_group = queries.shape[1] // keys.shape[1]
 
-    slots, uses, shift = gather_window(jnp.stack([keys, values]), n, window)
+    slots, shift = gather_window(jnp.stack([keys, values]), n, window)
 
     prompt_ids = jnp.arange(group_widths.shape[0], dtype=jnp.int32)
     offsets = jnp.sum(
@@ -178,7 +169,7 @@
     if n_tp == 2:
         me = lax.axis_index("tp")
         attended, peer_terms = attend(
-            query_pos, key_pos, key_limit, queries, slots, uses, heads_kv, out_weight, 1 - me
+            query_pos, key_pos, key_limit, queries, slots, list(range(len(slots))), heads_kv, out_weight, 1 - me
         )
         got = lax.ppermute(peer_terms, "tp", [(0, 1), (1, 0)])
         part = out_weight.shape[1] // 2
@@ -186,7 +177,7 @@
         own_terms = jnp.dot(attended, own_weight, preferred_element_type=jnp.float32)
         own_terms = lax.optimization_barrier(own_terms.astype(jnp.bfloat16)).astype(jnp.float32)
         return (own_terms + got.astype(jnp.float32)).astype(jnp.bfloat16)
-    (attended,) = attend(query_pos, key_pos, key_limit, queries, slots, uses, heads_kv, None, jnp.int32(0))
+    (attended,) = attend(query_pos, key_pos, key_limit, queries, slots, list(range(len(slots))), heads_kv, None, jnp.int32(0))
     terms = jnp.dot(attended, out_weight, preferred_element_type=jnp.float32)
     return lax.psum_scatter(terms.astype(jnp.bfloat16), "tp", scatter_dimension=1, tiled=True)
 

time: 68.4 us -> 63.2 us (0.924)
  the two profiles are of different devices: /device:TPU:11 before, /device:TPU:24 now
where the time goes in v10:
time: 63.2 us; the launch traced here: 62.8 us
  starting transfers between devices  16.1 us (25%)
  other arithmetic  13.8 us (22%)
  waiting for transfers between devices  13.7 us (22%)
  Pallas kernels  10.8 us (17%)
  matrix products  4.67 us (7%)
  between operations  2.71 us (4%)
  local copies, waits for them, and re-layouts  1.04 us (2%)
    pallas_call x1, Pallas kernels, attend(): pl.pallas_call(functools.partial(attention_kernel, n_slots, uses, heads_k...  10.8 us
    ppermute x5, starting transfers between devices, gather_window(): passed = [lax.ppermute(block, 'ctx', across) for block in [kv] + received]  8.35 us
    ppermute x1, waiting for transfers between devices, on_device(): got = lax.ppermute(peer_terms, 'tp', [(0, 1), (1, 0)])  7.98 us
    ppermute x4, starting transfers between devices, gather_window(): received.append(lax.ppermute(kv, 'ctx', pairs))  6.1 us
    ppermute x4, waiting for transfers between devices, gather_window(): received.append(lax.ppermute(kv, 'ctx', pairs))  5.02 us
    dot_general x1, matrix products, on_device(): jnp.dot(attended, own_weight, preferred_element_type=jnp.float32)  4.67 us
    neg x2, other arithmetic, tables(): -sine  4.57 us
    ppermute x1, starting transfers between devices, on_device(): got = lax.ppermute(peer_terms, 'tp', [(0, 1), (1, 0)])  1.61 us
  transfers between devices with their start and end apart: 10, of which 3 were waited for; matrix products, arithmetic and copies ran while one was open for 26% of the time, Pallas kernels for 0%

profile of v10, /device:TPU:24, one launch (start us, length us, event | category | flops | bytes accessed | tf_op | source)
XLA Modules:
  0.0 62.8 jit_solution(17099722690485005076)
XLA Ops:
  0.0 1.0 %pad_maximum_fusion.2.refs_0_ = bf16[2,128,512]{2,1,0:T(8,128)(2,1)S(1)} fusion(bf16[1,128,512]{2,1,0:T(8,128)(2,1)} %bitcast.12, bf16[1,128,512]{2,1,0:T(8,128)(2,1)} %bitcast.13), kind=kLoop, calls=%fused_computation.8 | loop fusion | flops 131072 | bytes 524288 | tf_op jit(solution)/shard_map/stack | solution.py:148
  1.0 1.3 %collective-permute-start = (bf16[2,128,512]{2,1,0:T(8,128)(2,1)S(1)}, bf16[2,128,512]{2,1,0:T(8,128)(2,1)S(1)}, u32[]{:S(2)}, u32[]{:S(2)}) collective-permute-start(bf16[2,128,512]{2,1,0:T(8,128)(2,1)S(1)} %pad_maximum_fusion.2.refs_0_), channel_id=1, source_target_pairs={{2,4},{6,8},{10,12},{14,16},{18,20},{22,24},{26,28},{3,5},{7,9},{1... | collective-permute-start | bytes 786440 | tf_op jit(solution)/shard_map/ppermute | solution.py:22
  2.3 2.2 %collective-permute-start.1 = (bf16[2,128,512]{2,1,0:T(8,128)(2,1)S(1)}, bf16[2,128,512]{2,1,0:T(8,128)(2,1)S(1)}, u32[]{:S(2)}, u32[]{:S(2)}) collective-permute-start(bf16[2,128,512]{2,1,0:T(8,128)(2,1)S(1)} %pad_maximum_fusion.2.refs_0_), channel_id=1, source_target_pairs={{0,6},{2,8},{4,10},{6,12},{8,14},{10,16},{12,18},{14,20},{16,22},{... | collective-permute-start | bytes 786440 | tf_op jit(solution)/shard_map/ppermute | solution.py:22
  4.5 1.3 %collective-permute-start.2 = (bf16[2,128,512]{2,1,0:T(8,128)(2,1)S(1)}, bf16[2,128,512]{2,1,0:T(8,128)(2,1)S(1)}, u32[]{:S(2)}, u32[]{:S(2)}) collective-permute-start(bf16[2,128,512]{2,1,0:T(8,128)(2,1)S(1)} %pad_maximum_fusion.2.refs_0_), channel_id=1, source_target_pairs={{0,10},{2,12},{4,14},{6,16},{8,18},{10,20},{12,22},{14,24},{16,26}... | collective-permute-start | bytes 786440 | tf_op jit(solution)/shard_map/ppermute | solution.py:22
  5.8 1.3 %collective-permute-start.3 = (bf16[2,128,512]{2,1,0:T(8,128)(2,1)S(1)}, bf16[2,128,512]{2,1,0:T(8,128)(2,1)S(1)}, u32[]{:S(2)}, u32[]{:S(2)}) collective-permute-start(bf16[2,128,512]{2,1,0:T(8,128)(2,1)S(1)} %pad_maximum_fusion.2.refs_0_), channel_id=1, source_target_pairs={{0,14},{2,16},{4,18},{6,20},{8,22},{10,24},{12,26},{14,28},{16,30}... | collective-permute-start | bytes 786440 | tf_op jit(solution)/shard_map/ppermute | solution.py:22
  7.1 1.4 %collective-permute-start.4 = (bf16[2,128,512]{2,1,0:T(8,128)(2,1)S(1)}, bf16[2,128,512]{2,1,0:T(8,128)(2,1)S(1)}, u32[]{:S(2)}, u32[]{:S(2)}) collective-permute-start(bf16[2,128,512]{2,1,0:T(8,128)(2,1)S(1)} %pad_maximum_fusion.2.refs_0_), channel_id=1, source_target_pairs={{0,2},{2,0},{4,6},{6,4},{8,10},{10,8},{12,14},{14,12},{16,18},{18,... | collective-permute-start | bytes 786440 | tf_op jit(solution)/shard_map/ppermute | solution.py:24
  8.5 0.5 multiply_power_fusion
  9.0 0.8 %select_reduce_fusion = s32[8]{0:T(128)S(1)} fusion(s32[8]{0:T(128)} %param.12), kind=kLoop, calls=%fused_computation.20 | loop fusion | flops 184 | bytes 64 | tf_op jit(solution)/shard_map/reduce_sum | solution.py:151
  9.8 0.6 %fusion.11 = s32[]{:T(128)} fusion(s32[8]{0:T(128)S(1)} %select_reduce_fusion, s32[]{:T(128)S(6)} %axis_index.33), kind=kLoop, calls=%fused_computation.27 | loop fusion | flops 23 | bytes 40 | tf_op jit(solution)/shard_map/reduce_sum | solution.py:154
  11.1 0.6 %select_reduce_fusion.3 = s32[]{:T(128)} fusion(s32[8]{0:T(128)S(1)} %select_reduce_fusion, s32[]{:T(128)S(6)} %sub.25), kind=kLoop, calls=%fused_computation.32 | loop fusion | flops 23 | bytes 40 | tf_op jit(solution)/shard_map/reduce_sum | solution.py:156
  12.4 1.3 %fusion.10 = s32[10]{0:T(128)S(1)} fusion(s32[10]{0:T(128)} %constant.46.clone, s32[10]{0:T(128)} %constant.47.clone, pred[]{:T(512)S(6)} %eq.14, s32[]{:T(128)} %select_reduce_fusion.3, s32[]{:T(128)S(6)} %axis_index.33), kind=kLoop, calls=%fused_computation.26 | loop fusion | flops 40 | bytes 129 | tf_op jit(solution)/shard_map/mul | solution.py:162
  13.8 1.3 %select_reduce_fusion.1 = (s32[]{:T(128)}, s32[]{:T(128)}) fusion(s32[8]{0:T(128)} %param.13, s32[]{:T(128)S(6)} %sub.25, s32[8]{0:T(128)} %param.12), kind=kLoop, calls=%fused_computation.30 | loop fusion | flops 38 | bytes 76 | tf_op jit(solution)/shard_map/reduce_sum | solution.py:158
  16.3 3.0 %fusion.5 = (f32[1280,64]{1,0:T(8,128)S(1)}, f32[1280,64]{1,0:T(8,128)S(1)}, f32[1280,64]{1,0:T(8,128)S(1)}) fusion(f32[64]{0:T(128)} %multiply_power_fusion, f32[1280]{0:T(1024)S(1)} %get-tuple-element.15), kind=kLoop, calls=%fused_computation.9 | loop fusion | flops 163840 | bytes 988416 | tf_op jit(solution)/shard_map/neg | solution.py:97
  19.9 1.6 %fusion.6 = (f32[128,64]{1,0:T(8,128)}, f32[128,64]{1,0:T(8,128)}, f32[128,64]{1,0:T(8,128)}) fusion(f32[64]{0:T(128)} %multiply_power_fusion, f32[128]{0:T(128)} %add_convert_fusion.1), kind=kLoop, calls=%fused_computation.15 | loop fusion | flops 16384 | bytes 99072 | tf_op jit(solution)/shard_map/neg | solution.py:97
  21.5 1.0 %pad_maximum_fusion.3 = (f32[128,128]{1,0:T(8,128)S(1)}, f32[128,128]{1,0:T(8,128)S(1)}) fusion(f32[128,64]{1,0:T(8,128)} %get-tuple-element.14, f32[128,64]{1,0:T(8,128)} %get-tuple-element.13, f32[128,64]{1,0:T(8,128)} %get-tuple-element.12), kind=kLoop, calls=%fused_computation.12 | loop fusion | flops 32768 | bytes 229376 | tf_op jit(solution)/shard_map/concatenate | solution.py:97
  23.1 5.0 %collective-permute-done.2.refs_3_ = bf16[2,128,512]{2,1,0:T(8,128)(2,1)S(1)} collective-permute-done((bf16[2,128,512]{2,1,0:T(8,128)(2,1)S(1)}, bf16[2,128,512]{2,1,0:T(8,128)(2,1)S(1)}, u32[]{:S(2)}, u32[]{:S(2)}) %collective-permute-start.2) | collective-permute-done | bytes 262176 | tf_op jit(solution)/shard_map/ppermute | solution.py:22
  28.2 6.4 %collective-permute-start.8 = (bf16[2,128,512]{2,1,0:T(8,128)(2,1)S(1)}, bf16[2,128,512]{2,1,0:T(8,128)(2,1)S(1)}, u32[]{:S(2)}, u32[]{:S(2)}) collective-permute-start(bf16[2,128,512]{2,1,0:T(8,128)(2,1)S(1)} %collective-permute-done.3.refs_4_), channel_id=1, source_target_pairs={{0,2},{2,0},{4,6},{6,4},{8,10},{10,8},{12,14},{14,12},{16,18},{18,... | collective-permute-start | bytes 786440 | tf_op jit(solution)/shard_map/ppermute | solution.py:24
  35.0 0.7 %collective-permute-done.8.refs_9_ = bf16[2,128,512]{2,1,0:T(8,128)(2,1)S(1)} collective-permute-done((bf16[2,128,512]{2,1,0:T(8,128)(2,1)S(1)}, bf16[2,128,512]{2,1,0:T(8,128)(2,1)S(1)}, u32[]{:S(2)}, u32[]{:S(2)}) %collective-permute-start.8) | collective-permute-done | bytes 262176 | tf_op jit(solution)/shard_map/ppermute | solution.py:24
  35.7 1.0 %copy-done = bf16[128,2048]{1,0:T(8,128)(2,1)S(1)} copy-done((bf16[128,2048]{1,0:T(8,128)(2,1)S(1)}, bf16[128,2048]{1,0:T(8,128)(2,1)}, u32[]{:S(2)}) %copy-start) | copy-done | bytes 524312
  36.8 10.8 %shard_map.82 = (bf16[128,2048]{1,0:T(8,128)(2,1)S(1)}, bf16[128,2048]{1,0:T(8,128)(2,1)S(1)}) custom-call(s32[1]{0:T(128)} %bitcast.peer_ref, s32[1]{0:T(128)} %bitcast.1.core_ref, s32[128,1]{1,0:T(8,128)S(1)} %iota_add_fusion.query_pos_ref, s32[1,1280]{1,0:T(1,128)S(1)} %and_select_fusion.key_limit_ref, f32[128,128]{1,0:T(8,128)S(1)} %get-tuple-element.19.query_cos_ref, ...), custom_call_target="tpu_custom_call" | custom-call | flops 2415919104 | bytes 12582912 | tf_op jit(solution)/shard_map/pallas_call | solution.py:127
  47.6 1.6 %collective-permute-start.9 = (bf16[128,2048]{1,0:T(8,128)(2,1)S(1)}, bf16[128,2048]{1,0:T(8,128)(2,1)S(1)}, u32[]{:S(2)}, u32[]{:S(2)}) collective-permute-start(bf16[128,2048]{1,0:T(8,128)(2,1)S(1)} %get-tuple-element.8), channel_id=1, source_target_pairs={{0,1},{1,0},{2,3},{3,2},{4,5},{5,4},{6,7},{7,6},{8,9},{9,8},{10,11... | collective-permute-start | bytes 1572872 | tf_op jit(solution)/shard_map/ppermute | solution.py:174
  49.2 4.7 %fusion.2 = bf16[128,2048]{1,0:T(8,128)(2,1)S(1)} fusion(bf16[128,2048]{1,0:T(8,128)(2,1)S(1)} %get-tuple-element.7, bf16[2048,4096]{1,0:T(8,128)(2,1)} %refs_10_.1, s32[]{:T(128)S(6)} %select_n.53), kind=kOutput, calls=%fused_computation.2 | convolution fusion | flops 1074003968 | bytes 9437188 | tf_op jit(solution)/shard_map/dot_general | solution.py:177
  53.9 8.0 %collective-permute-done.9 = bf16[128,2048]{1,0:T(8,128)(2,1)S(1)} collective-permute-done((bf16[128,2048]{1,0:T(8,128)(2,1)S(1)}, bf16[128,2048]{1,0:T(8,128)(2,1)S(1)}, u32[]{:S(2)}, u32[]{:S(2)}) %collective-permute-start.9) | collective-permute-done | bytes 524320 | tf_op jit(solution)/shard_map/ppermute | solution.py:174
  61.9 0.9 %add_convert_fusion = bf16[128,2048]{1,0:T(8,128)(2,1)} fusion(bf16[128,2048]{1,0:T(8,128)(2,1)S(1)} %collective-permute-done.9, bf16[128,2048]{1,0:T(8,128)(2,1)S(1)} %fusion.2), kind=kLoop, calls=%fused_computation.3 | loop fusion | flops 1048576 | bytes 1572864 | tf_op jit(solution)/shard_map/convert_element_type | solution.py:179
  (16 shorter events, 1.6 us)
Async XLA Ops:
  1.0 21.6 %collective-permute-start = (bf16[2,128,512]{2,1,0:T(8,128)(2,1)S(1)}, bf16[2,128,512]{2,1,0:T(8,128)(2,1)S(1)}, u32[]{:S(2)}, u32[]{:S(2)}) collective-permute-start(bf16[2,128,512]{2,1,0:T(8,128)(2,1)S(1)} %pad_maximum_fusion.2.refs_0_), channel_id=1, source_target_pairs={{2,4},{6,8},{10,12},{14,16},{18,20},{22,24},{26,28},{3,5},{7,9},{1... | collective-permute-start | bytes 786440 | tf_op jit(solution)/shard_map/ppermute | solution.py:22
  2.3 20.4 %collective-permute-start.1 = (bf16[2,128,512]{2,1,0:T(8,128)(2,1)S(1)}, bf16[2,128,512]{2,1,0:T(8,128)(2,1)S(1)}, u32[]{:S(2)}, u32[]{:S(2)}) collective-permute-start(bf16[2,128,512]{2,1,0:T(8,128)(2,1)S(1)} %pad_maximum_fusion.2.refs_0_), channel_id=1, source_target_pairs={{0,6},{2,8},{4,10},{6,12},{8,14},{10,16},{12,18},{14,20},{16,22},{... | collective-permute-start | bytes 786440 | tf_op jit(solution)/shard_map/ppermute | solution.py:22
  4.5 23.6 %collective-permute-start.2 = (bf16[2,128,512]{2,1,0:T(8,128)(2,1)S(1)}, bf16[2,128,512]{2,1,0:T(8,128)(2,1)S(1)}, u32[]{:S(2)}, u32[]{:S(2)}) collective-permute-start(bf16[2,128,512]{2,1,0:T(8,128)(2,1)S(1)} %pad_maximum_fusion.2.refs_0_), channel_id=1, source_target_pairs={{0,10},{2,12},{4,14},{6,16},{8,18},{10,20},{12,22},{14,24},{16,26}... | collective-permute-start | bytes 786440 | tf_op jit(solution)/shard_map/ppermute | solution.py:22
  5.8 22.3 %collective-permute-start.3 = (bf16[2,128,512]{2,1,0:T(8,128)(2,1)S(1)}, bf16[2,128,512]{2,1,0:T(8,128)(2,1)S(1)}, u32[]{:S(2)}, u32[]{:S(2)}) collective-permute-start(bf16[2,128,512]{2,1,0:T(8,128)(2,1)S(1)} %pad_maximum_fusion.2.refs_0_), channel_id=1, source_target_pairs={{0,14},{2,16},{4,18},{6,20},{8,22},{10,24},{12,26},{14,28},{16,30}... | collective-permute-start | bytes 786440 | tf_op jit(solution)/shard_map/ppermute | solution.py:22
  7.1 27.9 %collective-permute-start.4 = (bf16[2,128,512]{2,1,0:T(8,128)(2,1)S(1)}, bf16[2,128,512]{2,1,0:T(8,128)(2,1)S(1)}, u32[]{:S(2)}, u32[]{:S(2)}) collective-permute-start(bf16[2,128,512]{2,1,0:T(8,128)(2,1)S(1)} %pad_maximum_fusion.2.refs_0_), channel_id=1, source_target_pairs={{0,2},{2,0},{4,6},{6,4},{8,10},{10,8},{12,14},{14,12},{16,18},{18,... | collective-permute-start | bytes 786440 | tf_op jit(solution)/shard_map/ppermute | solution.py:24
  22.6 12.4 %collective-permute-start.5 = (bf16[2,128,512]{2,1,0:T(8,128)(2,1)S(1)}, bf16[2,128,512]{2,1,0:T(8,128)(2,1)S(1)}, u32[]{:S(2)}, u32[]{:S(2)}) collective-permute-start(bf16[2,128,512]{2,1,0:T(8,128)(2,1)S(1)} %collective-permute-done.refs_1_), channel_id=1, source_target_pairs={{0,2},{2,0},{4,6},{6,4},{8,10},{10,8},{12,14},{14,12},{16,18},{18,... | collective-permute-start | bytes 786440 | tf_op jit(solution)/shard_map/ppermute | solution.py:24
  22.7 12.3 %collective-permute-start.6 = (bf16[2,128,512]{2,1,0:T(8,128)(2,1)S(1)}, bf16[2,128,512]{2,1,0:T(8,128)(2,1)S(1)}, u32[]{:S(2)}, u32[]{:S(2)}) collective-permute-start(bf16[2,128,512]{2,1,0:T(8,128)(2,1)S(1)} %collective-permute-done.1.refs_2_), channel_id=1, source_target_pairs={{0,2},{2,0},{4,6},{6,4},{8,10},{10,8},{12,14},{14,12},{16,18},{18,... | collective-permute-start | bytes 786440 | tf_op jit(solution)/shard_map/ppermute | solution.py:24
  28.2 6.9 %collective-permute-start.7 = (bf16[2,128,512]{2,1,0:T(8,128)(2,1)S(1)}, bf16[2,128,512]{2,1,0:T(8,128)(2,1)S(1)}, u32[]{:S(2)}, u32[]{:S(2)}) collective-permute-start(bf16[2,128,512]{2,1,0:T(8,128)(2,1)S(1)} %collective-permute-done.2.refs_3_), channel_id=1, source_target_pairs={{0,2},{2,0},{4,6},{6,4},{8,10},{10,8},{12,14},{14,12},{16,18},{18,... | collective-permute-start | bytes 786440 | tf_op jit(solution)/shard_map/ppermute | solution.py:24
  28.2 7.6 %collective-permute-start.8 = (bf16[2,128,512]{2,1,0:T(8,128)(2,1)S(1)}, bf16[2,128,512]{2,1,0:T(8,128)(2,1)S(1)}, u32[]{:S(2)}, u32[]{:S(2)}) collective-permute-start(bf16[2,128,512]{2,1,0:T(8,128)(2,1)S(1)} %collective-permute-done.3.refs_4_), channel_id=1, source_target_pairs={{0,2},{2,0},{4,6},{6,4},{8,10},{10,8},{12,14},{14,12},{16,18},{18,... | collective-permute-start | bytes 786440 | tf_op jit(solution)/shard_map/ppermute | solution.py:24
  35.7 1.0 %copy-start = (bf16[128,2048]{1,0:T(8,128)(2,1)S(1)}, bf16[128,2048]{1,0:T(8,128)(2,1)}, u32[]{:S(2)}) copy-start(bf16[128,2048]{1,0:T(8,128)(2,1)} %query_ref.1) | copy-start | bytes 1572868
  47.6 14.3 %collective-permute-start.9 = (bf16[128,2048]{1,0:T(8,128)(2,1)S(1)}, bf16[128,2048]{1,0:T(8,128)(2,1)S(1)}, u32[]{:S(2)}, u32[]{:S(2)}) collective-permute-start(bf16[128,2048]{1,0:T(8,128)(2,1)S(1)} %get-tuple-element.8), channel_id=1, source_target_pairs={{0,1},{1,0},{2,3},{3,2},{4,5},{5,4},{6,7},{7,6},{8,9},{9,8},{10,11... | collective-permute-start | bytes 1572872 | tf_op jit(solution)/shard_map/ppermute | solution.py:174

commit v11 on v10

--- a/solution.py
+++ b/solution.py
@@ -23,11 +23,13 @@
     across = [(j, j ^ 1) for j in range(n)]
     passed = [lax.ppermute(block, "ctx", across) for block in [kv] + received]
     half = window // 2
-    even_shift = [0] + [2 * m + 1 for m in range(half)] + [FAR, FAR] + [2 * m for m in range(1, half)]
-    odd_shift = [0, FAR] + [2 * m + 1 for m in range(1, half)] + [1] + [2 * m + 2 for m in range(half)]
+    even = [(0, 0)] + [(1 + m, 2 * m + 1) for m in range(half)] + [(2 + half + m, 2 * m) for m in range(1, half)]
+    odd = [(0, 0)] + [(1 + m, 2 * m + 1) for m in range(1, half)] + [(1 + half, 1)]
+    odd += [(2 + half + m, 2 * m + 2) for m in range(half - 1)]
     core = lax.axis_index("ctx") % 2
-    shift = jnp.where(core == 0, jnp.array(even_shift, jnp.int32), jnp.array(odd_shift, jnp.int32))
-    return [kv] + received + passed, shift
+    shift = jnp.where(core == 0, jnp.array([t for _, t in even], jnp.int32),
+                      jnp.array([t for _, t in odd], jnp.int32))
+    return [kv] + received + passed, ([s for s, _ in even], [s for s, _ in odd]), shift
 
 
 def turn(rows, cosine, sine):
@@ -77,7 +79,8 @@
                 summed = jnp.dot(weights.astype(jnp.bfloat16), values, preferred_element_type=jnp.float32)
                 out_ref[:, columns] = (summed / totals).astype(out_ref.dtype)
 
-    body(uses)
+    for parity, use in enumerate(uses):
+        pl.when(core_ref[0] == parity)(functools.partial(body, use))
     if project:
         total = None
         for h in range(heads_kv):
@@ -145,7 +148,7 @@
     heads_kv = keys.shape[1] // HEAD_SIZE
     context_group = queries.shape[1] // keys.shape[1]
 
-    slots, shift = gather_window(jnp.stack([keys, values]), n, window)
+    slots, uses, shift = gather_window(jnp.stack([keys, values]), n, window)
 
     prompt_ids = jnp.arange(group_widths.shape[0], dtype=jnp.int32)
     offsets = jnp.sum(
@@ -169,7 +172,7 @@
     if n_tp == 2:
         me = lax.axis_index("tp")
         attended, peer_terms = attend(
-            query_pos, key_pos, key_limit, queries, slots, list(range(len(slots))), heads_kv, out_weight, 1 - me
+            query_pos, key_pos, key_limit, queries, slots, uses, heads_kv, out_weight, 1 - me
         )
         got = lax.ppermute(peer_terms, "tp", [(0, 1), (1, 0)])
         part = out_weight.shape[1] // 2
@@ -177,7 +180,7 @@
         own_terms = jnp.dot(attended, own_weight, preferred_element_type=jnp.float32)
         own_terms = lax.optimization_barrier(own_terms.astype(jnp.bfloat16)).astype(jnp.float32)
         return (own_terms + got.astype(jnp.float32)).astype(jnp.bfloat16)
-    (attended,) = attend(query_pos, key_pos, key_limit, queries, slots, list(range(len(slots))), heads_kv, None, jnp.int32(0))
+    (attended,) = attend(query_pos, key_pos, key_limit, queries, slots, uses, heads_kv, None, jnp.int32(0))
     terms = jnp.dot(attended, out_weight, preferred_element_type=jnp.float32)
     return lax.psum_scatter(terms.astype(jnp.bfloat16), "tp", scatter_dimension=1, tiled=True)
 

time: 63.2 us -> 67.6 us (1.070)
  waiting for transfers between devices: 13.7 us -> 18.9 us
  local copies, waits for them, and re-layouts: 1.04 us -> 5.19 us
  other arithmetic: 13.8 us -> 9.96 us
  Pallas kernels: 10.8 us -> 9.69 us
    ppermute x4, waiting for transfers between devices: 5.02 us -> 11 us  [gather_window(): received.append(lax.ppermute(kv, 'ctx', pairs))]
    unnamed x2 -> x12, local copies, waits for them, and re-layouts: 1.04 us -> 5.19 us
    neg x2, other arithmetic: 4.57 us -> 2.21 us  [tables(): -sine]
    pallas_call x1, Pallas kernels: 10.8 us -> 9.69 us  [attend(): pl.pallas_call(functools.partial(attention_kernel, n_slots, uses, heads_k...]
    concatenate x2, other arithmetic: 1.44 us -> 0.44 us  [tables(): jnp.concatenate([cosine, cosine], axis=1)]
    ppermute x5, waiting for transfers between devices: 0.72 us -> 0.01 us  [gather_window(): passed = [lax.ppermute(block, 'ctx', across) for block in [kv] + received]]
  transfers between devices with their start and end apart: 10 -> 10, of which waited for: 3 -> 2; matrix products, arithmetic and copies ran while one was open for 26% -> 19% of each run, Pallas kernels for 0% -> 0%
where the time goes in v11:
time: 67.6 us; the launch traced here: 67.1 us
  waiting for transfers between devices  18.9 us (28%)
  starting transfers between devices  16 us (24%)
  other arithmetic  9.96 us (15%)
  Pallas kernels  9.69 us (14%)
  local copies, waits for them, and re-layouts  5.19 us (8%)
  matrix products  4.63 us (7%)
  between operations  2.72 us (4%)
    ppermute x4, waiting for transfers between devices, gather_window(): received.append(lax.ppermute(kv, 'ctx', pairs))  11 us
    pallas_call x1, Pallas kernels, attend(): pl.pallas_call(functools.partial(attention_kernel, n_slots, uses, heads_k...  9.69 us
    ppermute x5, starting transfers between devices, gather_window(): passed = [lax.ppermute(block, 'ctx', across) for block in [kv] + received]  8.35 us
    ppermute x1, waiting for transfers between devices, on_device(): got = lax.ppermute(peer_terms, 'tp', [(0, 1), (1, 0)])  7.85 us
    ppermute x4, starting transfers between devices, gather_window(): received.append(lax.ppermute(kv, 'ctx', pairs))  6.1 us
    unnamed x12, local copies, waits for them, and re-layouts  5.19 us
    dot_general x1, matrix products, on_device(): jnp.dot(attended, own_weight, preferred_element_type=jnp.float32)  4.63 us
    neg x2, other arithmetic, tables(): -sine  2.21 us
  transfers between devices with their start and end apart: 10, of which 2 were waited for; matrix products, arithmetic and copies ran while one was open for 19% of the time, Pallas kernels for 0%

profile of v11, /device:TPU:24, one launch (start us, length us, event | category | flops | bytes accessed | tf_op | source)
XLA Modules:
  0.0 67.1 jit_solution(16909027203088548427)
XLA Ops:
  0.0 1.0 %pad_maximum_fusion.2.refs_0_ = bf16[2,128,512]{2,1,0:T(8,128)(2,1)S(1)} fusion(bf16[1,128,512]{2,1,0:T(8,128)(2,1)} %bitcast.8, bf16[1,128,512]{2,1,0:T(8,128)(2,1)} %bitcast.9), kind=kLoop, calls=%fused_computation.8 | loop fusion | flops 131072 | bytes 524288 | tf_op jit(solution)/shard_map/stack | solution.py:151
  1.0 1.3 %collective-permute-start = (bf16[2,128,512]{2,1,0:T(8,128)(2,1)S(1)}, bf16[2,128,512]{2,1,0:T(8,128)(2,1)S(1)}, u32[]{:S(2)}, u32[]{:S(2)}) collective-permute-start(bf16[2,128,512]{2,1,0:T(8,128)(2,1)S(1)} %pad_maximum_fusion.2.refs_0_), channel_id=1, source_target_pairs={{2,4},{6,8},{10,12},{14,16},{18,20},{22,24},{26,28},{3,5},{7,9},{1... | collective-permute-start | bytes 786440 | tf_op jit(solution)/shard_map/ppermute | solution.py:22
  2.3 2.2 %collective-permute-start.1 = (bf16[2,128,512]{2,1,0:T(8,128)(2,1)S(1)}, bf16[2,128,512]{2,1,0:T(8,128)(2,1)S(1)}, u32[]{:S(2)}, u32[]{:S(2)}) collective-permute-start(bf16[2,128,512]{2,1,0:T(8,128)(2,1)S(1)} %pad_maximum_fusion.2.refs_0_), channel_id=1, source_target_pairs={{0,6},{2,8},{4,10},{6,12},{8,14},{10,16},{12,18},{14,20},{16,22},{... | collective-permute-start | bytes 786440 | tf_op jit(solution)/shard_map/ppermute | solution.py:22
  4.5 1.3 %collective-permute-start.2 = (bf16[2,128,512]{2,1,0:T(8,128)(2,1)S(1)}, bf16[2,128,512]{2,1,0:T(8,128)(2,1)S(1)}, u32[]{:S(2)}, u32[]{:S(2)}) collective-permute-start(bf16[2,128,512]{2,1,0:T(8,128)(2,1)S(1)} %pad_maximum_fusion.2.refs_0_), channel_id=1, source_target_pairs={{0,10},{2,12},{4,14},{6,16},{8,18},{10,20},{12,22},{14,24},{16,26}... | collective-permute-start | bytes 786440 | tf_op jit(solution)/shard_map/ppermute | solution.py:22
  5.8 1.3 %collective-permute-start.3 = (bf16[2,128,512]{2,1,0:T(8,128)(2,1)S(1)}, bf16[2,128,512]{2,1,0:T(8,128)(2,1)S(1)}, u32[]{:S(2)}, u32[]{:S(2)}) collective-permute-start(bf16[2,128,512]{2,1,0:T(8,128)(2,1)S(1)} %pad_maximum_fusion.2.refs_0_), channel_id=1, source_target_pairs={{0,14},{2,16},{4,18},{6,20},{8,22},{10,24},{12,26},{14,28},{16,30}... | collective-permute-start | bytes 786440 | tf_op jit(solution)/shard_map/ppermute | solution.py:22
  7.1 1.4 %collective-permute-start.4 = (bf16[2,128,512]{2,1,0:T(8,128)(2,1)S(1)}, bf16[2,128,512]{2,1,0:T(8,128)(2,1)S(1)}, u32[]{:S(2)}, u32[]{:S(2)}) collective-permute-start(bf16[2,128,512]{2,1,0:T(8,128)(2,1)S(1)} %pad_maximum_fusion.2.refs_0_), channel_id=1, source_target_pairs={{0,2},{2,0},{4,6},{6,4},{8,10},{10,8},{12,14},{14,12},{16,18},{18,... | collective-permute-start | bytes 786440 | tf_op jit(solution)/shard_map/ppermute | solution.py:24
  8.5 0.8 %select_reduce_fusion = s32[8]{0:T(128)S(1)} fusion(s32[8]{0:T(128)} %param.12), kind=kLoop, calls=%fused_computation.19 | loop fusion | flops 184 | bytes 64 | tf_op jit(solution)/shard_map/reduce_sum | solution.py:154
  9.3 0.6 fusion.10
  11.9 1.3 %fusion.9 = s32[8]{0:T(128)S(1)} fusion(s32[8]{0:T(128)} %constant.46.clone, s32[8]{0:T(128)} %constant.47.clone, pred[]{:T(512)S(6)} %eq.14, s32[]{:T(128)} %select_reduce_fusion.3, s32[]{:T(128)S(6)} %axis_index.33), kind=kLoop, calls=%fused_computation.25 | loop fusion | flops 32 | bytes 105 | tf_op jit(solution)/shard_map/mul | solution.py:165
  13.2 1.9 %fusion.5 = (f32[1024,64]{1,0:T(8,128)S(1)}, f32[1024,64]{1,0:T(8,128)S(1)}, f32[1024,64]{1,0:T(8,128)S(1)}) fusion(f32[64]{0:T(128)S(1)} %multiply_power_fusion, f32[1024]{0:T(1024)S(1)} %get-tuple-element.15), kind=kLoop, calls=%fused_computation.9 | loop fusion | flops 131072 | bytes 790784 | tf_op jit(solution)/shard_map/neg | solution.py:100
  17.1 11.0 %collective-permute-done.2.refs_3_ = bf16[2,128,512]{2,1,0:T(8,128)(2,1)S(1)} collective-permute-done((bf16[2,128,512]{2,1,0:T(8,128)(2,1)S(1)}, bf16[2,128,512]{2,1,0:T(8,128)(2,1)S(1)}, u32[]{:S(2)}, u32[]{:S(2)}) %collective-permute-start.2) | collective-permute-done | bytes 262176 | tf_op jit(solution)/shard_map/ppermute | solution.py:22
  28.2 6.4 %collective-permute-start.8 = (bf16[2,128,512]{2,1,0:T(8,128)(2,1)S(1)}, bf16[2,128,512]{2,1,0:T(8,128)(2,1)}, u32[]{:S(2)}, u32[]{:S(2)}) collective-permute-start(bf16[2,128,512]{2,1,0:T(8,128)(2,1)S(1)} %collective-permute-done.3.refs_4_), channel_id=1, source_target_pairs={{0,2},{2,0},{4,6},{6,4},{8,10},{10,8},{12,14},{14,12},{16,18},{18,... | collective-permute-start | bytes 786440 | tf_op jit(solution)/shard_map/ppermute | solution.py:24
  34.6 1.3 %select_reduce_fusion.1 = (s32[]{:T(128)}, s32[]{:T(128)}) fusion(s32[8]{0:T(128)} %param.13, s32[]{:T(128)S(6)} %sub.23, s32[8]{0:T(128)} %param.12), kind=kLoop, calls=%fused_computation.29 | loop fusion | flops 38 | bytes 76 | tf_op jit(solution)/shard_map/reduce_sum | solution.py:161
  37.2 0.7 %copy-done.1 = bf16[2,128,512]{2,1,0:T(8,128)(2,1)} copy-done((bf16[2,128,512]{2,1,0:T(8,128)(2,1)}, bf16[2,128,512]{2,1,0:T(8,128)(2,1)S(1)}, u32[]{:S(2)}) %copy-start.1) | copy-done | bytes 262168
  37.9 0.7 %copy-done.3 = bf16[2,128,512]{2,1,0:T(8,128)(2,1)} copy-done((bf16[2,128,512]{2,1,0:T(8,128)(2,1)}, bf16[2,128,512]{2,1,0:T(8,128)(2,1)S(1)}, u32[]{:S(2)}) %copy-start.3) | copy-done | bytes 262168
  38.7 1.0 %copy-done = bf16[128,2048]{1,0:T(8,128)(2,1)S(1)} copy-done((bf16[128,2048]{1,0:T(8,128)(2,1)S(1)}, bf16[128,2048]{1,0:T(8,128)(2,1)}, u32[]{:S(2)}) %copy-start) | copy-done | bytes 524312
  39.7 0.9 %copy-done.2 = bf16[2,128,512]{2,1,0:T(8,128)(2,1)S(1)} copy-done((bf16[2,128,512]{2,1,0:T(8,128)(2,1)S(1)}, bf16[2,128,512]{2,1,0:T(8,128)(2,1)}, u32[]{:S(2)}) %copy-start.2) | copy-done | bytes 262168
  40.6 0.9 %copy-done.4 = bf16[2,128,512]{2,1,0:T(8,128)(2,1)S(1)} copy-done((bf16[2,128,512]{2,1,0:T(8,128)(2,1)S(1)}, bf16[2,128,512]{2,1,0:T(8,128)(2,1)}, u32[]{:S(2)}) %copy-start.4) | copy-done | bytes 262168
  41.6 0.8 %copy-done.5 = s32[128,1]{1,0:T(8,128)S(1)} copy-done((s32[128,1]{1,0:T(8,128)S(1)}, s32[128,1]{1,0:T(8,128)}, u32[]{:S(2)}) %copy-start.5) | copy-done | bytes 536
  42.4 9.7 %shard_map.82 = (bf16[128,2048]{1,0:T(8,128)(2,1)S(1)}, bf16[128,2048]{1,0:T(8,128)(2,1)}) custom-call(s32[1]{0:T(128)} %bitcast.peer_ref, s32[1]{0:T(128)} %bitcast.1.core_ref, s32[128,1]{1,0:T(8,128)S(1)} %copy-done.5, s32[1,1024]{1,0:T(1,128)S(1)} %and_select_fusion.key_limit_ref, f32[128,128]{1,0:T(8,128)S(1)} %get-tuple-element.19.query_cos_ref, ...), custom_call_target="tpu_custom_call" | custom-call | flops 2147483648 | bytes 12058624 | tf_op jit(solution)/shard_map/pallas_call | solution.py:130
  52.1 1.6 %collective-permute-start.9 = (bf16[128,2048]{1,0:T(8,128)(2,1)}, bf16[128,2048]{1,0:T(8,128)(2,1)S(1)}, u32[]{:S(2)}, u32[]{:S(2)}) collective-permute-start(bf16[128,2048]{1,0:T(8,128)(2,1)} %get-tuple-element.8), channel_id=1, source_target_pairs={{0,1},{1,0},{2,3},{3,2},{4,5},{5,4},{6,7},{7,6},{8,9},{9,8},{10,11... | collective-permute-start | bytes 1572872 | tf_op jit(solution)/shard_map/ppermute | solution.py:177
  53.7 4.6 %fusion.2 = bf16[128,2048]{1,0:T(8,128)(2,1)S(1)} fusion(bf16[128,2048]{1,0:T(8,128)(2,1)S(1)} %get-tuple-element.7, bf16[2048,4096]{1,0:T(8,128)(2,1)} %refs_10_.1, s32[]{:T(128)S(6)} %select_n.53), kind=kOutput, calls=%fused_computation.2 | convolution fusion | flops 1074003968 | bytes 9437188 | tf_op jit(solution)/shard_map/dot_general | solution.py:180
  58.4 7.8 %collective-permute-done.9 = bf16[128,2048]{1,0:T(8,128)(2,1)S(1)} collective-permute-done((bf16[128,2048]{1,0:T(8,128)(2,1)}, bf16[128,2048]{1,0:T(8,128)(2,1)S(1)}, u32[]{:S(2)}, u32[]{:S(2)}) %collective-permute-start.9) | collective-permute-done | bytes 524320 | tf_op jit(solution)/shard_map/ppermute | solution.py:177
  66.2 0.9 %add_convert_fusion = bf16[128,2048]{1,0:T(8,128)(2,1)} fusion(bf16[128,2048]{1,0:T(8,128)(2,1)S(1)} %collective-permute-done.9, bf16[128,2048]{1,0:T(8,128)(2,1)S(1)} %fusion.2), kind=kLoop, calls=%fused_computation.3 | loop fusion | flops 1048576 | bytes 1572864 | tf_op jit(solution)/shard_map/convert_element_type | solution.py:182
  (26 shorter events, 2.7 us)
Async XLA Ops:
  1.0 15.5 %collective-permute-start = (bf16[2,128,512]{2,1,0:T(8,128)(2,1)S(1)}, bf16[2,128,512]{2,1,0:T(8,128)(2,1)S(1)}, u32[]{:S(2)}, u32[]{:S(2)}) collective-permute-start(bf16[2,128,512]{2,1,0:T(8,128)(2,1)S(1)} %pad_maximum_fusion.2.refs_0_), channel_id=1, source_target_pairs={{2,4},{6,8},{10,12},{14,16},{18,20},{22,24},{26,28},{3,5},{7,9},{1... | collective-permute-start | bytes 786440 | tf_op jit(solution)/shard_map/ppermute | solution.py:22
  2.3 14.4 %collective-permute-start.1 = (bf16[2,128,512]{2,1,0:T(8,128)(2,1)S(1)}, bf16[2,128,512]{2,1,0:T(8,128)(2,1)S(1)}, u32[]{:S(2)}, u32[]{:S(2)}) collective-permute-start(bf16[2,128,512]{2,1,0:T(8,128)(2,1)S(1)} %pad_maximum_fusion.2.refs_0_), channel_id=1, source_target_pairs={{0,6},{2,8},{4,10},{6,12},{8,14},{10,16},{12,18},{14,20},{16,22},{... | collective-permute-start | bytes 786440 | tf_op jit(solution)/shard_map/ppermute | solution.py:22
  4.5 23.6 %collective-permute-start.2 = (bf16[2,128,512]{2,1,0:T(8,128)(2,1)S(1)}, bf16[2,128,512]{2,1,0:T(8,128)(2,1)S(1)}, u32[]{:S(2)}, u32[]{:S(2)}) collective-permute-start(bf16[2,128,512]{2,1,0:T(8,128)(2,1)S(1)} %pad_maximum_fusion.2.refs_0_), channel_id=1, source_target_pairs={{0,10},{2,12},{4,14},{6,16},{8,18},{10,20},{12,22},{14,24},{16,26}... | collective-permute-start | bytes 786440 | tf_op jit(solution)/shard_map/ppermute | solution.py:22
  5.8 22.3 %collective-permute-start.3 = (bf16[2,128,512]{2,1,0:T(8,128)(2,1)S(1)}, bf16[2,128,512]{2,1,0:T(8,128)(2,1)S(1)}, u32[]{:S(2)}, u32[]{:S(2)}) collective-permute-start(bf16[2,128,512]{2,1,0:T(8,128)(2,1)S(1)} %pad_maximum_fusion.2.refs_0_), channel_id=1, source_target_pairs={{0,14},{2,16},{4,18},{6,20},{8,22},{10,24},{12,26},{14,28},{16,30}... | collective-permute-start | bytes 786440 | tf_op jit(solution)/shard_map/ppermute | solution.py:22
  7.1 30.1 %collective-permute-start.4 = (bf16[2,128,512]{2,1,0:T(8,128)(2,1)S(1)}, bf16[2,128,512]{2,1,0:T(8,128)(2,1)S(1)}, u32[]{:S(2)}, u32[]{:S(2)}) collective-permute-start(bf16[2,128,512]{2,1,0:T(8,128)(2,1)S(1)} %pad_maximum_fusion.2.refs_0_), channel_id=1, source_target_pairs={{0,2},{2,0},{4,6},{6,4},{8,10},{10,8},{12,14},{14,12},{16,18},{18,... | collective-permute-start | bytes 786440 | tf_op jit(solution)/shard_map/ppermute | solution.py:24
  16.6 20.7 %collective-permute-start.5 = (bf16[2,128,512]{2,1,0:T(8,128)(2,1)S(1)}, bf16[2,128,512]{2,1,0:T(8,128)(2,1)S(1)}, u32[]{:S(2)}, u32[]{:S(2)}) collective-permute-start(bf16[2,128,512]{2,1,0:T(8,128)(2,1)S(1)} %collective-permute-done.refs_1_), channel_id=1, source_target_pairs={{0,2},{2,0},{4,6},{6,4},{8,10},{10,8},{12,14},{14,12},{16,18},{18,... | collective-permute-start | bytes 786440 | tf_op jit(solution)/shard_map/ppermute | solution.py:24
  16.7 20.6 %collective-permute-start.6 = (bf16[2,128,512]{2,1,0:T(8,128)(2,1)S(1)}, bf16[2,128,512]{2,1,0:T(8,128)(2,1)S(1)}, u32[]{:S(2)}, u32[]{:S(2)}) collective-permute-start(bf16[2,128,512]{2,1,0:T(8,128)(2,1)S(1)} %collective-permute-done.1.refs_2_), channel_id=1, source_target_pairs={{0,2},{2,0},{4,6},{6,4},{8,10},{10,8},{12,14},{14,12},{16,18},{18,... | collective-permute-start | bytes 786440 | tf_op jit(solution)/shard_map/ppermute | solution.py:24
  28.2 9.8 %collective-permute-start.7 = (bf16[2,128,512]{2,1,0:T(8,128)(2,1)S(1)}, bf16[2,128,512]{2,1,0:T(8,128)(2,1)S(1)}, u32[]{:S(2)}, u32[]{:S(2)}) collective-permute-start(bf16[2,128,512]{2,1,0:T(8,128)(2,1)S(1)} %collective-permute-done.2.refs_3_), channel_id=1, source_target_pairs={{0,2},{2,0},{4,6},{6,4},{8,10},{10,8},{12,14},{14,12},{16,18},{18,... | collective-permute-start | bytes 786440 | tf_op jit(solution)/shard_map/ppermute | solution.py:24
  28.2 10.5 %collective-permute-start.8 = (bf16[2,128,512]{2,1,0:T(8,128)(2,1)S(1)}, bf16[2,128,512]{2,1,0:T(8,128)(2,1)}, u32[]{:S(2)}, u32[]{:S(2)}) collective-permute-start(bf16[2,128,512]{2,1,0:T(8,128)(2,1)S(1)} %collective-permute-done.3.refs_4_), channel_id=1, source_target_pairs={{0,2},{2,0},{4,6},{6,4},{8,10},{10,8},{12,14},{14,12},{16,18},{18,... | collective-permute-start | bytes 786440 | tf_op jit(solution)/shard_map/ppermute | solution.py:24
  37.2 0.7 %copy-start.1 = (bf16[2,128,512]{2,1,0:T(8,128)(2,1)}, bf16[2,128,512]{2,1,0:T(8,128)(2,1)S(1)}, u32[]{:S(2)}) copy-start(bf16[2,128,512]{2,1,0:T(8,128)(2,1)S(1)} %collective-permute-done.6.refs_7_) | copy-start | bytes 786436
  37.9 0.7 %copy-start.3 = (bf16[2,128,512]{2,1,0:T(8,128)(2,1)}, bf16[2,128,512]{2,1,0:T(8,128)(2,1)S(1)}, u32[]{:S(2)}) copy-start(bf16[2,128,512]{2,1,0:T(8,128)(2,1)S(1)} %collective-permute-done.7.refs_8_) | copy-start | bytes 786436
  38.6 1.0 %copy-start = (bf16[128,2048]{1,0:T(8,128)(2,1)S(1)}, bf16[128,2048]{1,0:T(8,128)(2,1)}, u32[]{:S(2)}) copy-start(bf16[128,2048]{1,0:T(8,128)(2,1)} %query_ref.1) | copy-start | bytes 1572868
  39.7 0.9 %copy-start.2 = (bf16[2,128,512]{2,1,0:T(8,128)(2,1)S(1)}, bf16[2,128,512]{2,1,0:T(8,128)(2,1)}, u32[]{:S(2)}) copy-start(bf16[2,128,512]{2,1,0:T(8,128)(2,1)} %copy-done.1) | copy-start | bytes 786436
  40.6 0.9 %copy-start.4 = (bf16[2,128,512]{2,1,0:T(8,128)(2,1)S(1)}, bf16[2,128,512]{2,1,0:T(8,128)(2,1)}, u32[]{:S(2)}) copy-start(bf16[2,128,512]{2,1,0:T(8,128)(2,1)} %copy-done.3) | copy-start | bytes 786436
  41.6 0.8 %copy-start.5 = (s32[128,1]{1,0:T(8,128)S(1)}, s32[128,1]{1,0:T(8,128)}, u32[]{:S(2)}) copy-start(s32[128,1]{1,0:T(8,128)} %iota_add_fusion.query_pos_ref) | copy-start | bytes 1540
  52.1 14.1 %collective-permute-start.9 = (bf16[128,2048]{1,0:T(8,128)(2,1)}, bf16[128,2048]{1,0:T(8,128)(2,1)S(1)}, u32[]{:S(2)}, u32[]{:S(2)}) collective-permute-start(bf16[128,2048]{1,0:T(8,128)(2,1)} %get-tuple-element.8), channel_id=1, source_target_pairs={{0,1},{1,0},{2,3},{3,2},{4,5},{5,4},{6,7},{7,6},{8,9},{9,8},{10,11... | collective-permute-start | bytes 1572872 | tf_op jit(solution)/shard_map/ppermute | solution.py:177

commit v12 on v10

v12 whole, which is shorter than its diff:
```python
import functools
import math

import jax
import jax.numpy as jnp
from jax import lax
from jax.experimental import pallas as pl
from jax.experimental.pallas import tpu as pltpu
from jax.sharding import PartitionSpec as P

HEAD_SIZE = 128
FAR = 1 << 20


def gather_window(kv, n, window):
    received = []
    for s in range(1, window, 2):
        if s == 1:
            pairs = [(j, j + 1) for j in range(1, n - 1, 2)]
        else:
            pairs = [(j, j + s) for j in range(n - s)]
        received.append(lax.ppermute(kv, "ctx", pairs))
    across = [(j, j ^ 1) for j in range(n)]
    passed = [lax.ppermute(block, "ctx", across) for block in [kv] + received[:-1]]

    def pass_last(block):
        return lax.ppermute(block, "ctx", across)

    half = window // 2
    even_shift = [0] + [2 * m + 1 for m in range(half)] + [FAR, FAR] + [2 * m for m in range(1, half)]
    odd_shift = [0, FAR] + [2 * m + 1 for m in range(1, half)] + [1] + [2 * m + 2 for m in range(half)]
    core = lax.axis_index("ctx") % 2
    shift = jnp.where(core == 0, jnp.array(even_shift, jnp.int32), jnp.array(odd_shift, jnp.int32))
    return [kv] + received + passed, shift, pass_last


def turn(rows, cosine, sine):
    rows = rows.astype(jnp.float32)
    return (rows * cosine + pltpu.roll(rows, HEAD_SIZE // 2, 1) * sine).astype(jnp.bfloat16)


def attention_kernel(n_slots, heads_kv, late, project, peer_ref, query_pos_ref, key_limit_ref,
                     query_cos_ref, query_sin_ref, key_cos_ref, key_sin_ref, query_ref, *refs):
    if late:
        acc_in_ref, max_in_ref, sum_in_ref = refs[:3]
        refs = refs[3:]
    slot_refs = refs[:n_slots]
    rest = refs[n_slots:]
    if project:
        weight_hbm, out_ref, peer_out_ref, weight_ref, copy_sem = rest
        group = query_ref.shape[1] // heads_kv
        part = weight_ref.shape[1]
        copies = [
            pltpu.make_async_copy(
                weight_hbm.at[pl.ds(h * group, group), pl.ds(pl.multiple_of(peer_ref[0] * part, part), part)],
                weight_ref.at[pl.ds(h * group, group), :],
                copy_sem.at[h],
            )
            for h in range(heads_kv)
        ]
        for copy in copies:
            copy.start()
    elif late:
        (out_ref,) = rest
    else:
        acc_ref, max_ref, sum_ref = rest
    allowed = key_limit_ref[...] <= query_pos_ref[...]
    heads_here = query_ref.shape[1] // HEAD_SIZE // heads_kv
    for h in range(heads_kv):
        head = slice(h * HEAD_SIZE, (h + 1) * HEAD_SIZE)
        keys = turn(jnp.concatenate([r[0, :, head] for r in slot_refs], axis=0), key_cos_ref[...], key_sin_ref[...])
        values = jnp.concatenate([r[1, :, head] for r in slot_refs], axis=0)
        for g in range(heads_here):
            q = h * heads_here + g
            columns = slice(q * HEAD_SIZE, (q + 1) * HEAD_SIZE)
            query = turn(query_ref[:, columns], query_cos_ref[...], query_sin_ref[...])
            scores = lax.dot_general(
                query, keys, (((1,), (1,)), ((), ())), preferred_element_type=jnp.float32
            ) * (1.0 / math.sqrt(HEAD_SIZE))
            scores = jnp.where(allowed, scores, -1e30)
            highest = jnp.max(scores, axis=1, keepdims=True)
            if late:
                before = max_in_ref[:, q:q + 1]
                highest = jnp.maximum(before, highest)
                factor = jnp.exp(before - highest)
            weights = jnp.exp(scores - highest)
            totals = jnp.sum(weights, axis=1, keepdims=True)
            summed = jnp.dot(weights.astype(jnp.bfloat16), values, preferred_element_type=jnp.float32)
            if late:
                totals = sum_in_ref[:, q:q + 1] * factor + totals
                summed = acc_in_ref[:, columns] * factor + summed
                out_ref[:, columns] = (summed / totals).astype(out_ref.dtype)
            else:
                acc_ref[:, columns] = summed
                max_ref[:, q:q + 1] = highest
                sum_ref[:, q:q + 1] = totals
    if project:
        total = None
        for h in range(heads_kv):
            copies[h].wait()
            rows = slice(h * group, (h + 1) * group)
            term = jnp.dot(out_ref[:, rows], weight_ref[rows, :], preferred_element_type=jnp.float32)
            total = term if total is None else total + term
        peer_out_ref[...] = total.astype(peer_out_ref.dtype)


def tables(positions):
    half = HEAD_SIZE // 2
    freqs = 500000.0 ** (-jnp.arange(half, dtype=jnp.float32) / half)
    angles = positions.astype(jnp.float32)[:, None] * freqs[None, :]
    cosine = jnp.cos(angles)
    sine = jnp.sin(angles)
    return jnp.concatenate([cosine, cosine], axis=1), jnp.concatenate([-sine, sine], axis=1)


def attend(query_pos, key_pos, key_limit, queries, slots, heads_kv, carry=None, out_weight=None, peer=None):
    rows, width = queries.shape
    n_slots = len(slots)
    count = key_pos.shape[0]
    late = carry is not None
    project = out_weight is not None
    query_cos, query_sin = tables(query_pos)
    key_cos, key_sin = tables(key_pos)
    vmem = pl.BlockSpec(memory_space=pltpu.VMEM)
    smem = pl.BlockSpec(memory_space=pltpu.SMEM)
    args = [peer.reshape(1), query_pos.reshape(rows, 1), key_limit, query_cos, query_sin, key_cos, key_sin, queries]
    if late:
        args += list(carry)
    args += slots
    in_specs = [smem] + [vmem] * (len(args) - 1)
    heads = width // HEAD_SIZE
    if late:
        out_shape = [jax.ShapeDtypeStruct((rows, width), jnp.bfloat16)]
    else:
        out_shape = [jax.ShapeDtypeStruct((rows, width), jnp.float32),
                     jax.ShapeDtypeStruct((rows, heads), jnp.float32),
                     jax.ShapeDtypeStruct((rows, heads), jnp.float32)]
    scratch = []
    flops = 4 * rows * count * width
    moved = 2 * (2 * rows * width + 2 * count * heads_kv * HEAD_SIZE)
    if project:
        part = out_weight.shape[1] // 2
        args.append(out_weight)
        in_specs.append(pl.BlockSpec(memory_space=pl.ANY))
        out_shape.append(jax.ShapeDtypeStruct((rows, part), jnp.bfloat16))
        scratch += [pltpu.VMEM((width, part), jnp.bfloat16), pltpu.SemaphoreType.DMA((heads_kv,))]
        flops += 2 * rows * width * part
        moved += 2 * (width * part + rows * part)
    return pl.pallas_call(
        functools.partial(attention_kernel, n_slots, heads_kv, late, project),
        out_shape=out_shape,
        in_specs=in_specs,
        out_specs=[vmem] * len(out_shape),
        scratch_shapes=scratch,
        compiler_params=pltpu.CompilerParams(vmem_limit_bytes=48 * 1024 * 1024),
        cost_estimate=pl.CostEstimate(
            flops=flops, transcendentals=rows * count * width // HEAD_SIZE, bytes_accessed=moved
        ),
    )(*args)


def on_device(queries, keys, values, out_weight, group_widths, pad_tokens):
    n = lax.axis_size("ctx")
    window = n // 2
    group_index = lax.axis_index("ctx")
    rows_here = queries.shape[0]
    heads_kv = keys.shape[1] // HEAD_SIZE
    context_group = queries.shape[1] // keys.shape[1]

    slots, shift, pass_last = gather_window(jnp.stack([keys, values]), n, window)
    half = window // 2
    latest = [half, 2 * half + 1]
    early = [j for j in range(2 * half + 2) if j not in latest]

    prompt_ids = jnp.arange(group_widths.shape[0], dtype=jnp.int32)
    offsets = jnp.sum(
        jnp.where(prompt_ids[None, :] < prompt_ids[:, None], group_widths[None, :], 0), axis=1
    )
    owner = jnp.sum((offsets <= group_index).astype(jnp.int32)) - 1
    picked = prompt_ids == owner
    start = jnp.sum(jnp.where(picked, offsets, 0))
    width = jnp.sum(jnp.where(picked, group_widths, 0))
    padding = jnp.sum(jnp.where(picked, pad_tokens, 0))
    length = width * rows_here - padding
    local_rows = jnp.arange(rows_here, dtype=jnp.int32)
    query_pos = (group_index - start) * rows_here + local_rows

    def keys_at(chosen):
        key_pos = ((group_index - shift[jnp.array(chosen)] - start) * rows_here)[:, None] + local_rows[None, :]
        key_pos = key_pos.reshape(-1)
        usable = (key_pos >= 0) & (key_pos < length)
        return key_pos, jnp.where(usable, key_pos, FAR * rows_here).reshape(1, -1)

    zero = jnp.int32(0)
    carry = attend(query_pos, *keys_at(early), queries, [slots[j] for j in early], heads_kv, peer=zero)
    newest, carry = lax.optimization_barrier((slots[half], carry))
    last_slots = [newest, pass_last(newest)]

    n_tp = lax.axis_size("tp")
    if n_tp == 2:
        me = lax.axis_index("tp")
        attended, peer_terms = attend(
            query_pos, *keys_at(latest), queries, last_slots, heads_kv, carry=carry, out_weight=out_weight,
            peer=1 - me,
        )
        got = lax.ppermute(peer_terms, "tp", [(0, 1), (1, 0)])
        part = out_weight.shape[1] // 2
        own_weight = lax.dynamic_slice_in_dim(out_weight, me * part, part, 1)
        own_terms = jnp.dot(attended, own_weight, preferred_element_type=jnp.float32)
        own_terms = lax.optimization_barrier(own_terms.astype(jnp.bfloat16)).astype(jnp.float32)
        return (own_terms + got.astype(jnp.float32)).astype(jnp.bfloat16)
    (attended,) = attend(query_pos, *keys_at(latest), queries, last_slots, heads_kv, carry=carry, peer=zero)
    terms = jnp.dot(attended, out_weight, preferred_element_type=jnp.float32)
    return lax.psum_scatter(terms.astype(jnp.bfloat16), "tp", scatter_dimension=1, tiled=True)


def solution(mesh):
    return jax.shard_map(
        on_device,
        mesh=mesh,
        in_specs=(P("ctx", "tp"), P("ctx", "tp"), P("ctx", "tp"), P("tp", None), P(), P()),
        out_specs=P("ctx", "tp"),
        check_vma=False,
    )
```

time: 63.2 us -> 67.9 us (1.074)
  the two profiles are of different devices: /device:TPU:24 before, /device:TPU:0 now
where the time goes in v12:
time: 67.9 us; the launch traced here: 67.5 us
  Pallas kernels  17.2 us (25%)
  starting transfers between devices  17.1 us (25%)
  other arithmetic  12.1 us (18%)
  waiting for transfers between devices  10.3 us (15%)
  matrix products  4.63 us (7%)
  local copies, waits for them, and re-layouts  3.36 us (5%)
  between operations  2.84 us (4%)
    pallas_call x2, Pallas kernels, attend(): pl.pallas_call(functools.partial(attention_kernel, n_slots, heads_kv, lat...  17.2 us
    ppermute x4, starting transfers between devices, gather_window(): received.append(lax.ppermute(kv, 'ctx', pairs))  12 us
    ppermute x1, waiting for transfers between devices, on_device(): got = lax.ppermute(peer_terms, 'tp', [(0, 1), (1, 0)])  7.81 us
    dot_general x1, matrix products, on_device(): jnp.dot(attended, own_weight, preferred_element_type=jnp.float32)  4.63 us
    ppermute x4, starting transfers between devices, gather_window(): lax.ppermute(block, 'ctx', across)  3.31 us
    neg x3, other arithmetic, tables(): -sine  2.74 us
    unnamed x4, local copies, waits for them, and re-layouts  2.08 us
    ppermute x1, starting transfers between devices, on_device(): got = lax.ppermute(peer_terms, 'tp', [(0, 1), (1, 0)])  1.58 us
  transfers between devices with their start and end apart: 10, of which 5 were waited for; matrix products, arithmetic and copies ran while one was open for 24% of the time, Pallas kernels for 9%

profile of v12, /device:TPU:0, one launch (start us, length us, event | category | flops | bytes accessed | tf_op | source)
XLA Modules:
  0.0 67.5 jit_solution(16257937024188419807)
XLA Ops:
  0.0 1.0 %pad_maximum_fusion.2.refs_0_ = bf16[2,128,512]{2,1,0:T(8,128)(2,1)S(1)} fusion(bf16[1,128,512]{2,1,0:T(8,128)(2,1)} %bitcast.10, bf16[1,128,512]{2,1,0:T(8,128)(2,1)} %bitcast.11), kind=kLoop, calls=%fused_computation.10 | loop fusion | flops 131072 | bytes 524288 | tf_op jit(solution)/shard_map/stack | solution.py:170
  1.0 0.7 %collective-permute-start.1 = (bf16[2,128,512]{2,1,0:T(8,128)(2,1)S(1)}, bf16[2,128,512]{2,1,0:T(8,128)(2,1)S(1)}, u32[]{:S(2)}, u32[]{:S(2)}) collective-permute-start(bf16[2,128,512]{2,1,0:T(8,128)(2,1)S(1)} %pad_maximum_fusion.2.refs_0_), channel_id=1, source_target_pairs={{2,4},{6,8},{10,12},{14,16},{18,20},{22,24},{26,28},{3,5},{7,9},{1... | collective-permute-start | bytes 786440 | tf_op jit(solution)/shard_map/ppermute | solution.py:22
  1.7 7.4 %collective-permute-start.2 = (bf16[2,128,512]{2,1,0:T(8,128)(2,1)S(1)}, bf16[2,128,512]{2,1,0:T(8,128)(2,1)S(1)}, u32[]{:S(2)}, u32[]{:S(2)}) collective-permute-start(bf16[2,128,512]{2,1,0:T(8,128)(2,1)S(1)} %pad_maximum_fusion.2.refs_0_), channel_id=1, source_target_pairs={{0,6},{2,8},{4,10},{6,12},{8,14},{10,16},{12,18},{14,20},{16,22},{... | collective-permute-start | bytes 786440 | tf_op jit(solution)/shard_map/ppermute | solution.py:22
  9.1 1.9 %collective-permute-start.3 = (bf16[2,128,512]{2,1,0:T(8,128)(2,1)S(1)}, bf16[2,128,512]{2,1,0:T(8,128)(2,1)S(1)}, u32[]{:S(2)}, u32[]{:S(2)}) collective-permute-start(bf16[2,128,512]{2,1,0:T(8,128)(2,1)S(1)} %pad_maximum_fusion.2.refs_0_), channel_id=1, source_target_pairs={{0,10},{2,12},{4,14},{6,16},{8,18},{10,20},{12,22},{14,24},{16,26}... | collective-permute-start | bytes 786440 | tf_op jit(solution)/shard_map/ppermute | solution.py:22
  11.0 2.6 %collective-permute-start.4 = (bf16[2,128,512]{2,1,0:T(8,128)(2,1)S(1)}, bf16[2,128,512]{2,1,0:T(8,128)(2,1)S(1)}, u32[]{:S(2)}, u32[]{:S(2)}) collective-permute-start(bf16[2,128,512]{2,1,0:T(8,128)(2,1)S(1)} %pad_maximum_fusion.2.refs_0_), channel_id=1, source_target_pairs={{0,2},{2,0},{4,6},{6,4},{8,10},{10,8},{12,14},{14,12},{16,18},{18,... | collective-permute-start | bytes 786440 | tf_op jit(solution)/shard_map/ppermute | solution.py:24
  13.7 2.0 %collective-permute-start = (bf16[2,128,512]{2,1,0:T(8,128)(2,1)S(1)}, bf16[2,128,512]{2,1,0:T(8,128)(2,1)S(1)}, u32[]{:S(2)}, u32[]{:S(2)}) collective-permute-start(bf16[2,128,512]{2,1,0:T(8,128)(2,1)S(1)} %pad_maximum_fusion.2.refs_0_), channel_id=1, source_target_pairs={{0,14},{2,16},{4,18},{6,20},{8,22},{10,24},{12,26},{14,28},{16,30}... | collective-permute-start | bytes 786440 | tf_op jit(solution)/shard_map/ppermute | solution.py:22
  15.7 0.7 pad_clamp_fusion
  16.4 0.8 %select_reduce_fusion = s32[8]{0:T(128)S(1)} fusion(s32[8]{0:T(128)} %param.14), kind=kLoop, calls=%fused_computation.28 | loop fusion | flops 184 | bytes 64 | tf_op jit(solution)/shard_map/reduce_sum | solution.py:176
  19.7 0.7 broadcast_select_fusion
  20.4 0.6 gather_fusion.1
  21.0 0.7 subtract_multiply_fusion
  21.8 1.4 %select_reduce_fusion.1 = (s32[]{:T(128)}, s32[]{:T(128)}) fusion(s32[8]{0:T(128)} %param.15, s32[]{:T(128)S(6)} %sub.51, s32[8]{0:T(128)} %param.14), kind=kLoop, calls=%fused_computation.39 | loop fusion | flops 38 | bytes 76 | tf_op jit(solution)/shard_map/reduce_sum | solution.py:183
  23.8 0.7 pad_clamp_fusion.1
  25.1 0.7 subtract_multiply_fusion.1
  27.4 1.9 %fusion.5 = (f32[1024,64]{1,0:T(8,128)S(1)}, f32[1024,64]{1,0:T(8,128)S(1)}, f32[1024,64]{1,0:T(8,128)S(1)}) fusion(f32[64]{0:T(128)S(1)} %multiply_power_fusion, f32[1024]{0:T(1024)S(1)} %get-tuple-element.32), kind=kLoop, calls=%fused_computation.13 | loop fusion | flops 131072 | bytes 790784 | tf_op jit(solution)/shard_map/neg | solution.py:113
  31.6 1.0 %copy-done = bf16[128,2048]{1,0:T(8,128)(2,1)S(1)} copy-done((bf16[128,2048]{1,0:T(8,128)(2,1)S(1)}, bf16[128,2048]{1,0:T(8,128)(2,1)}, u32[]{:S(2)}) %copy-start) | copy-done | bytes 524312
  32.7 6.2 %shard_map.100 = (f32[128,2048]{1,0:T(8,128)S(1)}, f32[128,16]{1,0:T(8,128)S(1)}, f32[128,16]{1,0:T(8,128)S(1)}) custom-call(s32[1]{0:T(128)} %constant.54.clone.1.peer_ref, s32[128,1]{1,0:T(8,128)S(1)} %iota_add_fusion.query_pos_ref, s32[1,1024]{1,0:T(1,128)S(1)} %and_select_fusion.key_limit_ref, f32[128,128]{1,0:T(8,128)S(1)} %get-tuple-element.38.query_cos_ref, ...), custom_call_target="tpu_custom_call" | custom-call | flops 1073741824 | bytes 3145728 | tf_op jit(solution)/shard_map/pallas_call | solution.py:149
  39.3 1.2 %collective-permute-done.8.refs_4_ = bf16[2,128,512]{2,1,0:T(8,128)(2,1)S(1)} collective-permute-done((bf16[2,128,512]{2,1,0:T(8,128)(2,1)S(1)}, bf16[2,128,512]{2,1,0:T(8,128)(2,1)S(1)}, u32[]{:S(2)}, u32[]{:S(2)}) %collective-permute-start.8) | collective-permute-done | bytes 262176 | tf_op jit(solution)/shard_map/ppermute | solution.py:27
  40.5 1.0 %copy-done.1 = bf16[128,2048]{1,0:T(8,128)(2,1)S(1)} copy-done((bf16[128,2048]{1,0:T(8,128)(2,1)S(1)}, bf16[128,2048]{1,0:T(8,128)(2,1)}, u32[]{:S(2)}) %copy-start.1) | copy-done | bytes 524312
  41.6 10.9 %shard_map.101 = (bf16[128,2048]{1,0:T(8,128)(2,1)S(1)}, bf16[128,2048]{1,0:T(8,128)(2,1)S(1)}) custom-call(s32[1]{0:T(128)} %bitcast.peer_ref, s32[128,1]{1,0:T(8,128)S(1)} %iota_add_fusion.query_pos_ref, s32[1,256]{1,0:T(1,128)S(1)} %and_select_fusion.1.key_limit_ref, f32[128,128]{1,0:T(8,128)S(1)} %get-tuple-element.38.query_cos_ref, ...), custom_call_target="tpu_custom_call" | custom-call | flops 1342177280 | bytes 10485760 | tf_op jit(solution)/shard_map/pallas_call | solution.py:149
  52.5 1.6 %collective-permute-start.9 = (bf16[128,2048]{1,0:T(8,128)(2,1)S(1)}, bf16[128,2048]{1,0:T(8,128)(2,1)S(1)}, u32[]{:S(2)}, u32[]{:S(2)}) collective-permute-start(bf16[128,2048]{1,0:T(8,128)(2,1)S(1)} %get-tuple-element.22), channel_id=1, source_target_pairs={{0,1},{1,0},{2,3},{3,2},{4,5},{5,4},{6,7},{7,6},{8,9},{9,8},{10,11... | collective-permute-start | bytes 1572872 | tf_op jit(solution)/shard_map/ppermute | solution.py:206
  54.1 4.6 %fusion.2 = bf16[128,2048]{1,0:T(8,128)(2,1)S(1)} fusion(bf16[128,2048]{1,0:T(8,128)(2,1)S(1)} %get-tuple-element.21, bf16[2048,4096]{1,0:T(8,128)(2,1)} %refs_5_.1, s32[]{:T(128)S(6)} %select_n.71), kind=kOutput, calls=%fused_computation.4 | convolution fusion | flops 1074003968 | bytes 9437188 | tf_op jit(solution)/shard_map/dot_general | solution.py:209
  58.7 7.8 %collective-permute-done.9 = bf16[128,2048]{1,0:T(8,128)(2,1)S(1)} collective-permute-done((bf16[128,2048]{1,0:T(8,128)(2,1)S(1)}, bf16[128,2048]{1,0:T(8,128)(2,1)S(1)}, u32[]{:S(2)}, u32[]{:S(2)}) %collective-permute-start.9) | collective-permute-done | bytes 524320 | tf_op jit(solution)/shard_map/ppermute | solution.py:206
  66.6 0.9 %add_convert_fusion = bf16[128,2048]{1,0:T(8,128)(2,1)} fusion(bf16[128,2048]{1,0:T(8,128)(2,1)S(1)} %collective-permute-done.9, bf16[128,2048]{1,0:T(8,128)(2,1)S(1)} %fusion.2), kind=kLoop, calls=%fused_computation.5 | loop fusion | flops 1048576 | bytes 1572864 | tf_op jit(solution)/shard_map/convert_element_type | solution.py:211
  (29 shorter events, 5.6 us)
Async XLA Ops:
  1.0 28.3 %collective-permute-start.1 = (bf16[2,128,512]{2,1,0:T(8,128)(2,1)S(1)}, bf16[2,128,512]{2,1,0:T(8,128)(2,1)S(1)}, u32[]{:S(2)}, u32[]{:S(2)}) collective-permute-start(bf16[2,128,512]{2,1,0:T(8,128)(2,1)S(1)} %pad_maximum_fusion.2.refs_0_), channel_id=1, source_target_pairs={{2,4},{6,8},{10,12},{14,16},{18,20},{22,24},{26,28},{3,5},{7,9},{1... | collective-permute-start | bytes 786440 | tf_op jit(solution)/shard_map/ppermute | solution.py:22
  1.7 27.7 %collective-permute-start.2 = (bf16[2,128,512]{2,1,0:T(8,128)(2,1)S(1)}, bf16[2,128,512]{2,1,0:T(8,128)(2,1)S(1)}, u32[]{:S(2)}, u32[]{:S(2)}) collective-permute-start(bf16[2,128,512]{2,1,0:T(8,128)(2,1)S(1)} %pad_maximum_fusion.2.refs_0_), channel_id=1, source_target_pairs={{0,6},{2,8},{4,10},{6,12},{8,14},{10,16},{12,18},{14,20},{16,22},{... | collective-permute-start | bytes 786440 | tf_op jit(solution)/shard_map/ppermute | solution.py:22
  9.1 20.8 %collective-permute-start.3 = (bf16[2,128,512]{2,1,0:T(8,128)(2,1)S(1)}, bf16[2,128,512]{2,1,0:T(8,128)(2,1)S(1)}, u32[]{:S(2)}, u32[]{:S(2)}) collective-permute-start(bf16[2,128,512]{2,1,0:T(8,128)(2,1)S(1)} %pad_maximum_fusion.2.refs_0_), channel_id=1, source_target_pairs={{0,10},{2,12},{4,14},{6,16},{8,18},{10,20},{12,22},{14,24},{16,26}... | collective-permute-start | bytes 786440 | tf_op jit(solution)/shard_map/ppermute | solution.py:22
  11.0 19.4 %collective-permute-start.4 = (bf16[2,128,512]{2,1,0:T(8,128)(2,1)S(1)}, bf16[2,128,512]{2,1,0:T(8,128)(2,1)S(1)}, u32[]{:S(2)}, u32[]{:S(2)}) collective-permute-start(bf16[2,128,512]{2,1,0:T(8,128)(2,1)S(1)} %pad_maximum_fusion.2.refs_0_), channel_id=1, source_target_pairs={{0,2},{2,0},{4,6},{6,4},{8,10},{10,8},{12,14},{14,12},{16,18},{18,... | collective-permute-start | bytes 786440 | tf_op jit(solution)/shard_map/ppermute | solution.py:24
  13.7 25.3 %collective-permute-start = (bf16[2,128,512]{2,1,0:T(8,128)(2,1)S(1)}, bf16[2,128,512]{2,1,0:T(8,128)(2,1)S(1)}, u32[]{:S(2)}, u32[]{:S(2)}) collective-permute-start(bf16[2,128,512]{2,1,0:T(8,128)(2,1)S(1)} %pad_maximum_fusion.2.refs_0_), channel_id=1, source_target_pairs={{0,14},{2,16},{4,18},{6,20},{8,22},{10,24},{12,26},{14,28},{16,30}... | collective-permute-start | bytes 786440 | tf_op jit(solution)/shard_map/ppermute | solution.py:22
  29.3 1.6 %collective-permute-start.5 = (bf16[2,128,512]{2,1,0:T(8,128)(2,1)S(1)}, bf16[2,128,512]{2,1,0:T(8,128)(2,1)S(1)}, u32[]{:S(2)}, u32[]{:S(2)}) collective-permute-start(bf16[2,128,512]{2,1,0:T(8,128)(2,1)S(1)} %collective-permute-done.1.refs_1_), channel_id=1, source_target_pairs={{0,2},{2,0},{4,6},{6,4},{8,10},{10,8},{12,14},{14,12},{16,18},{18,... | collective-permute-start | bytes 786440 | tf_op jit(solution)/shard_map/ppermute | solution.py:24
  29.4 1.9 %collective-permute-start.6 = (bf16[2,128,512]{2,1,0:T(8,128)(2,1)S(1)}, bf16[2,128,512]{2,1,0:T(8,128)(2,1)S(1)}, u32[]{:S(2)}, u32[]{:S(2)}) collective-permute-start(bf16[2,128,512]{2,1,0:T(8,128)(2,1)S(1)} %collective-permute-done.2.refs_2_), channel_id=1, source_target_pairs={{0,2},{2,0},{4,6},{6,4},{8,10},{10,8},{12,14},{14,12},{16,18},{18,... | collective-permute-start | bytes 786440 | tf_op jit(solution)/shard_map/ppermute | solution.py:24
  29.9 1.8 %collective-permute-start.7 = (bf16[2,128,512]{2,1,0:T(8,128)(2,1)S(1)}, bf16[2,128,512]{2,1,0:T(8,128)(2,1)S(1)}, u32[]{:S(2)}, u32[]{:S(2)}) collective-permute-start(bf16[2,128,512]{2,1,0:T(8,128)(2,1)S(1)} %collective-permute-done.3.refs_3_), channel_id=1, source_target_pairs={{0,2},{2,0},{4,6},{6,4},{8,10},{10,8},{12,14},{14,12},{16,18},{18,... | collective-permute-start | bytes 786440 | tf_op jit(solution)/shard_map/ppermute | solution.py:24
  31.6 1.0 %copy-start = (bf16[128,2048]{1,0:T(8,128)(2,1)S(1)}, bf16[128,2048]{1,0:T(8,128)(2,1)}, u32[]{:S(2)}) copy-start(bf16[128,2048]{1,0:T(8,128)(2,1)} %query_ref.3) | copy-start | bytes 1572868
  38.9 1.6 %collective-permute-start.8 = (bf16[2,128,512]{2,1,0:T(8,128)(2,1)S(1)}, bf16[2,128,512]{2,1,0:T(8,128)(2,1)S(1)}, u32[]{:S(2)}, u32[]{:S(2)}) collective-permute-start(bf16[2,128,512]{2,1,0:T(8,128)(2,1)S(1)} %collective-permute-done.refs_3_), channel_id=1, source_target_pairs={{0,2},{2,0},{4,6},{6,4},{8,10},{10,8},{12,14},{14,12},{16,18},{18,... | collective-permute-start | bytes 786440 | tf_op jit(solution)/shard_map/ppermute | solution.py:27
  40.5 1.0 %copy-start.1 = (bf16[128,2048]{1,0:T(8,128)(2,1)S(1)}, bf16[128,2048]{1,0:T(8,128)(2,1)}, u32[]{:S(2)}) copy-start(bf16[128,2048]{1,0:T(8,128)(2,1)} %query_ref.3) | copy-start | bytes 1572868
  52.5 14.0 %collective-permute-start.9 = (bf16[128,2048]{1,0:T(8,128)(2,1)S(1)}, bf16[128,2048]{1,0:T(8,128)(2,1)S(1)}, u32[]{:S(2)}, u32[]{:S(2)}) collective-permute-start(bf16[128,2048]{1,0:T(8,128)(2,1)S(1)} %get-tuple-element.22), channel_id=1, source_target_pairs={{0,1},{1,0},{2,3},{3,2},{4,5},{5,4},{6,7},{7,6},{8,9},{9,8},{10,11... | collective-permute-start | bytes 1572872 | tf_op jit(solution)/shard_map/ppermute | solution.py:206

commit v13 on v10

--- a/solution.py
+++ b/solution.py
@@ -69,10 +69,10 @@
                 query = turn(query_ref[:, columns], query_cos_ref[...], query_sin_ref[...])
                 scores = lax.dot_general(
                     query, keys, (((1,), (1,)), ((), ())), preferred_element_type=jnp.float32
-                ) * (1.0 / math.sqrt(HEAD_SIZE))
+                )
                 scores = jnp.where(allowed, scores, -1e30)
                 highest = jnp.max(scores, axis=1, keepdims=True)
-                weights = jnp.exp(scores - highest)
+                weights = jnp.exp2((scores - highest) * (math.log2(math.e) / math.sqrt(HEAD_SIZE)))
                 totals = jnp.sum(weights, axis=1, keepdims=True)
                 summed = jnp.dot(weights.astype(jnp.bfloat16), values, preferred_element_type=jnp.float32)
                 out_ref[:, columns] = (summed / totals).astype(out_ref.dtype)

time: 63.2 us -> 63.2 us (level)
  no operation moved by 1% of the time
where the time goes in v13:
time: 63.2 us; the launch traced here: 62.8 us
  starting transfers between devices  16 us (25%)
  other arithmetic  13.8 us (22%)
  waiting for transfers between devices  13.7 us (22%)
  Pallas kernels  10.8 us (17%)
  matrix products  4.67 us (7%)
  between operations  2.71 us (4%)
  local copies, waits for them, and re-layouts  1.04 us (2%)
    pallas_call x1, Pallas kernels, attend(): pl.pallas_call(functools.partial(attention_kernel, n_slots, uses, heads_k...  10.8 us
    ppermute x5, starting transfers between devices, gather_window(): passed = [lax.ppermute(block, 'ctx', across) for block in [kv] + received]  8.35 us
    ppermute x1, waiting for transfers between devices, on_device(): got = lax.ppermute(peer_terms, 'tp', [(0, 1), (1, 0)])  7.99 us
    ppermute x4, starting transfers between devices, gather_window(): received.append(lax.ppermute(kv, 'ctx', pairs))  6.1 us
    ppermute x4, waiting for transfers between devices, gather_window(): received.append(lax.ppermute(kv, 'ctx', pairs))  5.02 us
    dot_general x1, matrix products, on_device(): jnp.dot(attended, own_weight, preferred_element_type=jnp.float32)  4.67 us
    neg x2, other arithmetic, tables(): -sine  4.57 us
    ppermute x1, starting transfers between devices, on_device(): got = lax.ppermute(peer_terms, 'tp', [(0, 1), (1, 0)])  1.6 us
  transfers between devices with their start and end apart: 10, of which 3 were waited for; matrix products, arithmetic and copies ran while one was open for 26% of the time, Pallas kernels for 0%

profile of v13, /device:TPU:24, one launch (start us, length us, event | category | flops | bytes accessed | tf_op | source)
XLA Modules:
  0.0 62.8 jit_solution(637463250081904745)
XLA Ops:
  0.0 1.0 %pad_maximum_fusion.2.refs_0_ = bf16[2,128,512]{2,1,0:T(8,128)(2,1)S(1)} fusion(bf16[1,128,512]{2,1,0:T(8,128)(2,1)} %bitcast.12, bf16[1,128,512]{2,1,0:T(8,128)(2,1)} %bitcast.13), kind=kLoop, calls=%fused_computation.8 | loop fusion | flops 131072 | bytes 524288 | tf_op jit(solution)/shard_map/stack | solution.py:148
  1.0 1.3 %collective-permute-start = (bf16[2,128,512]{2,1,0:T(8,128)(2,1)S(1)}, bf16[2,128,512]{2,1,0:T(8,128)(2,1)S(1)}, u32[]{:S(2)}, u32[]{:S(2)}) collective-permute-start(bf16[2,128,512]{2,1,0:T(8,128)(2,1)S(1)} %pad_maximum_fusion.2.refs_0_), channel_id=1, source_target_pairs={{2,4},{6,8},{10,12},{14,16},{18,20},{22,24},{26,28},{3,5},{7,9},{1... | collective-permute-start | bytes 786440 | tf_op jit(solution)/shard_map/ppermute | solution.py:22
  2.3 2.2 %collective-permute-start.1 = (bf16[2,128,512]{2,1,0:T(8,128)(2,1)S(1)}, bf16[2,128,512]{2,1,0:T(8,128)(2,1)S(1)}, u32[]{:S(2)}, u32[]{:S(2)}) collective-permute-start(bf16[2,128,512]{2,1,0:T(8,128)(2,1)S(1)} %pad_maximum_fusion.2.refs_0_), channel_id=1, source_target_pairs={{0,6},{2,8},{4,10},{6,12},{8,14},{10,16},{12,18},{14,20},{16,22},{... | collective-permute-start | bytes 786440 | tf_op jit(solution)/shard_map/ppermute | solution.py:22
  4.5 1.3 %collective-permute-start.2 = (bf16[2,128,512]{2,1,0:T(8,128)(2,1)S(1)}, bf16[2,128,512]{2,1,0:T(8,128)(2,1)S(1)}, u32[]{:S(2)}, u32[]{:S(2)}) collective-permute-start(bf16[2,128,512]{2,1,0:T(8,128)(2,1)S(1)} %pad_maximum_fusion.2.refs_0_), channel_id=1, source_target_pairs={{0,10},{2,12},{4,14},{6,16},{8,18},{10,20},{12,22},{14,24},{16,26}... | collective-permute-start | bytes 786440 | tf_op jit(solution)/shard_map/ppermute | solution.py:22
  5.8 1.3 %collective-permute-start.3 = (bf16[2,128,512]{2,1,0:T(8,128)(2,1)S(1)}, bf16[2,128,512]{2,1,0:T(8,128)(2,1)S(1)}, u32[]{:S(2)}, u32[]{:S(2)}) collective-permute-start(bf16[2,128,512]{2,1,0:T(8,128)(2,1)S(1)} %pad_maximum_fusion.2.refs_0_), channel_id=1, source_target_pairs={{0,14},{2,16},{4,18},{6,20},{8,22},{10,24},{12,26},{14,28},{16,30}... | collective-permute-start | bytes 786440 | tf_op jit(solution)/shard_map/ppermute | solution.py:22
  7.1 1.4 %collective-permute-start.4 = (bf16[2,128,512]{2,1,0:T(8,128)(2,1)S(1)}, bf16[2,128,512]{2,1,0:T(8,128)(2,1)S(1)}, u32[]{:S(2)}, u32[]{:S(2)}) collective-permute-start(bf16[2,128,512]{2,1,0:T(8,128)(2,1)S(1)} %pad_maximum_fusion.2.refs_0_), channel_id=1, source_target_pairs={{0,2},{2,0},{4,6},{6,4},{8,10},{10,8},{12,14},{14,12},{16,18},{18,... | collective-permute-start | bytes 786440 | tf_op jit(solution)/shard_map/ppermute | solution.py:24
  8.5 0.5 multiply_power_fusion
  9.0 0.8 %select_reduce_fusion = s32[8]{0:T(128)S(1)} fusion(s32[8]{0:T(128)} %param.12), kind=kLoop, calls=%fused_computation.20 | loop fusion | flops 184 | bytes 64 | tf_op jit(solution)/shard_map/reduce_sum | solution.py:151
  9.8 0.6 %fusion.11 = s32[]{:T(128)} fusion(s32[8]{0:T(128)S(1)} %select_reduce_fusion, s32[]{:T(128)S(6)} %axis_index.33), kind=kLoop, calls=%fused_computation.27 | loop fusion | flops 23 | bytes 40 | tf_op jit(solution)/shard_map/reduce_sum | solution.py:154
  11.1 0.6 %select_reduce_fusion.3 = s32[]{:T(128)} fusion(s32[8]{0:T(128)S(1)} %select_reduce_fusion, s32[]{:T(128)S(6)} %sub.25), kind=kLoop, calls=%fused_computation.32 | loop fusion | flops 23 | bytes 40 | tf_op jit(solution)/shard_map/reduce_sum | solution.py:156
  12.4 1.3 %fusion.10 = s32[10]{0:T(128)S(1)} fusion(s32[10]{0:T(128)} %constant.46.clone, s32[10]{0:T(128)} %constant.47.clone, pred[]{:T(512)S(6)} %eq.14, s32[]{:T(128)} %select_reduce_fusion.3, s32[]{:T(128)S(6)} %axis_index.33), kind=kLoop, calls=%fused_computation.26 | loop fusion | flops 40 | bytes 129 | tf_op jit(solution)/shard_map/mul | solution.py:162
  13.8 1.3 %select_reduce_fusion.1 = (s32[]{:T(128)}, s32[]{:T(128)}) fusion(s32[8]{0:T(128)} %param.13, s32[]{:T(128)S(6)} %sub.25, s32[8]{0:T(128)} %param.12), kind=kLoop, calls=%fused_computation.30 | loop fusion | flops 38 | bytes 76 | tf_op jit(solution)/shard_map/reduce_sum | solution.py:158
  16.3 3.0 %fusion.5 = (f32[1280,64]{1,0:T(8,128)S(1)}, f32[1280,64]{1,0:T(8,128)S(1)}, f32[1280,64]{1,0:T(8,128)S(1)}) fusion(f32[64]{0:T(128)} %multiply_power_fusion, f32[1280]{0:T(1024)S(1)} %get-tuple-element.15), kind=kLoop, calls=%fused_computation.9 | loop fusion | flops 163840 | bytes 988416 | tf_op jit(solution)/shard_map/neg | solution.py:97
  19.9 1.6 %fusion.6 = (f32[128,64]{1,0:T(8,128)}, f32[128,64]{1,0:T(8,128)}, f32[128,64]{1,0:T(8,128)}) fusion(f32[64]{0:T(128)} %multiply_power_fusion, f32[128]{0:T(128)} %add_convert_fusion.1), kind=kLoop, calls=%fused_computation.15 | loop fusion | flops 16384 | bytes 99072 | tf_op jit(solution)/shard_map/neg | solution.py:97
  21.5 1.0 %pad_maximum_fusion.3 = (f32[128,128]{1,0:T(8,128)S(1)}, f32[128,128]{1,0:T(8,128)S(1)}) fusion(f32[128,64]{1,0:T(8,128)} %get-tuple-element.14, f32[128,64]{1,0:T(8,128)} %get-tuple-element.13, f32[128,64]{1,0:T(8,128)} %get-tuple-element.12), kind=kLoop, calls=%fused_computation.12 | loop fusion | flops 32768 | bytes 229376 | tf_op jit(solution)/shard_map/concatenate | solution.py:97
  23.1 5.0 %collective-permute-done.2.refs_3_ = bf16[2,128,512]{2,1,0:T(8,128)(2,1)S(1)} collective-permute-done((bf16[2,128,512]{2,1,0:T(8,128)(2,1)S(1)}, bf16[2,128,512]{2,1,0:T(8,128)(2,1)S(1)}, u32[]{:S(2)}, u32[]{:S(2)}) %collective-permute-start.2) | collective-permute-done | bytes 262176 | tf_op jit(solution)/shard_map/ppermute | solution.py:22
  28.2 6.4 %collective-permute-start.8 = (bf16[2,128,512]{2,1,0:T(8,128)(2,1)S(1)}, bf16[2,128,512]{2,1,0:T(8,128)(2,1)S(1)}, u32[]{:S(2)}, u32[]{:S(2)}) collective-permute-start(bf16[2,128,512]{2,1,0:T(8,128)(2,1)S(1)} %collective-permute-done.3.refs_4_), channel_id=1, source_target_pairs={{0,2},{2,0},{4,6},{6,4},{8,10},{10,8},{12,14},{14,12},{16,18},{18,... | collective-permute-start | bytes 786440 | tf_op jit(solution)/shard_map/ppermute | solution.py:24
  35.0 0.7 %collective-permute-done.8.refs_9_ = bf16[2,128,512]{2,1,0:T(8,128)(2,1)S(1)} collective-permute-done((bf16[2,128,512]{2,1,0:T(8,128)(2,1)S(1)}, bf16[2,128,512]{2,1,0:T(8,128)(2,1)S(1)}, u32[]{:S(2)}, u32[]{:S(2)}) %collective-permute-start.8) | collective-permute-done | bytes 262176 | tf_op jit(solution)/shard_map/ppermute | solution.py:24
  35.7 1.0 %copy-done = bf16[128,2048]{1,0:T(8,128)(2,1)S(1)} copy-done((bf16[128,2048]{1,0:T(8,128)(2,1)S(1)}, bf16[128,2048]{1,0:T(8,128)(2,1)}, u32[]{:S(2)}) %copy-start) | copy-done | bytes 524312
  36.8 10.8 %shard_map.82 = (bf16[128,2048]{1,0:T(8,128)(2,1)S(1)}, bf16[128,2048]{1,0:T(8,128)(2,1)S(1)}) custom-call(s32[1]{0:T(128)} %bitcast.peer_ref, s32[1]{0:T(128)} %bitcast.1.core_ref, s32[128,1]{1,0:T(8,128)S(1)} %iota_add_fusion.query_pos_ref, s32[1,1280]{1,0:T(1,128)S(1)} %and_select_fusion.key_limit_ref, f32[128,128]{1,0:T(8,128)S(1)} %get-tuple-element.19.query_cos_ref, ...), custom_call_target="tpu_custom_call" | custom-call | flops 2415919104 | bytes 12582912 | tf_op jit(solution)/shard_map/pallas_call | solution.py:127
  47.6 1.6 %collective-permute-start.9 = (bf16[128,2048]{1,0:T(8,128)(2,1)S(1)}, bf16[128,2048]{1,0:T(8,128)(2,1)S(1)}, u32[]{:S(2)}, u32[]{:S(2)}) collective-permute-start(bf16[128,2048]{1,0:T(8,128)(2,1)S(1)} %get-tuple-element.8), channel_id=1, source_target_pairs={{0,1},{1,0},{2,3},{3,2},{4,5},{5,4},{6,7},{7,6},{8,9},{9,8},{10,11... | collective-permute-start | bytes 1572872 | tf_op jit(solution)/shard_map/ppermute | solution.py:174
  49.2 4.7 %fusion.2 = bf16[128,2048]{1,0:T(8,128)(2,1)S(1)} fusion(bf16[128,2048]{1,0:T(8,128)(2,1)S(1)} %get-tuple-element.7, bf16[2048,4096]{1,0:T(8,128)(2,1)} %refs_10_.1, s32[]{:T(128)S(6)} %select_n.53), kind=kOutput, calls=%fused_computation.2 | convolution fusion | flops 1074003968 | bytes 9437188 | tf_op jit(solution)/shard_map/dot_general | solution.py:177
  53.9 8.0 %collective-permute-done.9 = bf16[128,2048]{1,0:T(8,128)(2,1)S(1)} collective-permute-done((bf16[128,2048]{1,0:T(8,128)(2,1)S(1)}, bf16[128,2048]{1,0:T(8,128)(2,1)S(1)}, u32[]{:S(2)}, u32[]{:S(2)}) %collective-permute-start.9) | collective-permute-done | bytes 524320 | tf_op jit(solution)/shard_map/ppermute | solution.py:174
  61.9 0.9 %add_convert_fusion = bf16[128,2048]{1,0:T(8,128)(2,1)} fusion(bf16[128,2048]{1,0:T(8,128)(2,1)S(1)} %collective-permute-done.9, bf16[128,2048]{1,0:T(8,128)(2,1)S(1)} %fusion.2), kind=kLoop, calls=%fused_computation.3 | loop fusion | flops 1048576 | bytes 1572864 | tf_op jit(solution)/shard_map/convert_element_type | solution.py:179
  (16 shorter events, 1.6 us)
Async XLA Ops:
  1.0 21.6 %collective-permute-start = (bf16[2,128,512]{2,1,0:T(8,128)(2,1)S(1)}, bf16[2,128,512]{2,1,0:T(8,128)(2,1)S(1)}, u32[]{:S(2)}, u32[]{:S(2)}) collective-permute-start(bf16[2,128,512]{2,1,0:T(8,128)(2,1)S(1)} %pad_maximum_fusion.2.refs_0_), channel_id=1, source_target_pairs={{2,4},{6,8},{10,12},{14,16},{18,20},{22,24},{26,28},{3,5},{7,9},{1... | collective-permute-start | bytes 786440 | tf_op jit(solution)/shard_map/ppermute | solution.py:22
  2.3 20.4 %collective-permute-start.1 = (bf16[2,128,512]{2,1,0:T(8,128)(2,1)S(1)}, bf16[2,128,512]{2,1,0:T(8,128)(2,1)S(1)}, u32[]{:S(2)}, u32[]{:S(2)}) collective-permute-start(bf16[2,128,512]{2,1,0:T(8,128)(2,1)S(1)} %pad_maximum_fusion.2.refs_0_), channel_id=1, source_target_pairs={{0,6},{2,8},{4,10},{6,12},{8,14},{10,16},{12,18},{14,20},{16,22},{... | collective-permute-start | bytes 786440 | tf_op jit(solution)/shard_map/ppermute | solution.py:22
  4.5 23.6 %collective-permute-start.2 = (bf16[2,128,512]{2,1,0:T(8,128)(2,1)S(1)}, bf16[2,128,512]{2,1,0:T(8,128)(2,1)S(1)}, u32[]{:S(2)}, u32[]{:S(2)}) collective-permute-start(bf16[2,128,512]{2,1,0:T(8,128)(2,1)S(1)} %pad_maximum_fusion.2.refs_0_), channel_id=1, source_target_pairs={{0,10},{2,12},{4,14},{6,16},{8,18},{10,20},{12,22},{14,24},{16,26}... | collective-permute-start | bytes 786440 | tf_op jit(solution)/shard_map/ppermute | solution.py:22
  5.8 22.3 %collective-permute-start.3 = (bf16[2,128,512]{2,1,0:T(8,128)(2,1)S(1)}, bf16[2,128,512]{2,1,0:T(8,128)(2,1)S(1)}, u32[]{:S(2)}, u32[]{:S(2)}) collective-permute-start(bf16[2,128,512]{2,1,0:T(8,128)(2,1)S(1)} %pad_maximum_fusion.2.refs_0_), channel_id=1, source_target_pairs={{0,14},{2,16},{4,18},{6,20},{8,22},{10,24},{12,26},{14,28},{16,30}... | collective-permute-start | bytes 786440 | tf_op jit(solution)/shard_map/ppermute | solution.py:22
  7.1 27.9 %collective-permute-start.4 = (bf16[2,128,512]{2,1,0:T(8,128)(2,1)S(1)}, bf16[2,128,512]{2,1,0:T(8,128)(2,1)S(1)}, u32[]{:S(2)}, u32[]{:S(2)}) collective-permute-start(bf16[2,128,512]{2,1,0:T(8,128)(2,1)S(1)} %pad_maximum_fusion.2.refs_0_), channel_id=1, source_target_pairs={{0,2},{2,0},{4,6},{6,4},{8,10},{10,8},{12,14},{14,12},{16,18},{18,... | collective-permute-start | bytes 786440 | tf_op jit(solution)/shard_map/ppermute | solution.py:24
  22.6 12.4 %collective-permute-start.5 = (bf16[2,128,512]{2,1,0:T(8,128)(2,1)S(1)}, bf16[2,128,512]{2,1,0:T(8,128)(2,1)S(1)}, u32[]{:S(2)}, u32[]{:S(2)}) collective-permute-start(bf16[2,128,512]{2,1,0:T(8,128)(2,1)S(1)} %collective-permute-done.refs_1_), channel_id=1, source_target_pairs={{0,2},{2,0},{4,6},{6,4},{8,10},{10,8},{12,14},{14,12},{16,18},{18,... | collective-permute-start | bytes 786440 | tf_op jit(solution)/shard_map/ppermute | solution.py:24
  22.7 12.3 %collective-permute-start.6 = (bf16[2,128,512]{2,1,0:T(8,128)(2,1)S(1)}, bf16[2,128,512]{2,1,0:T(8,128)(2,1)S(1)}, u32[]{:S(2)}, u32[]{:S(2)}) collective-permute-start(bf16[2,128,512]{2,1,0:T(8,128)(2,1)S(1)} %collective-permute-done.1.refs_2_), channel_id=1, source_target_pairs={{0,2},{2,0},{4,6},{6,4},{8,10},{10,8},{12,14},{14,12},{16,18},{18,... | collective-permute-start | bytes 786440 | tf_op jit(solution)/shard_map/ppermute | solution.py:24
  28.2 6.9 %collective-permute-start.7 = (bf16[2,128,512]{2,1,0:T(8,128)(2,1)S(1)}, bf16[2,128,512]{2,1,0:T(8,128)(2,1)S(1)}, u32[]{:S(2)}, u32[]{:S(2)}) collective-permute-start(bf16[2,128,512]{2,1,0:T(8,128)(2,1)S(1)} %collective-permute-done.2.refs_3_), channel_id=1, source_target_pairs={{0,2},{2,0},{4,6},{6,4},{8,10},{10,8},{12,14},{14,12},{16,18},{18,... | collective-permute-start | bytes 786440 | tf_op jit(solution)/shard_map/ppermute | solution.py:24
  28.2 7.6 %collective-permute-start.8 = (bf16[2,128,512]{2,1,0:T(8,128)(2,1)S(1)}, bf16[2,128,512]{2,1,0:T(8,128)(2,1)S(1)}, u32[]{:S(2)}, u32[]{:S(2)}) collective-permute-start(bf16[2,128,512]{2,1,0:T(8,128)(2,1)S(1)} %collective-permute-done.3.refs_4_), channel_id=1, source_target_pairs={{0,2},{2,0},{4,6},{6,4},{8,10},{10,8},{12,14},{14,12},{16,18},{18,... | collective-permute-start | bytes 786440 | tf_op jit(solution)/shard_map/ppermute | solution.py:24
  35.7 1.0 %copy-start = (bf16[128,2048]{1,0:T(8,128)(2,1)S(1)}, bf16[128,2048]{1,0:T(8,128)(2,1)}, u32[]{:S(2)}) copy-start(bf16[128,2048]{1,0:T(8,128)(2,1)} %query_ref.1) | copy-start | bytes 1572868
  47.6 14.3 %collective-permute-start.9 = (bf16[128,2048]{1,0:T(8,128)(2,1)S(1)}, bf16[128,2048]{1,0:T(8,128)(2,1)S(1)}, u32[]{:S(2)}, u32[]{:S(2)}) collective-permute-start(bf16[128,2048]{1,0:T(8,128)(2,1)S(1)} %get-tuple-element.8), channel_id=1, source_target_pairs={{0,1},{1,0},{2,3},{3,2},{4,5},{5,4},{6,7},{7,6},{8,9},{9,8},{10,11... | collective-permute-start | bytes 1572872 | tf_op jit(solution)/shard_map/ppermute | solution.py:174

commit v14 on v10

--- a/solution.py
+++ b/solution.py
@@ -61,15 +61,13 @@
         for h in range(heads_kv):
             head = slice(h * HEAD_SIZE, (h + 1) * HEAD_SIZE)
             keys = turn(jnp.concatenate([slot_refs[j][0, :, head] for j in use], axis=0),
-                        key_cos_ref[...], key_sin_ref[...])
+                        key_cos_ref[...], key_sin_ref[...]).T
             values = jnp.concatenate([slot_refs[j][1, :, head] for j in use], axis=0)
             for g in range(heads_here):
                 q = h * heads_here + g
                 columns = slice(q * HEAD_SIZE, (q + 1) * HEAD_SIZE)
                 query = turn(query_ref[:, columns], query_cos_ref[...], query_sin_ref[...])
-                scores = lax.dot_general(
-                    query, keys, (((1,), (1,)), ((), ())), preferred_element_type=jnp.float32
-                ) * (1.0 / math.sqrt(HEAD_SIZE))
+                scores = jnp.dot(query, keys, preferred_element_type=jnp.float32) * (1.0 / math.sqrt(HEAD_SIZE))
                 scores = jnp.where(allowed, scores, -1e30)
                 highest = jnp.max(scores, axis=1, keepdims=True)
                 weights = jnp.exp(scores - highest)

time: 63.2 us -> 63.2 us (level)
  no operation moved by 1% of the time
where the time goes in v14:
time: 63.2 us; the launch traced here: 62.8 us
  starting transfers between devices  16.1 us (25%)
  other arithmetic  13.8 us (22%)
  waiting for transfers between devices  13.7 us (22%)
  Pallas kernels  10.8 us (17%)
  matrix products  4.67 us (7%)
  between operations  2.71 us (4%)
  local copies, waits for them, and re-layouts  1.04 us (2%)
    pallas_call x1, Pallas kernels, attend(): pl.pallas_call(functools.partial(attention_kernel, n_slots, uses, heads_k...  10.8 us
    ppermute x5, starting transfers between devices, gather_window(): passed = [lax.ppermute(block, 'ctx', across) for block in [kv] + received]  8.35 us
    ppermute x1, waiting for transfers between devices, on_device(): got = lax.ppermute(peer_terms, 'tp', [(0, 1), (1, 0)])  7.98 us
    ppermute x4, starting transfers between devices, gather_window(): received.append(lax.ppermute(kv, 'ctx', pairs))  6.1 us
    ppermute x4, waiting for transfers between devices, gather_window(): received.append(lax.ppermute(kv, 'ctx', pairs))  5.02 us
    dot_general x1, matrix products, on_device(): jnp.dot(attended, own_weight, preferred_element_type=jnp.float32)  4.67 us
    neg x2, other arithmetic, tables(): -sine  4.57 us
    ppermute x1, starting transfers between devices, on_device(): got = lax.ppermute(peer_terms, 'tp', [(0, 1), (1, 0)])  1.61 us
  transfers between devices with their start and end apart: 10, of which 3 were waited for; matrix products, arithmetic and copies ran while one was open for 26% of the time, Pallas kernels for 0%

profile of v14, /device:TPU:24, one launch (start us, length us, event | category | flops | bytes accessed | tf_op | source)
XLA Modules:
  0.0 62.8 jit_solution(17099722690485005076)
XLA Ops:
  0.0 1.0 %pad_maximum_fusion.2.refs_0_ = bf16[2,128,512]{2,1,0:T(8,128)(2,1)S(1)} fusion(bf16[1,128,512]{2,1,0:T(8,128)(2,1)} %bitcast.12, bf16[1,128,512]{2,1,0:T(8,128)(2,1)} %bitcast.13), kind=kLoop, calls=%fused_computation.8 | loop fusion | flops 131072 | bytes 524288 | tf_op jit(solution)/shard_map/stack | solution.py:146
  1.0 1.3 %collective-permute-start = (bf16[2,128,512]{2,1,0:T(8,128)(2,1)S(1)}, bf16[2,128,512]{2,1,0:T(8,128)(2,1)S(1)}, u32[]{:S(2)}, u32[]{:S(2)}) collective-permute-start(bf16[2,128,512]{2,1,0:T(8,128)(2,1)S(1)} %pad_maximum_fusion.2.refs_0_), channel_id=1, source_target_pairs={{2,4},{6,8},{10,12},{14,16},{18,20},{22,24},{26,28},{3,5},{7,9},{1... | collective-permute-start | bytes 786440 | tf_op jit(solution)/shard_map/ppermute | solution.py:22
  2.3 2.2 %collective-permute-start.1 = (bf16[2,128,512]{2,1,0:T(8,128)(2,1)S(1)}, bf16[2,128,512]{2,1,0:T(8,128)(2,1)S(1)}, u32[]{:S(2)}, u32[]{:S(2)}) collective-permute-start(bf16[2,128,512]{2,1,0:T(8,128)(2,1)S(1)} %pad_maximum_fusion.2.refs_0_), channel_id=1, source_target_pairs={{0,6},{2,8},{4,10},{6,12},{8,14},{10,16},{12,18},{14,20},{16,22},{... | collective-permute-start | bytes 786440 | tf_op jit(solution)/shard_map/ppermute | solution.py:22
  4.5 1.3 %collective-permute-start.2 = (bf16[2,128,512]{2,1,0:T(8,128)(2,1)S(1)}, bf16[2,128,512]{2,1,0:T(8,128)(2,1)S(1)}, u32[]{:S(2)}, u32[]{:S(2)}) collective-permute-start(bf16[2,128,512]{2,1,0:T(8,128)(2,1)S(1)} %pad_maximum_fusion.2.refs_0_), channel_id=1, source_target_pairs={{0,10},{2,12},{4,14},{6,16},{8,18},{10,20},{12,22},{14,24},{16,26}... | collective-permute-start | bytes 786440 | tf_op jit(solution)/shard_map/ppermute | solution.py:22
  5.8 1.3 %collective-permute-start.3 = (bf16[2,128,512]{2,1,0:T(8,128)(2,1)S(1)}, bf16[2,128,512]{2,1,0:T(8,128)(2,1)S(1)}, u32[]{:S(2)}, u32[]{:S(2)}) collective-permute-start(bf16[2,128,512]{2,1,0:T(8,128)(2,1)S(1)} %pad_maximum_fusion.2.refs_0_), channel_id=1, source_target_pairs={{0,14},{2,16},{4,18},{6,20},{8,22},{10,24},{12,26},{14,28},{16,30}... | collective-permute-start | bytes 786440 | tf_op jit(solution)/shard_map/ppermute | solution.py:22
  7.1 1.4 %collective-permute-start.4 = (bf16[2,128,512]{2,1,0:T(8,128)(2,1)S(1)}, bf16[2,128,512]{2,1,0:T(8,128)(2,1)S(1)}, u32[]{:S(2)}, u32[]{:S(2)}) collective-permute-start(bf16[2,128,512]{2,1,0:T(8,128)(2,1)S(1)} %pad_maximum_fusion.2.refs_0_), channel_id=1, source_target_pairs={{0,2},{2,0},{4,6},{6,4},{8,10},{10,8},{12,14},{14,12},{16,18},{18,... | collective-permute-start | bytes 786440 | tf_op jit(solution)/shard_map/ppermute | solution.py:24
  8.5 0.5 multiply_power_fusion
  9.0 0.8 %select_reduce_fusion = s32[8]{0:T(128)S(1)} fusion(s32[8]{0:T(128)} %param.12), kind=kLoop, calls=%fused_computation.20 | loop fusion | flops 184 | bytes 64 | tf_op jit(solution)/shard_map/reduce_sum | solution.py:149
  9.8 0.6 %fusion.11 = s32[]{:T(128)} fusion(s32[8]{0:T(128)S(1)} %select_reduce_fusion, s32[]{:T(128)S(6)} %axis_index.33), kind=kLoop, calls=%fused_computation.27 | loop fusion | flops 23 | bytes 40 | tf_op jit(solution)/shard_map/reduce_sum | solution.py:152
  11.1 0.6 %select_reduce_fusion.3 = s32[]{:T(128)} fusion(s32[8]{0:T(128)S(1)} %select_reduce_fusion, s32[]{:T(128)S(6)} %sub.25), kind=kLoop, calls=%fused_computation.32 | loop fusion | flops 23 | bytes 40 | tf_op jit(solution)/shard_map/reduce_sum | solution.py:154
  12.4 1.3 %fusion.10 = s32[10]{0:T(128)S(1)} fusion(s32[10]{0:T(128)} %constant.46.clone, s32[10]{0:T(128)} %constant.47.clone, pred[]{:T(512)S(6)} %eq.14, s32[]{:T(128)} %select_reduce_fusion.3, s32[]{:T(128)S(6)} %axis_index.33), kind=kLoop, calls=%fused_computation.26 | loop fusion | flops 40 | bytes 129 | tf_op jit(solution)/shard_map/mul | solution.py:160
  13.8 1.3 %select_reduce_fusion.1 = (s32[]{:T(128)}, s32[]{:T(128)}) fusion(s32[8]{0:T(128)} %param.13, s32[]{:T(128)S(6)} %sub.25, s32[8]{0:T(128)} %param.12), kind=kLoop, calls=%fused_computation.30 | loop fusion | flops 38 | bytes 76 | tf_op jit(solution)/shard_map/reduce_sum | solution.py:156
  16.3 3.0 %fusion.5 = (f32[1280,64]{1,0:T(8,128)S(1)}, f32[1280,64]{1,0:T(8,128)S(1)}, f32[1280,64]{1,0:T(8,128)S(1)}) fusion(f32[64]{0:T(128)} %multiply_power_fusion, f32[1280]{0:T(1024)S(1)} %get-tuple-element.15), kind=kLoop, calls=%fused_computation.9 | loop fusion | flops 163840 | bytes 988416 | tf_op jit(solution)/shard_map/neg | solution.py:95
  19.9 1.6 %fusion.6 = (f32[128,64]{1,0:T(8,128)}, f32[128,64]{1,0:T(8,128)}, f32[128,64]{1,0:T(8,128)}) fusion(f32[64]{0:T(128)} %multiply_power_fusion, f32[128]{0:T(128)} %add_convert_fusion.1), kind=kLoop, calls=%fused_computation.15 | loop fusion | flops 16384 | bytes 99072 | tf_op jit(solution)/shard_map/neg | solution.py:95
  21.5 1.0 %pad_maximum_fusion.3 = (f32[128,128]{1,0:T(8,128)S(1)}, f32[128,128]{1,0:T(8,128)S(1)}) fusion(f32[128,64]{1,0:T(8,128)} %get-tuple-element.14, f32[128,64]{1,0:T(8,128)} %get-tuple-element.13, f32[128,64]{1,0:T(8,128)} %get-tuple-element.12), kind=kLoop, calls=%fused_computation.12 | loop fusion | flops 32768 | bytes 229376 | tf_op jit(solution)/shard_map/concatenate | solution.py:95
  23.1 5.0 %collective-permute-done.2.refs_3_ = bf16[2,128,512]{2,1,0:T(8,128)(2,1)S(1)} collective-permute-done((bf16[2,128,512]{2,1,0:T(8,128)(2,1)S(1)}, bf16[2,128,512]{2,1,0:T(8,128)(2,1)S(1)}, u32[]{:S(2)}, u32[]{:S(2)}) %collective-permute-start.2) | collective-permute-done | bytes 262176 | tf_op jit(solution)/shard_map/ppermute | solution.py:22
  28.2 6.4 %collective-permute-start.8 = (bf16[2,128,512]{2,1,0:T(8,128)(2,1)S(1)}, bf16[2,128,512]{2,1,0:T(8,128)(2,1)S(1)}, u32[]{:S(2)}, u32[]{:S(2)}) collective-permute-start(bf16[2,128,512]{2,1,0:T(8,128)(2,1)S(1)} %collective-permute-done.3.refs_4_), channel_id=1, source_target_pairs={{0,2},{2,0},{4,6},{6,4},{8,10},{10,8},{12,14},{14,12},{16,18},{18,... | collective-permute-start | bytes 786440 | tf_op jit(solution)/shard_map/ppermute | solution.py:24
  35.0 0.7 %collective-permute-done.8.refs_9_ = bf16[2,128,512]{2,1,0:T(8,128)(2,1)S(1)} collective-permute-done((bf16[2,128,512]{2,1,0:T(8,128)(2,1)S(1)}, bf16[2,128,512]{2,1,0:T(8,128)(2,1)S(1)}, u32[]{:S(2)}, u32[]{:S(2)}) %collective-permute-start.8) | collective-permute-done | bytes 262176 | tf_op jit(solution)/shard_map/ppermute | solution.py:24
  35.7 1.0 %copy-done = bf16[128,2048]{1,0:T(8,128)(2,1)S(1)} copy-done((bf16[128,2048]{1,0:T(8,128)(2,1)S(1)}, bf16[128,2048]{1,0:T(8,128)(2,1)}, u32[]{:S(2)}) %copy-start) | copy-done | bytes 524312
  36.8 10.8 %shard_map.82 = (bf16[128,2048]{1,0:T(8,128)(2,1)S(1)}, bf16[128,2048]{1,0:T(8,128)(2,1)S(1)}) custom-call(s32[1]{0:T(128)} %bitcast.peer_ref, s32[1]{0:T(128)} %bitcast.1.core_ref, s32[128,1]{1,0:T(8,128)S(1)} %iota_add_fusion.query_pos_ref, s32[1,1280]{1,0:T(1,128)S(1)} %and_select_fusion.key_limit_ref, f32[128,128]{1,0:T(8,128)S(1)} %get-tuple-element.19.query_cos_ref, ...), custom_call_target="tpu_custom_call" | custom-call | flops 2415919104 | bytes 12582912 | tf_op jit(solution)/shard_map/pallas_call | solution.py:125
  47.6 1.6 %collective-permute-start.9 = (bf16[128,2048]{1,0:T(8,128)(2,1)S(1)}, bf16[128,2048]{1,0:T(8,128)(2,1)S(1)}, u32[]{:S(2)}, u32[]{:S(2)}) collective-permute-start(bf16[128,2048]{1,0:T(8,128)(2,1)S(1)} %get-tuple-element.8), channel_id=1, source_target_pairs={{0,1},{1,0},{2,3},{3,2},{4,5},{5,4},{6,7},{7,6},{8,9},{9,8},{10,11... | collective-permute-start | bytes 1572872 | tf_op jit(solution)/shard_map/ppermute | solution.py:172
  49.2 4.7 %fusion.2 = bf16[128,2048]{1,0:T(8,128)(2,1)S(1)} fusion(bf16[128,2048]{1,0:T(8,128)(2,1)S(1)} %get-tuple-element.7, bf16[2048,4096]{1,0:T(8,128)(2,1)} %refs_10_.1, s32[]{:T(128)S(6)} %select_n.53), kind=kOutput, calls=%fused_computation.2 | convolution fusion | flops 1074003968 | bytes 9437188 | tf_op jit(solution)/shard_map/dot_general | solution.py:175
  53.9 8.0 %collective-permute-done.9 = bf16[128,2048]{1,0:T(8,128)(2,1)S(1)} collective-permute-done((bf16[128,2048]{1,0:T(8,128)(2,1)S(1)}, bf16[128,2048]{1,0:T(8,128)(2,1)S(1)}, u32[]{:S(2)}, u32[]{:S(2)}) %collective-permute-start.9) | collective-permute-done | bytes 524320 | tf_op jit(solution)/shard_map/ppermute | solution.py:172
  61.9 0.9 %add_convert_fusion = bf16[128,2048]{1,0:T(8,128)(2,1)} fusion(bf16[128,2048]{1,0:T(8,128)(2,1)S(1)} %collective-permute-done.9, bf16[128,2048]{1,0:T(8,128)(2,1)S(1)} %fusion.2), kind=kLoop, calls=%fused_computation.3 | loop fusion | flops 1048576 | bytes 1572864 | tf_op jit(solution)/shard_map/convert_element_type | solution.py:177
  (16 shorter events, 1.6 us)
Async XLA Ops:
  1.0 21.6 %collective-permute-start = (bf16[2,128,512]{2,1,0:T(8,128)(2,1)S(1)}, bf16[2,128,512]{2,1,0:T(8,128)(2,1)S(1)}, u32[]{:S(2)}, u32[]{:S(2)}) collective-permute-start(bf16[2,128,512]{2,1,0:T(8,128)(2,1)S(1)} %pad_maximum_fusion.2.refs_0_), channel_id=1, source_target_pairs={{2,4},{6,8},{10,12},{14,16},{18,20},{22,24},{26,28},{3,5},{7,9},{1... | collective-permute-start | bytes 786440 | tf_op jit(solution)/shard_map/ppermute | solution.py:22
  2.3 20.4 %collective-permute-start.1 = (bf16[2,128,512]{2,1,0:T(8,128)(2,1)S(1)}, bf16[2,128,512]{2,1,0:T(8,128)(2,1)S(1)}, u32[]{:S(2)}, u32[]{:S(2)}) collective-permute-start(bf16[2,128,512]{2,1,0:T(8,128)(2,1)S(1)} %pad_maximum_fusion.2.refs_0_), channel_id=1, source_target_pairs={{0,6},{2,8},{4,10},{6,12},{8,14},{10,16},{12,18},{14,20},{16,22},{... | collective-permute-start | bytes 786440 | tf_op jit(solution)/shard_map/ppermute | solution.py:22
  4.5 23.6 %collective-permute-start.2 = (bf16[2,128,512]{2,1,0:T(8,128)(2,1)S(1)}, bf16[2,128,512]{2,1,0:T(8,128)(2,1)S(1)}, u32[]{:S(2)}, u32[]{:S(2)}) collective-permute-start(bf16[2,128,512]{2,1,0:T(8,128)(2,1)S(1)} %pad_maximum_fusion.2.refs_0_), channel_id=1, source_target_pairs={{0,10},{2,12},{4,14},{6,16},{8,18},{10,20},{12,22},{14,24},{16,26}... | collective-permute-start | bytes 786440 | tf_op jit(solution)/shard_map/ppermute | solution.py:22
  5.8 22.3 %collective-permute-start.3 = (bf16[2,128,512]{2,1,0:T(8,128)(2,1)S(1)}, bf16[2,128,512]{2,1,0:T(8,128)(2,1)S(1)}, u32[]{:S(2)}, u32[]{:S(2)}) collective-permute-start(bf16[2,128,512]{2,1,0:T(8,128)(2,1)S(1)} %pad_maximum_fusion.2.refs_0_), channel_id=1, source_target_pairs={{0,14},{2,16},{4,18},{6,20},{8,22},{10,24},{12,26},{14,28},{16,30}... | collective-permute-start | bytes 786440 | tf_op jit(solution)/shard_map/ppermute | solution.py:22
  7.1 27.9 %collective-permute-start.4 = (bf16[2,128,512]{2,1,0:T(8,128)(2,1)S(1)}, bf16[2,128,512]{2,1,0:T(8,128)(2,1)S(1)}, u32[]{:S(2)}, u32[]{:S(2)}) collective-permute-start(bf16[2,128,512]{2,1,0:T(8,128)(2,1)S(1)} %pad_maximum_fusion.2.refs_0_), channel_id=1, source_target_pairs={{0,2},{2,0},{4,6},{6,4},{8,10},{10,8},{12,14},{14,12},{16,18},{18,... | collective-permute-start | bytes 786440 | tf_op jit(solution)/shard_map/ppermute | solution.py:24
  22.6 12.4 %collective-permute-start.5 = (bf16[2,128,512]{2,1,0:T(8,128)(2,1)S(1)}, bf16[2,128,512]{2,1,0:T(8,128)(2,1)S(1)}, u32[]{:S(2)}, u32[]{:S(2)}) collective-permute-start(bf16[2,128,512]{2,1,0:T(8,128)(2,1)S(1)} %collective-permute-done.refs_1_), channel_id=1, source_target_pairs={{0,2},{2,0},{4,6},{6,4},{8,10},{10,8},{12,14},{14,12},{16,18},{18,... | collective-permute-start | bytes 786440 | tf_op jit(solution)/shard_map/ppermute | solution.py:24
  22.7 12.3 %collective-permute-start.6 = (bf16[2,128,512]{2,1,0:T(8,128)(2,1)S(1)}, bf16[2,128,512]{2,1,0:T(8,128)(2,1)S(1)}, u32[]{:S(2)}, u32[]{:S(2)}) collective-permute-start(bf16[2,128,512]{2,1,0:T(8,128)(2,1)S(1)} %collective-permute-done.1.refs_2_), channel_id=1, source_target_pairs={{0,2},{2,0},{4,6},{6,4},{8,10},{10,8},{12,14},{14,12},{16,18},{18,... | collective-permute-start | bytes 786440 | tf_op jit(solution)/shard_map/ppermute | solution.py:24
  28.2 6.9 %collective-permute-start.7 = (bf16[2,128,512]{2,1,0:T(8,128)(2,1)S(1)}, bf16[2,128,512]{2,1,0:T(8,128)(2,1)S(1)}, u32[]{:S(2)}, u32[]{:S(2)}) collective-permute-start(bf16[2,128,512]{2,1,0:T(8,128)(2,1)S(1)} %collective-permute-done.2.refs_3_), channel_id=1, source_target_pairs={{0,2},{2,0},{4,6},{6,4},{8,10},{10,8},{12,14},{14,12},{16,18},{18,... | collective-permute-start | bytes 786440 | tf_op jit(solution)/shard_map/ppermute | solution.py:24
  28.2 7.6 %collective-permute-start.8 = (bf16[2,128,512]{2,1,0:T(8,128)(2,1)S(1)}, bf16[2,128,512]{2,1,0:T(8,128)(2,1)S(1)}, u32[]{:S(2)}, u32[]{:S(2)}) collective-permute-start(bf16[2,128,512]{2,1,0:T(8,128)(2,1)S(1)} %collective-permute-done.3.refs_4_), channel_id=1, source_target_pairs={{0,2},{2,0},{4,6},{6,4},{8,10},{10,8},{12,14},{14,12},{16,18},{18,... | collective-permute-start | bytes 786440 | tf_op jit(solution)/shard_map/ppermute | solution.py:24
  35.7 1.0 %copy-start = (bf16[128,2048]{1,0:T(8,128)(2,1)S(1)}, bf16[128,2048]{1,0:T(8,128)(2,1)}, u32[]{:S(2)}) copy-start(bf16[128,2048]{1,0:T(8,128)(2,1)} %query_ref.1) | copy-start | bytes 1572868
  47.6 14.3 %collective-permute-start.9 = (bf16[128,2048]{1,0:T(8,128)(2,1)S(1)}, bf16[128,2048]{1,0:T(8,128)(2,1)S(1)}, u32[]{:S(2)}, u32[]{:S(2)}) collective-permute-start(bf16[128,2048]{1,0:T(8,128)(2,1)S(1)} %get-tuple-element.8), channel_id=1, source_target_pairs={{0,1},{1,0},{2,3},{3,2},{4,5},{5,4},{6,7},{7,6},{8,9},{9,8},{10,11... | collective-permute-start | bytes 1572872 | tf_op jit(solution)/shard_map/ppermute | solution.py:172

commit v15 on v10

--- a/solution.py
+++ b/solution.py
@@ -13,18 +13,18 @@
 
 
 def gather_window(kv, n, window):
+    half = window // 2
     received = []
     for s in range(1, window, 2):
-        if s == 1:
-            pairs = [(j, j + 1) for j in range(1, n - 1, 2)]
-        else:
-            pairs = [(j, j + s) for j in range(n - s)]
-        received.append(lax.ppermute(kv, "ctx", pairs))
-    across = [(j, j ^ 1) for j in range(n)]
-    passed = [lax.ppermute(block, "ctx", across) for block in [kv] + received]
-    half = window // 2
-    even_shift = [0] + [2 * m + 1 for m in range(half)] + [FAR, FAR] + [2 * m for m in range(1, half)]
-    odd_shift = [0, FAR] + [2 * m + 1 for m in range(1, half)] + [1] + [2 * m + 2 for m in range(half)]
+        received.append(lax.ppermute(kv, "ctx", [(j, j + s) for j in range(n - s)]))
+    up = [(j, j + 1) for j in range(0, n, 2)]
+    down = [(j + 1, j) for j in range(0, n, 2)]
+    passed = []
+    for m, block in enumerate(received):
+        pairs = (up if m < half - 1 else []) + (down if m > 0 else [])
+        passed.append(lax.ppermute(block, "ctx", pairs))
+    even_shift = [0] + [2 * m + 1 for m in range(half)] + [FAR] + [2 * m for m in range(1, half)]
+    odd_shift = [0] + [2 * m + 1 for m in range(half)] + [2 * m + 2 for m in range(half - 1)] + [FAR]
     core = lax.axis_index("ctx") % 2
     shift = jnp.where(core == 0, jnp.array(even_shift, jnp.int32), jnp.array(odd_shift, jnp.int32))
     return [kv] + received + passed, shift

time: 63.2 us -> 63.8 us (level)
  waiting for transfers between devices: 13.7 us -> 22.3 us
  other arithmetic: 13.8 us -> 9.63 us
  starting transfers between devices: 16.1 us -> 12.4 us
    ppermute x9 -> x8, waiting for transfers between devices: 5.74 us -> 14.6 us  [the longest x4 7.74 us: gather_window(): received.append(lax.ppermute(kv, 'ctx', [(j, j + s) for j in range(n - s)]))]
    ppermute x9 -> x8, starting transfers between devices: 14.4 us -> 10.9 us  [the longest x4 6.72 us: gather_window(): received.append(lax.ppermute(kv, 'ctx', [(j, j + s) for j in range(n - s)]))]
    neg x2, other arithmetic: 4.57 us -> 2.44 us  [tables(): -sine]
    concatenate x2, other arithmetic: 1.44 us -> 0.47 us  [tables(): jnp.concatenate([cosine, cosine], axis=1)]
  transfers between devices with their start and end apart: 10 -> 9, of which waited for: 3 -> 3; matrix products, arithmetic and copies ran while one was open for 26% -> 20% of each run, Pallas kernels for 0% -> 0%
where the time goes in v15:
time: 63.8 us; the launch traced here: 63.4 us
  waiting for transfers between devices  22.3 us (35%)
  starting transfers between devices  12.4 us (19%)
  Pallas kernels  10.6 us (17%)
  other arithmetic  9.63 us (15%)
  matrix products  4.67 us (7%)
  between operations  2.78 us (4%)
  local copies, waits for them, and re-layouts  1.04 us (2%)
    pallas_call x1, Pallas kernels, attend(): pl.pallas_call(functools.partial(attention_kernel, n_slots, uses, heads_k...  10.6 us
    ppermute x1, waiting for transfers between devices, on_device(): got = lax.ppermute(peer_terms, 'tp', [(0, 1), (1, 0)])  7.76 us
    ppermute x4, waiting for transfers between devices, gather_window(): received.append(lax.ppermute(kv, 'ctx', [(j, j + s) for j in range(n - s)]))  7.74 us
    ppermute x4, waiting for transfers between devices, gather_window(): passed.append(lax.ppermute(block, 'ctx', pairs))  6.81 us
    ppermute x4, starting transfers between devices, gather_window(): received.append(lax.ppermute(kv, 'ctx', [(j, j + s) for j in range(n - s)]))  6.72 us
    dot_general x1, matrix products, on_device(): jnp.dot(attended, own_weight, preferred_element_type=jnp.float32)  4.67 us
    ppermute x4, starting transfers between devices, gather_window(): passed.append(lax.ppermute(block, 'ctx', pairs))  4.14 us
    neg x2, other arithmetic, tables(): -sine  2.44 us
  transfers between devices with their start and end apart: 9, of which 3 were waited for; matrix products, arithmetic and copies ran while one was open for 20% of the time, Pallas kernels for 0%

profile of v15, /device:TPU:24, one launch (start us, length us, event | category | flops | bytes accessed | tf_op | source)
XLA Modules:
  0.0 63.4 jit_solution(9818856851517161093)
XLA Ops:
  0.0 1.0 %pad_maximum_fusion.2.refs_0_ = bf16[2,128,512]{2,1,0:T(8,128)(2,1)S(1)} fusion(bf16[1,128,512]{2,1,0:T(8,128)(2,1)} %bitcast.12, bf16[1,128,512]{2,1,0:T(8,128)(2,1)} %bitcast.13), kind=kLoop, calls=%fused_computation.8 | loop fusion | flops 131072 | bytes 524288 | tf_op jit(solution)/shard_map/stack | solution.py:148
  1.0 1.9 %collective-permute-start = (bf16[2,128,512]{2,1,0:T(8,128)(2,1)S(1)}, bf16[2,128,512]{2,1,0:T(8,128)(2,1)S(1)}, u32[]{:S(2)}, u32[]{:S(2)}) collective-permute-start(bf16[2,128,512]{2,1,0:T(8,128)(2,1)S(1)} %pad_maximum_fusion.2.refs_0_), channel_id=1, source_target_pairs={{0,2},{2,4},{4,6},{6,8},{8,10},{10,12},{12,14},{14,16},{16,18},{18... | collective-permute-start | bytes 786440 | tf_op jit(solution)/shard_map/ppermute | solution.py:19
  2.9 2.2 %collective-permute-start.1 = (bf16[2,128,512]{2,1,0:T(8,128)(2,1)S(1)}, bf16[2,128,512]{2,1,0:T(8,128)(2,1)S(1)}, u32[]{:S(2)}, u32[]{:S(2)}) collective-permute-start(bf16[2,128,512]{2,1,0:T(8,128)(2,1)S(1)} %pad_maximum_fusion.2.refs_0_), channel_id=1, source_target_pairs={{0,6},{2,8},{4,10},{6,12},{8,14},{10,16},{12,18},{14,20},{16,22},{... | collective-permute-start | bytes 786440 | tf_op jit(solution)/shard_map/ppermute | solution.py:19
  5.1 1.3 %collective-permute-start.2 = (bf16[2,128,512]{2,1,0:T(8,128)(2,1)S(1)}, bf16[2,128,512]{2,1,0:T(8,128)(2,1)S(1)}, u32[]{:S(2)}, u32[]{:S(2)}) collective-permute-start(bf16[2,128,512]{2,1,0:T(8,128)(2,1)S(1)} %pad_maximum_fusion.2.refs_0_), channel_id=1, source_target_pairs={{0,10},{2,12},{4,14},{6,16},{8,18},{10,20},{12,22},{14,24},{16,26}... | collective-permute-start | bytes 786440 | tf_op jit(solution)/shard_map/ppermute | solution.py:19
  6.4 1.3 %collective-permute-start.3 = (bf16[2,128,512]{2,1,0:T(8,128)(2,1)S(1)}, bf16[2,128,512]{2,1,0:T(8,128)(2,1)S(1)}, u32[]{:S(2)}, u32[]{:S(2)}) collective-permute-start(bf16[2,128,512]{2,1,0:T(8,128)(2,1)S(1)} %pad_maximum_fusion.2.refs_0_), channel_id=1, source_target_pairs={{0,14},{2,16},{4,18},{6,20},{8,22},{10,24},{12,26},{14,28},{16,30}... | collective-permute-start | bytes 786440 | tf_op jit(solution)/shard_map/ppermute | solution.py:19
  7.8 0.8 %select_reduce_fusion = s32[8]{0:T(128)S(1)} fusion(s32[8]{0:T(128)} %param.12), kind=kLoop, calls=%fused_computation.20 | loop fusion | flops 184 | bytes 64 | tf_op jit(solution)/shard_map/reduce_sum | solution.py:151
  8.6 0.6 %fusion.11 = s32[]{:T(128)} fusion(s32[8]{0:T(128)S(1)} %select_reduce_fusion, s32[]{:T(128)S(6)} %axis_index.33), kind=kLoop, calls=%fused_computation.27 | loop fusion | flops 23 | bytes 40 | tf_op jit(solution)/shard_map/reduce_sum | solution.py:154
  9.8 0.6 select_reduce_fusion.3
  11.1 1.3 %fusion.10 = s32[9]{0:T(128)S(1)} fusion(s32[9]{0:T(128)} %constant.46.clone, s32[9]{0:T(128)} %constant.47.clone, pred[]{:T(512)S(6)} %eq.14, s32[]{:T(128)} %select_reduce_fusion.3, s32[]{:T(128)S(6)} %axis_index.33), kind=kLoop, calls=%fused_computation.26 | loop fusion | flops 36 | bytes 117 | tf_op jit(solution)/shard_map/mul | solution.py:162
  12.5 1.3 %select_reduce_fusion.1 = (s32[]{:T(128)}, s32[]{:T(128)}) fusion(s32[8]{0:T(128)} %param.13, s32[]{:T(128)S(6)} %sub.25, s32[8]{0:T(128)} %param.12), kind=kLoop, calls=%fused_computation.30 | loop fusion | flops 38 | bytes 76 | tf_op jit(solution)/shard_map/reduce_sum | solution.py:158
  14.5 2.1 %fusion.5 = (f32[1152,64]{1,0:T(8,128)S(1)}, f32[1152,64]{1,0:T(8,128)S(1)}, f32[1152,64]{1,0:T(8,128)S(1)}) fusion(f32[64]{0:T(128)S(1)} %multiply_power_fusion, f32[1152]{0:T(1024)S(1)} %get-tuple-element.15), kind=kLoop, calls=%fused_computation.9 | loop fusion | flops 147456 | bytes 889600 | tf_op jit(solution)/shard_map/neg | solution.py:97
  17.3 0.3 fusion.6
  17.6 0.1 pad_maximum_fusion.3
  17.7 2.6 %collective-permute-start.4 = (bf16[2,128,512]{2,1,0:T(8,128)(2,1)S(1)}, bf16[2,128,512]{2,1,0:T(8,128)(2,1)S(1)}, u32[]{:S(2)}, u32[]{:S(2)}) collective-permute-start(bf16[2,128,512]{2,1,0:T(8,128)(2,1)S(1)} %collective-permute-done.refs_1_), channel_id=1, source_target_pairs={{0,2},{4,6},{8,10},{12,14},{16,18},{20,22},{24,26},{28,30},{1,3},{... | collective-permute-start | bytes 786440 | tf_op jit(solution)/shard_map/ppermute | solution.py:25
  20.4 7.7 %collective-permute-done.2.refs_3_ = bf16[2,128,512]{2,1,0:T(8,128)(2,1)S(1)} collective-permute-done((bf16[2,128,512]{2,1,0:T(8,128)(2,1)S(1)}, bf16[2,128,512]{2,1,0:T(8,128)(2,1)S(1)}, u32[]{:S(2)}, u32[]{:S(2)}) %collective-permute-start.2) | collective-permute-done | bytes 262176 | tf_op jit(solution)/shard_map/ppermute | solution.py:19
  28.2 1.5 %collective-permute-start.7 = (bf16[2,128,512]{2,1,0:T(8,128)(2,1)S(1)}, bf16[2,128,512]{2,1,0:T(8,128)(2,1)S(1)}, u32[]{:S(2)}, u32[]{:S(2)}) collective-permute-start(bf16[2,128,512]{2,1,0:T(8,128)(2,1)S(1)} %collective-permute-done.3.refs_4_), channel_id=1, source_target_pairs={{2,0},{6,4},{10,8},{14,12},{18,16},{22,20},{26,24},{30,28},{3,1},{... | collective-permute-start | bytes 786440 | tf_op jit(solution)/shard_map/ppermute | solution.py:25
  29.7 0.4 pad_maximum_fusion
  30.1 6.8 %collective-permute-done.7.refs_8_ = bf16[2,128,512]{2,1,0:T(8,128)(2,1)S(1)} collective-permute-done((bf16[2,128,512]{2,1,0:T(8,128)(2,1)S(1)}, bf16[2,128,512]{2,1,0:T(8,128)(2,1)S(1)}, u32[]{:S(2)}, u32[]{:S(2)}) %collective-permute-start.7) | collective-permute-done | bytes 262176 | tf_op jit(solution)/shard_map/ppermute | solution.py:25
  36.9 1.0 %copy-done = bf16[128,2048]{1,0:T(8,128)(2,1)S(1)} copy-done((bf16[128,2048]{1,0:T(8,128)(2,1)S(1)}, bf16[128,2048]{1,0:T(8,128)(2,1)}, u32[]{:S(2)}) %copy-start) | copy-done | bytes 524312
  37.9 10.6 %shard_map.82 = (bf16[128,2048]{1,0:T(8,128)(2,1)S(1)}, bf16[128,2048]{1,0:T(8,128)(2,1)S(1)}) custom-call(s32[1]{0:T(128)} %bitcast.peer_ref, s32[1]{0:T(128)} %bitcast.1.core_ref, s32[128,1]{1,0:T(8,128)S(1)} %iota_add_fusion.query_pos_ref, s32[1,1152]{1,0:T(1,128)S(1)} %and_select_fusion.key_limit_ref, f32[128,128]{1,0:T(8,128)S(1)} %get-tuple-element.19.query_cos_ref, ...), custom_call_target="tpu_custom_call" | custom-call | flops 2281701376 | bytes 12320768 | tf_op jit(solution)/shard_map/pallas_call | solution.py:127
  48.5 1.6 %collective-permute-start.8 = (bf16[128,2048]{1,0:T(8,128)(2,1)S(1)}, bf16[128,2048]{1,0:T(8,128)(2,1)S(1)}, u32[]{:S(2)}, u32[]{:S(2)}) collective-permute-start(bf16[128,2048]{1,0:T(8,128)(2,1)S(1)} %get-tuple-element.8), channel_id=1, source_target_pairs={{0,1},{1,0},{2,3},{3,2},{4,5},{5,4},{6,7},{7,6},{8,9},{9,8},{10,11... | collective-permute-start | bytes 1572872 | tf_op jit(solution)/shard_map/ppermute | solution.py:174
  50.1 4.7 %fusion.2 = bf16[128,2048]{1,0:T(8,128)(2,1)S(1)} fusion(bf16[128,2048]{1,0:T(8,128)(2,1)S(1)} %get-tuple-element.7, bf16[2048,4096]{1,0:T(8,128)(2,1)} %refs_9_.1, s32[]{:T(128)S(6)} %select_n.53), kind=kOutput, calls=%fused_computation.2 | convolution fusion | flops 1074003968 | bytes 9437188 | tf_op jit(solution)/shard_map/dot_general | solution.py:177
  54.7 7.8 %collective-permute-done.8 = bf16[128,2048]{1,0:T(8,128)(2,1)S(1)} collective-permute-done((bf16[128,2048]{1,0:T(8,128)(2,1)S(1)}, bf16[128,2048]{1,0:T(8,128)(2,1)S(1)}, u32[]{:S(2)}, u32[]{:S(2)}) %collective-permute-start.8) | collective-permute-done | bytes 524320 | tf_op jit(solution)/shard_map/ppermute | solution.py:174
  62.5 0.9 %add_convert_fusion = bf16[128,2048]{1,0:T(8,128)(2,1)} fusion(bf16[128,2048]{1,0:T(8,128)(2,1)S(1)} %collective-permute-done.8, bf16[128,2048]{1,0:T(8,128)(2,1)S(1)} %fusion.2), kind=kLoop, calls=%fused_computation.3 | loop fusion | flops 1048576 | bytes 1572864 | tf_op jit(solution)/shard_map/convert_element_type | solution.py:179
  (14 shorter events, 0.2 us)
Async XLA Ops:
  1.0 16.7 %collective-permute-start = (bf16[2,128,512]{2,1,0:T(8,128)(2,1)S(1)}, bf16[2,128,512]{2,1,0:T(8,128)(2,1)S(1)}, u32[]{:S(2)}, u32[]{:S(2)}) collective-permute-start(bf16[2,128,512]{2,1,0:T(8,128)(2,1)S(1)} %pad_maximum_fusion.2.refs_0_), channel_id=1, source_target_pairs={{0,2},{2,4},{4,6},{6,8},{8,10},{10,12},{12,14},{14,16},{16,18},{18... | collective-permute-start | bytes 786440 | tf_op jit(solution)/shard_map/ppermute | solution.py:19
  2.9 17.4 %collective-permute-start.1 = (bf16[2,128,512]{2,1,0:T(8,128)(2,1)S(1)}, bf16[2,128,512]{2,1,0:T(8,128)(2,1)S(1)}, u32[]{:S(2)}, u32[]{:S(2)}) collective-permute-start(bf16[2,128,512]{2,1,0:T(8,128)(2,1)S(1)} %pad_maximum_fusion.2.refs_0_), channel_id=1, source_target_pairs={{0,6},{2,8},{4,10},{6,12},{8,14},{10,16},{12,18},{14,20},{16,22},{... | collective-permute-start | bytes 786440 | tf_op jit(solution)/shard_map/ppermute | solution.py:19
  5.1 23.0 %collective-permute-start.2 = (bf16[2,128,512]{2,1,0:T(8,128)(2,1)S(1)}, bf16[2,128,512]{2,1,0:T(8,128)(2,1)S(1)}, u32[]{:S(2)}, u32[]{:S(2)}) collective-permute-start(bf16[2,128,512]{2,1,0:T(8,128)(2,1)S(1)} %pad_maximum_fusion.2.refs_0_), channel_id=1, source_target_pairs={{0,10},{2,12},{4,14},{6,16},{8,18},{10,20},{12,22},{14,24},{16,26}... | collective-permute-start | bytes 786440 | tf_op jit(solution)/shard_map/ppermute | solution.py:19
  6.4 21.7 %collective-permute-start.3 = (bf16[2,128,512]{2,1,0:T(8,128)(2,1)S(1)}, bf16[2,128,512]{2,1,0:T(8,128)(2,1)S(1)}, u32[]{:S(2)}, u32[]{:S(2)}) collective-permute-start(bf16[2,128,512]{2,1,0:T(8,128)(2,1)S(1)} %pad_maximum_fusion.2.refs_0_), channel_id=1, source_target_pairs={{0,14},{2,16},{4,18},{6,20},{8,22},{10,24},{12,26},{14,28},{16,30}... | collective-permute-start | bytes 786440 | tf_op jit(solution)/shard_map/ppermute | solution.py:19
  17.7 12.3 %collective-permute-start.4 = (bf16[2,128,512]{2,1,0:T(8,128)(2,1)S(1)}, bf16[2,128,512]{2,1,0:T(8,128)(2,1)S(1)}, u32[]{:S(2)}, u32[]{:S(2)}) collective-permute-start(bf16[2,128,512]{2,1,0:T(8,128)(2,1)S(1)} %collective-permute-done.refs_1_), channel_id=1, source_target_pairs={{0,2},{4,6},{8,10},{12,14},{16,18},{20,22},{24,26},{28,30},{1,3},{... | collective-permute-start | bytes 786440 | tf_op jit(solution)/shard_map/ppermute | solution.py:25
  20.4 9.7 %collective-permute-start.5 = (bf16[2,128,512]{2,1,0:T(8,128)(2,1)S(1)}, bf16[2,128,512]{2,1,0:T(8,128)(2,1)S(1)}, u32[]{:S(2)}, u32[]{:S(2)}) collective-permute-start(bf16[2,128,512]{2,1,0:T(8,128)(2,1)S(1)} %collective-permute-done.1.refs_2_), channel_id=1, source_target_pairs={{0,2},{4,6},{8,10},{12,14},{16,18},{20,22},{24,26},{28,30},{2,0},{... | collective-permute-start | bytes 786440 | tf_op jit(solution)/shard_map/ppermute | solution.py:25
  28.2 1.9 %collective-permute-start.6 = (bf16[2,128,512]{2,1,0:T(8,128)(2,1)S(1)}, bf16[2,128,512]{2,1,0:T(8,128)(2,1)S(1)}, u32[]{:S(2)}, u32[]{:S(2)}) collective-permute-start(bf16[2,128,512]{2,1,0:T(8,128)(2,1)S(1)} %collective-permute-done.2.refs_3_), channel_id=1, source_target_pairs={{0,2},{4,6},{8,10},{12,14},{16,18},{20,22},{24,26},{28,30},{2,0},{... | collective-permute-start | bytes 786440 | tf_op jit(solution)/shard_map/ppermute | solution.py:25
  28.2 8.7 %collective-permute-start.7 = (bf16[2,128,512]{2,1,0:T(8,128)(2,1)S(1)}, bf16[2,128,512]{2,1,0:T(8,128)(2,1)S(1)}, u32[]{:S(2)}, u32[]{:S(2)}) collective-permute-start(bf16[2,128,512]{2,1,0:T(8,128)(2,1)S(1)} %collective-permute-done.3.refs_4_), channel_id=1, source_target_pairs={{2,0},{6,4},{10,8},{14,12},{18,16},{22,20},{26,24},{30,28},{3,1},{... | collective-permute-start | bytes 786440 | tf_op jit(solution)/shard_map/ppermute | solution.py:25
  36.9 1.0 %copy-start = (bf16[128,2048]{1,0:T(8,128)(2,1)S(1)}, bf16[128,2048]{1,0:T(8,128)(2,1)}, u32[]{:S(2)}) copy-start(bf16[128,2048]{1,0:T(8,128)(2,1)} %query_ref.1) | copy-start | bytes 1572868
  48.5 14.0 %collective-permute-start.8 = (bf16[128,2048]{1,0:T(8,128)(2,1)S(1)}, bf16[128,2048]{1,0:T(8,128)(2,1)S(1)}, u32[]{:S(2)}, u32[]{:S(2)}) collective-permute-start(bf16[128,2048]{1,0:T(8,128)(2,1)S(1)} %get-tuple-element.8), channel_id=1, source_target_pairs={{0,1},{1,0},{2,3},{3,2},{4,5},{5,4},{6,7},{7,6},{8,9},{9,8},{10,11... | collective-permute-start | bytes 1572872 | tf_op jit(solution)/shard_map/ppermute | solution.py:174

commit v16 on v15

--- a/solution.py
+++ b/solution.py
@@ -21,7 +21,7 @@
     down = [(j + 1, j) for j in range(0, n, 2)]
     passed = []
     for m, block in enumerate(received):
-        pairs = (up if m < half - 1 else []) + (down if m > 0 else [])
+        pairs = up + (down if m > 0 else [])
         passed.append(lax.ppermute(block, "ctx", pairs))
     even_shift = [0] + [2 * m + 1 for m in range(half)] + [FAR] + [2 * m for m in range(1, half)]
     odd_shift = [0] + [2 * m + 1 for m in range(half)] + [2 * m + 2 for m in range(half - 1)] + [FAR]

time: 63.8 us -> 62.9 us (0.986)
  waiting for transfers between devices: 22.3 us -> 16.3 us
  starting transfers between devices: 12.4 us -> 17.6 us
    ppermute x4, waiting for transfers between devices: 6.81 us -> 0.76 us  [gather_window(): passed.append(lax.ppermute(block, 'ctx', pairs))]
    ppermute x4, starting transfers between devices: 4.14 us -> 9.25 us  [gather_window(): passed.append(lax.ppermute(block, 'ctx', pairs))]
where the time goes in v16:
time: 62.9 us; the launch traced here: 62.6 us
  starting transfers between devices  17.6 us (28%)
  waiting for transfers between devices  16.3 us (26%)
  Pallas kernels  10.6 us (17%)
  other arithmetic  9.63 us (15%)
  matrix products  4.67 us (7%)
  between operations  2.77 us (4%)
  local copies, waits for them, and re-layouts  1.04 us (2%)
    pallas_call x1, Pallas kernels, attend(): pl.pallas_call(functools.partial(attention_kernel, n_slots, uses, heads_k...  10.6 us
    ppermute x4, starting transfers between devices, gather_window(): passed.append(lax.ppermute(block, 'ctx', pairs))  9.25 us
    ppermute x1, waiting for transfers between devices, on_device(): got = lax.ppermute(peer_terms, 'tp', [(0, 1), (1, 0)])  7.99 us
    ppermute x4, waiting for transfers between devices, gather_window(): received.append(lax.ppermute(kv, 'ctx', [(j, j + s) for j in range(n - s)]))  7.56 us
    ppermute x4, starting transfers between devices, gather_window(): received.append(lax.ppermute(kv, 'ctx', [(j, j + s) for j in range(n - s)]))  6.72 us
    dot_general x1, matrix products, on_device(): jnp.dot(attended, own_weight, preferred_element_type=jnp.float32)  4.67 us
    neg x2, other arithmetic, tables(): -sine  2.44 us
    ppermute x1, starting transfers between devices, on_device(): got = lax.ppermute(peer_terms, 'tp', [(0, 1), (1, 0)])  1.62 us
  transfers between devices with their start and end apart: 9, of which 3 were waited for; matrix products, arithmetic and copies ran while one was open for 20% of the time, Pallas kernels for 0%

profile of v16, /device:TPU:24, one launch (start us, length us, event | category | flops | bytes accessed | tf_op | source)
XLA Modules:
  0.0 62.6 jit_solution(17057775164225399328)
XLA Ops:
  0.0 1.0 %pad_maximum_fusion.2.refs_0_ = bf16[2,128,512]{2,1,0:T(8,128)(2,1)S(1)} fusion(bf16[1,128,512]{2,1,0:T(8,128)(2,1)} %bitcast.12, bf16[1,128,512]{2,1,0:T(8,128)(2,1)} %bitcast.13), kind=kLoop, calls=%fused_computation.8 | loop fusion | flops 131072 | bytes 524288 | tf_op jit(solution)/shard_map/stack | solution.py:148
  1.0 1.9 %collective-permute-start = (bf16[2,128,512]{2,1,0:T(8,128)(2,1)S(1)}, bf16[2,128,512]{2,1,0:T(8,128)(2,1)S(1)}, u32[]{:S(2)}, u32[]{:S(2)}) collective-permute-start(bf16[2,128,512]{2,1,0:T(8,128)(2,1)S(1)} %pad_maximum_fusion.2.refs_0_), channel_id=1, source_target_pairs={{0,2},{2,4},{4,6},{6,8},{8,10},{10,12},{12,14},{14,16},{16,18},{18... | collective-permute-start | bytes 786440 | tf_op jit(solution)/shard_map/ppermute | solution.py:19
  2.9 2.2 %collective-permute-start.1 = (bf16[2,128,512]{2,1,0:T(8,128)(2,1)S(1)}, bf16[2,128,512]{2,1,0:T(8,128)(2,1)S(1)}, u32[]{:S(2)}, u32[]{:S(2)}) collective-permute-start(bf16[2,128,512]{2,1,0:T(8,128)(2,1)S(1)} %pad_maximum_fusion.2.refs_0_), channel_id=1, source_target_pairs={{0,6},{2,8},{4,10},{6,12},{8,14},{10,16},{12,18},{14,20},{16,22},{... | collective-permute-start | bytes 786440 | tf_op jit(solution)/shard_map/ppermute | solution.py:19
  5.1 1.3 %collective-permute-start.2 = (bf16[2,128,512]{2,1,0:T(8,128)(2,1)S(1)}, bf16[2,128,512]{2,1,0:T(8,128)(2,1)S(1)}, u32[]{:S(2)}, u32[]{:S(2)}) collective-permute-start(bf16[2,128,512]{2,1,0:T(8,128)(2,1)S(1)} %pad_maximum_fusion.2.refs_0_), channel_id=1, source_target_pairs={{0,10},{2,12},{4,14},{6,16},{8,18},{10,20},{12,22},{14,24},{16,26}... | collective-permute-start | bytes 786440 | tf_op jit(solution)/shard_map/ppermute | solution.py:19
  6.4 1.3 %collective-permute-start.3 = (bf16[2,128,512]{2,1,0:T(8,128)(2,1)S(1)}, bf16[2,128,512]{2,1,0:T(8,128)(2,1)S(1)}, u32[]{:S(2)}, u32[]{:S(2)}) collective-permute-start(bf16[2,128,512]{2,1,0:T(8,128)(2,1)S(1)} %pad_maximum_fusion.2.refs_0_), channel_id=1, source_target_pairs={{0,14},{2,16},{4,18},{6,20},{8,22},{10,24},{12,26},{14,28},{16,30}... | collective-permute-start | bytes 786440 | tf_op jit(solution)/shard_map/ppermute | solution.py:19
  7.8 0.8 %select_reduce_fusion = s32[8]{0:T(128)S(1)} fusion(s32[8]{0:T(128)} %param.12), kind=kLoop, calls=%fused_computation.20 | loop fusion | flops 184 | bytes 64 | tf_op jit(solution)/shard_map/reduce_sum | solution.py:151
  8.6 0.6 %fusion.11 = s32[]{:T(128)} fusion(s32[8]{0:T(128)S(1)} %select_reduce_fusion, s32[]{:T(128)S(6)} %axis_index.33), kind=kLoop, calls=%fused_computation.27 | loop fusion | flops 23 | bytes 40 | tf_op jit(solution)/shard_map/reduce_sum | solution.py:154
  9.8 0.6 %select_reduce_fusion.3 = s32[]{:T(128)} fusion(s32[8]{0:T(128)S(1)} %select_reduce_fusion, s32[]{:T(128)S(6)} %sub.25), kind=kLoop, calls=%fused_computation.32 | loop fusion | flops 23 | bytes 40 | tf_op jit(solution)/shard_map/reduce_sum | solution.py:156
  11.1 1.3 %fusion.10 = s32[9]{0:T(128)S(1)} fusion(s32[9]{0:T(128)} %constant.46.clone, s32[9]{0:T(128)} %constant.47.clone, pred[]{:T(512)S(6)} %eq.14, s32[]{:T(128)} %select_reduce_fusion.3, s32[]{:T(128)S(6)} %axis_index.33), kind=kLoop, calls=%fused_computation.26 | loop fusion | flops 36 | bytes 117 | tf_op jit(solution)/shard_map/mul | solution.py:162
  12.5 1.3 %select_reduce_fusion.1 = (s32[]{:T(128)}, s32[]{:T(128)}) fusion(s32[8]{0:T(128)} %param.13, s32[]{:T(128)S(6)} %sub.25, s32[8]{0:T(128)} %param.12), kind=kLoop, calls=%fused_computation.30 | loop fusion | flops 38 | bytes 76 | tf_op jit(solution)/shard_map/reduce_sum | solution.py:158
  14.5 2.1 %fusion.5 = (f32[1152,64]{1,0:T(8,128)S(1)}, f32[1152,64]{1,0:T(8,128)S(1)}, f32[1152,64]{1,0:T(8,128)S(1)}) fusion(f32[64]{0:T(128)S(1)} %multiply_power_fusion, f32[1152]{0:T(1024)S(1)} %get-tuple-element.15), kind=kLoop, calls=%fused_computation.9 | loop fusion | flops 147456 | bytes 889600 | tf_op jit(solution)/shard_map/neg | solution.py:97
  17.3 0.3 fusion.6
  17.6 0.1 pad_maximum_fusion.3
  17.7 2.8 %collective-permute-start.4 = (bf16[2,128,512]{2,1,0:T(8,128)(2,1)S(1)}, bf16[2,128,512]{2,1,0:T(8,128)(2,1)S(1)}, u32[]{:S(2)}, u32[]{:S(2)}) collective-permute-start(bf16[2,128,512]{2,1,0:T(8,128)(2,1)S(1)} %collective-permute-done.refs_1_), channel_id=1, source_target_pairs={{0,2},{4,6},{8,10},{12,14},{16,18},{20,22},{24,26},{28,30},{1,3},{... | collective-permute-start | bytes 786440 | tf_op jit(solution)/shard_map/ppermute | solution.py:25
  20.6 7.5 %collective-permute-done.2.refs_3_ = bf16[2,128,512]{2,1,0:T(8,128)(2,1)S(1)} collective-permute-done((bf16[2,128,512]{2,1,0:T(8,128)(2,1)S(1)}, bf16[2,128,512]{2,1,0:T(8,128)(2,1)S(1)}, u32[]{:S(2)}, u32[]{:S(2)}) %collective-permute-start.2) | collective-permute-done | bytes 262176 | tf_op jit(solution)/shard_map/ppermute | solution.py:19
  28.2 6.4 %collective-permute-start.7 = (bf16[2,128,512]{2,1,0:T(8,128)(2,1)S(1)}, bf16[2,128,512]{2,1,0:T(8,128)(2,1)S(1)}, u32[]{:S(2)}, u32[]{:S(2)}) collective-permute-start(bf16[2,128,512]{2,1,0:T(8,128)(2,1)S(1)} %collective-permute-done.3.refs_4_), channel_id=1, source_target_pairs={{0,2},{4,6},{8,10},{12,14},{16,18},{20,22},{24,26},{28,30},{2,0},{... | collective-permute-start | bytes 786440 | tf_op jit(solution)/shard_map/ppermute | solution.py:25
  34.6 0.4 pad_maximum_fusion
  35.0 0.8 %collective-permute-done.7.refs_8_ = bf16[2,128,512]{2,1,0:T(8,128)(2,1)S(1)} collective-permute-done((bf16[2,128,512]{2,1,0:T(8,128)(2,1)S(1)}, bf16[2,128,512]{2,1,0:T(8,128)(2,1)S(1)}, u32[]{:S(2)}, u32[]{:S(2)}) %collective-permute-start.7) | collective-permute-done | bytes 262176 | tf_op jit(solution)/shard_map/ppermute | solution.py:25
  35.7 1.0 %copy-done = bf16[128,2048]{1,0:T(8,128)(2,1)S(1)} copy-done((bf16[128,2048]{1,0:T(8,128)(2,1)S(1)}, bf16[128,2048]{1,0:T(8,128)(2,1)}, u32[]{:S(2)}) %copy-start) | copy-done | bytes 524312
  36.8 10.6 %shard_map.82 = (bf16[128,2048]{1,0:T(8,128)(2,1)S(1)}, bf16[128,2048]{1,0:T(8,128)(2,1)S(1)}) custom-call(s32[1]{0:T(128)} %bitcast.peer_ref, s32[1]{0:T(128)} %bitcast.1.core_ref, s32[128,1]{1,0:T(8,128)S(1)} %iota_add_fusion.query_pos_ref, s32[1,1152]{1,0:T(1,128)S(1)} %and_select_fusion.key_limit_ref, f32[128,128]{1,0:T(8,128)S(1)} %get-tuple-element.19.query_cos_ref, ...), custom_call_target="tpu_custom_call" | custom-call | flops 2281701376 | bytes 12320768 | tf_op jit(solution)/shard_map/pallas_call | solution.py:127
  47.3 1.6 %collective-permute-start.8 = (bf16[128,2048]{1,0:T(8,128)(2,1)S(1)}, bf16[128,2048]{1,0:T(8,128)(2,1)S(1)}, u32[]{:S(2)}, u32[]{:S(2)}) collective-permute-start(bf16[128,2048]{1,0:T(8,128)(2,1)S(1)} %get-tuple-element.8), channel_id=1, source_target_pairs={{0,1},{1,0},{2,3},{3,2},{4,5},{5,4},{6,7},{7,6},{8,9},{9,8},{10,11... | collective-permute-start | bytes 1572872 | tf_op jit(solution)/shard_map/ppermute | solution.py:174
  49.0 4.7 %fusion.2 = bf16[128,2048]{1,0:T(8,128)(2,1)S(1)} fusion(bf16[128,2048]{1,0:T(8,128)(2,1)S(1)} %get-tuple-element.7, bf16[2048,4096]{1,0:T(8,128)(2,1)} %refs_9_.1, s32[]{:T(128)S(6)} %select_n.53), kind=kOutput, calls=%fused_computation.2 | convolution fusion | flops 1074003968 | bytes 9437188 | tf_op jit(solution)/shard_map/dot_general | solution.py:177
  53.6 8.0 %collective-permute-done.8 = bf16[128,2048]{1,0:T(8,128)(2,1)S(1)} collective-permute-done((bf16[128,2048]{1,0:T(8,128)(2,1)S(1)}, bf16[128,2048]{1,0:T(8,128)(2,1)S(1)}, u32[]{:S(2)}, u32[]{:S(2)}) %collective-permute-start.8) | collective-permute-done | bytes 524320 | tf_op jit(solution)/shard_map/ppermute | solution.py:174
  61.6 0.9 %add_convert_fusion = bf16[128,2048]{1,0:T(8,128)(2,1)} fusion(bf16[128,2048]{1,0:T(8,128)(2,1)S(1)} %collective-permute-done.8, bf16[128,2048]{1,0:T(8,128)(2,1)S(1)} %fusion.2), kind=kLoop, calls=%fused_computation.3 | loop fusion | flops 1048576 | bytes 1572864 | tf_op jit(solution)/shard_map/convert_element_type | solution.py:179
  (14 shorter events, 0.2 us)
Async XLA Ops:
  1.0 16.7 %collective-permute-start = (bf16[2,128,512]{2,1,0:T(8,128)(2,1)S(1)}, bf16[2,128,512]{2,1,0:T(8,128)(2,1)S(1)}, u32[]{:S(2)}, u32[]{:S(2)}) collective-permute-start(bf16[2,128,512]{2,1,0:T(8,128)(2,1)S(1)} %pad_maximum_fusion.2.refs_0_), channel_id=1, source_target_pairs={{0,2},{2,4},{4,6},{6,8},{8,10},{10,12},{12,14},{14,16},{16,18},{18... | collective-permute-start | bytes 786440 | tf_op jit(solution)/shard_map/ppermute | solution.py:19
  2.9 17.6 %collective-permute-start.1 = (bf16[2,128,512]{2,1,0:T(8,128)(2,1)S(1)}, bf16[2,128,512]{2,1,0:T(8,128)(2,1)S(1)}, u32[]{:S(2)}, u32[]{:S(2)}) collective-permute-start(bf16[2,128,512]{2,1,0:T(8,128)(2,1)S(1)} %pad_maximum_fusion.2.refs_0_), channel_id=1, source_target_pairs={{0,6},{2,8},{4,10},{6,12},{8,14},{10,16},{12,18},{14,20},{16,22},{... | collective-permute-start | bytes 786440 | tf_op jit(solution)/shard_map/ppermute | solution.py:19
  5.1 23.0 %collective-permute-start.2 = (bf16[2,128,512]{2,1,0:T(8,128)(2,1)S(1)}, bf16[2,128,512]{2,1,0:T(8,128)(2,1)S(1)}, u32[]{:S(2)}, u32[]{:S(2)}) collective-permute-start(bf16[2,128,512]{2,1,0:T(8,128)(2,1)S(1)} %pad_maximum_fusion.2.refs_0_), channel_id=1, source_target_pairs={{0,10},{2,12},{4,14},{6,16},{8,18},{10,20},{12,22},{14,24},{16,26}... | collective-permute-start | bytes 786440 | tf_op jit(solution)/shard_map/ppermute | solution.py:19
  6.4 21.7 %collective-permute-start.3 = (bf16[2,128,512]{2,1,0:T(8,128)(2,1)S(1)}, bf16[2,128,512]{2,1,0:T(8,128)(2,1)S(1)}, u32[]{:S(2)}, u32[]{:S(2)}) collective-permute-start(bf16[2,128,512]{2,1,0:T(8,128)(2,1)S(1)} %pad_maximum_fusion.2.refs_0_), channel_id=1, source_target_pairs={{0,14},{2,16},{4,18},{6,20},{8,22},{10,24},{12,26},{14,28},{16,30}... | collective-permute-start | bytes 786440 | tf_op jit(solution)/shard_map/ppermute | solution.py:19
  17.7 17.2 %collective-permute-start.4 = (bf16[2,128,512]{2,1,0:T(8,128)(2,1)S(1)}, bf16[2,128,512]{2,1,0:T(8,128)(2,1)S(1)}, u32[]{:S(2)}, u32[]{:S(2)}) collective-permute-start(bf16[2,128,512]{2,1,0:T(8,128)(2,1)S(1)} %collective-permute-done.refs_1_), channel_id=1, source_target_pairs={{0,2},{4,6},{8,10},{12,14},{16,18},{20,22},{24,26},{28,30},{1,3},{... | collective-permute-start | bytes 786440 | tf_op jit(solution)/shard_map/ppermute | solution.py:25
  20.5 14.4 %collective-permute-start.5 = (bf16[2,128,512]{2,1,0:T(8,128)(2,1)S(1)}, bf16[2,128,512]{2,1,0:T(8,128)(2,1)S(1)}, u32[]{:S(2)}, u32[]{:S(2)}) collective-permute-start(bf16[2,128,512]{2,1,0:T(8,128)(2,1)S(1)} %collective-permute-done.1.refs_2_), channel_id=1, source_target_pairs={{0,2},{4,6},{8,10},{12,14},{16,18},{20,22},{24,26},{28,30},{2,0},{... | collective-permute-start | bytes 786440 | tf_op jit(solution)/shard_map/ppermute | solution.py:25
  28.2 6.8 %collective-permute-start.6 = (bf16[2,128,512]{2,1,0:T(8,128)(2,1)S(1)}, bf16[2,128,512]{2,1,0:T(8,128)(2,1)S(1)}, u32[]{:S(2)}, u32[]{:S(2)}) collective-permute-start(bf16[2,128,512]{2,1,0:T(8,128)(2,1)S(1)} %collective-permute-done.2.refs_3_), channel_id=1, source_target_pairs={{0,2},{4,6},{8,10},{12,14},{16,18},{20,22},{24,26},{28,30},{2,0},{... | collective-permute-start | bytes 786440 | tf_op jit(solution)/shard_map/ppermute | solution.py:25
  28.2 7.6 %collective-permute-start.7 = (bf16[2,128,512]{2,1,0:T(8,128)(2,1)S(1)}, bf16[2,128,512]{2,1,0:T(8,128)(2,1)S(1)}, u32[]{:S(2)}, u32[]{:S(2)}) collective-permute-start(bf16[2,128,512]{2,1,0:T(8,128)(2,1)S(1)} %collective-permute-done.3.refs_4_), channel_id=1, source_target_pairs={{0,2},{4,6},{8,10},{12,14},{16,18},{20,22},{24,26},{28,30},{2,0},{... | collective-permute-start | bytes 786440 | tf_op jit(solution)/shard_map/ppermute | solution.py:25
  35.7 1.0 %copy-start = (bf16[128,2048]{1,0:T(8,128)(2,1)S(1)}, bf16[128,2048]{1,0:T(8,128)(2,1)}, u32[]{:S(2)}) copy-start(bf16[128,2048]{1,0:T(8,128)(2,1)} %query_ref.1) | copy-start | bytes 1572868
  47.3 14.3 %collective-permute-start.8 = (bf16[128,2048]{1,0:T(8,128)(2,1)S(1)}, bf16[128,2048]{1,0:T(8,128)(2,1)S(1)}, u32[]{:S(2)}, u32[]{:S(2)}) collective-permute-start(bf16[128,2048]{1,0:T(8,128)(2,1)S(1)} %get-tuple-element.8), channel_id=1, source_target_pairs={{0,1},{1,0},{2,3},{3,2},{4,5},{5,4},{6,7},{7,6},{8,9},{9,8},{10,11... | collective-permute-start | bytes 1572872 | tf_op jit(solution)/shard_map/ppermute | solution.py:174

commit v17 on v16

--- a/solution.py
+++ b/solution.py
@@ -17,17 +17,17 @@
     received = []
     for s in range(1, window, 2):
         received.append(lax.ppermute(kv, "ctx", [(j, j + s) for j in range(n - s)]))
+    direct = lax.ppermute(kv, "ctx", [(j, j + window - 2) for j in range(0, n - window + 2, 2)])
     up = [(j, j + 1) for j in range(0, n, 2)]
     down = [(j + 1, j) for j in range(0, n, 2)]
     passed = []
-    for m, block in enumerate(received):
-        pairs = up + (down if m > 0 else [])
-        passed.append(lax.ppermute(block, "ctx", pairs))
-    even_shift = [0] + [2 * m + 1 for m in range(half)] + [FAR] + [2 * m for m in range(1, half)]
+    for m, block in enumerate(received[:-1]):
+        passed.append(lax.ppermute(block, "ctx", up + (down if m > 0 else [])))
+    even_shift = [0] + [2 * m + 1 for m in range(half)] + [FAR] + [2 * m for m in range(1, half - 1)] + [window - 2]
     odd_shift = [0] + [2 * m + 1 for m in range(half)] + [2 * m + 2 for m in range(half - 1)] + [FAR]
     core = lax.axis_index("ctx") % 2
     shift = jnp.where(core == 0, jnp.array(even_shift, jnp.int32), jnp.array(odd_shift, jnp.int32))
-    return [kv] + received + passed, shift
+    return [kv] + received + passed + [direct], shift
 
 
 def turn(rows, cosine, sine):

time: 62.9 us -> 64.2 us (1.021)
  waiting for transfers between devices: 16.3 us -> 23.3 us
  starting transfers between devices: 17.6 us -> 11.8 us
    ppermute x4, waiting for transfers between devices: 0.76 us -> 9 us  [the longest x1 9 us: gather_window(): lax.ppermute(kv, 'ctx', [(j, j + window - 2) for j in range(0, n - window...]
    ppermute x4, starting transfers between devices: 9.25 us -> 3.53 us  [the longest x3 2.24 us: gather_window(): passed.append(lax.ppermute(block, 'ctx', up + (down if m > 0 else [])))]
    ppermute x1, waiting for transfers between devices: 7.99 us -> 4.66 us  [on_device(): got = lax.ppermute(peer_terms, 'tp', [(0, 1), (1, 0)])]
    ppermute x4, waiting for transfers between devices: 7.56 us -> 9.68 us  [gather_window(): received.append(lax.ppermute(kv, 'ctx', [(j, j + s) for j in range(n - s)]))]
  transfers between devices with their start and end apart: 9 -> 9, of which waited for: 3 -> 3; matrix products, arithmetic and copies ran while one was open for 20% -> 19% of each run, Pallas kernels for 0% -> 0%
where the time goes in v17:
time: 64.2 us; the launch traced here: 63.8 us
  waiting for transfers between devices  23.3 us (36%)
  starting transfers between devices  11.8 us (18%)
  Pallas kernels  10.6 us (17%)
  other arithmetic  9.63 us (15%)
  matrix products  4.67 us (7%)
  between operations  2.77 us (4%)
  local copies, waits for them, and re-layouts  1.04 us (2%)
    pallas_call x1, Pallas kernels, attend(): pl.pallas_call(functools.partial(attention_kernel, n_slots, uses, heads_k...  10.6 us
    ppermute x4, waiting for transfers between devices, gather_window(): received.append(lax.ppermute(kv, 'ctx', [(j, j + s) for j in range(n - s)]))  9.68 us
    ppermute x1, waiting for transfers between devices, gather_window(): lax.ppermute(kv, 'ctx', [(j, j + window - 2) for j in range(0, n - window...  9 us
    ppermute x4, starting transfers between devices, gather_window(): received.append(lax.ppermute(kv, 'ctx', [(j, j + s) for j in range(n - s)]))  6.72 us
    dot_general x1, matrix products, on_device(): jnp.dot(attended, own_weight, preferred_element_type=jnp.float32)  4.67 us
    ppermute x1, waiting for transfers between devices, on_device(): got = lax.ppermute(peer_terms, 'tp', [(0, 1), (1, 0)])  4.66 us
    neg x2, other arithmetic, tables(): -sine  2.44 us
    ppermute x3, starting transfers between devices, gather_window(): passed.append(lax.ppermute(block, 'ctx', up + (down if m > 0 else [])))  2.24 us
  transfers between devices with their start and end apart: 9, of which 3 were waited for; matrix products, arithmetic and copies ran while one was open for 19% of the time, Pallas kernels for 0%

profile of v17, /device:TPU:24, one launch (start us, length us, event | category | flops | bytes accessed | tf_op | source)
XLA Modules:
  0.0 63.8 jit_solution(14796965006084210966)
XLA Ops:
  0.0 1.0 %pad_maximum_fusion.2.refs_0_ = bf16[2,128,512]{2,1,0:T(8,128)(2,1)S(1)} fusion(bf16[1,128,512]{2,1,0:T(8,128)(2,1)} %bitcast.12, bf16[1,128,512]{2,1,0:T(8,128)(2,1)} %bitcast.13), kind=kLoop, calls=%fused_computation.8 | loop fusion | flops 131072 | bytes 524288 | tf_op jit(solution)/shard_map/stack | solution.py:148
  1.0 1.9 %collective-permute-start = (bf16[2,128,512]{2,1,0:T(8,128)(2,1)S(1)}, bf16[2,128,512]{2,1,0:T(8,128)(2,1)S(1)}, u32[]{:S(2)}, u32[]{:S(2)}) collective-permute-start(bf16[2,128,512]{2,1,0:T(8,128)(2,1)S(1)} %pad_maximum_fusion.2.refs_0_), channel_id=1, source_target_pairs={{0,2},{2,4},{4,6},{6,8},{8,10},{10,12},{12,14},{14,16},{16,18},{18... | collective-permute-start | bytes 786440 | tf_op jit(solution)/shard_map/ppermute | solution.py:19
  2.9 2.2 %collective-permute-start.1 = (bf16[2,128,512]{2,1,0:T(8,128)(2,1)S(1)}, bf16[2,128,512]{2,1,0:T(8,128)(2,1)S(1)}, u32[]{:S(2)}, u32[]{:S(2)}) collective-permute-start(bf16[2,128,512]{2,1,0:T(8,128)(2,1)S(1)} %pad_maximum_fusion.2.refs_0_), channel_id=1, source_target_pairs={{0,6},{2,8},{4,10},{6,12},{8,14},{10,16},{12,18},{14,20},{16,22},{... | collective-permute-start | bytes 786440 | tf_op jit(solution)/shard_map/ppermute | solution.py:19
  5.1 1.3 %collective-permute-start.2 = (bf16[2,128,512]{2,1,0:T(8,128)(2,1)S(1)}, bf16[2,128,512]{2,1,0:T(8,128)(2,1)S(1)}, u32[]{:S(2)}, u32[]{:S(2)}) collective-permute-start(bf16[2,128,512]{2,1,0:T(8,128)(2,1)S(1)} %pad_maximum_fusion.2.refs_0_), channel_id=1, source_target_pairs={{0,10},{2,12},{4,14},{6,16},{8,18},{10,20},{12,22},{14,24},{16,26}... | collective-permute-start | bytes 786440 | tf_op jit(solution)/shard_map/ppermute | solution.py:19
  6.4 1.3 %collective-permute-start.3 = (bf16[2,128,512]{2,1,0:T(8,128)(2,1)S(1)}, bf16[2,128,512]{2,1,0:T(8,128)(2,1)S(1)}, u32[]{:S(2)}, u32[]{:S(2)}) collective-permute-start(bf16[2,128,512]{2,1,0:T(8,128)(2,1)S(1)} %pad_maximum_fusion.2.refs_0_), channel_id=1, source_target_pairs={{0,14},{2,16},{4,18},{6,20},{8,22},{10,24},{12,26},{14,28},{16,30}... | collective-permute-start | bytes 786440 | tf_op jit(solution)/shard_map/ppermute | solution.py:19
  7.7 1.3 %collective-permute-start.7 = (bf16[2,128,512]{2,1,0:T(8,128)(2,1)S(1)}, bf16[2,128,512]{2,1,0:T(8,128)(2,1)S(1)}, u32[]{:S(2)}, u32[]{:S(2)}) collective-permute-start(bf16[2,128,512]{2,1,0:T(8,128)(2,1)S(1)} %pad_maximum_fusion.2.refs_0_), channel_id=1, source_target_pairs={{0,12},{4,16},{8,20},{12,24},{16,28},{1,13},{5,17},{9,21},{13,25},... | collective-permute-start | bytes 786440 | tf_op jit(solution)/shard_map/ppermute | solution.py:20
  9.1 0.8 %select_reduce_fusion = s32[8]{0:T(128)S(1)} fusion(s32[8]{0:T(128)} %param.12), kind=kLoop, calls=%fused_computation.20 | loop fusion | flops 184 | bytes 64 | tf_op jit(solution)/shard_map/reduce_sum | solution.py:151
  9.9 0.6 fusion.11
  11.1 0.6 select_reduce_fusion.3
  12.4 1.3 %fusion.10 = s32[9]{0:T(128)S(1)} fusion(s32[9]{0:T(128)} %constant.46.clone, s32[9]{0:T(128)} %constant.47.clone, pred[]{:T(512)S(6)} %eq.14, s32[]{:T(128)} %select_reduce_fusion.3, s32[]{:T(128)S(6)} %axis_index.33), kind=kLoop, calls=%fused_computation.26 | loop fusion | flops 36 | bytes 117 | tf_op jit(solution)/shard_map/mul | solution.py:162
  13.8 1.3 %select_reduce_fusion.1 = (s32[]{:T(128)}, s32[]{:T(128)}) fusion(s32[8]{0:T(128)} %param.13, s32[]{:T(128)S(6)} %sub.25, s32[8]{0:T(128)} %param.12), kind=kLoop, calls=%fused_computation.30 | loop fusion | flops 38 | bytes 76 | tf_op jit(solution)/shard_map/reduce_sum | solution.py:158
  15.8 2.1 %fusion.5 = (f32[1152,64]{1,0:T(8,128)S(1)}, f32[1152,64]{1,0:T(8,128)S(1)}, f32[1152,64]{1,0:T(8,128)S(1)}) fusion(f32[64]{0:T(128)S(1)} %multiply_power_fusion, f32[1152]{0:T(1024)S(1)} %get-tuple-element.15), kind=kLoop, calls=%fused_computation.9 | loop fusion | flops 147456 | bytes 889600 | tf_op jit(solution)/shard_map/neg | solution.py:97
  18.6 0.3 fusion.6
  18.9 0.1 pad_maximum_fusion.3
  19.0 2.2 %collective-permute-start.4 = (bf16[2,128,512]{2,1,0:T(8,128)(2,1)S(1)}, bf16[2,128,512]{2,1,0:T(8,128)(2,1)S(1)}, u32[]{:S(2)}, u32[]{:S(2)}) collective-permute-start(bf16[2,128,512]{2,1,0:T(8,128)(2,1)S(1)} %collective-permute-done.refs_1_), channel_id=1, source_target_pairs={{0,2},{4,6},{8,10},{12,14},{16,18},{20,22},{24,26},{28,30},{1,3},{... | collective-permute-start | bytes 786440 | tf_op jit(solution)/shard_map/ppermute | solution.py:25
  21.3 9.7 %collective-permute-done.2.refs_3_ = bf16[2,128,512]{2,1,0:T(8,128)(2,1)S(1)} collective-permute-done((bf16[2,128,512]{2,1,0:T(8,128)(2,1)S(1)}, bf16[2,128,512]{2,1,0:T(8,128)(2,1)S(1)}, u32[]{:S(2)}, u32[]{:S(2)}) %collective-permute-start.2) | collective-permute-done | bytes 262176 | tf_op jit(solution)/shard_map/ppermute | solution.py:19
  31.0 0.4 pad_maximum_fusion
  31.4 9.0 %collective-permute-done.7.refs_8_ = bf16[2,128,512]{2,1,0:T(8,128)(2,1)S(1)} collective-permute-done((bf16[2,128,512]{2,1,0:T(8,128)(2,1)S(1)}, bf16[2,128,512]{2,1,0:T(8,128)(2,1)S(1)}, u32[]{:S(2)}, u32[]{:S(2)}) %collective-permute-start.7) | collective-permute-done | bytes 262176 | tf_op jit(solution)/shard_map/ppermute | solution.py:20
  40.4 1.0 %copy-done = bf16[128,2048]{1,0:T(8,128)(2,1)S(1)} copy-done((bf16[128,2048]{1,0:T(8,128)(2,1)S(1)}, bf16[128,2048]{1,0:T(8,128)(2,1)}, u32[]{:S(2)}) %copy-start) | copy-done | bytes 524312
  41.4 10.6 %shard_map.82 = (bf16[128,2048]{1,0:T(8,128)(2,1)S(1)}, bf16[128,2048]{1,0:T(8,128)(2,1)S(1)}) custom-call(s32[1]{0:T(128)} %bitcast.peer_ref, s32[1]{0:T(128)} %bitcast.1.core_ref, s32[128,1]{1,0:T(8,128)S(1)} %iota_add_fusion.query_pos_ref, s32[1,1152]{1,0:T(1,128)S(1)} %and_select_fusion.key_limit_ref, f32[128,128]{1,0:T(8,128)S(1)} %get-tuple-element.19.query_cos_ref, ...), custom_call_target="tpu_custom_call" | custom-call | flops 2281701376 | bytes 12320768 | tf_op jit(solution)/shard_map/pallas_call | solution.py:127
  52.0 1.6 %collective-permute-start.8 = (bf16[128,2048]{1,0:T(8,128)(2,1)S(1)}, bf16[128,2048]{1,0:T(8,128)(2,1)S(1)}, u32[]{:S(2)}, u32[]{:S(2)}) collective-permute-start(bf16[128,2048]{1,0:T(8,128)(2,1)S(1)} %get-tuple-element.8), channel_id=1, source_target_pairs={{0,1},{1,0},{2,3},{3,2},{4,5},{5,4},{6,7},{7,6},{8,9},{9,8},{10,11... | collective-permute-start | bytes 1572872 | tf_op jit(solution)/shard_map/ppermute | solution.py:174
  53.6 4.7 %fusion.2 = bf16[128,2048]{1,0:T(8,128)(2,1)S(1)} fusion(bf16[128,2048]{1,0:T(8,128)(2,1)S(1)} %get-tuple-element.7, bf16[2048,4096]{1,0:T(8,128)(2,1)} %refs_9_.1, s32[]{:T(128)S(6)} %select_n.53), kind=kOutput, calls=%fused_computation.2 | convolution fusion | flops 1074003968 | bytes 9437188 | tf_op jit(solution)/shard_map/dot_general | solution.py:177
  58.3 4.7 %collective-permute-done.8 = bf16[128,2048]{1,0:T(8,128)(2,1)S(1)} collective-permute-done((bf16[128,2048]{1,0:T(8,128)(2,1)S(1)}, bf16[128,2048]{1,0:T(8,128)(2,1)S(1)}, u32[]{:S(2)}, u32[]{:S(2)}) %collective-permute-start.8) | collective-permute-done | bytes 524320 | tf_op jit(solution)/shard_map/ppermute | solution.py:174
  62.9 0.9 %add_convert_fusion = bf16[128,2048]{1,0:T(8,128)(2,1)} fusion(bf16[128,2048]{1,0:T(8,128)(2,1)S(1)} %collective-permute-done.8, bf16[128,2048]{1,0:T(8,128)(2,1)S(1)} %fusion.2), kind=kLoop, calls=%fused_computation.3 | loop fusion | flops 1048576 | bytes 1572864 | tf_op jit(solution)/shard_map/convert_element_type | solution.py:179
  (14 shorter events, 0.2 us)
Async XLA Ops:
  1.0 18.0 %collective-permute-start = (bf16[2,128,512]{2,1,0:T(8,128)(2,1)S(1)}, bf16[2,128,512]{2,1,0:T(8,128)(2,1)S(1)}, u32[]{:S(2)}, u32[]{:S(2)}) collective-permute-start(bf16[2,128,512]{2,1,0:T(8,128)(2,1)S(1)} %pad_maximum_fusion.2.refs_0_), channel_id=1, source_target_pairs={{0,2},{2,4},{4,6},{6,8},{8,10},{10,12},{12,14},{14,16},{16,18},{18... | collective-permute-start | bytes 786440 | tf_op jit(solution)/shard_map/ppermute | solution.py:19
  2.9 18.3 %collective-permute-start.1 = (bf16[2,128,512]{2,1,0:T(8,128)(2,1)S(1)}, bf16[2,128,512]{2,1,0:T(8,128)(2,1)S(1)}, u32[]{:S(2)}, u32[]{:S(2)}) collective-permute-start(bf16[2,128,512]{2,1,0:T(8,128)(2,1)S(1)} %pad_maximum_fusion.2.refs_0_), channel_id=1, source_target_pairs={{0,6},{2,8},{4,10},{6,12},{8,14},{10,16},{12,18},{14,20},{16,22},{... | collective-permute-start | bytes 786440 | tf_op jit(solution)/shard_map/ppermute | solution.py:19
  5.1 25.8 %collective-permute-start.2 = (bf16[2,128,512]{2,1,0:T(8,128)(2,1)S(1)}, bf16[2,128,512]{2,1,0:T(8,128)(2,1)S(1)}, u32[]{:S(2)}, u32[]{:S(2)}) collective-permute-start(bf16[2,128,512]{2,1,0:T(8,128)(2,1)S(1)} %pad_maximum_fusion.2.refs_0_), channel_id=1, source_target_pairs={{0,10},{2,12},{4,14},{6,16},{8,18},{10,20},{12,22},{14,24},{16,26}... | collective-permute-start | bytes 786440 | tf_op jit(solution)/shard_map/ppermute | solution.py:19
  6.4 24.9 %collective-permute-start.3 = (bf16[2,128,512]{2,1,0:T(8,128)(2,1)S(1)}, bf16[2,128,512]{2,1,0:T(8,128)(2,1)S(1)}, u32[]{:S(2)}, u32[]{:S(2)}) collective-permute-start(bf16[2,128,512]{2,1,0:T(8,128)(2,1)S(1)} %pad_maximum_fusion.2.refs_0_), channel_id=1, source_target_pairs={{0,14},{2,16},{4,18},{6,20},{8,22},{10,24},{12,26},{14,28},{16,30}... | collective-permute-start | bytes 786440 | tf_op jit(solution)/shard_map/ppermute | solution.py:19
  7.7 32.6 %collective-permute-start.7 = (bf16[2,128,512]{2,1,0:T(8,128)(2,1)S(1)}, bf16[2,128,512]{2,1,0:T(8,128)(2,1)S(1)}, u32[]{:S(2)}, u32[]{:S(2)}) collective-permute-start(bf16[2,128,512]{2,1,0:T(8,128)(2,1)S(1)} %pad_maximum_fusion.2.refs_0_), channel_id=1, source_target_pairs={{0,12},{4,16},{8,20},{12,24},{16,28},{1,13},{5,17},{9,21},{13,25},... | collective-permute-start | bytes 786440 | tf_op jit(solution)/shard_map/ppermute | solution.py:20
  19.0 21.3 %collective-permute-start.4 = (bf16[2,128,512]{2,1,0:T(8,128)(2,1)S(1)}, bf16[2,128,512]{2,1,0:T(8,128)(2,1)S(1)}, u32[]{:S(2)}, u32[]{:S(2)}) collective-permute-start(bf16[2,128,512]{2,1,0:T(8,128)(2,1)S(1)} %collective-permute-done.refs_1_), channel_id=1, source_target_pairs={{0,2},{4,6},{8,10},{12,14},{16,18},{20,22},{24,26},{28,30},{1,3},{... | collective-permute-start | bytes 786440 | tf_op jit(solution)/shard_map/ppermute | solution.py:25
  21.2 19.1 %collective-permute-start.5 = (bf16[2,128,512]{2,1,0:T(8,128)(2,1)S(1)}, bf16[2,128,512]{2,1,0:T(8,128)(2,1)S(1)}, u32[]{:S(2)}, u32[]{:S(2)}) collective-permute-start(bf16[2,128,512]{2,1,0:T(8,128)(2,1)S(1)} %collective-permute-done.1.refs_2_), channel_id=1, source_target_pairs={{0,2},{4,6},{8,10},{12,14},{16,18},{20,22},{24,26},{28,30},{2,0},{... | collective-permute-start | bytes 786440 | tf_op jit(solution)/shard_map/ppermute | solution.py:25
  31.0 9.4 %collective-permute-start.6 = (bf16[2,128,512]{2,1,0:T(8,128)(2,1)S(1)}, bf16[2,128,512]{2,1,0:T(8,128)(2,1)S(1)}, u32[]{:S(2)}, u32[]{:S(2)}) collective-permute-start(bf16[2,128,512]{2,1,0:T(8,128)(2,1)S(1)} %collective-permute-done.2.refs_3_), channel_id=1, source_target_pairs={{0,2},{4,6},{8,10},{12,14},{16,18},{20,22},{24,26},{28,30},{2,0},{... | collective-permute-start | bytes 786440 | tf_op jit(solution)/shard_map/ppermute | solution.py:25
  40.4 1.0 %copy-start = (bf16[128,2048]{1,0:T(8,128)(2,1)S(1)}, bf16[128,2048]{1,0:T(8,128)(2,1)}, u32[]{:S(2)}) copy-start(bf16[128,2048]{1,0:T(8,128)(2,1)} %query_ref.1) | copy-start | bytes 1572868
  52.0 10.9 %collective-permute-start.8 = (bf16[128,2048]{1,0:T(8,128)(2,1)S(1)}, bf16[128,2048]{1,0:T(8,128)(2,1)S(1)}, u32[]{:S(2)}, u32[]{:S(2)}) collective-permute-start(bf16[128,2048]{1,0:T(8,128)(2,1)S(1)} %get-tuple-element.8), channel_id=1, source_target_pairs={{0,1},{1,0},{2,3},{3,2},{4,5},{5,4},{6,7},{7,6},{8,9},{9,8},{10,11... | collective-permute-start | bytes 1572872 | tf_op jit(solution)/shard_map/ppermute | solution.py:174

commit v18 on v16

--- a/solution.py
+++ b/solution.py
@@ -58,6 +58,7 @@
     heads_here = query_ref.shape[1] // HEAD_SIZE // heads_kv
 
     def body(use):
+        total = None
         for h in range(heads_kv):
             head = slice(h * HEAD_SIZE, (h + 1) * HEAD_SIZE)
             keys = turn(jnp.concatenate([slot_refs[j][0, :, head] for j in use], axis=0),
@@ -76,16 +77,15 @@
                 totals = jnp.sum(weights, axis=1, keepdims=True)
                 summed = jnp.dot(weights.astype(jnp.bfloat16), values, preferred_element_type=jnp.float32)
                 out_ref[:, columns] = (summed / totals).astype(out_ref.dtype)
+            if project:
+                copies[h].wait()
+                rows = slice(h * group, (h + 1) * group)
+                term = jnp.dot(out_ref[:, rows], weight_ref[rows, :], preferred_element_type=jnp.float32)
+                total = term if total is None else total + term
+        if project:
+            peer_out_ref[...] = total.astype(peer_out_ref.dtype)
 
     body(uses)
-    if project:
-        total = None
-        for h in range(heads_kv):
-            copies[h].wait()
-            rows = slice(h * group, (h + 1) * group)
-            term = jnp.dot(out_ref[:, rows], weight_ref[rows, :], preferred_element_type=jnp.float32)
-            total = term if total is None else total + term
-        peer_out_ref[...] = total.astype(peer_out_ref.dtype)
 
 
 def tables(positions):

time: 62.9 us -> 61.3 us (0.975)
  Pallas kernels: 10.6 us -> 8.99 us
    pallas_call x1, Pallas kernels: 10.6 us -> 8.99 us  [attend(): pl.pallas_call(functools.partial(attention_kernel, n_slots, uses, heads_k...]
where the time goes in v18:
time: 61.3 us; the launch traced here: 61 us
  starting transfers between devices  17.6 us (29%)
  waiting for transfers between devices  16.3 us (27%)
  other arithmetic  9.63 us (16%)
  Pallas kernels  8.99 us (15%)
  matrix products  4.67 us (8%)
  between operations  2.77 us (5%)
  local copies, waits for them, and re-layouts  1.04 us (2%)
    ppermute x4, starting transfers between devices, gather_window(): passed.append(lax.ppermute(block, 'ctx', pairs))  9.25 us
    pallas_call x1, Pallas kernels, attend(): pl.pallas_call(functools.partial(attention_kernel, n_slots, uses, heads_k...  8.99 us
    ppermute x1, waiting for transfers between devices, on_device(): got = lax.ppermute(peer_terms, 'tp', [(0, 1), (1, 0)])  7.99 us
    ppermute x4, waiting for transfers between devices, gather_window(): received.append(lax.ppermute(kv, 'ctx', [(j, j + s) for j in range(n - s)]))  7.56 us
    ppermute x4, starting transfers between devices, gather_window(): received.append(lax.ppermute(kv, 'ctx', [(j, j + s) for j in range(n - s)]))  6.72 us
    dot_general x1, matrix products, on_device(): jnp.dot(attended, own_weight, preferred_element_type=jnp.float32)  4.67 us
    neg x2, other arithmetic, tables(): -sine  2.44 us
    ppermute x1, starting transfers between devices, on_device(): got = lax.ppermute(peer_terms, 'tp', [(0, 1), (1, 0)])  1.6 us
  transfers between devices with their start and end apart: 9, of which 3 were waited for; matrix products, arithmetic and copies ran while one was open for 20% of the time, Pallas kernels for 0%

profile of v18, /device:TPU:24, one launch (start us, length us, event | category | flops | bytes accessed | tf_op | source)
XLA Modules:
  0.0 61.0 jit_solution(16239322627989900165)
XLA Ops:
  0.0 1.0 %pad_maximum_fusion.2.refs_0_ = bf16[2,128,512]{2,1,0:T(8,128)(2,1)S(1)} fusion(bf16[1,128,512]{2,1,0:T(8,128)(2,1)} %bitcast.12, bf16[1,128,512]{2,1,0:T(8,128)(2,1)} %bitcast.13), kind=kLoop, calls=%fused_computation.8 | loop fusion | flops 131072 | bytes 524288 | tf_op jit(solution)/shard_map/stack | solution.py:148
  1.0 1.9 %collective-permute-start = (bf16[2,128,512]{2,1,0:T(8,128)(2,1)S(1)}, bf16[2,128,512]{2,1,0:T(8,128)(2,1)S(1)}, u32[]{:S(2)}, u32[]{:S(2)}) collective-permute-start(bf16[2,128,512]{2,1,0:T(8,128)(2,1)S(1)} %pad_maximum_fusion.2.refs_0_), channel_id=1, source_target_pairs={{0,2},{2,4},{4,6},{6,8},{8,10},{10,12},{12,14},{14,16},{16,18},{18... | collective-permute-start | bytes 786440 | tf_op jit(solution)/shard_map/ppermute | solution.py:19
  2.9 2.2 %collective-permute-start.1 = (bf16[2,128,512]{2,1,0:T(8,128)(2,1)S(1)}, bf16[2,128,512]{2,1,0:T(8,128)(2,1)S(1)}, u32[]{:S(2)}, u32[]{:S(2)}) collective-permute-start(bf16[2,128,512]{2,1,0:T(8,128)(2,1)S(1)} %pad_maximum_fusion.2.refs_0_), channel_id=1, source_target_pairs={{0,6},{2,8},{4,10},{6,12},{8,14},{10,16},{12,18},{14,20},{16,22},{... | collective-permute-start | bytes 786440 | tf_op jit(solution)/shard_map/ppermute | solution.py:19
  5.1 1.3 %collective-permute-start.2 = (bf16[2,128,512]{2,1,0:T(8,128)(2,1)S(1)}, bf16[2,128,512]{2,1,0:T(8,128)(2,1)S(1)}, u32[]{:S(2)}, u32[]{:S(2)}) collective-permute-start(bf16[2,128,512]{2,1,0:T(8,128)(2,1)S(1)} %pad_maximum_fusion.2.refs_0_), channel_id=1, source_target_pairs={{0,10},{2,12},{4,14},{6,16},{8,18},{10,20},{12,22},{14,24},{16,26}... | collective-permute-start | bytes 786440 | tf_op jit(solution)/shard_map/ppermute | solution.py:19
  6.4 1.3 %collective-permute-start.3 = (bf16[2,128,512]{2,1,0:T(8,128)(2,1)S(1)}, bf16[2,128,512]{2,1,0:T(8,128)(2,1)S(1)}, u32[]{:S(2)}, u32[]{:S(2)}) collective-permute-start(bf16[2,128,512]{2,1,0:T(8,128)(2,1)S(1)} %pad_maximum_fusion.2.refs_0_), channel_id=1, source_target_pairs={{0,14},{2,16},{4,18},{6,20},{8,22},{10,24},{12,26},{14,28},{16,30}... | collective-permute-start | bytes 786440 | tf_op jit(solution)/shard_map/ppermute | solution.py:19
  7.8 0.8 %select_reduce_fusion = s32[8]{0:T(128)S(1)} fusion(s32[8]{0:T(128)} %param.12), kind=kLoop, calls=%fused_computation.20 | loop fusion | flops 184 | bytes 64 | tf_op jit(solution)/shard_map/reduce_sum | solution.py:151
  8.6 0.6 %fusion.11 = s32[]{:T(128)} fusion(s32[8]{0:T(128)S(1)} %select_reduce_fusion, s32[]{:T(128)S(6)} %axis_index.33), kind=kLoop, calls=%fused_computation.27 | loop fusion | flops 23 | bytes 40 | tf_op jit(solution)/shard_map/reduce_sum | solution.py:154
  9.8 0.6 %select_reduce_fusion.3 = s32[]{:T(128)} fusion(s32[8]{0:T(128)S(1)} %select_reduce_fusion, s32[]{:T(128)S(6)} %sub.25), kind=kLoop, calls=%fused_computation.32 | loop fusion | flops 23 | bytes 40 | tf_op jit(solution)/shard_map/reduce_sum | solution.py:156
  11.1 1.3 %fusion.10 = s32[9]{0:T(128)S(1)} fusion(s32[9]{0:T(128)} %constant.46.clone, s32[9]{0:T(128)} %constant.47.clone, pred[]{:T(512)S(6)} %eq.14, s32[]{:T(128)} %select_reduce_fusion.3, s32[]{:T(128)S(6)} %axis_index.33), kind=kLoop, calls=%fused_computation.26 | loop fusion | flops 36 | bytes 117 | tf_op jit(solution)/shard_map/mul | solution.py:162
  12.5 1.3 %select_reduce_fusion.1 = (s32[]{:T(128)}, s32[]{:T(128)}) fusion(s32[8]{0:T(128)} %param.13, s32[]{:T(128)S(6)} %sub.25, s32[8]{0:T(128)} %param.12), kind=kLoop, calls=%fused_computation.30 | loop fusion | flops 38 | bytes 76 | tf_op jit(solution)/shard_map/reduce_sum | solution.py:158
  14.5 2.1 %fusion.5 = (f32[1152,64]{1,0:T(8,128)S(1)}, f32[1152,64]{1,0:T(8,128)S(1)}, f32[1152,64]{1,0:T(8,128)S(1)}) fusion(f32[64]{0:T(128)S(1)} %multiply_power_fusion, f32[1152]{0:T(1024)S(1)} %get-tuple-element.15), kind=kLoop, calls=%fused_computation.9 | loop fusion | flops 147456 | bytes 889600 | tf_op jit(solution)/shard_map/neg | solution.py:97
  17.3 0.3 fusion.6
  17.6 0.1 pad_maximum_fusion.3
  17.7 2.8 %collective-permute-start.4 = (bf16[2,128,512]{2,1,0:T(8,128)(2,1)S(1)}, bf16[2,128,512]{2,1,0:T(8,128)(2,1)S(1)}, u32[]{:S(2)}, u32[]{:S(2)}) collective-permute-start(bf16[2,128,512]{2,1,0:T(8,128)(2,1)S(1)} %collective-permute-done.refs_1_), channel_id=1, source_target_pairs={{0,2},{4,6},{8,10},{12,14},{16,18},{20,22},{24,26},{28,30},{1,3},{... | collective-permute-start | bytes 786440 | tf_op jit(solution)/shard_map/ppermute | solution.py:25
  20.6 7.5 %collective-permute-done.2.refs_3_ = bf16[2,128,512]{2,1,0:T(8,128)(2,1)S(1)} collective-permute-done((bf16[2,128,512]{2,1,0:T(8,128)(2,1)S(1)}, bf16[2,128,512]{2,1,0:T(8,128)(2,1)S(1)}, u32[]{:S(2)}, u32[]{:S(2)}) %collective-permute-start.2) | collective-permute-done | bytes 262176 | tf_op jit(solution)/shard_map/ppermute | solution.py:19
  28.2 6.4 %collective-permute-start.7 = (bf16[2,128,512]{2,1,0:T(8,128)(2,1)S(1)}, bf16[2,128,512]{2,1,0:T(8,128)(2,1)S(1)}, u32[]{:S(2)}, u32[]{:S(2)}) collective-permute-start(bf16[2,128,512]{2,1,0:T(8,128)(2,1)S(1)} %collective-permute-done.3.refs_4_), channel_id=1, source_target_pairs={{0,2},{4,6},{8,10},{12,14},{16,18},{20,22},{24,26},{28,30},{2,0},{... | collective-permute-start | bytes 786440 | tf_op jit(solution)/shard_map/ppermute | solution.py:25
  34.6 0.4 pad_maximum_fusion
  35.0 0.8 %collective-permute-done.7.refs_8_ = bf16[2,128,512]{2,1,0:T(8,128)(2,1)S(1)} collective-permute-done((bf16[2,128,512]{2,1,0:T(8,128)(2,1)S(1)}, bf16[2,128,512]{2,1,0:T(8,128)(2,1)S(1)}, u32[]{:S(2)}, u32[]{:S(2)}) %collective-permute-start.7) | collective-permute-done | bytes 262176 | tf_op jit(solution)/shard_map/ppermute | solution.py:25
  35.7 1.0 %copy-done = bf16[128,2048]{1,0:T(8,128)(2,1)S(1)} copy-done((bf16[128,2048]{1,0:T(8,128)(2,1)S(1)}, bf16[128,2048]{1,0:T(8,128)(2,1)}, u32[]{:S(2)}) %copy-start) | copy-done | bytes 524312
  36.8 9.0 %shard_map.82 = (bf16[128,2048]{1,0:T(8,128)(2,1)S(1)}, bf16[128,2048]{1,0:T(8,128)(2,1)S(1)}) custom-call(s32[1]{0:T(128)} %bitcast.peer_ref, s32[1]{0:T(128)} %bitcast.1.core_ref, s32[128,1]{1,0:T(8,128)S(1)} %iota_add_fusion.query_pos_ref, s32[1,1152]{1,0:T(1,128)S(1)} %and_select_fusion.key_limit_ref, f32[128,128]{1,0:T(8,128)S(1)} %get-tuple-element.19.query_cos_ref, ...), custom_call_target="tpu_custom_call" | custom-call | flops 2281701376 | bytes 12320768 | tf_op jit(solution)/shard_map/pallas_call | solution.py:127
  45.8 1.6 %collective-permute-start.8 = (bf16[128,2048]{1,0:T(8,128)(2,1)S(1)}, bf16[128,2048]{1,0:T(8,128)(2,1)S(1)}, u32[]{:S(2)}, u32[]{:S(2)}) collective-permute-start(bf16[128,2048]{1,0:T(8,128)(2,1)S(1)} %get-tuple-element.8), channel_id=1, source_target_pairs={{0,1},{1,0},{2,3},{3,2},{4,5},{5,4},{6,7},{7,6},{8,9},{9,8},{10,11... | collective-permute-start | bytes 1572872 | tf_op jit(solution)/shard_map/ppermute | solution.py:174
  47.4 4.7 %fusion.2 = bf16[128,2048]{1,0:T(8,128)(2,1)S(1)} fusion(bf16[128,2048]{1,0:T(8,128)(2,1)S(1)} %get-tuple-element.7, bf16[2048,4096]{1,0:T(8,128)(2,1)} %refs_9_.1, s32[]{:T(128)S(6)} %select_n.53), kind=kOutput, calls=%fused_computation.2 | convolution fusion | flops 1074003968 | bytes 9437188 | tf_op jit(solution)/shard_map/dot_general | solution.py:177
  52.1 8.0 %collective-permute-done.8 = bf16[128,2048]{1,0:T(8,128)(2,1)S(1)} collective-permute-done((bf16[128,2048]{1,0:T(8,128)(2,1)S(1)}, bf16[128,2048]{1,0:T(8,128)(2,1)S(1)}, u32[]{:S(2)}, u32[]{:S(2)}) %collective-permute-start.8) | collective-permute-done | bytes 524320 | tf_op jit(solution)/shard_map/ppermute | solution.py:174
  60.0 0.9 %add_convert_fusion = bf16[128,2048]{1,0:T(8,128)(2,1)} fusion(bf16[128,2048]{1,0:T(8,128)(2,1)S(1)} %collective-permute-done.8, bf16[128,2048]{1,0:T(8,128)(2,1)S(1)} %fusion.2), kind=kLoop, calls=%fused_computation.3 | loop fusion | flops 1048576 | bytes 1572864 | tf_op jit(solution)/shard_map/convert_element_type | solution.py:179
  (14 shorter events, 0.2 us)
Async XLA Ops:
  1.0 16.7 %collective-permute-start = (bf16[2,128,512]{2,1,0:T(8,128)(2,1)S(1)}, bf16[2,128,512]{2,1,0:T(8,128)(2,1)S(1)}, u32[]{:S(2)}, u32[]{:S(2)}) collective-permute-start(bf16[2,128,512]{2,1,0:T(8,128)(2,1)S(1)} %pad_maximum_fusion.2.refs_0_), channel_id=1, source_target_pairs={{0,2},{2,4},{4,6},{6,8},{8,10},{10,12},{12,14},{14,16},{16,18},{18... | collective-permute-start | bytes 786440 | tf_op jit(solution)/shard_map/ppermute | solution.py:19
  2.9 17.6 %collective-permute-start.1 = (bf16[2,128,512]{2,1,0:T(8,128)(2,1)S(1)}, bf16[2,128,512]{2,1,0:T(8,128)(2,1)S(1)}, u32[]{:S(2)}, u32[]{:S(2)}) collective-permute-start(bf16[2,128,512]{2,1,0:T(8,128)(2,1)S(1)} %pad_maximum_fusion.2.refs_0_), channel_id=1, source_target_pairs={{0,6},{2,8},{4,10},{6,12},{8,14},{10,16},{12,18},{14,20},{16,22},{... | collective-permute-start | bytes 786440 | tf_op jit(solution)/shard_map/ppermute | solution.py:19
  5.1 23.0 %collective-permute-start.2 = (bf16[2,128,512]{2,1,0:T(8,128)(2,1)S(1)}, bf16[2,128,512]{2,1,0:T(8,128)(2,1)S(1)}, u32[]{:S(2)}, u32[]{:S(2)}) collective-permute-start(bf16[2,128,512]{2,1,0:T(8,128)(2,1)S(1)} %pad_maximum_fusion.2.refs_0_), channel_id=1, source_target_pairs={{0,10},{2,12},{4,14},{6,16},{8,18},{10,20},{12,22},{14,24},{16,26}... | collective-permute-start | bytes 786440 | tf_op jit(solution)/shard_map/ppermute | solution.py:19
  6.4 21.7 %collective-permute-start.3 = (bf16[2,128,512]{2,1,0:T(8,128)(2,1)S(1)}, bf16[2,128,512]{2,1,0:T(8,128)(2,1)S(1)}, u32[]{:S(2)}, u32[]{:S(2)}) collective-permute-start(bf16[2,128,512]{2,1,0:T(8,128)(2,1)S(1)} %pad_maximum_fusion.2.refs_0_), channel_id=1, source_target_pairs={{0,14},{2,16},{4,18},{6,20},{8,22},{10,24},{12,26},{14,28},{16,30}... | collective-permute-start | bytes 786440 | tf_op jit(solution)/shard_map/ppermute | solution.py:19
  17.7 17.2 %collective-permute-start.4 = (bf16[2,128,512]{2,1,0:T(8,128)(2,1)S(1)}, bf16[2,128,512]{2,1,0:T(8,128)(2,1)S(1)}, u32[]{:S(2)}, u32[]{:S(2)}) collective-permute-start(bf16[2,128,512]{2,1,0:T(8,128)(2,1)S(1)} %collective-permute-done.refs_1_), channel_id=1, source_target_pairs={{0,2},{4,6},{8,10},{12,14},{16,18},{20,22},{24,26},{28,30},{1,3},{... | collective-permute-start | bytes 786440 | tf_op jit(solution)/shard_map/ppermute | solution.py:25
  20.5 14.4 %collective-permute-start.5 = (bf16[2,128,512]{2,1,0:T(8,128)(2,1)S(1)}, bf16[2,128,512]{2,1,0:T(8,128)(2,1)S(1)}, u32[]{:S(2)}, u32[]{:S(2)}) collective-permute-start(bf16[2,128,512]{2,1,0:T(8,128)(2,1)S(1)} %collective-permute-done.1.refs_2_), channel_id=1, source_target_pairs={{0,2},{4,6},{8,10},{12,14},{16,18},{20,22},{24,26},{28,30},{2,0},{... | collective-permute-start | bytes 786440 | tf_op jit(solution)/shard_map/ppermute | solution.py:25
  28.2 6.8 %collective-permute-start.6 = (bf16[2,128,512]{2,1,0:T(8,128)(2,1)S(1)}, bf16[2,128,512]{2,1,0:T(8,128)(2,1)S(1)}, u32[]{:S(2)}, u32[]{:S(2)}) collective-permute-start(bf16[2,128,512]{2,1,0:T(8,128)(2,1)S(1)} %collective-permute-done.2.refs_3_), channel_id=1, source_target_pairs={{0,2},{4,6},{8,10},{12,14},{16,18},{20,22},{24,26},{28,30},{2,0},{... | collective-permute-start | bytes 786440 | tf_op jit(solution)/shard_map/ppermute | solution.py:25
  28.2 7.6 %collective-permute-start.7 = (bf16[2,128,512]{2,1,0:T(8,128)(2,1)S(1)}, bf16[2,128,512]{2,1,0:T(8,128)(2,1)S(1)}, u32[]{:S(2)}, u32[]{:S(2)}) collective-permute-start(bf16[2,128,512]{2,1,0:T(8,128)(2,1)S(1)} %collective-permute-done.3.refs_4_), channel_id=1, source_target_pairs={{0,2},{4,6},{8,10},{12,14},{16,18},{20,22},{24,26},{28,30},{2,0},{... | collective-permute-start | bytes 786440 | tf_op jit(solution)/shard_map/ppermute | solution.py:25
  35.7 1.0 %copy-start = (bf16[128,2048]{1,0:T(8,128)(2,1)S(1)}, bf16[128,2048]{1,0:T(8,128)(2,1)}, u32[]{:S(2)}) copy-start(bf16[128,2048]{1,0:T(8,128)(2,1)} %query_ref.1) | copy-start | bytes 1572868
  45.8 14.3 %collective-permute-start.8 = (bf16[128,2048]{1,0:T(8,128)(2,1)S(1)}, bf16[128,2048]{1,0:T(8,128)(2,1)S(1)}, u32[]{:S(2)}, u32[]{:S(2)}) collective-permute-start(bf16[128,2048]{1,0:T(8,128)(2,1)S(1)} %get-tuple-element.8), channel_id=1, source_target_pairs={{0,1},{1,0},{2,3},{3,2},{4,5},{5,4},{6,7},{7,6},{8,9},{9,8},{10,11... | collective-permute-start | bytes 1572872 | tf_op jit(solution)/shard_map/ppermute | solution.py:174

commit v19 on v18

--- a/solution.py
+++ b/solution.py
@@ -77,11 +77,14 @@
                 totals = jnp.sum(weights, axis=1, keepdims=True)
                 summed = jnp.dot(weights.astype(jnp.bfloat16), values, preferred_element_type=jnp.float32)
                 out_ref[:, columns] = (summed / totals).astype(out_ref.dtype)
-            if project:
-                copies[h].wait()
-                rows = slice(h * group, (h + 1) * group)
-                term = jnp.dot(out_ref[:, rows], weight_ref[rows, :], preferred_element_type=jnp.float32)
-                total = term if total is None else total + term
+            if project and (h % 2 == 1 or h == heads_kv - 1):
+                done = range(h - h % 2, h + 1)
+                for k in done:
+                    copies[k].wait()
+                for k in done:
+                    rows = slice(k * group, (k + 1) * group)
+                    term = jnp.dot(out_ref[:, rows], weight_ref[rows, :], preferred_element_type=jnp.float32)
+                    total = term if total is None else total + term
         if project:
             peer_out_ref[...] = total.astype(peer_out_ref.dtype)
 

time: 61.3 us -> 60.6 us (0.989)
  Pallas kernels: 8.99 us -> 8.23 us
    pallas_call x1, Pallas kernels: 8.99 us -> 8.23 us  [attend(): pl.pallas_call(functools.partial(attention_kernel, n_slots, uses, heads_k...]
  transfers between devices with their start and end apart: 9 -> 9, of which waited for: 3 -> 3; matrix products, arithmetic and copies ran while one was open for 20% -> 21% of each run, Pallas kernels for 0% -> 0%
where the time goes in v19:
time: 60.6 us; the launch traced here: 60.2 us
  starting transfers between devices  17.6 us (29%)
  waiting for transfers between devices  16.3 us (27%)
  other arithmetic  9.63 us (16%)
  Pallas kernels  8.23 us (14%)
  matrix products  4.67 us (8%)
  between operations  2.77 us (5%)
  local copies, waits for them, and re-layouts  1.04 us (2%)
    ppermute x4, starting transfers between devices, gather_window(): passed.append(lax.ppermute(block, 'ctx', pairs))  9.25 us
    pallas_call x1, Pallas kernels, attend(): pl.pallas_call(functools.partial(attention_kernel, n_slots, uses, heads_k...  8.23 us
    ppermute x1, waiting for transfers between devices, on_device(): got = lax.ppermute(peer_terms, 'tp', [(0, 1), (1, 0)])  8 us
    ppermute x4, waiting for transfers between devices, gather_window(): received.append(lax.ppermute(kv, 'ctx', [(j, j + s) for j in range(n - s)]))  7.56 us
    ppermute x4, starting transfers between devices, gather_window(): received.append(lax.ppermute(kv, 'ctx', [(j, j + s) for j in range(n - s)]))  6.72 us
    dot_general x1, matrix products, on_device(): jnp.dot(attended, own_weight, preferred_element_type=jnp.float32)  4.67 us
    neg x2, other arithmetic, tables(): -sine  2.44 us
    ppermute x1, starting transfers between devices, on_device(): got = lax.ppermute(peer_terms, 'tp', [(0, 1), (1, 0)])  1.59 us
  transfers between devices with their start and end apart: 9, of which 3 were waited for; matrix products, arithmetic and copies ran while one was open for 21% of the time, Pallas kernels for 0%

profile of v19, /device:TPU:24, one launch (start us, length us, event | category | flops | bytes accessed | tf_op | source)
XLA Modules:
  0.0 60.2 jit_solution(6883304201704514495)
XLA Ops:
  0.0 1.0 %pad_maximum_fusion.2.refs_0_ = bf16[2,128,512]{2,1,0:T(8,128)(2,1)S(1)} fusion(bf16[1,128,512]{2,1,0:T(8,128)(2,1)} %bitcast.12, bf16[1,128,512]{2,1,0:T(8,128)(2,1)} %bitcast.13), kind=kLoop, calls=%fused_computation.8 | loop fusion | flops 131072 | bytes 524288 | tf_op jit(solution)/shard_map/stack | solution.py:151
  1.0 1.9 %collective-permute-start = (bf16[2,128,512]{2,1,0:T(8,128)(2,1)S(1)}, bf16[2,128,512]{2,1,0:T(8,128)(2,1)S(1)}, u32[]{:S(2)}, u32[]{:S(2)}) collective-permute-start(bf16[2,128,512]{2,1,0:T(8,128)(2,1)S(1)} %pad_maximum_fusion.2.refs_0_), channel_id=1, source_target_pairs={{0,2},{2,4},{4,6},{6,8},{8,10},{10,12},{12,14},{14,16},{16,18},{18... | collective-permute-start | bytes 786440 | tf_op jit(solution)/shard_map/ppermute | solution.py:19
  2.9 2.2 %collective-permute-start.1 = (bf16[2,128,512]{2,1,0:T(8,128)(2,1)S(1)}, bf16[2,128,512]{2,1,0:T(8,128)(2,1)S(1)}, u32[]{:S(2)}, u32[]{:S(2)}) collective-permute-start(bf16[2,128,512]{2,1,0:T(8,128)(2,1)S(1)} %pad_maximum_fusion.2.refs_0_), channel_id=1, source_target_pairs={{0,6},{2,8},{4,10},{6,12},{8,14},{10,16},{12,18},{14,20},{16,22},{... | collective-permute-start | bytes 786440 | tf_op jit(solution)/shard_map/ppermute | solution.py:19
  5.1 1.3 %collective-permute-start.2 = (bf16[2,128,512]{2,1,0:T(8,128)(2,1)S(1)}, bf16[2,128,512]{2,1,0:T(8,128)(2,1)S(1)}, u32[]{:S(2)}, u32[]{:S(2)}) collective-permute-start(bf16[2,128,512]{2,1,0:T(8,128)(2,1)S(1)} %pad_maximum_fusion.2.refs_0_), channel_id=1, source_target_pairs={{0,10},{2,12},{4,14},{6,16},{8,18},{10,20},{12,22},{14,24},{16,26}... | collective-permute-start | bytes 786440 | tf_op jit(solution)/shard_map/ppermute | solution.py:19
  6.4 1.3 %collective-permute-start.3 = (bf16[2,128,512]{2,1,0:T(8,128)(2,1)S(1)}, bf16[2,128,512]{2,1,0:T(8,128)(2,1)S(1)}, u32[]{:S(2)}, u32[]{:S(2)}) collective-permute-start(bf16[2,128,512]{2,1,0:T(8,128)(2,1)S(1)} %pad_maximum_fusion.2.refs_0_), channel_id=1, source_target_pairs={{0,14},{2,16},{4,18},{6,20},{8,22},{10,24},{12,26},{14,28},{16,30}... | collective-permute-start | bytes 786440 | tf_op jit(solution)/shard_map/ppermute | solution.py:19
  7.8 0.8 %select_reduce_fusion = s32[8]{0:T(128)S(1)} fusion(s32[8]{0:T(128)} %param.12), kind=kLoop, calls=%fused_computation.20 | loop fusion | flops 184 | bytes 64 | tf_op jit(solution)/shard_map/reduce_sum | solution.py:154
  8.6 0.6 %fusion.11 = s32[]{:T(128)} fusion(s32[8]{0:T(128)S(1)} %select_reduce_fusion, s32[]{:T(128)S(6)} %axis_index.33), kind=kLoop, calls=%fused_computation.27 | loop fusion | flops 23 | bytes 40 | tf_op jit(solution)/shard_map/reduce_sum | solution.py:157
  9.8 0.6 %select_reduce_fusion.3 = s32[]{:T(128)} fusion(s32[8]{0:T(128)S(1)} %select_reduce_fusion, s32[]{:T(128)S(6)} %sub.25), kind=kLoop, calls=%fused_computation.32 | loop fusion | flops 23 | bytes 40 | tf_op jit(solution)/shard_map/reduce_sum | solution.py:159
  11.1 1.3 %fusion.10 = s32[9]{0:T(128)S(1)} fusion(s32[9]{0:T(128)} %constant.46.clone, s32[9]{0:T(128)} %constant.47.clone, pred[]{:T(512)S(6)} %eq.14, s32[]{:T(128)} %select_reduce_fusion.3, s32[]{:T(128)S(6)} %axis_index.33), kind=kLoop, calls=%fused_computation.26 | loop fusion | flops 36 | bytes 117 | tf_op jit(solution)/shard_map/mul | solution.py:165
  12.5 1.3 %select_reduce_fusion.1 = (s32[]{:T(128)}, s32[]{:T(128)}) fusion(s32[8]{0:T(128)} %param.13, s32[]{:T(128)S(6)} %sub.25, s32[8]{0:T(128)} %param.12), kind=kLoop, calls=%fused_computation.30 | loop fusion | flops 38 | bytes 76 | tf_op jit(solution)/shard_map/reduce_sum | solution.py:161
  14.5 2.1 %fusion.5 = (f32[1152,64]{1,0:T(8,128)S(1)}, f32[1152,64]{1,0:T(8,128)S(1)}, f32[1152,64]{1,0:T(8,128)S(1)}) fusion(f32[64]{0:T(128)S(1)} %multiply_power_fusion, f32[1152]{0:T(1024)S(1)} %get-tuple-element.15), kind=kLoop, calls=%fused_computation.9 | loop fusion | flops 147456 | bytes 889600 | tf_op jit(solution)/shard_map/neg | solution.py:100
  17.3 0.3 fusion.6
  17.6 0.1 pad_maximum_fusion.3
  17.7 2.8 %collective-permute-start.4 = (bf16[2,128,512]{2,1,0:T(8,128)(2,1)S(1)}, bf16[2,128,512]{2,1,0:T(8,128)(2,1)S(1)}, u32[]{:S(2)}, u32[]{:S(2)}) collective-permute-start(bf16[2,128,512]{2,1,0:T(8,128)(2,1)S(1)} %collective-permute-done.refs_1_), channel_id=1, source_target_pairs={{0,2},{4,6},{8,10},{12,14},{16,18},{20,22},{24,26},{28,30},{1,3},{... | collective-permute-start | bytes 786440 | tf_op jit(solution)/shard_map/ppermute | solution.py:25
  20.6 7.5 %collective-permute-done.2.refs_3_ = bf16[2,128,512]{2,1,0:T(8,128)(2,1)S(1)} collective-permute-done((bf16[2,128,512]{2,1,0:T(8,128)(2,1)S(1)}, bf16[2,128,512]{2,1,0:T(8,128)(2,1)S(1)}, u32[]{:S(2)}, u32[]{:S(2)}) %collective-permute-start.2) | collective-permute-done | bytes 262176 | tf_op jit(solution)/shard_map/ppermute | solution.py:19
  28.2 6.4 %collective-permute-start.7 = (bf16[2,128,512]{2,1,0:T(8,128)(2,1)S(1)}, bf16[2,128,512]{2,1,0:T(8,128)(2,1)S(1)}, u32[]{:S(2)}, u32[]{:S(2)}) collective-permute-start(bf16[2,128,512]{2,1,0:T(8,128)(2,1)S(1)} %collective-permute-done.3.refs_4_), channel_id=1, source_target_pairs={{0,2},{4,6},{8,10},{12,14},{16,18},{20,22},{24,26},{28,30},{2,0},{... | collective-permute-start | bytes 786440 | tf_op jit(solution)/shard_map/ppermute | solution.py:25
  34.6 0.4 pad_maximum_fusion
  35.0 0.8 %collective-permute-done.7.refs_8_ = bf16[2,128,512]{2,1,0:T(8,128)(2,1)S(1)} collective-permute-done((bf16[2,128,512]{2,1,0:T(8,128)(2,1)S(1)}, bf16[2,128,512]{2,1,0:T(8,128)(2,1)S(1)}, u32[]{:S(2)}, u32[]{:S(2)}) %collective-permute-start.7) | collective-permute-done | bytes 262176 | tf_op jit(solution)/shard_map/ppermute | solution.py:25
  35.7 1.0 %copy-done = bf16[128,2048]{1,0:T(8,128)(2,1)S(1)} copy-done((bf16[128,2048]{1,0:T(8,128)(2,1)S(1)}, bf16[128,2048]{1,0:T(8,128)(2,1)}, u32[]{:S(2)}) %copy-start) | copy-done | bytes 524312
  36.8 8.2 %shard_map.82 = (bf16[128,2048]{1,0:T(8,128)(2,1)S(1)}, bf16[128,2048]{1,0:T(8,128)(2,1)S(1)}) custom-call(s32[1]{0:T(128)} %bitcast.peer_ref, s32[1]{0:T(128)} %bitcast.1.core_ref, s32[128,1]{1,0:T(8,128)S(1)} %iota_add_fusion.query_pos_ref, s32[1,1152]{1,0:T(1,128)S(1)} %and_select_fusion.key_limit_ref, f32[128,128]{1,0:T(8,128)S(1)} %get-tuple-element.19.query_cos_ref, ...), custom_call_target="tpu_custom_call" | custom-call | flops 2281701376 | bytes 12320768 | tf_op jit(solution)/shard_map/pallas_call | solution.py:130
  45.0 1.6 %collective-permute-start.8 = (bf16[128,2048]{1,0:T(8,128)(2,1)S(1)}, bf16[128,2048]{1,0:T(8,128)(2,1)S(1)}, u32[]{:S(2)}, u32[]{:S(2)}) collective-permute-start(bf16[128,2048]{1,0:T(8,128)(2,1)S(1)} %get-tuple-element.8), channel_id=1, source_target_pairs={{0,1},{1,0},{2,3},{3,2},{4,5},{5,4},{6,7},{7,6},{8,9},{9,8},{10,11... | collective-permute-start | bytes 1572872 | tf_op jit(solution)/shard_map/ppermute | solution.py:177
  46.6 4.7 %fusion.2 = bf16[128,2048]{1,0:T(8,128)(2,1)S(1)} fusion(bf16[128,2048]{1,0:T(8,128)(2,1)S(1)} %get-tuple-element.7, bf16[2048,4096]{1,0:T(8,128)(2,1)} %refs_9_.1, s32[]{:T(128)S(6)} %select_n.53), kind=kOutput, calls=%fused_computation.2 | convolution fusion | flops 1074003968 | bytes 9437188 | tf_op jit(solution)/shard_map/dot_general | solution.py:180
  51.3 8.0 %collective-permute-done.8 = bf16[128,2048]{1,0:T(8,128)(2,1)S(1)} collective-permute-done((bf16[128,2048]{1,0:T(8,128)(2,1)S(1)}, bf16[128,2048]{1,0:T(8,128)(2,1)S(1)}, u32[]{:S(2)}, u32[]{:S(2)}) %collective-permute-start.8) | collective-permute-done | bytes 524320 | tf_op jit(solution)/shard_map/ppermute | solution.py:177
  59.3 0.9 %add_convert_fusion = bf16[128,2048]{1,0:T(8,128)(2,1)} fusion(bf16[128,2048]{1,0:T(8,128)(2,1)S(1)} %collective-permute-done.8, bf16[128,2048]{1,0:T(8,128)(2,1)S(1)} %fusion.2), kind=kLoop, calls=%fused_computation.3 | loop fusion | flops 1048576 | bytes 1572864 | tf_op jit(solution)/shard_map/convert_element_type | solution.py:182
  (14 shorter events, 0.2 us)
Async XLA Ops:
  1.0 16.7 %collective-permute-start = (bf16[2,128,512]{2,1,0:T(8,128)(2,1)S(1)}, bf16[2,128,512]{2,1,0:T(8,128)(2,1)S(1)}, u32[]{:S(2)}, u32[]{:S(2)}) collective-permute-start(bf16[2,128,512]{2,1,0:T(8,128)(2,1)S(1)} %pad_maximum_fusion.2.refs_0_), channel_id=1, source_target_pairs={{0,2},{2,4},{4,6},{6,8},{8,10},{10,12},{12,14},{14,16},{16,18},{18... | collective-permute-start | bytes 786440 | tf_op jit(solution)/shard_map/ppermute | solution.py:19
  2.9 17.6 %collective-permute-start.1 = (bf16[2,128,512]{2,1,0:T(8,128)(2,1)S(1)}, bf16[2,128,512]{2,1,0:T(8,128)(2,1)S(1)}, u32[]{:S(2)}, u32[]{:S(2)}) collective-permute-start(bf16[2,128,512]{2,1,0:T(8,128)(2,1)S(1)} %pad_maximum_fusion.2.refs_0_), channel_id=1, source_target_pairs={{0,6},{2,8},{4,10},{6,12},{8,14},{10,16},{12,18},{14,20},{16,22},{... | collective-permute-start | bytes 786440 | tf_op jit(solution)/shard_map/ppermute | solution.py:19
  5.1 23.0 %collective-permute-start.2 = (bf16[2,128,512]{2,1,0:T(8,128)(2,1)S(1)}, bf16[2,128,512]{2,1,0:T(8,128)(2,1)S(1)}, u32[]{:S(2)}, u32[]{:S(2)}) collective-permute-start(bf16[2,128,512]{2,1,0:T(8,128)(2,1)S(1)} %pad_maximum_fusion.2.refs_0_), channel_id=1, source_target_pairs={{0,10},{2,12},{4,14},{6,16},{8,18},{10,20},{12,22},{14,24},{16,26}... | collective-permute-start | bytes 786440 | tf_op jit(solution)/shard_map/ppermute | solution.py:19
  6.4 21.7 %collective-permute-start.3 = (bf16[2,128,512]{2,1,0:T(8,128)(2,1)S(1)}, bf16[2,128,512]{2,1,0:T(8,128)(2,1)S(1)}, u32[]{:S(2)}, u32[]{:S(2)}) collective-permute-start(bf16[2,128,512]{2,1,0:T(8,128)(2,1)S(1)} %pad_maximum_fusion.2.refs_0_), channel_id=1, source_target_pairs={{0,14},{2,16},{4,18},{6,20},{8,22},{10,24},{12,26},{14,28},{16,30}... | collective-permute-start | bytes 786440 | tf_op jit(solution)/shard_map/ppermute | solution.py:19
  17.7 17.2 %collective-permute-start.4 = (bf16[2,128,512]{2,1,0:T(8,128)(2,1)S(1)}, bf16[2,128,512]{2,1,0:T(8,128)(2,1)S(1)}, u32[]{:S(2)}, u32[]{:S(2)}) collective-permute-start(bf16[2,128,512]{2,1,0:T(8,128)(2,1)S(1)} %collective-permute-done.refs_1_), channel_id=1, source_target_pairs={{0,2},{4,6},{8,10},{12,14},{16,18},{20,22},{24,26},{28,30},{1,3},{... | collective-permute-start | bytes 786440 | tf_op jit(solution)/shard_map/ppermute | solution.py:25
  20.5 14.4 %collective-permute-start.5 = (bf16[2,128,512]{2,1,0:T(8,128)(2,1)S(1)}, bf16[2,128,512]{2,1,0:T(8,128)(2,1)S(1)}, u32[]{:S(2)}, u32[]{:S(2)}) collective-permute-start(bf16[2,128,512]{2,1,0:T(8,128)(2,1)S(1)} %collective-permute-done.1.refs_2_), channel_id=1, source_target_pairs={{0,2},{4,6},{8,10},{12,14},{16,18},{20,22},{24,26},{28,30},{2,0},{... | collective-permute-start | bytes 786440 | tf_op jit(solution)/shard_map/ppermute | solution.py:25
  28.2 6.8 %collective-permute-start.6 = (bf16[2,128,512]{2,1,0:T(8,128)(2,1)S(1)}, bf16[2,128,512]{2,1,0:T(8,128)(2,1)S(1)}, u32[]{:S(2)}, u32[]{:S(2)}) collective-permute-start(bf16[2,128,512]{2,1,0:T(8,128)(2,1)S(1)} %collective-permute-done.2.refs_3_), channel_id=1, source_target_pairs={{0,2},{4,6},{8,10},{12,14},{16,18},{20,22},{24,26},{28,30},{2,0},{... | collective-permute-start | bytes 786440 | tf_op jit(solution)/shard_map/ppermute | solution.py:25
  28.2 7.6 %collective-permute-start.7 = (bf16[2,128,512]{2,1,0:T(8,128)(2,1)S(1)}, bf16[2,128,512]{2,1,0:T(8,128)(2,1)S(1)}, u32[]{:S(2)}, u32[]{:S(2)}) collective-permute-start(bf16[2,128,512]{2,1,0:T(8,128)(2,1)S(1)} %collective-permute-done.3.refs_4_), channel_id=1, source_target_pairs={{0,2},{4,6},{8,10},{12,14},{16,18},{20,22},{24,26},{28,30},{2,0},{... | collective-permute-start | bytes 786440 | tf_op jit(solution)/shard_map/ppermute | solution.py:25
  35.7 1.0 %copy-start = (bf16[128,2048]{1,0:T(8,128)(2,1)S(1)}, bf16[128,2048]{1,0:T(8,128)(2,1)}, u32[]{:S(2)}) copy-start(bf16[128,2048]{1,0:T(8,128)(2,1)} %query_ref.1) | copy-start | bytes 1572868
  45.0 14.3 %collective-permute-start.8 = (bf16[128,2048]{1,0:T(8,128)(2,1)S(1)}, bf16[128,2048]{1,0:T(8,128)(2,1)S(1)}, u32[]{:S(2)}, u32[]{:S(2)}) collective-permute-start(bf16[128,2048]{1,0:T(8,128)(2,1)S(1)} %get-tuple-element.8), channel_id=1, source_target_pairs={{0,1},{1,0},{2,3},{3,2},{4,5},{5,4},{6,7},{7,6},{8,9},{9,8},{10,11... | collective-permute-start | bytes 1572872 | tf_op jit(solution)/shard_map/ppermute | solution.py:177

commit v20 on v19

--- a/solution.py
+++ b/solution.py
@@ -77,11 +77,12 @@
                 totals = jnp.sum(weights, axis=1, keepdims=True)
                 summed = jnp.dot(weights.astype(jnp.bfloat16), values, preferred_element_type=jnp.float32)
                 out_ref[:, columns] = (summed / totals).astype(out_ref.dtype)
-            if project and (h % 2 == 1 or h == heads_kv - 1):
-                done = range(h - h % 2, h + 1)
-                for k in done:
-                    copies[k].wait()
-                for k in done:
+            landing = max(heads_kv - 2, 0)
+            if project and h >= landing:
+                if h == landing:
+                    for copy in copies:
+                        copy.wait()
+                for k in (range(h + 1) if h == landing else [h]):
                     rows = slice(k * group, (k + 1) * group)
                     term = jnp.dot(out_ref[:, rows], weight_ref[rows, :], preferred_element_type=jnp.float32)
                     total = term if total is None else total + term

time: 60.6 us -> 60.6 us (level)
  no operation moved by 1% of the time
where the time goes in v20:
time: 60.6 us; the launch traced here: 60.2 us
  starting transfers between devices  17.6 us (29%)
  waiting for transfers between devices  16.3 us (27%)
  other arithmetic  9.63 us (16%)
  Pallas kernels  8.24 us (14%)
  matrix products  4.67 us (8%)
  between operations  2.77 us (5%)
  local copies, waits for them, and re-layouts  1.04 us (2%)
    ppermute x4, starting transfers between devices, gather_window(): passed.append(lax.ppermute(block, 'ctx', pairs))  9.25 us
    pallas_call x1, Pallas kernels, attend(): pl.pallas_call(functools.partial(attention_kernel, n_slots, uses, heads_k...  8.24 us
    ppermute x1, waiting for transfers between devices, on_device(): got = lax.ppermute(peer_terms, 'tp', [(0, 1), (1, 0)])  7.99 us
    ppermute x4, waiting for transfers between devices, gather_window(): received.append(lax.ppermute(kv, 'ctx', [(j, j + s) for j in range(n - s)]))  7.56 us
    ppermute x4, starting transfers between devices, gather_window(): received.append(lax.ppermute(kv, 'ctx', [(j, j + s) for j in range(n - s)]))  6.72 us
    dot_general x1, matrix products, on_device(): jnp.dot(attended, own_weight, preferred_element_type=jnp.float32)  4.67 us
    neg x2, other arithmetic, tables(): -sine  2.44 us
    ppermute x1, starting transfers between devices, on_device(): got = lax.ppermute(peer_terms, 'tp', [(0, 1), (1, 0)])  1.6 us
  transfers between devices with their start and end apart: 9, of which 3 were waited for; matrix products, arithmetic and copies ran while one was open for 21% of the time, Pallas kernels for 0%

profile of v20, /device:TPU:24, one launch (start us, length us, event | category | flops | bytes accessed | tf_op | source)
XLA Modules:
  0.0 60.2 jit_solution(9712747311011095462)
XLA Ops:
  0.0 1.0 %pad_maximum_fusion.2.refs_0_ = bf16[2,128,512]{2,1,0:T(8,128)(2,1)S(1)} fusion(bf16[1,128,512]{2,1,0:T(8,128)(2,1)} %bitcast.12, bf16[1,128,512]{2,1,0:T(8,128)(2,1)} %bitcast.13), kind=kLoop, calls=%fused_computation.8 | loop fusion | flops 131072 | bytes 524288 | tf_op jit(solution)/shard_map/stack | solution.py:152
  1.0 1.9 %collective-permute-start = (bf16[2,128,512]{2,1,0:T(8,128)(2,1)S(1)}, bf16[2,128,512]{2,1,0:T(8,128)(2,1)S(1)}, u32[]{:S(2)}, u32[]{:S(2)}) collective-permute-start(bf16[2,128,512]{2,1,0:T(8,128)(2,1)S(1)} %pad_maximum_fusion.2.refs_0_), channel_id=1, source_target_pairs={{0,2},{2,4},{4,6},{6,8},{8,10},{10,12},{12,14},{14,16},{16,18},{18... | collective-permute-start | bytes 786440 | tf_op jit(solution)/shard_map/ppermute | solution.py:19
  2.9 2.2 %collective-permute-start.1 = (bf16[2,128,512]{2,1,0:T(8,128)(2,1)S(1)}, bf16[2,128,512]{2,1,0:T(8,128)(2,1)S(1)}, u32[]{:S(2)}, u32[]{:S(2)}) collective-permute-start(bf16[2,128,512]{2,1,0:T(8,128)(2,1)S(1)} %pad_maximum_fusion.2.refs_0_), channel_id=1, source_target_pairs={{0,6},{2,8},{4,10},{6,12},{8,14},{10,16},{12,18},{14,20},{16,22},{... | collective-permute-start | bytes 786440 | tf_op jit(solution)/shard_map/ppermute | solution.py:19
  5.1 1.3 %collective-permute-start.2 = (bf16[2,128,512]{2,1,0:T(8,128)(2,1)S(1)}, bf16[2,128,512]{2,1,0:T(8,128)(2,1)S(1)}, u32[]{:S(2)}, u32[]{:S(2)}) collective-permute-start(bf16[2,128,512]{2,1,0:T(8,128)(2,1)S(1)} %pad_maximum_fusion.2.refs_0_), channel_id=1, source_target_pairs={{0,10},{2,12},{4,14},{6,16},{8,18},{10,20},{12,22},{14,24},{16,26}... | collective-permute-start | bytes 786440 | tf_op jit(solution)/shard_map/ppermute | solution.py:19
  6.4 1.3 %collective-permute-start.3 = (bf16[2,128,512]{2,1,0:T(8,128)(2,1)S(1)}, bf16[2,128,512]{2,1,0:T(8,128)(2,1)S(1)}, u32[]{:S(2)}, u32[]{:S(2)}) collective-permute-start(bf16[2,128,512]{2,1,0:T(8,128)(2,1)S(1)} %pad_maximum_fusion.2.refs_0_), channel_id=1, source_target_pairs={{0,14},{2,16},{4,18},{6,20},{8,22},{10,24},{12,26},{14,28},{16,30}... | collective-permute-start | bytes 786440 | tf_op jit(solution)/shard_map/ppermute | solution.py:19
  7.8 0.8 %select_reduce_fusion = s32[8]{0:T(128)S(1)} fusion(s32[8]{0:T(128)} %param.12), kind=kLoop, calls=%fused_computation.20 | loop fusion | flops 184 | bytes 64 | tf_op jit(solution)/shard_map/reduce_sum | solution.py:155
  8.6 0.6 %fusion.11 = s32[]{:T(128)} fusion(s32[8]{0:T(128)S(1)} %select_reduce_fusion, s32[]{:T(128)S(6)} %axis_index.33), kind=kLoop, calls=%fused_computation.27 | loop fusion | flops 23 | bytes 40 | tf_op jit(solution)/shard_map/reduce_sum | solution.py:158
  9.8 0.6 %select_reduce_fusion.3 = s32[]{:T(128)} fusion(s32[8]{0:T(128)S(1)} %select_reduce_fusion, s32[]{:T(128)S(6)} %sub.25), kind=kLoop, calls=%fused_computation.32 | loop fusion | flops 23 | bytes 40 | tf_op jit(solution)/shard_map/reduce_sum | solution.py:160
  11.1 1.3 %fusion.10 = s32[9]{0:T(128)S(1)} fusion(s32[9]{0:T(128)} %constant.46.clone, s32[9]{0:T(128)} %constant.47.clone, pred[]{:T(512)S(6)} %eq.14, s32[]{:T(128)} %select_reduce_fusion.3, s32[]{:T(128)S(6)} %axis_index.33), kind=kLoop, calls=%fused_computation.26 | loop fusion | flops 36 | bytes 117 | tf_op jit(solution)/shard_map/mul | solution.py:166
  12.5 1.3 %select_reduce_fusion.1 = (s32[]{:T(128)}, s32[]{:T(128)}) fusion(s32[8]{0:T(128)} %param.13, s32[]{:T(128)S(6)} %sub.25, s32[8]{0:T(128)} %param.12), kind=kLoop, calls=%fused_computation.30 | loop fusion | flops 38 | bytes 76 | tf_op jit(solution)/shard_map/reduce_sum | solution.py:162
  14.5 2.1 %fusion.5 = (f32[1152,64]{1,0:T(8,128)S(1)}, f32[1152,64]{1,0:T(8,128)S(1)}, f32[1152,64]{1,0:T(8,128)S(1)}) fusion(f32[64]{0:T(128)S(1)} %multiply_power_fusion, f32[1152]{0:T(1024)S(1)} %get-tuple-element.15), kind=kLoop, calls=%fused_computation.9 | loop fusion | flops 147456 | bytes 889600 | tf_op jit(solution)/shard_map/neg | solution.py:101
  17.3 0.3 fusion.6
  17.6 0.1 pad_maximum_fusion.3
  17.7 2.8 %collective-permute-start.4 = (bf16[2,128,512]{2,1,0:T(8,128)(2,1)S(1)}, bf16[2,128,512]{2,1,0:T(8,128)(2,1)S(1)}, u32[]{:S(2)}, u32[]{:S(2)}) collective-permute-start(bf16[2,128,512]{2,1,0:T(8,128)(2,1)S(1)} %collective-permute-done.refs_1_), channel_id=1, source_target_pairs={{0,2},{4,6},{8,10},{12,14},{16,18},{20,22},{24,26},{28,30},{1,3},{... | collective-permute-start | bytes 786440 | tf_op jit(solution)/shard_map/ppermute | solution.py:25
  20.6 7.5 %collective-permute-done.2.refs_3_ = bf16[2,128,512]{2,1,0:T(8,128)(2,1)S(1)} collective-permute-done((bf16[2,128,512]{2,1,0:T(8,128)(2,1)S(1)}, bf16[2,128,512]{2,1,0:T(8,128)(2,1)S(1)}, u32[]{:S(2)}, u32[]{:S(2)}) %collective-permute-start.2) | collective-permute-done | bytes 262176 | tf_op jit(solution)/shard_map/ppermute | solution.py:19
  28.2 6.4 %collective-permute-start.7 = (bf16[2,128,512]{2,1,0:T(8,128)(2,1)S(1)}, bf16[2,128,512]{2,1,0:T(8,128)(2,1)S(1)}, u32[]{:S(2)}, u32[]{:S(2)}) collective-permute-start(bf16[2,128,512]{2,1,0:T(8,128)(2,1)S(1)} %collective-permute-done.3.refs_4_), channel_id=1, source_target_pairs={{0,2},{4,6},{8,10},{12,14},{16,18},{20,22},{24,26},{28,30},{2,0},{... | collective-permute-start | bytes 786440 | tf_op jit(solution)/shard_map/ppermute | solution.py:25
  34.6 0.4 pad_maximum_fusion
  35.0 0.8 %collective-permute-done.7.refs_8_ = bf16[2,128,512]{2,1,0:T(8,128)(2,1)S(1)} collective-permute-done((bf16[2,128,512]{2,1,0:T(8,128)(2,1)S(1)}, bf16[2,128,512]{2,1,0:T(8,128)(2,1)S(1)}, u32[]{:S(2)}, u32[]{:S(2)}) %collective-permute-start.7) | collective-permute-done | bytes 262176 | tf_op jit(solution)/shard_map/ppermute | solution.py:25
  35.7 1.0 %copy-done = bf16[128,2048]{1,0:T(8,128)(2,1)S(1)} copy-done((bf16[128,2048]{1,0:T(8,128)(2,1)S(1)}, bf16[128,2048]{1,0:T(8,128)(2,1)}, u32[]{:S(2)}) %copy-start) | copy-done | bytes 524312
  36.8 8.2 %shard_map.82 = (bf16[128,2048]{1,0:T(8,128)(2,1)S(1)}, bf16[128,2048]{1,0:T(8,128)(2,1)S(1)}) custom-call(s32[1]{0:T(128)} %bitcast.peer_ref, s32[1]{0:T(128)} %bitcast.1.core_ref, s32[128,1]{1,0:T(8,128)S(1)} %iota_add_fusion.query_pos_ref, s32[1,1152]{1,0:T(1,128)S(1)} %and_select_fusion.key_limit_ref, f32[128,128]{1,0:T(8,128)S(1)} %get-tuple-element.19.query_cos_ref, ...), custom_call_target="tpu_custom_call" | custom-call | flops 2281701376 | bytes 12320768 | tf_op jit(solution)/shard_map/pallas_call | solution.py:131
  45.0 1.6 %collective-permute-start.8 = (bf16[128,2048]{1,0:T(8,128)(2,1)S(1)}, bf16[128,2048]{1,0:T(8,128)(2,1)S(1)}, u32[]{:S(2)}, u32[]{:S(2)}) collective-permute-start(bf16[128,2048]{1,0:T(8,128)(2,1)S(1)} %get-tuple-element.8), channel_id=1, source_target_pairs={{0,1},{1,0},{2,3},{3,2},{4,5},{5,4},{6,7},{7,6},{8,9},{9,8},{10,11... | collective-permute-start | bytes 1572872 | tf_op jit(solution)/shard_map/ppermute | solution.py:178
  46.6 4.7 %fusion.2 = bf16[128,2048]{1,0:T(8,128)(2,1)S(1)} fusion(bf16[128,2048]{1,0:T(8,128)(2,1)S(1)} %get-tuple-element.7, bf16[2048,4096]{1,0:T(8,128)(2,1)} %refs_9_.1, s32[]{:T(128)S(6)} %select_n.53), kind=kOutput, calls=%fused_computation.2 | convolution fusion | flops 1074003968 | bytes 9437188 | tf_op jit(solution)/shard_map/dot_general | solution.py:181
  51.3 8.0 %collective-permute-done.8 = bf16[128,2048]{1,0:T(8,128)(2,1)S(1)} collective-permute-done((bf16[128,2048]{1,0:T(8,128)(2,1)S(1)}, bf16[128,2048]{1,0:T(8,128)(2,1)S(1)}, u32[]{:S(2)}, u32[]{:S(2)}) %collective-permute-start.8) | collective-permute-done | bytes 524320 | tf_op jit(solution)/shard_map/ppermute | solution.py:178
  59.3 0.9 %add_convert_fusion = bf16[128,2048]{1,0:T(8,128)(2,1)} fusion(bf16[128,2048]{1,0:T(8,128)(2,1)S(1)} %collective-permute-done.8, bf16[128,2048]{1,0:T(8,128)(2,1)S(1)} %fusion.2), kind=kLoop, calls=%fused_computation.3 | loop fusion | flops 1048576 | bytes 1572864 | tf_op jit(solution)/shard_map/convert_element_type | solution.py:183
  (14 shorter events, 0.2 us)
Async XLA Ops:
  1.0 16.7 %collective-permute-start = (bf16[2,128,512]{2,1,0:T(8,128)(2,1)S(1)}, bf16[2,128,512]{2,1,0:T(8,128)(2,1)S(1)}, u32[]{:S(2)}, u32[]{:S(2)}) collective-permute-start(bf16[2,128,512]{2,1,0:T(8,128)(2,1)S(1)} %pad_maximum_fusion.2.refs_0_), channel_id=1, source_target_pairs={{0,2},{2,4},{4,6},{6,8},{8,10},{10,12},{12,14},{14,16},{16,18},{18... | collective-permute-start | bytes 786440 | tf_op jit(solution)/shard_map/ppermute | solution.py:19
  2.9 17.6 %collective-permute-start.1 = (bf16[2,128,512]{2,1,0:T(8,128)(2,1)S(1)}, bf16[2,128,512]{2,1,0:T(8,128)(2,1)S(1)}, u32[]{:S(2)}, u32[]{:S(2)}) collective-permute-start(bf16[2,128,512]{2,1,0:T(8,128)(2,1)S(1)} %pad_maximum_fusion.2.refs_0_), channel_id=1, source_target_pairs={{0,6},{2,8},{4,10},{6,12},{8,14},{10,16},{12,18},{14,20},{16,22},{... | collective-permute-start | bytes 786440 | tf_op jit(solution)/shard_map/ppermute | solution.py:19
  5.1 23.0 %collective-permute-start.2 = (bf16[2,128,512]{2,1,0:T(8,128)(2,1)S(1)}, bf16[2,128,512]{2,1,0:T(8,128)(2,1)S(1)}, u32[]{:S(2)}, u32[]{:S(2)}) collective-permute-start(bf16[2,128,512]{2,1,0:T(8,128)(2,1)S(1)} %pad_maximum_fusion.2.refs_0_), channel_id=1, source_target_pairs={{0,10},{2,12},{4,14},{6,16},{8,18},{10,20},{12,22},{14,24},{16,26}... | collective-permute-start | bytes 786440 | tf_op jit(solution)/shard_map/ppermute | solution.py:19
  6.4 21.7 %collective-permute-start.3 = (bf16[2,128,512]{2,1,0:T(8,128)(2,1)S(1)}, bf16[2,128,512]{2,1,0:T(8,128)(2,1)S(1)}, u32[]{:S(2)}, u32[]{:S(2)}) collective-permute-start(bf16[2,128,512]{2,1,0:T(8,128)(2,1)S(1)} %pad_maximum_fusion.2.refs_0_), channel_id=1, source_target_pairs={{0,14},{2,16},{4,18},{6,20},{8,22},{10,24},{12,26},{14,28},{16,30}... | collective-permute-start | bytes 786440 | tf_op jit(solution)/shard_map/ppermute | solution.py:19
  17.7 17.2 %collective-permute-start.4 = (bf16[2,128,512]{2,1,0:T(8,128)(2,1)S(1)}, bf16[2,128,512]{2,1,0:T(8,128)(2,1)S(1)}, u32[]{:S(2)}, u32[]{:S(2)}) collective-permute-start(bf16[2,128,512]{2,1,0:T(8,128)(2,1)S(1)} %collective-permute-done.refs_1_), channel_id=1, source_target_pairs={{0,2},{4,6},{8,10},{12,14},{16,18},{20,22},{24,26},{28,30},{1,3},{... | collective-permute-start | bytes 786440 | tf_op jit(solution)/shard_map/ppermute | solution.py:25
  20.5 14.4 %collective-permute-start.5 = (bf16[2,128,512]{2,1,0:T(8,128)(2,1)S(1)}, bf16[2,128,512]{2,1,0:T(8,128)(2,1)S(1)}, u32[]{:S(2)}, u32[]{:S(2)}) collective-permute-start(bf16[2,128,512]{2,1,0:T(8,128)(2,1)S(1)} %collective-permute-done.1.refs_2_), channel_id=1, source_target_pairs={{0,2},{4,6},{8,10},{12,14},{16,18},{20,22},{24,26},{28,30},{2,0},{... | collective-permute-start | bytes 786440 | tf_op jit(solution)/shard_map/ppermute | solution.py:25
  28.2 6.8 %collective-permute-start.6 = (bf16[2,128,512]{2,1,0:T(8,128)(2,1)S(1)}, bf16[2,128,512]{2,1,0:T(8,128)(2,1)S(1)}, u32[]{:S(2)}, u32[]{:S(2)}) collective-permute-start(bf16[2,128,512]{2,1,0:T(8,128)(2,1)S(1)} %collective-permute-done.2.refs_3_), channel_id=1, source_target_pairs={{0,2},{4,6},{8,10},{12,14},{16,18},{20,22},{24,26},{28,30},{2,0},{... | collective-permute-start | bytes 786440 | tf_op jit(solution)/shard_map/ppermute | solution.py:25
  28.2 7.6 %collective-permute-start.7 = (bf16[2,128,512]{2,1,0:T(8,128)(2,1)S(1)}, bf16[2,128,512]{2,1,0:T(8,128)(2,1)S(1)}, u32[]{:S(2)}, u32[]{:S(2)}) collective-permute-start(bf16[2,128,512]{2,1,0:T(8,128)(2,1)S(1)} %collective-permute-done.3.refs_4_), channel_id=1, source_target_pairs={{0,2},{4,6},{8,10},{12,14},{16,18},{20,22},{24,26},{28,30},{2,0},{... | collective-permute-start | bytes 786440 | tf_op jit(solution)/shard_map/ppermute | solution.py:25
  35.7 1.0 %copy-start = (bf16[128,2048]{1,0:T(8,128)(2,1)S(1)}, bf16[128,2048]{1,0:T(8,128)(2,1)}, u32[]{:S(2)}) copy-start(bf16[128,2048]{1,0:T(8,128)(2,1)} %query_ref.1) | copy-start | bytes 1572868
  45.0 14.3 %collective-permute-start.8 = (bf16[128,2048]{1,0:T(8,128)(2,1)S(1)}, bf16[128,2048]{1,0:T(8,128)(2,1)S(1)}, u32[]{:S(2)}, u32[]{:S(2)}) collective-permute-start(bf16[128,2048]{1,0:T(8,128)(2,1)S(1)} %get-tuple-element.8), channel_id=1, source_target_pairs={{0,1},{1,0},{2,3},{3,2},{4,5},{5,4},{6,7},{7,6},{8,9},{9,8},{10,11... | collective-permute-start | bytes 1572872 | tf_op jit(solution)/shard_map/ppermute | solution.py:178
